TPU v7x, 32 devices: a whole 2x2x4 slice. The times are simulated.
32 devices in a mesh: blk: 8 (over y, x, core), slab: 4 (over z).
Axes of the slice: x: 2, y: 2, z: 4, core: 2. Of those that a mesh axis runs over, the one named last changes fastest.
Arguments:
- queries: bfloat16 [4096, 4096], P(('blk', 'slab')), may hold values from -8 to 8
- passages: bfloat16 [2816, 4096], P(('blk', 'slab')), may hold values from -6 to 6
- positive: int32 [4096], P(('blk', 'slab')), may hold values from 0 to 703
- hard_ids: int32 [4096, 8], P(('blk', 'slab')), may hold values from 0 to 2815, as said below
Outputs:
- query_loss: float32 [4096], P(('blk', 'slab'))
- query_grad: float32 [4096, 4096], P(('blk', 'slab'))
- passage_grad: float32 [2816, 4096], P(('blk', 'slab'))
Inputs may be any that keep to these rules, and one draw needn't show every extreme that they name: `hard_ids`: passage row f * 88 + t lies on the device of flat index f = b * 4 + s. Of the hard-negative ids of the 128 queries of one device, at most 36 name rows that lie on any one device, and in every draw some device has exactly 36 ids on some one device.
All inputs are finite; a program needn't handle non-finite values.
Results may differ from a plain program's by a relative error of at most 0.008.
Values may be sent and summed in bfloat16 or wider, within the bound.
No kernel may reach another device: no remote copies, remote signals or barrier semaphores. Data moves between devices by JAX's collectives and lax.ppermute only.
A program may use at most 192 MiB of HBM per device.

v0:
```python
import math

import jax
import jax.numpy as jnp
from jax import lax
from jax.sharding import PartitionSpec as P


def per_device(queries, passages, positive, hard_ids):
    block_list = lax.axis_size("blk")
    devices = block_list * lax.axis_size("slab")
    query_rows_dev, model_width = queries.shape
    passage_rows_dev = passages.shape[0]
    hard_count = hard_ids.shape[1]
    pool_size = block_list * passage_rows_dev
    logit_scale = 3.0 / math.sqrt(model_width)
    contract_rows = (((1,), (1,)), ((), ()))
    pooled = (
        lax.dot_general(
            queries,
            lax.all_gather(passages, "blk", axis=0, tiled=True),
            contract_rows,
            preferred_element_type=jnp.float32,
        )
        * logit_scale
    )
    entries = query_rows_dev * hard_count
    slot_count = max(2, 9 * entries // (8 * devices))
    flat_ids = hard_ids.reshape(entries)
    owner_dev = flat_ids // passage_rows_dev
    member = (owner_dev[:, None] == jnp.arange(devices, dtype=jnp.int32)[None, :]).astype(jnp.int32)
    before = jnp.sum((jnp.cumsum(member, axis=0) - member) * member, axis=1)
    slot_of = owner_dev * slot_count + before
    wanted = (
        jnp.full((devices * slot_count,), -1, jnp.int32)
        .at[slot_of]
        .set(flat_ids % passage_rows_dev)
    )
    wanted = wanted.reshape(devices, slot_count)
    asked_rows = lax.all_to_all(wanted, ("blk", "slab"), split_axis=0, concat_axis=0, tiled=True)
    served = jnp.where(
        (asked_rows >= 0)[:, :, None],
        passages[jnp.maximum(asked_rows, 0)],
        jnp.zeros((), jnp.bfloat16),
    )
    arrived = lax.all_to_all(served, ("blk", "slab"), split_axis=0, concat_axis=0, tiled=True)
    hard_rows = arrived.reshape(devices * slot_count, model_width)[slot_of].reshape(
        query_rows_dev, hard_count, model_width
    )
    hard_logits = (
        jnp.einsum("qd,qkd->qk", queries, hard_rows, preferred_element_type=jnp.float32)
        * logit_scale
    )
    row_top = jnp.maximum(jnp.max(pooled, axis=1), jnp.max(hard_logits, axis=1))
    row_total = jnp.sum(jnp.exp(pooled - row_top[:, None]), axis=1) + jnp.sum(
        jnp.exp(hard_logits - row_top[:, None]), axis=1
    )
    row_lse = row_top + jnp.log(row_total)
    onehot = (jnp.arange(pool_size, dtype=jnp.int32)[None, :] == positive[:, None]).astype(
        jnp.float32
    )
    query_loss = row_lse - jnp.sum(onehot * pooled, axis=1)
    coef_pool = (jnp.exp(pooled - row_lse[:, None]) - onehot).astype(jnp.bfloat16)
    coef_hard = jnp.exp(hard_logits - row_lse[:, None]).astype(jnp.bfloat16)
    grad_hard = jnp.einsum("qk,qkd->qd", coef_hard, hard_rows, preferred_element_type=jnp.float32)
    coef_part = coef_pool
    grad_pool = jnp.dot(
        coef_part,
        lax.all_gather(passages, "blk", axis=0, tiled=True),
        preferred_element_type=jnp.float32,
    )
    query_grad = grad_pool + grad_hard
    hard_terms = (coef_hard[:, :, None] * queries[:, None, :]).reshape(entries, model_width)
    outgoing = (
        jnp.zeros((devices * slot_count, model_width), jnp.bfloat16).at[slot_of].set(hard_terms)
    )
    returned = lax.all_to_all(
        outgoing.reshape(devices, slot_count, model_width),
        ("blk", "slab"),
        split_axis=0,
        concat_axis=0,
        tiled=True,
    )
    matching = (
        jnp.arange(passage_rows_dev, dtype=jnp.int32)[:, None]
        == asked_rows.reshape(1, devices * slot_count)
    ).astype(jnp.bfloat16)
    hard_sum = jnp.dot(
        matching,
        returned.reshape(devices * slot_count, model_width),
        preferred_element_type=jnp.float32,
    )
    coef_part = coef_pool
    pool_sum = lax.psum_scatter(
        lax.dot_general(
            coef_part, queries, (((0,), (0,)), ((), ())), preferred_element_type=jnp.float32
        ).astype(jnp.bfloat16),
        "blk",
        scatter_dimension=0,
        tiled=True,
    ).astype(jnp.float32)
    passage_grad = pool_sum + hard_sum
    return (query_loss, query_grad, passage_grad)


def solution(mesh):
    return jax.shard_map(
        per_device,
        mesh=mesh,
        in_specs=(
            P(("blk", "slab"), None),
            P(("blk", "slab"), None),
            P(("blk", "slab")),
            P(("blk", "slab"), None),
        ),
        out_specs=(P(("blk", "slab")), P(("blk", "slab"), None), P(("blk", "slab"), None)),
        check_vma=False,
    )
```

profile of v0, /device:TPU:0, one launch (start us, length us, event | category | flops | bytes accessed | tf_op | source)
XLA Modules:
  0.0 633.4 jit_solution(17178039438803658981)
XLA Ops:
  7.2 0.0 copy-start
  7.2 0.8 compare_and_fusion
  7.9 0.7 broadcast_remainder_fusion
  8.6 0.1 copy.25
  8.8 0.1 and.30
  8.9 0.1 and.28
  9.0 0.1 copy.26
  9.1 0.1 div.29
  9.2 0.1 div.28
  9.3 0.1 div.27
  9.4 0.1 copy.27
  9.5 0.1 ne.61
  9.6 0.1 copy.28
  9.7 0.1 rem.32
  9.8 9.0 %reduce-window.6 = s32[32,8,128]{2,1,0:T(8,128)S(1)} reduce-window(s32[32,8,128]{2,1,0:T(8,128)S(1)} %fusion.13, s32[]{:T(128)} %constant.40.clone.1), window={size=1x1x128 pad=0_0x0_0x127_0}, to_apply=%region_1.2 | reduce-window | flops 4161536 | bytes 262148 | tf_op jit(solution)/shard_map/reduce-window
  18.8 0.1 slice.12
  18.9 0.1 copy.32
  19.1 0.1 copy.33
  19.2 0.1 broadcast_add_fusion
  19.4 4.3 scatter_custom_fusion
  23.7 0.1 all_to_all.12
  23.8 14.3 %all_to_all.19 = s32[32,1,36]{2,1,0:T(1,128)S(1)} all-to-all(s32[32,1,36]{2,1,0:T(1,128)S(1)} %all_to_all.12), channel_id=1, replica_groups=mesh['blk'=8,'slab'=4] {'blk','slab'}, dimensions={0} | all-to-all | bytes 9216 | tf_op jit(solution)/shard_map/all_to_all | solution.py:40
  38.1 0.1 reshape.190
  38.2 0.0 copy-done
  38.2 8.0 %gather_fusion = bf16[1152,4096]{1,0:T(8,128)(2,1)} fusion(bf16[88,4096]{1,0:T(8,128)(2,1)S(1)} %copy-done, s32[2048]{0:T(1024)S(1)} %pad_clamp_fusion), kind=kCustom, calls=%fused_computation | custom fusion | bytes 18878976 | tf_op jit(solution)/shard_map/gather | solution.py:43
  46.3 13.1 %reshape.189 = bf16[32,36,4096]{2,1,0:T(8,128)(2,1)} reshape(bf16[1152,4096]{1,0:T(8,128)(2,1)} %gather_fusion) | data formatting | bytes 18874368 | tf_op jit(solution)/shard_map/gather | solution.py:43
  59.4 10.0 %broadcast_select_fusion = bf16[32,36,4096]{2,1,0:T(8,128)(2,1)} fusion(bf16[32,36,4096]{2,1,0:T(8,128)(2,1)} %reshape.189, pred[32,36]{1,0:T(8,128)(4,1)S(1)} %compare_bitcast_fusion), kind=kLoop, calls=%fused_computation.4 | loop fusion | flops 4718592 | bytes 18875520 | tf_op jit(solution)/shard_map/jit(_where)/select_n | solution.py:41
  69.4 0.0 copy-start.1
  69.4 3.8 all-to-all-start.1
  73.3 0.2 all-gather.2.cloned.1.call-start
  73.5 0.5 all-gather.2.cloned.1.call-update
  74.0 113.4 %all-gather.2.cloned.1.call-done = bf16[704,4096]{1,0:T(8,128)(2,1)} async-done(((bf16[88,4096]{1,0:T(8,128)(2,1)}), bf16[704,4096]{1,0:T(8,128)(2,1)}) %all-gather.2.cloned.1.call-update) | async-done | bytes 5767184 | tf_op jit(solution)/shard_map/all_gather | solution.py:21
  187.5 0.0 copy-done.1
  187.5 4.3 fusion.20
  191.8 103.5 %all-to-all-done.1 = bf16[32,36,4096]{2,1,0:T(8,128)(2,1)} async-done(((bf16[32,36,4096]{2,1,0:T(8,128)(2,1)}), bf16[32,36,4096]{2,1,0:T(8,128)(2,1)}, u32[]{:S(2)}, u32[]{:S(2)}) %all-to-all-start.1) | async-done | bytes 9437216 | tf_op jit(solution)/shard_map/all_to_all | solution.py:46
  295.3 13.2 %reshape.184 = bf16[1152,4096]{1,0:T(8,128)(2,1)} reshape(bf16[32,36,4096]{2,1,0:T(8,128)(2,1)} %all-to-all-done.1) | data formatting | bytes 18874368 | tf_op jit(solution)/shard_map/reshape | solution.py:47
  308.5 19.9 %gather_fusion.1 = bf16[1024,4096]{1,0:T(8,128)(2,1)} fusion(bf16[1152,4096]{1,0:T(8,128)(2,1)} %reshape.184, s32[1024]{0:T(1024)S(1)} %broadcast_clamp_fusion), kind=kCustom, calls=%fused_computation.1 | custom fusion | bytes 16781312 | tf_op jit(solution)/shard_map/gather | solution.py:47
  328.5 0.0 copy-start.2
  328.5 8.9 %fusion.3 = f32[128,1,8]{2,1,0:T(1,128)S(1)} fusion(bf16[1024,4096]{1,0:T(8,128)(2,1)} %gather_fusion.1, bf16[128,4096,1]{1,0,2:T(8,128)(2,1)S(1)} %bitcast.50), kind=kOutput, calls=%fused_computation.9 | convolution fusion | flops 8388608 | bytes 9441280 | tf_op jit(solution)/shard_map/qd,qkd->qk/dot_general | solution.py:51
  337.3 0.1 multiply_reduce_fusion
  337.5 0.2 exponential_reduce_fusion.1
  337.7 0.0 copy-done.2
  337.7 0.1 select_reduce_fusion
  337.8 0.5 fusion.19
  338.3 0.1 exponential_convert_fusion
  338.4 0.1 mul.57
  338.5 17.3 %scatter_custom_fusion.1 = bf16[1152,4096]{1,0:T(8,128)(2,1)} fusion(s32[1024]{0:T(1024)S(1)} %bitcast.62, bf16[]{:T(256)} %constant.43.clone.1, bf16[128,4096]{1,0:T(8,128)(2,1)S(1)} %copy-done.1, bf16[1024]{0:T(1024)(128)(2,1)S(1)} %mul.57), kind=kCustom, calls=%fused_computation.6 | custom fusion | flops 4194304 | bytes 10487810 | tf_op jit(solution)/shard_map/scatter | solution.py:75
  355.8 13.1 %reshape.186 = bf16[32,36,4096]{2,1,0:T(8,128)(2,1)} reshape(bf16[1152,4096]{1,0:T(8,128)(2,1)} %scatter_custom_fusion.1) | data formatting | bytes 18874368 | tf_op jit(solution)/shard_map/reshape | solution.py:78
  369.0 15.0 %all-to-all-start.2 = ((bf16[32,36,4096]{2,1,0:T(8,128)(2,1)}), bf16[32,36,4096]{2,1,0:T(8,128)(2,1)}, u32[]{:S(2)}, u32[]{:S(2)}) async-start(bf16[32,36,4096]{2,1,0:T(8,128)(2,1)} %reshape.186), calls=%async_computation.3 | async-start | bytes 20971520 | tf_op jit(solution)/shard_map/all_to_all | solution.py:77
  384.0 0.3 reduce-scatter.2.cloned.1.call-start
  384.3 4.1 convolution_convert_fusion
  388.4 0.0 reduce-scatter.2.cloned.1.call-update
  388.4 0.5 broadcast.164
  389.0 0.7 reduce.3
  389.7 0.1 eq.61
  389.8 0.1 fusion.26
  389.9 0.0 slice-start.1
  389.9 5.9 fusion.1
  395.7 0.0 slice-done
  395.7 0.0 slice-done.1
  395.8 3.4 convolution_add_fusion
  399.2 207.4 %all-to-all-done.2 = bf16[32,36,4096]{2,1,0:T(8,128)(2,1)} async-done(((bf16[32,36,4096]{2,1,0:T(8,128)(2,1)}), bf16[32,36,4096]{2,1,0:T(8,128)(2,1)}, u32[]{:S(2)}, u32[]{:S(2)}) %all-to-all-start.2) | async-done | bytes 9437216 | tf_op jit(solution)/shard_map/all_to_all | solution.py:77
  606.6 13.2 %reshape.187 = bf16[1152,4096]{1,0:T(8,128)(2,1)} reshape(bf16[32,36,4096]{2,1,0:T(8,128)(2,1)} %all-to-all-done.2) | data formatting | bytes 18874368 | tf_op jit(solution)/shard_map/reshape | solution.py:90
  619.8 6.8 %convolution_add_fusion.1 = f32[88,4096]{1,0:T(8,128)} fusion(bf16[1152,4096]{1,0:T(8,128)(2,1)} %reshape.187, bf16[88,4096]{1,0:T(8,128)(2,1)} %reduce-scatter.2.cloned.1.call-done, s32[1152]{0:T(1024)S(1)} %eq.61), kind=kOutput, calls=%fused_computation.13 | convolution fusion | flops 831294464 | bytes 11604480 | tf_op jit(solution)/shard_map/dot_general | solution.py:88
  (15 shorter events, 0.1 us)
Async XLA Ops:
  7.2 31.1 %copy-start = (bf16[88,4096]{1,0:T(8,128)(2,1)S(1)}, bf16[88,4096]{1,0:T(8,128)(2,1)}, u32[]{:S(2)}) copy-start(bf16[88,4096]{1,0:T(8,128)(2,1)} %param.5) | copy-start | bytes 2162692
  69.4 118.0 %copy-start.1 = (bf16[128,4096]{1,0:T(8,128)(2,1)S(1)}, bf16[128,4096]{1,0:T(8,128)(2,1)}, u32[]{:S(2)}) copy-start(bf16[128,4096]{1,0:T(8,128)(2,1)} %param.4) | copy-start | bytes 3145732
  69.4 225.9 %all-to-all-start.1 = ((bf16[32,36,4096]{2,1,0:T(8,128)(2,1)}), bf16[32,36,4096]{2,1,0:T(8,128)(2,1)}, u32[]{:S(2)}, u32[]{:S(2)}) async-start(bf16[32,36,4096]{2,1,0:T(8,128)(2,1)} %broadcast_select_fusion), calls=%async_computation.1 | async-start | bytes 20971520 | tf_op jit(solution)/shard_map/all_to_all | solution.py:46
  73.3 114.2 %all-gather.2.cloned.1.call-start = ((), (), s32[]{:S(2)}) async-start(), calls=%async_computation.4 | async-start | bytes 6488064 | tf_op jit(solution)/shard_map/all_gather | solution.py:21
  328.5 9.2 %copy-start.2 = (s32[128]{0:T(128)S(1)}, s32[128]{0:T(128)}, u32[]{:S(2)}) copy-start(s32[128]{0:T(128)} %param.6) | copy-start | bytes 1540
  369.0 237.6 %all-to-all-start.2 = ((bf16[32,36,4096]{2,1,0:T(8,128)(2,1)}), bf16[32,36,4096]{2,1,0:T(8,128)(2,1)}, u32[]{:S(2)}, u32[]{:S(2)}) async-start(bf16[32,36,4096]{2,1,0:T(8,128)(2,1)} %reshape.186), calls=%async_computation.3 | async-start | bytes 20971520 | tf_op jit(solution)/shard_map/all_to_all | solution.py:77
  384.0 235.8 %reduce-scatter.2.cloned.1.call-start = ((), (), s32[]{:S(2)}) async-start(), calls=%async_computation.5 | async-start | bytes 6488064 | tf_op jit(solution)/shard_map/reduce_scatter | solution.py:94
  388.4 7.3 %slice-start = ((s8[5767168]{0:T(1024)(128)(4,1)}), s8[1572864]{0:T(1024)(128)(4,1)S(1)}, s32[]{:S(2)}) async-start(s8[5767168]{0:T(1024)(128)(4,1)} %bitcast.48), calls=%async_computation.6 | async-start | bytes 3145728
  389.9 5.9 slice-start.1
Sparse Core Ops, SparseCore 0:
  76.0 111.4 all-gather.1
  388.6 139.4 reduce-scatter.1
where the time goes:
time: 644 us; the launch traced here: 633 us
  waiting for transfers between devices  425 us (66%)
  local copies, waits for them, and re-layouts  87.4 us (14%)
  other arithmetic  39.8 us (6%)
  matrix products  33.4 us (5%)
  starting transfers between devices  19.4 us (3%)
  blocking collectives  14.3 us (2%)
  between operations  14.3 us (2%)
    all_to_all x1, waiting for transfers between devices, per_device(): lax.all_to_all(outgoing.reshape(devices, slot_count, model_width), ('blk'...  207 us
    all_gather x1, waiting for transfers between devices, per_device(): lax.all_gather(passages, 'blk', axis=0, tiled=True)  113 us
    all_to_all x1, waiting for transfers between devices, per_device(): lax.all_to_all(served, ('blk', 'slab'), split_axis=0, concat_axis=0, tile...  104 us
    gather x2, local copies, waits for them, and re-layouts, per_device(): passages[jnp.maximum(asked_rows, 0)]  21.2 us
    gather x1, local copies, waits for them, and re-layouts, per_device(): arrived.reshape(devices * slot_count, model_width)[slot_of]  19.9 us
    scatter x1, other arithmetic, per_device(): jnp.zeros((devices * slot_count, model_width), jnp.bfloat16).at[slot_of]  17.3 us
    all_to_all x1, starting transfers between devices, per_device(): lax.all_to_all(outgoing.reshape(devices, slot_count, model_width), ('blk'...  15 us
    all_to_all x1, blocking collectives, per_device(): lax.all_to_all(wanted, ('blk', 'slab'), split_axis=0, concat_axis=0, tile...  14.3 us
  transfers between devices with their start and end apart: 4, of which 3 were waited for; matrix products, arithmetic and copies ran while one was open for 5% of the time, Pallas kernels for 0%

commit v1 on v0

v1 whole, which is shorter than its diff:
```python
import math

import jax
import jax.numpy as jnp
from jax import lax
from jax.sharding import PartitionSpec as P


def per_device(queries, passages, positive, hard_ids):
    slabs = lax.axis_size("slab")
    my_slab = lax.axis_index("slab")
    query_rows_dev, model_width = queries.shape
    passage_rows_dev = passages.shape[0]
    hard_count = hard_ids.shape[1]
    logit_scale = 3.0 / math.sqrt(model_width)
    contract_rows = (((1,), (1,)), ((), ()))
    contract_cols = (((0,), (0,)), ((), ()))

    pool = lax.all_gather(passages, "blk", axis=0, tiled=True)
    pool_size = pool.shape[0]
    column_queries = lax.all_gather(queries, "slab", axis=0, tiled=True)
    column_ids = lax.all_gather(hard_ids, "slab", axis=0, tiled=True)
    column_rows = column_queries.shape[0]

    scores = (
        lax.dot_general(column_queries, pool, contract_rows, preferred_element_type=jnp.float32)
        * logit_scale
    )
    own_start = my_slab * query_rows_dev
    pooled = lax.dynamic_slice_in_dim(scores, own_start, query_rows_dev, axis=0)

    owner_dev = column_ids // passage_rows_dev
    owner_slab = owner_dev % slabs
    hard_pos = (owner_dev // slabs) * passage_rows_dev + column_ids % passage_rows_dev
    mine = owner_slab == my_slab
    hard_mine = jnp.where(mine, jnp.take_along_axis(scores, hard_pos, axis=1), 0.0)

    pool_max = jnp.max(pooled, axis=1)
    pool_sum = jnp.sum(jnp.exp(pooled - pool_max[:, None]), axis=1)
    payload = jnp.concatenate([hard_mine.reshape(-1), pool_max, pool_sum])
    gathered = lax.all_gather(payload, "slab", axis=0)
    hard_split = column_rows * hard_count
    hard_all = jnp.take_along_axis(
        gathered[:, :hard_split].reshape(slabs, column_rows, hard_count),
        owner_slab[None],
        axis=0,
    )[0]
    stats = gathered[:, hard_split:].reshape(slabs, 2, query_rows_dev)
    max_all = stats[:, 0].reshape(column_rows)
    sum_all = stats[:, 1].reshape(column_rows)

    row_top = jnp.maximum(max_all, jnp.max(hard_all, axis=1))
    row_total = sum_all * jnp.exp(max_all - row_top) + jnp.sum(
        jnp.exp(hard_all - row_top[:, None]), axis=1
    )
    lse_all = row_top + jnp.log(row_total)
    row_lse = lax.dynamic_slice_in_dim(lse_all, own_start, query_rows_dev)

    onehot = (jnp.arange(pool_size, dtype=jnp.int32)[None, :] == positive[:, None]).astype(
        jnp.float32
    )
    query_loss = row_lse - jnp.sum(onehot * pooled, axis=1)
    coef_pool = (jnp.exp(pooled - row_lse[:, None]) - onehot).astype(jnp.bfloat16)
    coef_hard = jnp.where(
        mine, jnp.exp(hard_mine - lse_all[:, None]).astype(jnp.bfloat16), jnp.zeros((), jnp.bfloat16)
    )
    hard_matrix = jnp.sum(
        jnp.where(
            hard_pos[:, :, None] == jnp.arange(pool_size, dtype=jnp.int32)[None, None, :],
            coef_hard.astype(jnp.float32)[:, :, None],
            0.0,
        ),
        axis=1,
    ).astype(jnp.bfloat16)

    hard_grad = jnp.dot(hard_matrix, pool, preferred_element_type=jnp.float32).astype(jnp.bfloat16)
    hard_grad = lax.psum_scatter(hard_grad, "slab", scatter_dimension=0, tiled=True)
    pool_grad = jnp.dot(coef_pool, pool, preferred_element_type=jnp.float32)
    query_grad = pool_grad + hard_grad.astype(jnp.float32)

    partial = lax.dot_general(
        coef_pool, queries, contract_cols, preferred_element_type=jnp.float32
    ) + lax.dot_general(hard_matrix, column_queries, contract_cols, preferred_element_type=jnp.float32)
    passage_grad = lax.psum_scatter(
        partial.astype(jnp.bfloat16), "blk", scatter_dimension=0, tiled=True
    ).astype(jnp.float32)
    return (query_loss, query_grad, passage_grad)


def solution(mesh):
    return jax.shard_map(
        per_device,
        mesh=mesh,
        in_specs=(
            P(("blk", "slab"), None),
            P(("blk", "slab"), None),
            P(("blk", "slab")),
            P(("blk", "slab"), None),
        ),
        out_specs=(P(("blk", "slab")), P(("blk", "slab"), None), P(("blk", "slab"), None)),
        check_vma=False,
    )
```

time: 644 us -> 383 us (0.59); the launches traced: 633 us -> 383 us
  waiting for transfers between devices: 425 us -> 239 us
  other arithmetic: 39.8 us -> 4.86 us
  local copies, waits for them, and re-layouts: 87.4 us -> 68.1 us
  starting transfers between devices: 19.4 us -> 0.34 us
  blocking collectives: 14.3 us -> 28.2 us
    all_to_all x2 -> x0, waiting for transfers between devices: 311 us -> none  [the longest x1 207 us: per_device(): lax.all_to_all(outgoing.reshape(devices, slot_count, model_width), ('blk'...]
    reduce_scatter x1 -> x2, waiting for transfers between devices: 0.01 us -> 125 us  [the longest x1 66.7 us: per_device(): lax.psum_scatter(hard_grad, 'slab', scatter_dimension=0, tiled=True)]
    reshape x3, local copies, waits for them, and re-layouts: 39.6 us -> 0.76 us  [the longest x1 0.59 us: per_device(): gathered[:, :hard_split].reshape(slabs, column_rows, hard_count)]
    all_gather x0 -> x2, blocking collectives: none -> 28.2 us  [the longest x1 14.9 us: per_device(): column_ids = lax.all_gather(hard_ids, 'slab', axis=0, tiled=True)]
    gather x3 -> x10, local copies, waits for them, and re-layouts: 41.1 us -> 67.2 us  [the longest x5 33.6 us: per_device(): jnp.take_along_axis(gathered[:, :hard_split].reshape(slabs, column_rows,...]
    all_to_all x2 -> x0, starting transfers between devices: 18.8 us -> none  [the longest x1 15 us: per_device(): lax.all_to_all(outgoing.reshape(devices, slot_count, model_width), ('blk'...]
    scatter x1 -> x0, other arithmetic: 17.3 us -> none  [per_device(): jnp.zeros((devices * slot_count, model_width), jnp.bfloat16).at[slot_of]]
    all_to_all x1 -> x0, blocking collectives: 14.3 us -> none  [per_device(): lax.all_to_all(wanted, ('blk', 'slab'), split_axis=0, concat_axis=0, tile...]
  transfers between devices with their start and end apart: 4 -> 4, of which waited for: 3 -> 4; matrix products, arithmetic and copies ran while one was open for 5% -> 4% of each run, Pallas kernels for 0% -> 0%
where the time goes in v1:
time: 383 us
  waiting for transfers between devices  239 us (62%)
  local copies, waits for them, and re-layouts  68.1 us (18%)
  matrix products  28.7 us (7%)
  blocking collectives  28.2 us (7%)
  between operations  14 us (4%)
  other arithmetic  4.86 us (1%)
    all_gather x1, waiting for transfers between devices, per_device(): column_queries = lax.all_gather(queries, 'slab', axis=0, tiled=True)  68.7 us
    reduce_scatter x1, waiting for transfers between devices, per_device(): lax.psum_scatter(hard_grad, 'slab', scatter_dimension=0, tiled=True)  66.7 us
    reduce_scatter x1, waiting for transfers between devices, per_device(): lax.psum_scatter(partial.astype(jnp.bfloat16), 'blk', scatter_dimension=0...  58 us
    all_gather x1, waiting for transfers between devices, per_device(): pool = lax.all_gather(passages, 'blk', axis=0, tiled=True)  43.8 us
    gather x5, local copies, waits for them, and re-layouts, per_device(): jnp.take_along_axis(gathered[:, :hard_split].reshape(slabs, column_rows,...  33.6 us
    gather x5, local copies, waits for them, and re-layouts, per_device(): jnp.take_along_axis(scores, hard_pos, axis=1)  33.6 us
    all_gather x1, blocking collectives, per_device(): column_ids = lax.all_gather(hard_ids, 'slab', axis=0, tiled=True)  14.9 us
    all_gather x1, blocking collectives, per_device(): gathered = lax.all_gather(payload, 'slab', axis=0)  13.3 us
  transfers between devices with their start and end apart: 4, of which 4 were waited for; matrix products, arithmetic and copies ran while one was open for 4% of the time, Pallas kernels for 0%

profile of v1, /device:TPU:0, one launch (start us, length us, event | category | flops | bytes accessed | tf_op | source)
XLA Modules:
  0.0 382.8 jit_solution(10937758230135534292)
XLA Ops:
  7.2 0.0 all-gather.5.cloned.1.call-start
  7.2 0.7 all-gather.5.cloned.1.call-update
  7.9 0.0 all-gather.7.cloned.1.call-start
  7.9 0.7 all-gather.7.cloned.1.call-update
  8.6 0.0 reduce-scatter.3.cloned.1.call-start
  8.7 14.9 %all_gather.15 = s32[512,8]{0,1:T(8,128)S(1)} all-gather(s32[128,8]{0,1:T(8,128)} %param.7), channel_id=1, replica_groups=mesh['blk'=8,'slab'=4] {'slab'}, dimensions={0}, use_global_device_ids=true | all-gather | bytes 20480 | tf_op jit(solution)/shard_map/all_gather | solution.py:22
  23.7 0.1 copy.19
  23.9 0.2 reshape.91
  24.1 0.1 copy.16
  24.2 0.2 reshape.83
  24.3 68.7 %all-gather.5.cloned.1.call-done = bf16[512,4096]{1,0:T(8,128)(2,1)} async-done(((bf16[128,4096]{1,0:T(8,128)(2,1)}), bf16[512,4096]{1,0:T(8,128)(2,1)}) %all-gather.5.cloned.1.call-update) | async-done | bytes 4194320 | tf_op jit(solution)/shard_map/all_gather | solution.py:21
  93.1 43.8 %all-gather.7.cloned.1.call-done = bf16[704,4096]{1,0:T(8,128)(2,1)} async-done(((bf16[88,4096]{1,0:T(8,128)(2,1)}), bf16[704,4096]{1,0:T(8,128)(2,1)}) %all-gather.7.cloned.1.call-update) | async-done | bytes 5767184 | tf_op jit(solution)/shard_map/all_gather | solution.py:19
  136.8 6.5 %convolution_multiply_fusion = f32[512,704]{0,1:T(8,128)S(1)} fusion(bf16[512,4096]{1,0:T(8,128)(2,1)} %all-gather.5.cloned.1.call-done, bf16[704,4096]{1,0:T(8,128)(2,1)} %all-gather.7.cloned.1.call-done), kind=kOutput, calls=%fused_computation.7 | convolution fusion | flops 2953150464 | bytes 11403264 | tf_op jit(solution)/shard_map/dot_general | solution.py:26
  143.3 0.0 copy-start.1
  143.3 33.0 %gather_fusion = f32[4096]{0:T(1024)S(1)} fusion(f32[512,704]{0,1:T(8,128)S(1)} %convolution_multiply_fusion, s32[4096]{0:T(1024)S(1)} %reshape.83), kind=kCustom, calls=%fused_computation | custom fusion | bytes 65536 | tf_op jit(solution)/shard_map/jit(take_along_axis)/gather | solution.py:36
  176.4 0.1 dynamic-slice_reduce_fusion
  176.5 0.2 reshape.86
  176.6 0.1 copy.17
  176.8 0.1 copy.18
  176.9 0.2 reshape.79
  177.0 0.0 copy-done.1
  177.1 0.1 select_reduce_fusion.1
  177.2 13.3 %all-gather.1 = f32[4,1,4352]{2,1,0:T(1,128)S(1)} all-gather(f32[1,1,4352]{2,1,0:T(1,128)S(1)} %reshape.105), channel_id=2, replica_groups=mesh['blk'=8,'slab'=4] {'slab'}, dimensions={0}, use_global_device_ids=true | all-gather | bytes 87040 | tf_op jit(solution)/shard_map/all_gather | solution.py:41
  190.5 0.6 reshape.81
  191.1 33.1 %gather_fusion.1 = f32[4096]{0:T(1024)S(1)} fusion(f32[4,512,8]{2,1,0:T(8,128)S(1)} %reshape.81, s32[4096]{0:T(1024)S(1)} %reshape.91), kind=kCustom, calls=%fused_computation.1 | custom fusion | bytes 81920 | tf_op jit(solution)/shard_map/jit(take_along_axis)/gather | solution.py:43
  224.3 0.2 gather.12
  224.4 0.1 copy.20
  224.6 1.5 select_reduce_fusion
  226.1 7.6 %convolution_convert_fusion = bf16[512,4096]{1,0:T(8,128)(2,1)} fusion(bf16[704,4096]{1,0:T(8,128)(2,1)} %all-gather.7.cloned.1.call-done, bf16[512,704]{0,1:T(8,128)(2,1)S(1)} %select_reduce_fusion), kind=kOutput, calls=%fused_computation.5 | convolution fusion | flops 2954887168 | bytes 10682368 | tf_op jit(solution)/shard_map/dot_general | solution.py:76
  233.8 0.0 reduce-scatter.3.cloned.1.call-update
  233.8 0.2 reduce-scatter.5.cloned.1.call-start
  234.0 0.6 fusion.17
  234.6 0.0 copy-start
  234.6 5.1 %fusion.20 = f32[704,4096]{1,0:T(8,128)S(1)} fusion(bf16[512,704]{0,1:T(8,128)(2,1)S(1)} %select_reduce_fusion, bf16[512,4096]{1,0:T(8,128)(2,1)} %all-gather.5.cloned.1.call-done), kind=kOutput, calls=%fused_computation.57 | convolution fusion | flops 2952790016 | bytes 16449536 | tf_op jit(solution)/shard_map/dot_general | solution.py:83
  239.7 0.0 copy-done
  239.7 4.2 %add_convert_fusion = bf16[704,4096]{1,0:T(8,128)(2,1)} fusion(f32[704,4096]{1,0:T(8,128)S(1)} %fusion.20, bf16[128,4096]{1,0:T(8,128)(2,1)S(1)} %copy-done, f32[512,704]{0,1:T(8,128)S(1)} %convolution_multiply_fusion, s32[]{:T(128)S(6)} %select_n.62, f32[128]{0:T(128)S(1)} %get-tuple-element.6, s32[128]{0:T(128)S(1)} %copy-done.1), kind=kOutput, calls=%fused_computation.2 | convolution fusion | flops 744415232 | bytes 18711556 | tf_op jit(solution)/shard_map/dot_general | solution.py:81
  243.9 0.0 reduce-scatter.5.cloned.1.call-update
  244.0 66.7 %reduce-scatter.3.cloned.1.call-done = bf16[128,4096]{1,0:T(8,128)(2,1)} async-done(((bf16[512,4096]{1,0:T(8,128)(2,1)}), bf16[128,4096]{1,0:T(8,128)(2,1)}) %reduce-scatter.3.cloned.1.call-update) | async-done | bytes 1048592 | tf_op jit(solution)/shard_map/reduce_scatter | solution.py:77
  310.6 5.3 %convolution_add_fusion = f32[128,4096]{1,0:T(8,128)} fusion(bf16[704,4096]{1,0:T(8,128)(2,1)} %all-gather.7.cloned.1.call-done, bf16[128,4096]{1,0:T(8,128)(2,1)} %reduce-scatter.3.cloned.1.call-done, f32[512,704]{0,1:T(8,128)S(1)} %convolution_multiply_fusion, s32[]{:T(128)S(6)} %select_n.62, f32[128]{0:T(128)S(1)} %get-tuple-element.6, s32[128]{0:T(128)S(1)} %copy-done.1), kind=kOutput, calls=%fused_computation.6 | convolution fusion | flops 739696640 | bytes 9274372 | tf_op jit(solution)/shard_map/dot_general | solution.py:78
  315.9 58.0 %reduce-scatter.5.cloned.1.call-done = bf16[88,4096]{1,0:T(8,128)(2,1)} async-done(((bf16[704,4096]{1,0:T(8,128)(2,1)}), bf16[88,4096]{1,0:T(8,128)(2,1)}) %reduce-scatter.5.cloned.1.call-update) | async-done | bytes 720912 | tf_op jit(solution)/shard_map/reduce_scatter | solution.py:84
  373.9 2.3 convert_element_type.35
  (19 shorter events, 0.3 us)
Async XLA Ops:
  7.2 85.9 %all-gather.5.cloned.1.call-start = ((), (), s32[]{:S(2)}) async-start(), calls=%async_computation.2 | async-start | bytes 5242880 | tf_op jit(solution)/shard_map/all_gather | solution.py:21
  7.9 128.9 %all-gather.7.cloned.1.call-start = ((), (), s32[]{:S(2)}) async-start(), calls=%async_computation.3 | async-start | bytes 6488064 | tf_op jit(solution)/shard_map/all_gather | solution.py:19
  8.6 302.0 %reduce-scatter.3.cloned.1.call-start = ((), (), s32[]{:S(2)}) async-start(), calls=%async_computation.4 | async-start | bytes 5242880 | tf_op jit(solution)/shard_map/reduce_scatter | solution.py:77
  143.3 33.7 %copy-start.1 = (s32[128]{0:T(128)S(1)}, s32[128]{0:T(128)}, u32[]{:S(2)}) copy-start(s32[128]{0:T(128)} %param.6) | copy-start | bytes 1540
  233.8 140.1 %reduce-scatter.5.cloned.1.call-start = ((), (), s32[]{:S(2)}) async-start(), calls=%async_computation.5 | async-start | bytes 6488064 | tf_op jit(solution)/shard_map/reduce_scatter | solution.py:84
  234.6 5.1 %copy-start = (bf16[128,4096]{1,0:T(8,128)(2,1)S(1)}, bf16[128,4096]{1,0:T(8,128)(2,1)}, u32[]{:S(2)}) copy-start(bf16[128,4096]{1,0:T(8,128)(2,1)} %param.4) | copy-start | bytes 3145732
Sparse Core Ops, SparseCore 0:
  9.6 83.4 all-gather.4
  94.9 41.8 all-gather.6
  233.9 76.6 reduce-scatter.2
  314.3 59.5 reduce-scatter.4

commit v2 on v1

--- a/solution.py
+++ b/solution.py
@@ -18,7 +18,9 @@
 
     pool = lax.all_gather(passages, "blk", axis=0, tiled=True)
     pool_size = pool.shape[0]
-    column_queries = lax.all_gather(queries, "slab", axis=0, tiled=True)
+    column_queries = lax.all_to_all(
+        jnp.broadcast_to(queries[None], (slabs,) + queries.shape), "slab", 0, 0, tiled=True
+    ).reshape(slabs * query_rows_dev, model_width)
     column_ids = lax.all_gather(hard_ids, "slab", axis=0, tiled=True)
     column_rows = column_queries.shape[0]
 
@@ -33,18 +35,24 @@
     owner_slab = owner_dev % slabs
     hard_pos = (owner_dev // slabs) * passage_rows_dev + column_ids % passage_rows_dev
     mine = owner_slab == my_slab
-    hard_mine = jnp.where(mine, jnp.take_along_axis(scores, hard_pos, axis=1), 0.0)
+    pool_iota = jnp.arange(pool_size, dtype=jnp.int32)[None, None, :]
+    hard_hit = (hard_pos[:, :, None] == pool_iota) & mine[:, :, None]
+    hard_mine = jnp.sum(jnp.where(hard_hit, scores[:, None, :], 0.0), axis=2)
 
     pool_max = jnp.max(pooled, axis=1)
     pool_sum = jnp.sum(jnp.exp(pooled - pool_max[:, None]), axis=1)
     payload = jnp.concatenate([hard_mine.reshape(-1), pool_max, pool_sum])
     gathered = lax.all_gather(payload, "slab", axis=0)
     hard_split = column_rows * hard_count
-    hard_all = jnp.take_along_axis(
-        gathered[:, :hard_split].reshape(slabs, column_rows, hard_count),
-        owner_slab[None],
+    slab_iota = jnp.arange(slabs, dtype=jnp.int32)[:, None, None]
+    hard_all = jnp.sum(
+        jnp.where(
+            owner_slab[None] == slab_iota,
+            gathered[:, :hard_split].reshape(slabs, column_rows, hard_count),
+            0.0,
+        ),
         axis=0,
-    )[0]
+    )
     stats = gathered[:, hard_split:].reshape(slabs, 2, query_rows_dev)
     max_all = stats[:, 0].reshape(column_rows)
     sum_all = stats[:, 1].reshape(column_rows)
@@ -65,18 +73,15 @@
         mine, jnp.exp(hard_mine - lse_all[:, None]).astype(jnp.bfloat16), jnp.zeros((), jnp.bfloat16)
     )
     hard_matrix = jnp.sum(
-        jnp.where(
-            hard_pos[:, :, None] == jnp.arange(pool_size, dtype=jnp.int32)[None, None, :],
-            coef_hard.astype(jnp.float32)[:, :, None],
-            0.0,
-        ),
-        axis=1,
+        jnp.where(hard_hit, coef_hard.astype(jnp.float32)[:, :, None], 0.0), axis=1
     ).astype(jnp.bfloat16)
 
     hard_grad = jnp.dot(hard_matrix, pool, preferred_element_type=jnp.float32).astype(jnp.bfloat16)
-    hard_grad = lax.psum_scatter(hard_grad, "slab", scatter_dimension=0, tiled=True)
+    hard_grad = lax.all_to_all(
+        hard_grad.reshape(slabs, query_rows_dev, model_width), "slab", 0, 0, tiled=True
+    )
     pool_grad = jnp.dot(coef_pool, pool, preferred_element_type=jnp.float32)
-    query_grad = pool_grad + hard_grad.astype(jnp.float32)
+    query_grad = pool_grad + jnp.sum(hard_grad.astype(jnp.float32), axis=0)
 
     partial = lax.dot_general(
         coef_pool, queries, contract_cols, preferred_element_type=jnp.float32

time: 383 us -> 264 us (0.69)
  waiting for transfers between devices: 239 us -> 0.72 us
  blocking collectives: 28.2 us -> 203 us
  local copies, waits for them, and re-layouts: 68.1 us -> 4.6 us
  starting transfers between devices: 0.34 us -> 6.49 us
  other arithmetic: 4.86 us -> 9.93 us
  matrix products: 28.7 us -> 24.6 us
    all_to_all x0 -> x1, blocking collectives: none -> 91.4 us  [per_device(): lax.all_to_all(hard_grad.reshape(slabs, query_rows_dev, model_width), 'sl...]
    all_gather x1, blocking collectives: 14.9 us -> 98.6 us  [per_device(): column_ids = lax.all_gather(hard_ids, 'slab', axis=0, tiled=True)]
    all_gather x1 -> x0, waiting for transfers between devices: 68.7 us -> none  [per_device(): column_queries = lax.all_gather(queries, 'slab', axis=0, tiled=True)]
    gather x10 -> x0, local copies, waits for them, and re-layouts: 67.2 us -> none  [the longest x5 33.6 us: per_device(): jnp.take_along_axis(gathered[:, :hard_split].reshape(slabs, column_rows,...]
    reduce_scatter x1 -> x0, waiting for transfers between devices: 66.7 us -> none  [per_device(): lax.psum_scatter(hard_grad, 'slab', scatter_dimension=0, tiled=True)]
    reduce_scatter x1, waiting for transfers between devices: 58 us -> 0.01 us  [per_device(): lax.psum_scatter(partial.astype(jnp.bfloat16), 'blk', scatter_dimension=0...]
    all_gather x1, waiting for transfers between devices: 43.8 us -> 0.02 us  [per_device(): pool = lax.all_gather(passages, 'blk', axis=0, tiled=True)]
    all_to_all x0 -> x1, starting transfers between devices: none -> 6.45 us  [per_device(): lax.all_to_all(jnp.broadcast_to(queries[None], (slabs,) + queries.shape),...]
  transfers between devices with their start and end apart: 4 -> 3, of which waited for: 4 -> 0; matrix products, arithmetic and copies ran while one was open for 4% -> 5% of each run, Pallas kernels for 0% -> 0%
where the time goes in v2:
time: 264 us
  blocking collectives  203 us (77%)
  matrix products  24.6 us (9%)
  between operations  14.2 us (5%)
  other arithmetic  9.93 us (4%)
  starting transfers between devices  6.49 us (2%)
  local copies, waits for them, and re-layouts  4.6 us (2%)
    all_gather x1, blocking collectives, per_device(): column_ids = lax.all_gather(hard_ids, 'slab', axis=0, tiled=True)  98.6 us
    all_to_all x1, blocking collectives, per_device(): lax.all_to_all(hard_grad.reshape(slabs, query_rows_dev, model_width), 'sl...  91.4 us
    all_gather x1, blocking collectives, per_device(): gathered = lax.all_gather(payload, 'slab', axis=0)  13.3 us
    dot_general x1, matrix products, per_device(): jnp.dot(hard_matrix, pool, preferred_element_type=jnp.float32)  6.5 us
    dot_general x1, matrix products, per_device(): lax.dot_general(column_queries, pool, contract_rows, preferred_element_ty...  6.49 us
    all_to_all x1, starting transfers between devices, per_device(): lax.all_to_all(jnp.broadcast_to(queries[None], (slabs,) + queries.shape),...  6.45 us
  transfers between devices with their start and end apart: 3, of which 0 were waited for; matrix products, arithmetic and copies ran while one was open for 5% of the time, Pallas kernels for 0%

profile of v2, /device:TPU:0, one launch (start us, length us, event | category | flops | bytes accessed | tf_op | source)
XLA Modules:
  0.0 264.0 jit_solution(16685934172144126649)
XLA Ops:
  7.2 0.0 all-gather.4.cloned.1.call-start
  7.2 0.7 all-gather.4.cloned.1.call-update
  7.9 3.8 %broadcast_in_dim.28 = bf16[4,128,4096]{2,1,0:T(8,128)(2,1)} broadcast(bf16[128,4096]{1,0:T(8,128)(2,1)} %param.4), dimensions={1,2} | broadcast | bytes 5242880 | tf_op jit(solution)/shard_map/broadcast_in_dim | solution.py:22
  11.7 0.0 copy-start.2
  11.7 6.4 %all-to-all-start = ((bf16[4,128,4096]{2,1,0:T(8,128)(2,1)}), bf16[4,128,4096]{2,1,0:T(8,128)(2,1)}, u32[]{:S(2)}, u32[]{:S(2)}) async-start(bf16[4,128,4096]{2,1,0:T(8,128)(2,1)} %broadcast_in_dim.28), calls=%async_computation | async-start | bytes 8388608 | tf_op jit(solution)/shard_map/all_to_all | solution.py:21
  18.2 0.0 reduce-scatter.2.cloned.1.call-start
  18.2 0.0 copy-done.2
  18.2 98.6 %all_gather.12 = s32[512,8]{0,1:T(8,128)S(1)} all-gather(s32[128,8]{0,1:T(8,128)S(1)} %copy-done.2), channel_id=1, replica_groups=mesh['blk'=8,'slab'=4] {'slab'}, dimensions={0}, use_global_device_ids=true | all-gather | bytes 20480 | tf_op jit(solution)/shard_map/all_gather | solution.py:24
  116.8 0.1 copy.24
  116.9 0.2 eq.56
  117.1 0.0 all-to-all-done
  117.1 0.0 all-gather.4.cloned.1.call-done
  117.2 0.0 copy-start.1
  117.2 6.5 %convolution_multiply_fusion = f32[512,704]{0,1:T(8,128)S(1)} fusion(bf16[512,4096]{1,0:T(8,128)(2,1)} %bitcast, bf16[704,4096]{1,0:T(8,128)(2,1)} %all-gather.4.cloned.1.call-done), kind=kOutput, calls=%fused_computation.8 | convolution fusion | flops 2953150464 | bytes 11403264 | tf_op jit(solution)/shard_map/dot_general | solution.py:28
  123.7 0.1 dynamic-slice_reduce_fusion
  123.8 2.7 %select_reduce_fusion.1 = f32[512,8]{0,1:T(8,128)S(1)} fusion(f32[512,704]{0,1:T(8,128)S(1)} %convolution_multiply_fusion, s32[512,8]{0,1:T(8,128)S(1)} %fusion.6, pred[512,8]{0,1:T(8,128)(4,1)S(1)} %get-tuple-element.7), kind=kLoop, calls=%fused_computation.2 | loop fusion | flops 11530240 | bytes 1478656 | tf_op jit(solution)/shard_map/reduce_sum | solution.py:40
  126.4 0.1 copy.23
  126.6 0.2 reshape.59
  126.7 0.0 copy-done.1
  126.7 0.1 select_reduce_fusion.2
  126.9 13.3 %all-gather.1 = f32[4,1,4352]{2,1,0:T(1,128)S(1)} all-gather(f32[1,1,4352]{2,1,0:T(1,128)S(1)} %reshape.63), channel_id=2, replica_groups=mesh['blk'=8,'slab'=4] {'slab'}, dimensions={0}, use_global_device_ids=true | all-gather | bytes 87040 | tf_op jit(solution)/shard_map/all_gather | solution.py:45
  140.3 0.1 fusion.4
  140.3 0.2 reduce_sum.68
  140.5 0.1 reduce_max.19
  140.7 0.2 exponential_reduce_fusion.1
  141.0 0.6 fusion.12
  141.5 2.8 %select_reduce_fusion = bf16[512,704]{0,1:T(8,128)(2,1)S(1)} fusion(f32[512,8]{0,1:T(8,128)S(1)} %fusion.11, s32[512,8]{0,1:T(8,128)S(1)} %fusion.6, pred[512,8]{0,1:T(8,128)(4,1)S(1)} %get-tuple-element.7), kind=kLoop, calls=%fused_computation.1 | loop fusion | flops 11173888 | bytes 757760 | tf_op jit(solution)/shard_map/reduce_sum | solution.py:75
  144.3 0.0 copy-start
  144.3 5.0 %fusion.14 = f32[704,4096]{1,0:T(8,128)S(1)} fusion(bf16[512,704]{0,1:T(8,128)(2,1)S(1)} %select_reduce_fusion, bf16[512,4096]{1,0:T(8,128)(2,1)} %bitcast), kind=kOutput, calls=%fused_computation.45 | convolution fusion | flops 2952790016 | bytes 16449536 | tf_op jit(solution)/shard_map/dot_general | solution.py:88
  149.4 0.0 copy-done
  149.4 4.2 %add_convert_fusion = bf16[704,4096]{1,0:T(8,128)(2,1)} fusion(f32[704,4096]{1,0:T(8,128)S(1)} %fusion.14, bf16[128,4096]{1,0:T(8,128)(2,1)S(1)} %copy-done, f32[512,704]{0,1:T(8,128)S(1)} %convolution_multiply_fusion, s32[]{:T(128)S(6)} %select_n.45, f32[128]{0:T(128)S(1)} %get-tuple-element.6, s32[128]{0:T(128)S(1)} %copy-done.1), kind=kOutput, calls=%fused_computation | convolution fusion | flops 744415232 | bytes 18711556 | tf_op jit(solution)/shard_map/dot_general | solution.py:86
  153.6 0.0 reduce-scatter.2.cloned.1.call-update
  153.7 0.0 slice-start
  153.7 6.5 %convolution_convert_fusion = bf16[512,4096]{1,0:T(8,128)(2,1)S(1)} fusion(bf16[704,4096]{1,0:T(8,128)(2,1)} %all-gather.4.cloned.1.call-done, bf16[512,704]{0,1:T(8,128)(2,1)S(1)} %select_reduce_fusion), kind=kOutput, calls=%fused_computation.6 | convolution fusion | flops 2954887168 | bytes 10682368 | tf_op jit(solution)/shard_map/dot_general | solution.py:79
  160.2 0.0 slice-start.1
  160.2 91.4 %all_to_all.10 = bf16[4,128,4096]{2,1,0:T(8,128)(2,1)S(1)} all-to-all(bf16[4,128,4096]{2,1,0:T(8,128)(2,1)S(1)} %bitcast.17), channel_id=1, replica_groups=mesh['blk'=8,'slab'=4] {'slab'}, dimensions={0} | all-to-all | bytes 8388608 | tf_op jit(solution)/shard_map/all_to_all | solution.py:80
  251.6 0.8 convert_reduce_fusion
  252.4 0.0 slice-done
  252.4 0.0 slice-done.1
  252.4 2.4 convolution_add_fusion
  254.8 0.0 reduce-scatter.2.cloned.1.call-done
  254.8 2.3 convert_element_type.35
  (12 shorter events, 0.2 us)
Async XLA Ops:
  7.2 110.0 %all-gather.4.cloned.1.call-start = ((), (), s32[]{:S(2)}) async-start(), calls=%async_computation.3 | async-start | bytes 6488064 | tf_op jit(solution)/shard_map/all_gather | solution.py:19
  11.7 6.5 %copy-start.2 = (s32[128,8]{0,1:T(8,128)S(1)}, s32[128,8]{0,1:T(8,128)}, u32[]{:S(2)}) copy-start(s32[128,8]{0,1:T(8,128)} %param.7) | copy-start | bytes 12292
  11.7 105.4 %all-to-all-start = ((bf16[4,128,4096]{2,1,0:T(8,128)(2,1)}), bf16[4,128,4096]{2,1,0:T(8,128)(2,1)}, u32[]{:S(2)}, u32[]{:S(2)}) async-start(bf16[4,128,4096]{2,1,0:T(8,128)(2,1)} %broadcast_in_dim.28), calls=%async_computation | async-start | bytes 8388608 | tf_op jit(solution)/shard_map/all_to_all | solution.py:21
  18.2 236.6 %reduce-scatter.2.cloned.1.call-start = ((), (), s32[]{:S(2)}) async-start(), calls=%async_computation.4 | async-start | bytes 6488064 | tf_op jit(solution)/shard_map/reduce_scatter | solution.py:89
  117.2 9.6 %copy-start.1 = (s32[128]{0:T(128)S(1)}, s32[128]{0:T(128)}, u32[]{:S(2)}) copy-start(s32[128]{0:T(128)} %param.6) | copy-start | bytes 1540
  144.3 5.1 %copy-start = (bf16[128,4096]{1,0:T(8,128)(2,1)S(1)}, bf16[128,4096]{1,0:T(8,128)(2,1)}, u32[]{:S(2)}) copy-start(bf16[128,4096]{1,0:T(8,128)(2,1)} %param.4) | copy-start | bytes 3145732
  153.7 98.7 %slice-start = ((s8[5767168]{0:T(1024)(128)(4,1)}), s8[4194304]{0:T(1024)(128)(4,1)S(1)}, s32[]{:S(2)}) async-start(s8[5767168]{0:T(1024)(128)(4,1)} %bitcast.15), calls=%async_computation.5 | async-start | bytes 8388608
  160.2 92.2 %slice-start.1 = ((s8[5767168]{0:T(1024)(128)(4,1)}), s8[1572864]{0:T(1024)(128)(4,1)S(1)}, s32[]{:S(2)}) async-start(s8[5767168]{0:T(1024)(128)(4,1)} %bitcast.15), calls=%async_computation.6 | async-start | bytes 3145728
Sparse Core Ops, SparseCore 0:
  9.9 46.0 all-gather.3
  153.8 59.3 reduce-scatter.1

commit v3 on v2

--- a/solution.py
+++ b/solution.py
@@ -18,10 +18,20 @@
 
     pool = lax.all_gather(passages, "blk", axis=0, tiled=True)
     pool_size = pool.shape[0]
-    column_queries = lax.all_to_all(
-        jnp.broadcast_to(queries[None], (slabs,) + queries.shape), "slab", 0, 0, tiled=True
-    ).reshape(slabs * query_rows_dev, model_width)
-    column_ids = lax.all_gather(hard_ids, "slab", axis=0, tiled=True)
+    ring_down = [(i, (i - 1) % slabs) for i in range(slabs)]
+    query_blocks = [queries]
+    id_blocks = [hard_ids]
+    for _ in range(slabs - 1):
+        query_blocks.append(lax.ppermute(query_blocks[-1], "slab", ring_down))
+        id_blocks.append(lax.ppermute(id_blocks[-1], "slab", ring_down))
+
+    def to_origin(blocks):
+        doubled = jnp.concatenate(blocks + blocks, axis=0)
+        start = ((slabs - my_slab) % slabs) * blocks[0].shape[0]
+        return lax.dynamic_slice_in_dim(doubled, start, slabs * blocks[0].shape[0], axis=0)
+
+    column_queries = to_origin(query_blocks)
+    column_ids = to_origin(id_blocks)
     column_rows = column_queries.shape[0]
 
     scores = (
@@ -76,12 +86,19 @@
         jnp.where(hard_hit, coef_hard.astype(jnp.float32)[:, :, None], 0.0), axis=1
     ).astype(jnp.bfloat16)
 
-    hard_grad = jnp.dot(hard_matrix, pool, preferred_element_type=jnp.float32).astype(jnp.bfloat16)
-    hard_grad = lax.all_to_all(
-        hard_grad.reshape(slabs, query_rows_dev, model_width), "slab", 0, 0, tiled=True
+    hard_grad = jnp.dot(hard_matrix, pool, preferred_element_type=jnp.float32).reshape(
+        slabs, query_rows_dev, model_width
     )
+
+    def grad_for(offset):
+        return lax.dynamic_index_in_dim(hard_grad, (my_slab + offset) % slabs, keepdims=False)
+
+    carried = grad_for(1)
+    for step in range(1, slabs):
+        carried = lax.ppermute(carried.astype(jnp.bfloat16), "slab", ring_down).astype(jnp.float32)
+        carried = carried + grad_for((step + 1) % slabs)
     pool_grad = jnp.dot(coef_pool, pool, preferred_element_type=jnp.float32)
-    query_grad = pool_grad + jnp.sum(hard_grad.astype(jnp.float32), axis=0)
+    query_grad = pool_grad + carried
 
     partial = lax.dot_general(
         coef_pool, queries, contract_cols, preferred_element_type=jnp.float32

time: 264 us -> 221 us (0.84)
  blocking collectives: 203 us -> 13.8 us
  waiting for transfers between devices: 0.72 us -> 103 us
  starting transfers between devices: 6.49 us -> 31.3 us
  local copies, waits for them, and re-layouts: 4.6 us -> 16.4 us
  other arithmetic: 9.93 us -> 16.9 us
    ppermute x0 -> x9, waiting for transfers between devices: none -> 103 us  [the longest x3 43.6 us: per_device(): lax.ppermute(carried.astype(jnp.bfloat16), 'slab', ring_down)]
    all_gather x1 -> x0, blocking collectives: 98.6 us -> none  [per_device(): column_ids = lax.all_gather(hard_ids, 'slab', axis=0, tiled=True)]
    all_to_all x1 -> x0, blocking collectives: 91.4 us -> none  [per_device(): lax.all_to_all(hard_grad.reshape(slabs, query_rows_dev, model_width), 'sl...]
    ppermute x0 -> x9, starting transfers between devices: none -> 31.2 us  [the longest x3 13.4 us: per_device(): query_blocks.append(lax.ppermute(query_blocks[-1], 'slab', ring_down))]
    unnamed x12 -> x32, local copies, waits for them, and re-layouts: 0.06 us -> 13.9 us
    all_to_all x1 -> x0, starting transfers between devices: 6.45 us -> none  [per_device(): lax.all_to_all(jnp.broadcast_to(queries[None], (slabs,) + queries.shape),...]
    convert_element_type x0 -> x2, other arithmetic: none -> 3.87 us  [per_device(): carried.astype(jnp.bfloat16)]
    broadcast_in_dim x1 -> x0, local copies, waits for them, and re-layouts: 3.81 us -> none  [per_device(): jnp.broadcast_to(queries[None], (slabs,) + queries.shape)]
  transfers between devices with their start and end apart: 3 -> 11, of which waited for: 0 -> 7; matrix products, arithmetic and copies ran while one was open for 5% -> 13% of each run, Pallas kernels for 0% -> 0%
where the time goes in v3:
time: 221 us
  waiting for transfers between devices  103 us (47%)
  starting transfers between devices  31.3 us (14%)
  matrix products  24.7 us (11%)
  other arithmetic  16.9 us (8%)
  local copies, waits for them, and re-layouts  16.4 us (7%)
  between operations  14.3 us (6%)
  blocking collectives  13.8 us (6%)
    ppermute x3, waiting for transfers between devices, per_device(): lax.ppermute(carried.astype(jnp.bfloat16), 'slab', ring_down)  43.6 us
    ppermute x3, waiting for transfers between devices, per_device(): query_blocks.append(lax.ppermute(query_blocks[-1], 'slab', ring_down))  39.5 us
    ppermute x3, waiting for transfers between devices, per_device(): id_blocks.append(lax.ppermute(id_blocks[-1], 'slab', ring_down))  19.6 us
    unnamed x32, local copies, waits for them, and re-layouts  13.9 us
    all_gather x1, blocking collectives, per_device(): gathered = lax.all_gather(payload, 'slab', axis=0)  13.8 us
    ppermute x3, starting transfers between devices, per_device(): query_blocks.append(lax.ppermute(query_blocks[-1], 'slab', ring_down))  13.4 us
    ppermute x3, starting transfers between devices, per_device(): lax.ppermute(carried.astype(jnp.bfloat16), 'slab', ring_down)  12.8 us
    dot_general x1, matrix products, per_device(): lax.dot_general(hard_matrix, column_queries, contract_cols, preferred_ele...  7.29 us
  transfers between devices with their start and end apart: 11, of which 7 were waited for; matrix products, arithmetic and copies ran while one was open for 13% of the time, Pallas kernels for 0%

profile of v3, /device:TPU:0, one launch (start us, length us, event | category | flops | bytes accessed | tf_op | source)
XLA Modules:
  0.0 220.9 jit_solution(6146449346247533851)
XLA Ops:
  7.2 0.0 copy-start.1
  7.2 0.0 all-gather.4.cloned.1.call-start
  7.2 0.7 all-gather.4.cloned.1.call-update
  7.9 0.0 reduce-scatter.2.cloned.1.call-start
  8.0 5.1 %collective-permute-start.3 = (bf16[128,4096]{1,0:T(8,128)(2,1)}, bf16[128,4096]{1,0:T(8,128)(2,1)S(1)}, u32[]{:S(2)}, u32[]{:S(2)}) collective-permute-start(bf16[128,4096]{1,0:T(8,128)(2,1)} %param.4), channel_id=1, source_target_pairs={{0,3},{1,0},{2,1},{3,2},{4,7},{5,4},{6,5},{7,6},{8,11},{9,8},{10,9... | collective-permute-start | bytes 3145736 | tf_op jit(solution)/shard_map/ppermute | solution.py:25
  13.1 0.4 collective-permute-start
  13.5 22.3 %collective-permute-done.3 = bf16[128,4096]{1,0:T(8,128)(2,1)S(1)} collective-permute-done((bf16[128,4096]{1,0:T(8,128)(2,1)}, bf16[128,4096]{1,0:T(8,128)(2,1)S(1)}, u32[]{:S(2)}, u32[]{:S(2)}) %collective-permute-start.3) | collective-permute-done | bytes 1048608 | tf_op jit(solution)/shard_map/ppermute | solution.py:25
  35.8 4.2 %collective-permute-start.4 = (bf16[128,4096]{1,0:T(8,128)(2,1)S(1)}, bf16[128,4096]{1,0:T(8,128)(2,1)S(1)}, u32[]{:S(2)}, u32[]{:S(2)}) collective-permute-start(bf16[128,4096]{1,0:T(8,128)(2,1)S(1)} %collective-permute-done.3), channel_id=1, source_target_pairs={{0,3},{1,0},{2,1},{3,2},{4,7},{5,4},{6,5},{7,6},{8,11},{9,8},{10,9... | collective-permute-start | bytes 3145736 | tf_op jit(solution)/shard_map/ppermute | solution.py:25
  40.0 2.3 %constant_dynamic-update-slice_fusion.15 = bf16[1024,4096]{1,0:T(8,128)(2,1)} fusion(bf16[128,4096]{1,0:T(8,128)(2,1)} %param.4), kind=kLoop, calls=%fused_computation.45 | loop fusion | bytes 2097152
  42.3 0.7 constant_dynamic-update-slice_fusion.7
  43.0 0.0 collective-permute-done
  43.0 0.3 collective-permute-start.1
  43.3 18.3 %collective-permute-done.1 = s32[128,8]{0,1:T(8,128)S(1)} collective-permute-done((s32[128,8]{0,1:T(8,128)S(1)}, s32[128,8]{0,1:T(8,128)S(1)}, u32[]{:S(2)}, u32[]{:S(2)}) %collective-permute-start.1) | collective-permute-done | bytes 4128 | tf_op jit(solution)/shard_map/ppermute | solution.py:26
  61.6 4.3 %collective-permute-start.2 = (s32[128,8]{0,1:T(8,128)S(1)}, s32[128,8]{0,1:T(8,128)S(1)}, u32[]{:S(2)}, u32[]{:S(2)}) collective-permute-start(s32[128,8]{0,1:T(8,128)S(1)} %collective-permute-done.1), channel_id=1, source_target_pairs={{0,3},{1,0},{2,1},{3,2},{4,7},{5,4},{6,5},{7,6},{8,11},{9,8},{10,9... | collective-permute-start | bytes 12296 | tf_op jit(solution)/shard_map/ppermute | solution.py:26
  65.9 1.3 collective-permute-done.2
  67.2 0.7 constant_dynamic-update-slice_fusion.3
  67.9 0.6 broadcast_compare_fusion
  68.5 0.1 copy.24
  68.6 0.8 eq.63
  69.4 0.0 collective-permute-done.4
  69.4 4.1 %collective-permute-start.5 = (bf16[128,4096]{1,0:T(8,128)(2,1)S(1)}, bf16[128,4096]{1,0:T(8,128)(2,1)S(1)}, u32[]{:S(2)}, u32[]{:S(2)}) collective-permute-start(bf16[128,4096]{1,0:T(8,128)(2,1)S(1)} %collective-permute-done.4), channel_id=1, source_target_pairs={{0,3},{1,0},{2,1},{3,2},{4,7},{5,4},{6,5},{7,6},{8,11},{9,8},{10,9... | collective-permute-start | bytes 3145736 | tf_op jit(solution)/shard_map/ppermute | solution.py:25
  73.5 1.1 constant_dynamic-update-slice_fusion.14
  74.6 1.1 constant_dynamic-update-slice_fusion.13
  75.7 17.2 %collective-permute-done.5 = bf16[128,4096]{1,0:T(8,128)(2,1)S(1)} collective-permute-done((bf16[128,4096]{1,0:T(8,128)(2,1)S(1)}, bf16[128,4096]{1,0:T(8,128)(2,1)S(1)}, u32[]{:S(2)}, u32[]{:S(2)}) %collective-permute-start.5) | collective-permute-done | bytes 1048608 | tf_op jit(solution)/shard_map/ppermute | solution.py:25
  92.9 1.1 constant_dynamic-update-slice_fusion.12
  94.0 1.1 constant_dynamic-update-slice_fusion.11
  95.0 1.1 constant_dynamic-update-slice_fusion.10
  96.2 1.1 constant_dynamic-update-slice_fusion.9
  97.2 1.1 constant_dynamic-update-slice_fusion.8
  98.3 6.5 %fusion.7 = f32[512,704]{0,1:T(8,128)S(1)} fusion(bf16[704,4096]{1,0:T(8,128)(2,1)} %all-gather.4.cloned.1.call-done, bf16[1024,4096]{1,0:T(8,128)(2,1)} %constant_dynamic-update-slice_fusion.8, s32[]{:T(128)S(6)} %select_n.82), kind=kOutput, calls=%fused_computation.15 | convolution fusion | flops 2953150464 | bytes 11403268 | tf_op jit(solution)/shard_map/dot_general | solution.py:38
  104.8 0.1 dynamic-slice_reduce_fusion
  104.9 2.7 %select_reduce_fusion.1 = f32[512,8]{0,1:T(8,128)S(1)} fusion(f32[512,704]{0,1:T(8,128)S(1)} %fusion.7, s32[512,8]{0,1:T(8,128)S(1)} %fusion.16, pred[512,8]{0,1:T(8,128)(4,1)S(1)} %copy-done.2), kind=kLoop, calls=%fused_computation.2 | loop fusion | flops 11530240 | bytes 1478656 | tf_op jit(solution)/shard_map/reduce_sum | solution.py:50
  107.6 0.1 copy.23
  107.7 0.2 reshape.55
  107.9 0.0 copy-done.4
  107.9 0.1 select_reduce_fusion.2
  108.1 13.8 %all-gather.1 = f32[4,1,4352]{2,1,0:T(1,128)S(1)} all-gather(f32[1,1,4352]{2,1,0:T(1,128)S(1)} %reshape.59), channel_id=2, replica_groups=mesh['blk'=8,'slab'=4] {'slab'}, dimensions={0}, use_global_device_ids=true | all-gather | bytes 87040 | tf_op jit(solution)/shard_map/all_gather | solution.py:55
  121.9 0.0 copy-done.3
  121.9 0.1 fusion.14
  122.0 0.2 reduce_sum.59
  122.1 0.1 reduce_max.19
  122.3 0.2 exponential_reduce_fusion.1
  122.6 0.6 fusion.26
  123.2 2.8 %select_reduce_fusion = bf16[512,704]{0,1:T(8,128)(2,1)S(1)} fusion(f32[512,8]{0,1:T(8,128)S(1)} %fusion.21, s32[512,8]{0,1:T(8,128)S(1)} %fusion.16, pred[512,8]{0,1:T(8,128)(4,1)S(1)} %copy-done.2), kind=kLoop, calls=%fused_computation.1 | loop fusion | flops 11173888 | bytes 757760 | tf_op jit(solution)/shard_map/reduce_sum | solution.py:85
  126.0 1.7 fusion.24
  127.6 7.3 %add_convert_fusion = bf16[704,4096]{1,0:T(8,128)(2,1)} fusion(f32[704,4096]{1,0:T(8,128)S(1)} %fusion.24, bf16[1024,4096]{1,0:T(8,128)(2,1)} %constant_dynamic-update-slice_fusion.8, s32[]{:T(128)S(6)} %select_n.82, bf16[512,704]{0,1:T(8,128)(2,1)S(1)} %select_reduce_fusion), kind=kOutput, calls=%fused_computation | convolution fusion | flops 2958557184 | bytes 22216708 | tf_op jit(solution)/shard_map/dot_general | solution.py:105
  134.9 0.0 copy-done.6
  134.9 0.0 reduce-scatter.2.cloned.1.call-update
  135.0 5.5 %fusion.28 = f32[512,4096]{1,0:T(8,128)S(1)} fusion(bf16[512,704]{0,1:T(8,128)(2,1)S(1)} %select_reduce_fusion, bf16[704,4096]{1,0:T(8,128)(2,1)} %all-gather.4.cloned.1.call-done), kind=kOutput, calls=%fused_computation.73 | convolution fusion | flops 2952790016 | bytes 14876672 | tf_op jit(solution)/shard_map/dot_general | solution.py:89
  140.5 0.0 copy-start.5
  140.5 0.0 copy-start.7
  140.5 3.7 %copy-done = f32[512,4096]{1,0:T(8,128)} copy-done((f32[512,4096]{1,0:T(8,128)}, f32[512,4096]{1,0:T(8,128)S(1)}, u32[]{:S(2)}) %copy-start) | copy-done | bytes 8388632
  144.2 0.1 fusion.10
  144.3 4.0 %collective-permute-start.6 = (bf16[128,4096]{1,0:T(8,128)(2,1)S(1)}, bf16[128,4096]{1,0:T(8,128)(2,1)S(1)}, u32[]{:S(2)}, u32[]{:S(2)}) collective-permute-start(bf16[128,4096]{1,0:T(8,128)(2,1)S(1)} %fusion.10), channel_id=1, source_target_pairs={{0,3},{1,0},{2,1},{3,2},{4,7},{5,4},{6,5},{7,6},{8,11},{9,8},{10,9... | collective-permute-start | bytes 3145736 | tf_op jit(solution)/shard_map/ppermute | solution.py:98
  148.3 17.2 %collective-permute-done.6 = bf16[128,4096]{1,0:T(8,128)(2,1)S(1)} collective-permute-done((bf16[128,4096]{1,0:T(8,128)(2,1)S(1)}, bf16[128,4096]{1,0:T(8,128)(2,1)S(1)}, u32[]{:S(2)}, u32[]{:S(2)}) %collective-permute-start.6) | collective-permute-done | bytes 1048608 | tf_op jit(solution)/shard_map/ppermute | solution.py:98
  165.5 1.8 fusion.6
  167.3 4.4 %collective-permute-start.7 = (bf16[128,4096]{1,0:T(8,128)(2,1)S(1)}, bf16[128,4096]{1,0:T(8,128)(2,1)}, u32[]{:S(2)}, u32[]{:S(2)}) collective-permute-start(bf16[128,4096]{1,0:T(8,128)(2,1)S(1)} %fusion.6), channel_id=1, source_target_pairs={{0,3},{1,0},{2,1},{3,2},{4,7},{5,4},{6,5},{7,6},{8,11},{9,8},{10,9... | collective-permute-start | bytes 3145736 | tf_op jit(solution)/shard_map/ppermute | solution.py:98
  171.7 16.7 %collective-permute-done.7 = bf16[128,4096]{1,0:T(8,128)(2,1)} collective-permute-done((bf16[128,4096]{1,0:T(8,128)(2,1)S(1)}, bf16[128,4096]{1,0:T(8,128)(2,1)}, u32[]{:S(2)}, u32[]{:S(2)}) %collective-permute-start.7) | collective-permute-done | bytes 1048608 | tf_op jit(solution)/shard_map/ppermute | solution.py:98
  188.4 2.1 fusion.5
  190.5 4.5 %collective-permute-start.8 = (bf16[128,4096]{1,0:T(8,128)(2,1)S(1)}, bf16[128,4096]{1,0:T(8,128)(2,1)S(1)}, u32[]{:S(2)}, u32[]{:S(2)}) collective-permute-start(bf16[128,4096]{1,0:T(8,128)(2,1)S(1)} %fusion.5), channel_id=1, source_target_pairs={{0,3},{1,0},{2,1},{3,2},{4,7},{5,4},{6,5},{7,6},{8,11},{9,8},{10,9... | collective-permute-start | bytes 3145736 | tf_op jit(solution)/shard_map/ppermute | solution.py:98
  194.9 3.7 %fusion.25 = f32[128,4096]{1,0:T(8,128)S(1)} fusion(bf16[704,4096]{1,0:T(8,128)(2,1)} %all-gather.4.cloned.1.call-done, f32[512,704]{0,1:T(8,128)S(1)} %fusion.7, s32[]{:T(128)S(6)} %select_n.88, f32[128]{0:T(128)S(1)} %copy-done.7, s32[128]{0:T(128)S(1)} %copy-done.5), kind=kOutput, calls=%fused_computation.70 | convolution fusion | flops 738648064 | bytes 8225796 | tf_op jit(solution)/shard_map/dot_general | solution.py:100
  198.7 9.7 %collective-permute-done.8 = bf16[128,4096]{1,0:T(8,128)(2,1)S(1)} collective-permute-done((bf16[128,4096]{1,0:T(8,128)(2,1)S(1)}, bf16[128,4096]{1,0:T(8,128)(2,1)S(1)}, u32[]{:S(2)}, u32[]{:S(2)}) %collective-permute-start.8) | collective-permute-done | bytes 1048608 | tf_op jit(solution)/shard_map/ppermute | solution.py:98
  208.4 3.3 %fusion.4 = f32[128,4096]{1,0:T(8,128)} fusion(f32[128,4096]{1,0:T(8,128)S(1)} %fusion.25, f32[4,128,4096]{2,1,0:T(8,128)} %bitcast.29, s32[]{:T(128)S(6)} %select_n.99, bf16[128,4096]{1,0:T(8,128)(2,1)S(1)} %collective-permute-done.8), kind=kLoop, calls=%fused_computation.9 | loop fusion | flops 1572864 | bytes 7340036 | tf_op jit(solution)/shard_map/add | solution.py:101
  211.7 2.3 %convert_element_type.55 = f32[88,4096]{1,0:T(8,128)} convert(bf16[88,4096]{1,0:T(8,128)(2,1)} %reduce-scatter.2.cloned.1.call-done) | non-fusion elementwise | flops 360448 | bytes 2162688 | tf_op jit(solution)/shard_map/convert_element_type | solution.py:108
  (27 shorter events, 0.2 us)
Async XLA Ops:
  7.2 86.8 %copy-start.1 = (bf16[128,4096]{1,0:T(8,128)(2,1)S(1)}, bf16[128,4096]{1,0:T(8,128)(2,1)}, u32[]{:S(2)}) copy-start(bf16[128,4096]{1,0:T(8,128)(2,1)} %param.4) | copy-start | bytes 3145732
  7.2 91.1 %all-gather.4.cloned.1.call-start = ((), (), s32[]{:S(2)}) async-start(), calls=%async_computation.1 | async-start | bytes 6488064 | tf_op jit(solution)/shard_map/all_gather | solution.py:19
  7.9 203.8 %reduce-scatter.2.cloned.1.call-start = ((), (), s32[]{:S(2)}) async-start(), calls=%async_computation.2 | async-start | bytes 6488064 | tf_op jit(solution)/shard_map/reduce_scatter | solution.py:106
  8.0 27.9 %collective-permute-start.3 = (bf16[128,4096]{1,0:T(8,128)(2,1)}, bf16[128,4096]{1,0:T(8,128)(2,1)S(1)}, u32[]{:S(2)}, u32[]{:S(2)}) collective-permute-start(bf16[128,4096]{1,0:T(8,128)(2,1)} %param.4), channel_id=1, source_target_pairs={{0,3},{1,0},{2,1},{3,2},{4,7},{5,4},{6,5},{7,6},{8,11},{9,8},{10,9... | collective-permute-start | bytes 3145736 | tf_op jit(solution)/shard_map/ppermute | solution.py:25
  13.1 29.9 %collective-permute-start = (s32[128,8]{0,1:T(8,128)}, s32[128,8]{0,1:T(8,128)S(1)}, u32[]{:S(2)}, u32[]{:S(2)}) collective-permute-start(s32[128,8]{0,1:T(8,128)} %param.7), channel_id=1, source_target_pairs={{0,3},{1,0},{2,1},{3,2},{4,7},{5,4},{6,5},{7,6},{8,11},{9,8},{10,9... | collective-permute-start | bytes 12296 | tf_op jit(solution)/shard_map/ppermute | solution.py:26
  35.8 33.6 %collective-permute-start.4 = (bf16[128,4096]{1,0:T(8,128)(2,1)S(1)}, bf16[128,4096]{1,0:T(8,128)(2,1)S(1)}, u32[]{:S(2)}, u32[]{:S(2)}) collective-permute-start(bf16[128,4096]{1,0:T(8,128)(2,1)S(1)} %collective-permute-done.3), channel_id=1, source_target_pairs={{0,3},{1,0},{2,1},{3,2},{4,7},{5,4},{6,5},{7,6},{8,11},{9,8},{10,9... | collective-permute-start | bytes 3145736 | tf_op jit(solution)/shard_map/ppermute | solution.py:25
  43.0 18.6 %collective-permute-start.1 = (s32[128,8]{0,1:T(8,128)S(1)}, s32[128,8]{0,1:T(8,128)S(1)}, u32[]{:S(2)}, u32[]{:S(2)}) collective-permute-start(s32[128,8]{0,1:T(8,128)S(1)} %collective-permute-done), channel_id=1, source_target_pairs={{0,3},{1,0},{2,1},{3,2},{4,7},{5,4},{6,5},{7,6},{8,11},{9,8},{10,9... | collective-permute-start | bytes 12296 | tf_op jit(solution)/shard_map/ppermute | solution.py:26
  61.6 5.6 %collective-permute-start.2 = (s32[128,8]{0,1:T(8,128)S(1)}, s32[128,8]{0,1:T(8,128)S(1)}, u32[]{:S(2)}, u32[]{:S(2)}) collective-permute-start(s32[128,8]{0,1:T(8,128)S(1)} %collective-permute-done.1), channel_id=1, source_target_pairs={{0,3},{1,0},{2,1},{3,2},{4,7},{5,4},{6,5},{7,6},{8,11},{9,8},{10,9... | collective-permute-start | bytes 12296 | tf_op jit(solution)/shard_map/ppermute | solution.py:26
  69.4 23.5 %collective-permute-start.5 = (bf16[128,4096]{1,0:T(8,128)(2,1)S(1)}, bf16[128,4096]{1,0:T(8,128)(2,1)S(1)}, u32[]{:S(2)}, u32[]{:S(2)}) collective-permute-start(bf16[128,4096]{1,0:T(8,128)(2,1)S(1)} %collective-permute-done.4), channel_id=1, source_target_pairs={{0,3},{1,0},{2,1},{3,2},{4,7},{5,4},{6,5},{7,6},{8,11},{9,8},{10,9... | collective-permute-start | bytes 3145736 | tf_op jit(solution)/shard_map/ppermute | solution.py:25
  98.3 6.6 %copy-start.2 = (pred[512,8]{0,1:T(8,128)(4,1)S(1)}, pred[512,8]{0,1:T(8,128)(4,1)}, u32[]{:S(2)}) copy-start(pred[512,8]{0,1:T(8,128)(4,1)} %get-tuple-element.7) | copy-start | bytes 12292
  98.3 9.6 %copy-start.4 = (s32[128]{0:T(128)S(1)}, s32[128]{0:T(128)}, u32[]{:S(2)}) copy-start(s32[128]{0:T(128)} %param.6) | copy-start | bytes 1540
  98.3 23.6 %copy-start.3 = (s32[4096]{0:T(1024)S(1)}, s32[4096]{0:T(1024)}, u32[]{:S(2)}) copy-start(s32[4096]{0:T(1024)} %eq.63) | copy-start | bytes 49156
  123.2 11.8 %copy-start.6 = (f32[128]{0:T(128)}, f32[128]{0:T(128)S(1)}, u32[]{:S(2)}) copy-start(f32[128]{0:T(128)S(1)} %get-tuple-element.6) | copy-start | bytes 1540
  140.5 3.7 %copy-start = (f32[512,4096]{1,0:T(8,128)}, f32[512,4096]{1,0:T(8,128)S(1)}, u32[]{:S(2)}) copy-start(f32[512,4096]{1,0:T(8,128)S(1)} %fusion.28) | copy-start | bytes 25165828
  140.5 54.4 %copy-start.5 = (s32[128]{0:T(128)S(1)}, s32[128]{0:T(128)}, u32[]{:S(2)}) copy-start(s32[128]{0:T(128)} %param.6) | copy-start | bytes 1540
  140.5 54.4 %copy-start.7 = (f32[128]{0:T(128)S(1)}, f32[128]{0:T(128)}, u32[]{:S(2)}) copy-start(f32[128]{0:T(128)} %copy-done.6) | copy-start | bytes 1540
  144.3 21.2 %collective-permute-start.6 = (bf16[128,4096]{1,0:T(8,128)(2,1)S(1)}, bf16[128,4096]{1,0:T(8,128)(2,1)S(1)}, u32[]{:S(2)}, u32[]{:S(2)}) collective-permute-start(bf16[128,4096]{1,0:T(8,128)(2,1)S(1)} %fusion.10), channel_id=1, source_target_pairs={{0,3},{1,0},{2,1},{3,2},{4,7},{5,4},{6,5},{7,6},{8,11},{9,8},{10,9... | collective-permute-start | bytes 3145736 | tf_op jit(solution)/shard_map/ppermute | solution.py:98
  167.3 21.1 %collective-permute-start.7 = (bf16[128,4096]{1,0:T(8,128)(2,1)S(1)}, bf16[128,4096]{1,0:T(8,128)(2,1)}, u32[]{:S(2)}, u32[]{:S(2)}) collective-permute-start(bf16[128,4096]{1,0:T(8,128)(2,1)S(1)} %fusion.6), channel_id=1, source_target_pairs={{0,3},{1,0},{2,1},{3,2},{4,7},{5,4},{6,5},{7,6},{8,11},{9,8},{10,9... | collective-permute-start | bytes 3145736 | tf_op jit(solution)/shard_map/ppermute | solution.py:98
  190.5 17.9 %collective-permute-start.8 = (bf16[128,4096]{1,0:T(8,128)(2,1)S(1)}, bf16[128,4096]{1,0:T(8,128)(2,1)S(1)}, u32[]{:S(2)}, u32[]{:S(2)}) collective-permute-start(bf16[128,4096]{1,0:T(8,128)(2,1)S(1)} %fusion.5), channel_id=1, source_target_pairs={{0,3},{1,0},{2,1},{3,2},{4,7},{5,4},{6,5},{7,6},{8,11},{9,8},{10,9... | collective-permute-start | bytes 3145736 | tf_op jit(solution)/shard_map/ppermute | solution.py:98
Sparse Core Ops, SparseCore 0:
  9.9 46.0 all-gather.3
  135.1 60.5 reduce-scatter.1

commit v4 on v3

--- a/solution.py
+++ b/solution.py
@@ -18,6 +18,7 @@
 
     pool = lax.all_gather(passages, "blk", axis=0, tiled=True)
     pool_size = pool.shape[0]
+
     ring_down = [(i, (i - 1) % slabs) for i in range(slabs)]
     query_blocks = [queries]
     id_blocks = [hard_ids]
@@ -25,21 +26,24 @@
         query_blocks.append(lax.ppermute(query_blocks[-1], "slab", ring_down))
         id_blocks.append(lax.ppermute(id_blocks[-1], "slab", ring_down))
 
-    def to_origin(blocks):
-        doubled = jnp.concatenate(blocks + blocks, axis=0)
-        start = ((slabs - my_slab) % slabs) * blocks[0].shape[0]
-        return lax.dynamic_slice_in_dim(doubled, start, slabs * blocks[0].shape[0], axis=0)
+    def to_origin(x):
+        doubled = jnp.concatenate([x, x], axis=0)
+        return lax.dynamic_slice_in_dim(doubled, (slabs - my_slab) % slabs, slabs, axis=0)
 
-    column_queries = to_origin(query_blocks)
-    column_ids = to_origin(id_blocks)
-    column_rows = column_queries.shape[0]
+    def to_ring(x):
+        doubled = jnp.concatenate([x, x], axis=0)
+        return lax.dynamic_slice_in_dim(doubled, my_slab, slabs, axis=0)
 
-    scores = (
-        lax.dot_general(column_queries, pool, contract_rows, preferred_element_type=jnp.float32)
-        * logit_scale
-    )
-    own_start = my_slab * query_rows_dev
-    pooled = lax.dynamic_slice_in_dim(scores, own_start, query_rows_dev, axis=0)
+    scores = jnp.concatenate(
+        [
+            lax.dot_general(block, pool, contract_rows, preferred_element_type=jnp.float32)
+            for block in query_blocks
+        ],
+        axis=0,
+    ) * logit_scale
+    column_ids = jnp.concatenate(id_blocks, axis=0)
+    column_rows = column_ids.shape[0]
+    pooled = scores[:query_rows_dev]
 
     owner_dev = column_ids // passage_rows_dev
     owner_slab = owner_dev % slabs
@@ -51,19 +55,22 @@
 
     pool_max = jnp.max(pooled, axis=1)
     pool_sum = jnp.sum(jnp.exp(pooled - pool_max[:, None]), axis=1)
-    payload = jnp.concatenate([hard_mine.reshape(-1), pool_max, pool_sum])
+    hard_origin = to_origin(hard_mine.reshape(slabs, query_rows_dev * hard_count))
+    payload = jnp.concatenate([hard_origin.reshape(-1), pool_max, pool_sum])
     gathered = lax.all_gather(payload, "slab", axis=0)
     hard_split = column_rows * hard_count
+    owner_origin = to_origin(owner_slab.reshape(slabs, query_rows_dev * hard_count))
     slab_iota = jnp.arange(slabs, dtype=jnp.int32)[:, None, None]
     hard_all = jnp.sum(
         jnp.where(
-            owner_slab[None] == slab_iota,
-            gathered[:, :hard_split].reshape(slabs, column_rows, hard_count),
+            owner_origin[None] == slab_iota,
+            gathered[:, :hard_split].reshape(slabs, slabs, query_rows_dev * hard_count),
             0.0,
         ),
         axis=0,
     )
-    stats = gathered[:, hard_split:].reshape(slabs, 2, query_rows_dev)
+    hard_all = to_ring(hard_all).reshape(column_rows, hard_count)
+    stats = to_ring(gathered[:, hard_split:].reshape(slabs, 2, query_rows_dev))
     max_all = stats[:, 0].reshape(column_rows)
     sum_all = stats[:, 1].reshape(column_rows)
 
@@ -72,7 +79,7 @@
         jnp.exp(hard_all - row_top[:, None]), axis=1
     )
     lse_all = row_top + jnp.log(row_total)
-    row_lse = lax.dynamic_slice_in_dim(lse_all, own_start, query_rows_dev)
+    row_lse = lse_all[:query_rows_dev]
 
     onehot = (jnp.arange(pool_size, dtype=jnp.int32)[None, :] == positive[:, None]).astype(
         jnp.float32
@@ -86,12 +93,9 @@
         jnp.where(hard_hit, coef_hard.astype(jnp.float32)[:, :, None], 0.0), axis=1
     ).astype(jnp.bfloat16)
 
-    hard_grad = jnp.dot(hard_matrix, pool, preferred_element_type=jnp.float32).reshape(
-        slabs, query_rows_dev, model_width
-    )
-
-    def grad_for(offset):
-        return lax.dynamic_index_in_dim(hard_grad, (my_slab + offset) % slabs, keepdims=False)
+    def grad_for(block):
+        rows = hard_matrix[block * query_rows_dev : (block + 1) * query_rows_dev]
+        return jnp.dot(rows, pool, preferred_element_type=jnp.float32)
 
     carried = grad_for(1)
     for step in range(1, slabs):
@@ -100,6 +104,7 @@
     pool_grad = jnp.dot(coef_pool, pool, preferred_element_type=jnp.float32)
     query_grad = pool_grad + carried
 
+    column_queries = jnp.concatenate(query_blocks, axis=0)
     partial = lax.dot_general(
         coef_pool, queries, contract_cols, preferred_element_type=jnp.float32
     ) + lax.dot_general(hard_matrix, column_queries, contract_cols, preferred_element_type=jnp.float32)

time: 221 us -> 200 us (0.905)
  local copies, waits for them, and re-layouts: 16.4 us -> 3.3 us
  other arithmetic: 16.9 us -> 9.3 us
  starting transfers between devices: 31.3 us -> 28.9 us
    ppermute x3, waiting for transfers between devices: 39.5 us -> 12.5 us  [per_device(): query_blocks.append(lax.ppermute(query_blocks[-1], 'slab', ring_down))]
    ppermute x3, waiting for transfers between devices: 19.6 us -> 41.2 us  [per_device(): id_blocks.append(lax.ppermute(id_blocks[-1], 'slab', ring_down))]
    unnamed x32 -> x33, local copies, waits for them, and re-layouts: 13.9 us -> 2.19 us
    ppermute x3, waiting for transfers between devices: 43.6 us -> 49.9 us  [per_device(): lax.ppermute(carried.astype(jnp.bfloat16), 'slab', ring_down)]
    dot_general x2 -> x8, matrix products: 12 us -> 18.1 us  [the longest x4 9.74 us: per_device(): lax.dot_general(block, pool, contract_rows, preferred_element_type=jnp.fl...]
    ppermute x3, starting transfers between devices: 13.4 us -> 7.39 us  [per_device(): query_blocks.append(lax.ppermute(query_blocks[-1], 'slab', ring_down))]
    convert_element_type x2 -> x0, other arithmetic: 3.87 us -> none  [per_device(): carried.astype(jnp.bfloat16)]
    ppermute x3, starting transfers between devices: 5.05 us -> 8.85 us  [per_device(): id_blocks.append(lax.ppermute(id_blocks[-1], 'slab', ring_down))]
  transfers between devices with their start and end apart: 11 -> 11, of which waited for: 7 -> 7; matrix products, arithmetic and copies ran while one was open for 13% -> 9% of each run, Pallas kernels for 0% -> 0%
where the time goes in v4:
time: 200 us
  waiting for transfers between devices  104 us (52%)
  starting transfers between devices  28.9 us (14%)
  matrix products  25.7 us (13%)
  between operations  14.4 us (7%)
  blocking collectives  13.8 us (7%)
  other arithmetic  9.3 us (5%)
  local copies, waits for them, and re-layouts  3.3 us (2%)
    ppermute x3, waiting for transfers between devices, per_device(): lax.ppermute(carried.astype(jnp.bfloat16), 'slab', ring_down)  49.9 us
    ppermute x3, waiting for transfers between devices, per_device(): id_blocks.append(lax.ppermute(id_blocks[-1], 'slab', ring_down))  41.2 us
    all_gather x1, blocking collectives, per_device(): gathered = lax.all_gather(payload, 'slab', axis=0)  13.8 us
    ppermute x3, starting transfers between devices, per_device(): lax.ppermute(carried.astype(jnp.bfloat16), 'slab', ring_down)  12.5 us
    ppermute x3, waiting for transfers between devices, per_device(): query_blocks.append(lax.ppermute(query_blocks[-1], 'slab', ring_down))  12.5 us
    dot_general x4, matrix products, per_device(): lax.dot_general(block, pool, contract_rows, preferred_element_type=jnp.fl...  9.74 us
    ppermute x3, starting transfers between devices, per_device(): id_blocks.append(lax.ppermute(id_blocks[-1], 'slab', ring_down))  8.85 us
    dot_general x4, matrix products, grad_for(): return jnp.dot(rows, pool, preferred_element_type=jnp.float32)  8.35 us
  transfers between devices with their start and end apart: 11, of which 7 were waited for; matrix products, arithmetic and copies ran while one was open for 9% of the time, Pallas kernels for 0%

profile of v4, /device:TPU:0, one launch (start us, length us, event | category | flops | bytes accessed | tf_op | source)
XLA Modules:
  0.0 199.8 jit_solution(1303245688549433503)
XLA Ops:
  7.2 0.0 all-gather.4.cloned.1.call-start
  7.2 0.7 all-gather.4.cloned.1.call-update
  7.9 0.0 reduce-scatter.2.cloned.1.call-start
  7.9 5.1 %collective-permute-start.3 = (bf16[128,4096]{1,0:T(8,128)(2,1)}, bf16[128,4096]{1,0:T(8,128)(2,1)S(1)}, u32[]{:S(2)}, u32[]{:S(2)}) collective-permute-start(bf16[128,4096]{1,0:T(8,128)(2,1)} %param.4), channel_id=1, source_target_pairs={{0,3},{1,0},{2,1},{3,2},{4,7},{5,4},{6,5},{7,6},{8,11},{9,8},{10,9... | collective-permute-start | bytes 3145736 | tf_op jit(solution)/shard_map/ppermute | solution.py:26
  13.0 0.4 collective-permute-start
  13.5 0.7 constant_dynamic-update-slice_fusion.3
  14.2 21.6 %collective-permute-done = s32[128,8]{0,1:T(8,128)S(1)} collective-permute-done((s32[128,8]{0,1:T(8,128)}, s32[128,8]{0,1:T(8,128)S(1)}, u32[]{:S(2)}, u32[]{:S(2)}) %collective-permute-start) | collective-permute-done | bytes 4128 | tf_op jit(solution)/shard_map/ppermute | solution.py:27
  35.8 4.2 %collective-permute-start.1 = (s32[128,8]{0,1:T(8,128)S(1)}, s32[128,8]{0,1:T(8,128)S(1)}, u32[]{:S(2)}, u32[]{:S(2)}) collective-permute-start(s32[128,8]{0,1:T(8,128)S(1)} %collective-permute-done), channel_id=1, source_target_pairs={{0,3},{1,0},{2,1},{3,2},{4,7},{5,4},{6,5},{7,6},{8,11},{9,8},{10,9... | collective-permute-start | bytes 12296 | tf_op jit(solution)/shard_map/ppermute | solution.py:27
  40.0 0.0 collective-permute-done.3
  40.0 0.1 collective-permute-start.4
  40.1 1.3 collective-permute-done.1
  41.4 4.2 %collective-permute-start.2 = (s32[128,8]{0,1:T(8,128)S(1)}, s32[128,8]{0,1:T(8,128)S(1)}, u32[]{:S(2)}, u32[]{:S(2)}) collective-permute-start(s32[128,8]{0,1:T(8,128)S(1)} %collective-permute-done.1), channel_id=1, source_target_pairs={{0,3},{1,0},{2,1},{3,2},{4,7},{5,4},{6,5},{7,6},{8,11},{9,8},{10,9... | collective-permute-start | bytes 12296 | tf_op jit(solution)/shard_map/ppermute | solution.py:27
  45.6 18.3 %collective-permute-done.2 = s32[128,8]{0,1:T(8,128)S(1)} collective-permute-done((s32[128,8]{0,1:T(8,128)S(1)}, s32[128,8]{0,1:T(8,128)S(1)}, u32[]{:S(2)}, u32[]{:S(2)}) %collective-permute-start.2) | collective-permute-done | bytes 4128 | tf_op jit(solution)/shard_map/ppermute | solution.py:27
  63.9 0.2 copy.26
  64.1 0.2 and.80
  64.3 0.1 copy.27
  64.4 0.2 div.35
  64.7 0.0 collective-permute-done.4
  64.7 0.0 copy-start.6
  64.7 2.2 %collective-permute-start.5 = (bf16[128,4096]{1,0:T(8,128)(2,1)S(1)}, bf16[128,4096]{1,0:T(8,128)(2,1)S(1)}, u32[]{:S(2)}, u32[]{:S(2)}) collective-permute-start(bf16[128,4096]{1,0:T(8,128)(2,1)S(1)} %collective-permute-done.4), channel_id=1, source_target_pairs={{0,3},{1,0},{2,1},{3,2},{4,7},{5,4},{6,5},{7,6},{8,11},{9,8},{10,9... | collective-permute-start | bytes 3145736 | tf_op jit(solution)/shard_map/ppermute | solution.py:26
  66.9 4.8 %fusion.38 = f32[128,704]{0,1:T(8,128)S(1)} fusion(bf16[128,4096]{1,0:T(8,128)(2,1)} %param.4, bf16[704,4096]{1,0:T(8,128)(2,1)} %all-gather.4.cloned.1.call-done), kind=kOutput, calls=%fused_computation.87 | convolution fusion | flops 738197504 | bytes 7176192 | tf_op jit(solution)/shard_map/dot_general | solution.py:39
  71.7 1.7 fusion.39
  73.4 0.0 copy-done.4
  73.4 0.0 copy-done.6
  73.4 1.7 fusion.40
  75.1 0.0 copy-start.10
  75.1 0.0 copy-start.3
  75.1 12.5 %collective-permute-done.5 = bf16[128,4096]{1,0:T(8,128)(2,1)S(1)} collective-permute-done((bf16[128,4096]{1,0:T(8,128)(2,1)S(1)}, bf16[128,4096]{1,0:T(8,128)(2,1)S(1)}, u32[]{:S(2)}, u32[]{:S(2)}) %collective-permute-start.5) | collective-permute-done | bytes 1048608 | tf_op jit(solution)/shard_map/ppermute | solution.py:26
  87.6 1.0 copy-done.8
  88.6 1.7 fusion.41
  90.2 0.1 maximum_multiply_fusion
  90.3 0.1 slice_reduce_fusion
  90.4 2.7 %select_reduce_fusion.1 = f32[512,8]{0,1:T(8,128)S(1)} fusion(f32[512,704]{0,1:T(8,128)S(1)} %maximum_multiply_fusion, s32[512,8]{0,1:T(8,128)S(1)} %get-tuple-element.8, pred[512,8]{0,1:T(8,128)(4,1)S(1)} %get-tuple-element.5), kind=kLoop, calls=%fused_computation.2 | loop fusion | flops 11530240 | bytes 1478656 | tf_op jit(solution)/shard_map/reduce_sum | solution.py:54
  93.1 0.1 copy.25
  93.2 0.2 reshape.312
  93.5 0.1 exponential_reduce_fusion
  93.6 13.8 %all-gather.1 = f32[4,1,4352]{2,1,0:T(1,128)S(1)} all-gather(f32[1,1,4352]{2,1,0:T(1,128)S(1)} %reshape.317), channel_id=2, replica_groups=mesh['blk'=8,'slab'=4] {'slab'}, dimensions={0}, use_global_device_ids=true | all-gather | bytes 87040 | tf_op jit(solution)/shard_map/all_gather | solution.py:60
  107.4 0.1 fusion.17
  107.6 0.2 reshape.315
  107.8 0.1 reduce_max.19
  107.9 0.2 exponential_reduce_fusion.1
  108.2 0.5 fusion.37
  108.7 2.8 %select_reduce_fusion = bf16[512,704]{0,1:T(8,128)(2,1)S(1)} fusion(f32[512,8]{0,1:T(8,128)S(1)} %fusion.30, s32[512,8]{0,1:T(8,128)S(1)} %get-tuple-element.8, pred[512,8]{0,1:T(8,128)(4,1)S(1)} %get-tuple-element.5), kind=kLoop, calls=%fused_computation.1 | loop fusion | flops 11173888 | bytes 757760 | tf_op jit(solution)/shard_map/reduce_sum | solution.py:92
  111.6 0.0 copy-start.7
  111.6 0.0 copy-start.9
  111.6 1.7 fusion.33
  113.2 0.0 copy-done.1
  113.3 0.1 copy-done.7
  113.3 0.3 copy-done.9
  113.7 4.9 %add_convert_fusion = bf16[704,4096]{1,0:T(8,128)(2,1)} fusion(f32[704,4096]{1,0:T(8,128)S(1)} %fusion.33, bf16[512,704]{0,1:T(8,128)(2,1)S(1)} %select_reduce_fusion, bf16[128,4096]{1,0:T(8,128)(2,1)S(1)} %copy-done.9, bf16[128,4096]{1,0:T(8,128)(2,1)S(1)} %copy-done.7, bf16[128,4096]{1,0:T(8,128)(2,1)S(1)} %copy-done.5, bf16[128,4096]{1,0:T(8,128)(2,1)S(1)} %copy-done.3), kind=kOutput, calls=%fused_computation | convolution fusion | flops 2975334400 | bytes 22216704 | tf_op jit(solution)/shard_map/dot_general | solution.py:110
  118.6 0.0 reduce-scatter.2.cloned.1.call-update
  118.6 0.0 slice-start.1
  118.6 3.9 %convolution_convert_fusion = bf16[128,4096]{1,0:T(8,128)(2,1)S(1)} fusion(bf16[704,4096]{1,0:T(8,128)(2,1)} %all-gather.4.cloned.1.call-done, bf16[512,704]{0,1:T(8,128)(2,1)} %copy-done.1), kind=kOutput, calls=%fused_computation.5 | convolution fusion | flops 738721792 | bytes 6995968 | tf_op jit(solution)/shard_map/dot_general | solution.py:98
  122.5 3.9 %collective-permute-start.6 = (bf16[128,4096]{1,0:T(8,128)(2,1)S(1)}, bf16[128,4096]{1,0:T(8,128)(2,1)S(1)}, u32[]{:S(2)}, u32[]{:S(2)}) collective-permute-start(bf16[128,4096]{1,0:T(8,128)(2,1)S(1)} %convolution_convert_fusion), channel_id=1, source_target_pairs={{0,3},{1,0},{2,1},{3,2},{4,7},{5,4},{6,5},{7,6},{8,11},{9,8},{10,9... | collective-permute-start | bytes 3145736 | tf_op jit(solution)/shard_map/ppermute | solution.py:102
  126.4 17.9 %collective-permute-done.6 = bf16[128,4096]{1,0:T(8,128)(2,1)S(1)} collective-permute-done((bf16[128,4096]{1,0:T(8,128)(2,1)S(1)}, bf16[128,4096]{1,0:T(8,128)(2,1)S(1)}, u32[]{:S(2)}, u32[]{:S(2)}) %collective-permute-start.6) | collective-permute-done | bytes 1048608 | tf_op jit(solution)/shard_map/ppermute | solution.py:102
  144.4 1.0 add_convert_fusion.2
  145.4 4.3 %collective-permute-start.7 = (bf16[128,4096]{1,0:T(8,128)(2,1)S(1)}, bf16[128,4096]{1,0:T(8,128)(2,1)S(1)}, u32[]{:S(2)}, u32[]{:S(2)}) collective-permute-start(bf16[128,4096]{1,0:T(8,128)(2,1)S(1)} %add_convert_fusion.2), channel_id=1, source_target_pairs={{0,3},{1,0},{2,1},{3,2},{4,7},{5,4},{6,5},{7,6},{8,11},{9,8},{10,9... | collective-permute-start | bytes 3145736 | tf_op jit(solution)/shard_map/ppermute | solution.py:102
  149.7 18.0 %collective-permute-done.7 = bf16[128,4096]{1,0:T(8,128)(2,1)S(1)} collective-permute-done((bf16[128,4096]{1,0:T(8,128)(2,1)S(1)}, bf16[128,4096]{1,0:T(8,128)(2,1)S(1)}, u32[]{:S(2)}, u32[]{:S(2)}) %collective-permute-start.7) | collective-permute-done | bytes 1048608 | tf_op jit(solution)/shard_map/ppermute | solution.py:102
  167.7 1.0 add_convert_fusion.1
  168.7 4.3 %collective-permute-start.8 = (bf16[128,4096]{1,0:T(8,128)(2,1)S(1)}, bf16[128,4096]{1,0:T(8,128)(2,1)S(1)}, u32[]{:S(2)}, u32[]{:S(2)}) collective-permute-start(bf16[128,4096]{1,0:T(8,128)(2,1)S(1)} %add_convert_fusion.1), channel_id=1, source_target_pairs={{0,3},{1,0},{2,1},{3,2},{4,7},{5,4},{6,5},{7,6},{8,11},{9,8},{10,9... | collective-permute-start | bytes 3145736 | tf_op jit(solution)/shard_map/ppermute | solution.py:102
  173.1 1.0 fusion.34
  174.1 14.1 %collective-permute-done.8 = bf16[128,4096]{1,0:T(8,128)(2,1)S(1)} collective-permute-done((bf16[128,4096]{1,0:T(8,128)(2,1)S(1)}, bf16[128,4096]{1,0:T(8,128)(2,1)S(1)}, u32[]{:S(2)}, u32[]{:S(2)}) %collective-permute-start.8) | collective-permute-done | bytes 1048608 | tf_op jit(solution)/shard_map/ppermute | solution.py:102
  188.2 2.4 %add_add_fusion = f32[128,4096]{1,0:T(8,128)} fusion(f32[128,4096]{1,0:T(8,128)S(1)} %fusion.34, bf16[128,4096]{1,0:T(8,128)(2,1)S(1)} %collective-permute-done.8, bf16[704,4096]{1,0:T(8,128)(2,1)S(1)} %bitcast.31, bf16[512,704]{0,1:T(8,128)(2,1)S(1)} %copy-done.2), kind=kOutput, calls=%fused_computation.13 | convolution fusion | flops 739770368 | bytes 11190272 | tf_op jit(solution)/shard_map/dot_general | solution.py:98
  190.6 2.3 %convert_element_type.59 = f32[88,4096]{1,0:T(8,128)} convert(bf16[88,4096]{1,0:T(8,128)(2,1)} %reduce-scatter.2.cloned.1.call-done) | non-fusion elementwise | flops 360448 | bytes 2162688 | tf_op jit(solution)/shard_map/convert_element_type | solution.py:113
  (39 shorter events, 0.3 us)
Async XLA Ops:
  7.2 59.8 %all-gather.4.cloned.1.call-start = ((), (), s32[]{:S(2)}) async-start(), calls=%async_computation.1 | async-start | bytes 6488064 | tf_op jit(solution)/shard_map/all_gather | solution.py:19
  7.9 182.7 %reduce-scatter.2.cloned.1.call-start = ((), (), s32[]{:S(2)}) async-start(), calls=%async_computation.2 | async-start | bytes 6488064 | tf_op jit(solution)/shard_map/reduce_scatter | solution.py:111
  7.9 32.1 %collective-permute-start.3 = (bf16[128,4096]{1,0:T(8,128)(2,1)}, bf16[128,4096]{1,0:T(8,128)(2,1)S(1)}, u32[]{:S(2)}, u32[]{:S(2)}) collective-permute-start(bf16[128,4096]{1,0:T(8,128)(2,1)} %param.4), channel_id=1, source_target_pairs={{0,3},{1,0},{2,1},{3,2},{4,7},{5,4},{6,5},{7,6},{8,11},{9,8},{10,9... | collective-permute-start | bytes 3145736 | tf_op jit(solution)/shard_map/ppermute | solution.py:26
  13.0 22.8 %collective-permute-start = (s32[128,8]{0,1:T(8,128)}, s32[128,8]{0,1:T(8,128)S(1)}, u32[]{:S(2)}, u32[]{:S(2)}) collective-permute-start(s32[128,8]{0,1:T(8,128)} %param.7), channel_id=1, source_target_pairs={{0,3},{1,0},{2,1},{3,2},{4,7},{5,4},{6,5},{7,6},{8,11},{9,8},{10,9... | collective-permute-start | bytes 12296 | tf_op jit(solution)/shard_map/ppermute | solution.py:27
  35.8 5.5 %collective-permute-start.1 = (s32[128,8]{0,1:T(8,128)S(1)}, s32[128,8]{0,1:T(8,128)S(1)}, u32[]{:S(2)}, u32[]{:S(2)}) collective-permute-start(s32[128,8]{0,1:T(8,128)S(1)} %collective-permute-done), channel_id=1, source_target_pairs={{0,3},{1,0},{2,1},{3,2},{4,7},{5,4},{6,5},{7,6},{8,11},{9,8},{10,9... | collective-permute-start | bytes 12296 | tf_op jit(solution)/shard_map/ppermute | solution.py:27
  40.0 33.3 %copy-start.4 = (bf16[128,4096]{1,0:T(8,128)(2,1)}, bf16[128,4096]{1,0:T(8,128)(2,1)S(1)}, u32[]{:S(2)}) copy-start(bf16[128,4096]{1,0:T(8,128)(2,1)S(1)} %collective-permute-done.3) | copy-start | bytes 3145732
  40.0 24.6 %collective-permute-start.4 = (bf16[128,4096]{1,0:T(8,128)(2,1)S(1)}, bf16[128,4096]{1,0:T(8,128)(2,1)S(1)}, u32[]{:S(2)}, u32[]{:S(2)}) collective-permute-start(bf16[128,4096]{1,0:T(8,128)(2,1)S(1)} %collective-permute-done.3), channel_id=1, source_target_pairs={{0,3},{1,0},{2,1},{3,2},{4,7},{5,4},{6,5},{7,6},{8,11},{9,8},{10,9... | collective-permute-start | bytes 3145736 | tf_op jit(solution)/shard_map/ppermute | solution.py:26
  41.4 22.5 %collective-permute-start.2 = (s32[128,8]{0,1:T(8,128)S(1)}, s32[128,8]{0,1:T(8,128)S(1)}, u32[]{:S(2)}, u32[]{:S(2)}) collective-permute-start(s32[128,8]{0,1:T(8,128)S(1)} %collective-permute-done.1), channel_id=1, source_target_pairs={{0,3},{1,0},{2,1},{3,2},{4,7},{5,4},{6,5},{7,6},{8,11},{9,8},{10,9... | collective-permute-start | bytes 12296 | tf_op jit(solution)/shard_map/ppermute | solution.py:27
  64.7 8.7 %copy-start.6 = (bf16[128,4096]{1,0:T(8,128)(2,1)}, bf16[128,4096]{1,0:T(8,128)(2,1)S(1)}, u32[]{:S(2)}) copy-start(bf16[128,4096]{1,0:T(8,128)(2,1)S(1)} %collective-permute-done.4) | copy-start | bytes 3145732
  64.7 22.9 %collective-permute-start.5 = (bf16[128,4096]{1,0:T(8,128)(2,1)S(1)}, bf16[128,4096]{1,0:T(8,128)(2,1)S(1)}, u32[]{:S(2)}, u32[]{:S(2)}) collective-permute-start(bf16[128,4096]{1,0:T(8,128)(2,1)S(1)} %collective-permute-done.4), channel_id=1, source_target_pairs={{0,3},{1,0},{2,1},{3,2},{4,7},{5,4},{6,5},{7,6},{8,11},{9,8},{10,9... | collective-permute-start | bytes 3145736 | tf_op jit(solution)/shard_map/ppermute | solution.py:26
  66.9 4.8 %copy-start = (bf16[704,4096]{1,0:T(8,128)(2,1)S(1)}, bf16[704,4096]{1,0:T(8,128)(2,1)}, u32[]{:S(2)}) copy-start(bf16[704,4096]{1,0:T(8,128)(2,1)} %all-gather.4.cloned.1.call-done) | copy-start | bytes 17301508
  75.1 18.4 %copy-start.10 = (s32[128]{0:T(128)S(1)}, s32[128]{0:T(128)}, u32[]{:S(2)}) copy-start(s32[128]{0:T(128)} %param.6) | copy-start | bytes 1540
  75.1 36.5 %copy-start.3 = (bf16[128,4096]{1,0:T(8,128)(2,1)S(1)}, bf16[128,4096]{1,0:T(8,128)(2,1)}, u32[]{:S(2)}) copy-start(bf16[128,4096]{1,0:T(8,128)(2,1)} %param.4) | copy-start | bytes 3145732
  87.6 1.0 copy-start.8
  111.5 1.7 copy-start.1
  111.5 1.7 copy-start.5
  111.6 1.8 copy-start.7
  111.6 2.1 %copy-start.9 = (bf16[128,4096]{1,0:T(8,128)(2,1)S(1)}, bf16[128,4096]{1,0:T(8,128)(2,1)}, u32[]{:S(2)}) copy-start(bf16[128,4096]{1,0:T(8,128)(2,1)} %copy-done.8) | copy-start | bytes 3145732
  118.6 25.7 %slice-start = ((s8[5767168]{0:T(1024)(128)(4,1)}), s8[1572864]{0:T(1024)(128)(4,1)S(1)}, s32[]{:S(2)}) async-start(s8[5767168]{0:T(1024)(128)(4,1)} %bitcast.30), calls=%async_computation.3 | async-start | bytes 3145728
  118.6 25.7 %slice-start.1 = ((s8[5767168]{0:T(1024)(128)(4,1)}), s8[4194304]{0:T(1024)(128)(4,1)S(1)}, s32[]{:S(2)}) async-start(s8[5767168]{0:T(1024)(128)(4,1)} %bitcast.30), calls=%async_computation.4 | async-start | bytes 8388608
  118.6 25.7 %copy-start.2 = (bf16[512,704]{0,1:T(8,128)(2,1)S(1)}, bf16[512,704]{0,1:T(8,128)(2,1)}, u32[]{:S(2)}) copy-start(bf16[512,704]{0,1:T(8,128)(2,1)} %copy-done.1) | copy-start | bytes 2162692
  122.5 21.8 %collective-permute-start.6 = (bf16[128,4096]{1,0:T(8,128)(2,1)S(1)}, bf16[128,4096]{1,0:T(8,128)(2,1)S(1)}, u32[]{:S(2)}, u32[]{:S(2)}) collective-permute-start(bf16[128,4096]{1,0:T(8,128)(2,1)S(1)} %convolution_convert_fusion), channel_id=1, source_target_pairs={{0,3},{1,0},{2,1},{3,2},{4,7},{5,4},{6,5},{7,6},{8,11},{9,8},{10,9... | collective-permute-start | bytes 3145736 | tf_op jit(solution)/shard_map/ppermute | solution.py:102
  145.4 22.3 %collective-permute-start.7 = (bf16[128,4096]{1,0:T(8,128)(2,1)S(1)}, bf16[128,4096]{1,0:T(8,128)(2,1)S(1)}, u32[]{:S(2)}, u32[]{:S(2)}) collective-permute-start(bf16[128,4096]{1,0:T(8,128)(2,1)S(1)} %add_convert_fusion.2), channel_id=1, source_target_pairs={{0,3},{1,0},{2,1},{3,2},{4,7},{5,4},{6,5},{7,6},{8,11},{9,8},{10,9... | collective-permute-start | bytes 3145736 | tf_op jit(solution)/shard_map/ppermute | solution.py:102
  168.7 19.4 %collective-permute-start.8 = (bf16[128,4096]{1,0:T(8,128)(2,1)S(1)}, bf16[128,4096]{1,0:T(8,128)(2,1)S(1)}, u32[]{:S(2)}, u32[]{:S(2)}) collective-permute-start(bf16[128,4096]{1,0:T(8,128)(2,1)S(1)} %add_convert_fusion.1), channel_id=1, source_target_pairs={{0,3},{1,0},{2,1},{3,2},{4,7},{5,4},{6,5},{7,6},{8,11},{9,8},{10,9... | collective-permute-start | bytes 3145736 | tf_op jit(solution)/shard_map/ppermute | solution.py:102
Sparse Core Ops, SparseCore 0:
  9.9 46.0 all-gather.3
  118.7 60.5 reduce-scatter.1

commit v5 on v4

--- a/solution.py
+++ b/solution.py
@@ -20,11 +20,19 @@
     pool_size = pool.shape[0]
 
     ring_down = [(i, (i - 1) % slabs) for i in range(slabs)]
-    query_blocks = [queries]
-    id_blocks = [hard_ids]
-    for _ in range(slabs - 1):
-        query_blocks.append(lax.ppermute(query_blocks[-1], "slab", ring_down))
-        id_blocks.append(lax.ppermute(id_blocks[-1], "slab", ring_down))
+    chunks = 2
+    chunk_rows = query_rows_dev // chunks
+
+    def ring_gather(x):
+        parts = [x[c * chunk_rows : (c + 1) * chunk_rows] for c in range(chunks)]
+        blocks = [x]
+        for _ in range(slabs - 1):
+            parts = [lax.ppermute(part, "slab", ring_down) for part in parts]
+            blocks.append(jnp.concatenate(parts, axis=0))
+        return blocks
+
+    query_blocks = ring_gather(queries)
+    id_blocks = ring_gather(hard_ids)
 
     def to_origin(x):
         doubled = jnp.concatenate([x, x], axis=0)
@@ -97,10 +105,18 @@
         rows = hard_matrix[block * query_rows_dev : (block + 1) * query_rows_dev]
         return jnp.dot(rows, pool, preferred_element_type=jnp.float32)
 
-    carried = grad_for(1)
+    def chunk_of(x, c):
+        return x[c * chunk_rows : (c + 1) * chunk_rows]
+
+    carried = [chunk_of(grad_for(1), c) for c in range(chunks)]
     for step in range(1, slabs):
-        carried = lax.ppermute(carried.astype(jnp.bfloat16), "slab", ring_down).astype(jnp.float32)
-        carried = carried + grad_for((step + 1) % slabs)
+        nxt = grad_for((step + 1) % slabs)
+        carried = [
+            lax.ppermute(part.astype(jnp.bfloat16), "slab", ring_down).astype(jnp.float32)
+            + chunk_of(nxt, c)
+            for c, part in enumerate(carried)
+        ]
+    carried = jnp.concatenate(carried, axis=0)
     pool_grad = jnp.dot(coef_pool, pool, preferred_element_type=jnp.float32)
     query_grad = pool_grad + carried
 

time: 200 us -> 212 us (1.060)
  local copies, waits for them, and re-layouts: 3.3 us -> 13.4 us
  starting transfers between devices: 28.9 us -> 37.7 us
  waiting for transfers between devices: 104 us -> 97.6 us
    ppermute x9 -> x18, starting transfers between devices: 28.8 us -> 37.6 us  [the longest x12 24.9 us: ring_gather(): parts = [lax.ppermute(part, 'slab', ring_down) for part in parts]]
    ppermute x9 -> x18, waiting for transfers between devices: 104 us -> 96.9 us  [the longest x6 49.2 us: per_device(): lax.ppermute(part.astype(jnp.bfloat16), 'slab', ring_down)]
    unnamed x33 -> x36, local copies, waits for them, and re-layouts: 2.19 us -> 8.26 us
    slice x0 -> x3, local copies, waits for them, and re-layouts: none -> 3.09 us  [the longest x2 3 us: ring_gather(): parts = [x[c * chunk_rows:(c + 1) * chunk_rows] for c in range(chunks)]]
  transfers between devices with their start and end apart: 11 -> 20, of which waited for: 7 -> 12; matrix products, arithmetic and copies ran while one was open for 9% -> 10% of each run, Pallas kernels for 0% -> 0%
where the time goes in v5:
time: 212 us
  waiting for transfers between devices  97.6 us (46%)
  starting transfers between devices  37.7 us (18%)
  matrix products  25.4 us (12%)
  between operations  14.4 us (7%)
  blocking collectives  13.7 us (6%)
  local copies, waits for them, and re-layouts  13.4 us (6%)
  other arithmetic  9.96 us (5%)
    ppermute x6, waiting for transfers between devices, per_device(): lax.ppermute(part.astype(jnp.bfloat16), 'slab', ring_down)  49.2 us
    ppermute x12, waiting for transfers between devices, ring_gather(): parts = [lax.ppermute(part, 'slab', ring_down) for part in parts]  47.7 us
    ppermute x12, starting transfers between devices, ring_gather(): parts = [lax.ppermute(part, 'slab', ring_down) for part in parts]  24.9 us
    all_gather x1, blocking collectives, per_device(): gathered = lax.all_gather(payload, 'slab', axis=0)  13.7 us
    ppermute x6, starting transfers between devices, per_device(): lax.ppermute(part.astype(jnp.bfloat16), 'slab', ring_down)  12.7 us
    dot_general x4, matrix products, per_device(): lax.dot_general(block, pool, contract_rows, preferred_element_type=jnp.fl...  9.43 us
    unnamed x36, local copies, waits for them, and re-layouts  8.26 us
    dot_general x4, matrix products, grad_for(): return jnp.dot(rows, pool, preferred_element_type=jnp.float32)  6.94 us
  transfers between devices with their start and end apart: 20, of which 12 were waited for; matrix products, arithmetic and copies ran while one was open for 10% of the time, Pallas kernels for 0%

profile of v5, /device:TPU:0, one launch (start us, length us, event | category | flops | bytes accessed | tf_op | source)
XLA Modules:
  0.0 212.2 jit_solution(10776105315410266461)
XLA Ops:
  7.2 0.7 all-gather.4.cloned.1.call-update
  8.0 0.8 fusion.48
  8.8 5.0 %collective-permute-start.1 = (s32[64,8]{0,1:T(8,128)S(1)}, s32[64,8]{0,1:T(8,128)S(1)}, u32[]{:S(2)}, u32[]{:S(2)}) collective-permute-start(s32[64,8]{0,1:T(8,128)S(1)} %get-tuple-element.21), channel_id=1, source_target_pairs={{0,3},{1,0},{2,1},{3,2},{4,7},{5,4},{6,5},{7,6},{8,11},{9,8},{10,9... | collective-permute-start | bytes 6152 | tf_op jit(solution)/shard_map/ppermute | solution.py:30
  13.8 0.4 collective-permute-start
  14.3 0.9 collective-permute-done.1
  15.2 4.1 %collective-permute-start.3 = (s32[64,8]{0,1:T(8,128)S(1)}, s32[64,8]{0,1:T(8,128)S(1)}, u32[]{:S(2)}, u32[]{:S(2)}) collective-permute-start(s32[64,8]{0,1:T(8,128)S(1)} %collective-permute-done.1), channel_id=1, source_target_pairs={{0,3},{1,0},{2,1},{3,2},{4,7},{5,4},{6,5},{7,6},{8,11},{9,8},{10,9... | collective-permute-start | bytes 6152 | tf_op jit(solution)/shard_map/ppermute | solution.py:30
  19.2 0.4 collective-permute-start.2
  19.7 2.2 %fusion.46 = (bf16[64,4096]{1,0:T(8,128)(2,1)}, bf16[64,4096]{1,0:T(8,128)(2,1)S(1)}) fusion(bf16[128,4096]{1,0:T(8,128)(2,1)} %param.4), kind=kLoop, calls=%fused_computation.104 | loop fusion | bytes 2097152 | tf_op jit(solution)/shard_map/slice | solution.py:27
  21.9 0.3 collective-permute-start.7
  22.2 4.2 %collective-permute-start.5 = (s32[64,8]{0,1:T(8,128)S(1)}, s32[64,8]{0,1:T(8,128)S(1)}, u32[]{:S(2)}, u32[]{:S(2)}) collective-permute-start(s32[64,8]{0,1:T(8,128)S(1)} %collective-permute-done.3), channel_id=1, source_target_pairs={{0,3},{1,0},{2,1},{3,2},{4,7},{5,4},{6,5},{7,6},{8,11},{9,8},{10,9... | collective-permute-start | bytes 6152 | tf_op jit(solution)/shard_map/ppermute | solution.py:30
  26.4 0.4 collective-permute-start.4
  26.8 2.3 %constant_dynamic-update-slice_fusion.6 = bf16[512,4096]{1,0:T(8,128)(2,1)} fusion(bf16[128,4096]{1,0:T(8,128)(2,1)} %param.4), kind=kLoop, calls=%fused_computation.82 | loop fusion | bytes 2097152
  29.1 16.2 %collective-permute-done.5 = s32[64,8]{0,1:T(8,128)S(1)} collective-permute-done((s32[64,8]{0,1:T(8,128)S(1)}, s32[64,8]{0,1:T(8,128)S(1)}, u32[]{:S(2)}, u32[]{:S(2)}) %collective-permute-start.5) | collective-permute-done | bytes 2080 | tf_op jit(solution)/shard_map/ppermute | solution.py:30
  45.5 0.2 copy.26
  45.7 0.2 and.80
  45.9 0.1 copy.27
  46.0 0.2 div.35
  46.3 2.1 %collective-permute-start.8 = (bf16[64,4096]{1,0:T(8,128)(2,1)S(1)}, bf16[64,4096]{1,0:T(8,128)(2,1)S(1)}, u32[]{:S(2)}, u32[]{:S(2)}) collective-permute-start(bf16[64,4096]{1,0:T(8,128)(2,1)S(1)} %collective-permute-done.6), channel_id=1, source_target_pairs={{0,3},{1,0},{2,1},{3,2},{4,7},{5,4},{6,5},{7,6},{8,11},{9,8},{10,9... | collective-permute-start | bytes 1572872 | tf_op jit(solution)/shard_map/ppermute | solution.py:30
  48.5 0.8 constant_dynamic-update-slice_fusion.5
  49.3 0.8 constant_dynamic-update-slice_fusion.4
  50.1 11.1 %collective-permute-done.8 = bf16[64,4096]{1,0:T(8,128)(2,1)S(1)} collective-permute-done((bf16[64,4096]{1,0:T(8,128)(2,1)S(1)}, bf16[64,4096]{1,0:T(8,128)(2,1)S(1)}, u32[]{:S(2)}, u32[]{:S(2)}) %collective-permute-start.8) | collective-permute-done | bytes 524320 | tf_op jit(solution)/shard_map/ppermute | solution.py:30
  61.2 3.9 %collective-permute-start.10 = (bf16[64,4096]{1,0:T(8,128)(2,1)S(1)}, bf16[64,4096]{1,0:T(8,128)(2,1)S(1)}, u32[]{:S(2)}, u32[]{:S(2)}) collective-permute-start(bf16[64,4096]{1,0:T(8,128)(2,1)S(1)} %collective-permute-done.8), channel_id=1, source_target_pairs={{0,3},{1,0},{2,1},{3,2},{4,7},{5,4},{6,5},{7,6},{8,11},{9,8},{10,9... | collective-permute-start | bytes 1572872 | tf_op jit(solution)/shard_map/ppermute | solution.py:30
  65.1 7.4 %collective-permute-done.9 = bf16[64,4096]{1,0:T(8,128)(2,1)S(1)} collective-permute-done((bf16[64,4096]{1,0:T(8,128)(2,1)S(1)}, bf16[64,4096]{1,0:T(8,128)(2,1)S(1)}, u32[]{:S(2)}, u32[]{:S(2)}) %collective-permute-start.9) | collective-permute-done | bytes 524320 | tf_op jit(solution)/shard_map/ppermute | solution.py:30
  72.4 3.9 %collective-permute-start.11 = (bf16[64,4096]{1,0:T(8,128)(2,1)S(1)}, bf16[64,4096]{1,0:T(8,128)(2,1)S(1)}, u32[]{:S(2)}, u32[]{:S(2)}) collective-permute-start(bf16[64,4096]{1,0:T(8,128)(2,1)S(1)} %collective-permute-done.9), channel_id=1, source_target_pairs={{0,3},{1,0},{2,1},{3,2},{4,7},{5,4},{6,5},{7,6},{8,11},{9,8},{10,9... | collective-permute-start | bytes 1572872 | tf_op jit(solution)/shard_map/ppermute | solution.py:30
  76.3 0.9 constant_dynamic-update-slice_fusion.3
  77.2 0.9 constant_dynamic-update-slice_fusion.2
  78.1 5.6 %collective-permute-done.10 = bf16[64,4096]{1,0:T(8,128)(2,1)S(1)} collective-permute-done((bf16[64,4096]{1,0:T(8,128)(2,1)S(1)}, bf16[64,4096]{1,0:T(8,128)(2,1)S(1)}, u32[]{:S(2)}, u32[]{:S(2)}) %collective-permute-start.10) | collective-permute-done | bytes 524320 | tf_op jit(solution)/shard_map/ppermute | solution.py:30
  83.7 0.9 constant_dynamic-update-slice_fusion.1
  84.6 6.6 %collective-permute-done.11 = bf16[64,4096]{1,0:T(8,128)(2,1)S(1)} collective-permute-done((bf16[64,4096]{1,0:T(8,128)(2,1)S(1)}, bf16[64,4096]{1,0:T(8,128)(2,1)S(1)}, u32[]{:S(2)}, u32[]{:S(2)}) %collective-permute-start.11) | collective-permute-done | bytes 524320 | tf_op jit(solution)/shard_map/ppermute | solution.py:30
  91.1 0.8 copy-done.6
  91.9 0.8 constant_dynamic-update-slice_fusion
  92.8 4.4 %fusion.50 = f32[128,704]{0,1:T(8,128)S(1)} fusion(bf16[128,4096]{1,0:T(8,128)(2,1)S(1)} %copy-done.1, bf16[704,4096]{1,0:T(8,128)(2,1)} %all-gather.4.cloned.1.call-done), kind=kOutput, calls=%fused_computation.108 | convolution fusion | flops 738197504 | bytes 7176192 | tf_op jit(solution)/shard_map/dot_general | solution.py:47
  97.2 1.7 fusion.5
  98.9 1.7 fusion.9
  100.6 1.7 fusion.13
  102.5 2.7 %select_reduce_fusion.1 = f32[512,8]{0,1:T(8,128)S(1)} fusion(f32[512,704]{0,1:T(8,128)S(1)} %maximum_multiply_fusion, s32[512,8]{0,1:T(8,128)S(1)} %get-tuple-element.18, pred[512,8]{0,1:T(8,128)(4,1)S(1)} %get-tuple-element.5), kind=kLoop, calls=%fused_computation.2 | loop fusion | flops 11530240 | bytes 1478656 | tf_op jit(solution)/shard_map/reduce_sum | solution.py:62
  105.3 0.2 reshape.429
  105.7 13.7 %all-gather.1 = f32[4,1,4352]{2,1,0:T(1,128)S(1)} all-gather(f32[1,1,4352]{2,1,0:T(1,128)S(1)} %reshape.434), channel_id=2, replica_groups=mesh['blk'=8,'slab'=4] {'slab'}, dimensions={0}, use_global_device_ids=true | all-gather | bytes 87040 | tf_op jit(solution)/shard_map/all_gather | solution.py:68
  119.5 0.2 reshape.432
  119.7 0.1 reduce_max.19
  119.9 0.2 exponential_reduce_fusion.1
  120.1 0.5 fusion.49
  120.7 2.8 %select_reduce_fusion = bf16[512,704]{0,1:T(8,128)(2,1)S(1)} fusion(f32[512,8]{0,1:T(8,128)S(1)} %fusion.37, s32[512,8]{0,1:T(8,128)S(1)} %get-tuple-element.18, pred[512,8]{0,1:T(8,128)(4,1)S(1)} %get-tuple-element.5), kind=kLoop, calls=%fused_computation.1 | loop fusion | flops 11173888 | bytes 757760 | tf_op jit(solution)/shard_map/reduce_sum | solution.py:100
  123.5 1.7 fusion.42
  125.1 0.8 copy-done.8
  125.9 5.0 %add_convert_fusion = bf16[704,4096]{1,0:T(8,128)(2,1)} fusion(f32[704,4096]{1,0:T(8,128)S(1)} %fusion.42, bf16[512,704]{0,1:T(8,128)(2,1)S(1)} %select_reduce_fusion, bf16[512,4096]{1,0:T(8,128)(2,1)S(1)} %copy-done.8), kind=kOutput, calls=%fused_computation | convolution fusion | flops 2958557184 | bytes 22216704 | tf_op jit(solution)/shard_map/dot_general | solution.py:126
  131.0 3.9 %convolution_convert_fusion = bf16[128,4096]{1,0:T(8,128)(2,1)S(1)} fusion(bf16[704,4096]{1,0:T(8,128)(2,1)} %all-gather.4.cloned.1.call-done, bf16[512,704]{0,1:T(8,128)(2,1)} %copy-done.2), kind=kOutput, calls=%fused_computation.5 | convolution fusion | flops 738721792 | bytes 6995968 | tf_op jit(solution)/shard_map/dot_general | solution.py:106
  135.0 3.8 %collective-permute-start.12 = (bf16[64,4096]{1,0:T(8,128)(2,1)S(1)}, bf16[64,4096]{1,0:T(8,128)(2,1)S(1)}, u32[]{:S(2)}, u32[]{:S(2)}) collective-permute-start(bf16[64,4096]{1,0:T(8,128)(2,1)S(1)} %get-tuple-element.13), channel_id=1, source_target_pairs={{0,3},{1,0},{2,1},{3,2},{4,7},{5,4},{6,5},{7,6},{8,11},{9,8},{10,9... | collective-permute-start | bytes 1572872 | tf_op jit(solution)/shard_map/ppermute | solution.py:115
  138.9 1.0 fusion.21
  139.9 9.9 %collective-permute-done.12 = bf16[64,4096]{1,0:T(8,128)(2,1)S(1)} collective-permute-done((bf16[64,4096]{1,0:T(8,128)(2,1)S(1)}, bf16[64,4096]{1,0:T(8,128)(2,1)S(1)}, u32[]{:S(2)}, u32[]{:S(2)}) %collective-permute-start.12) | collective-permute-done | bytes 524320 | tf_op jit(solution)/shard_map/ppermute | solution.py:115
  149.8 7.8 %collective-permute-done.15 = bf16[64,4096]{1,0:T(8,128)(2,1)S(1)} collective-permute-done((bf16[64,4096]{1,0:T(8,128)(2,1)S(1)}, bf16[64,4096]{1,0:T(8,128)(2,1)S(1)}, u32[]{:S(2)}, u32[]{:S(2)}) %collective-permute-start.15) | collective-permute-done | bytes 524320 | tf_op jit(solution)/shard_map/ppermute | solution.py:115
  157.6 0.2 fusion.4
  157.8 4.3 %collective-permute-start.13 = (bf16[64,4096]{1,0:T(8,128)(2,1)S(1)}, bf16[64,4096]{1,0:T(8,128)(2,1)S(1)}, u32[]{:S(2)}, u32[]{:S(2)}) collective-permute-start(bf16[64,4096]{1,0:T(8,128)(2,1)S(1)} %get-tuple-element.11), channel_id=1, source_target_pairs={{0,3},{1,0},{2,1},{3,2},{4,7},{5,4},{6,5},{7,6},{8,11},{9,8},{10,9... | collective-permute-start | bytes 1572872 | tf_op jit(solution)/shard_map/ppermute | solution.py:115
  162.2 1.0 fusion.19
  163.2 9.0 %collective-permute-done.13 = bf16[64,4096]{1,0:T(8,128)(2,1)S(1)} collective-permute-done((bf16[64,4096]{1,0:T(8,128)(2,1)S(1)}, bf16[64,4096]{1,0:T(8,128)(2,1)S(1)}, u32[]{:S(2)}, u32[]{:S(2)}) %collective-permute-start.13) | collective-permute-done | bytes 524320 | tf_op jit(solution)/shard_map/ppermute | solution.py:115
  172.2 8.7 %collective-permute-done.16 = bf16[64,4096]{1,0:T(8,128)(2,1)S(1)} collective-permute-done((bf16[64,4096]{1,0:T(8,128)(2,1)S(1)}, bf16[64,4096]{1,0:T(8,128)(2,1)S(1)}, u32[]{:S(2)}, u32[]{:S(2)}) %collective-permute-start.16) | collective-permute-done | bytes 524320 | tf_op jit(solution)/shard_map/ppermute | solution.py:115
  180.9 0.2 fusion.3
  181.1 4.3 %collective-permute-start.14 = (bf16[64,4096]{1,0:T(8,128)(2,1)S(1)}, bf16[64,4096]{1,0:T(8,128)(2,1)S(1)}, u32[]{:S(2)}, u32[]{:S(2)}) collective-permute-start(bf16[64,4096]{1,0:T(8,128)(2,1)S(1)} %get-tuple-element.9), channel_id=1, source_target_pairs={{0,3},{1,0},{2,1},{3,2},{4,7},{5,4},{6,5},{7,6},{8,11},{9,8},{10,9... | collective-permute-start | bytes 1572872 | tf_op jit(solution)/shard_map/ppermute | solution.py:115
  185.5 1.0 fusion.17
  186.5 8.2 %collective-permute-done.14 = bf16[64,4096]{1,0:T(8,128)(2,1)S(1)} collective-permute-done((bf16[64,4096]{1,0:T(8,128)(2,1)S(1)}, bf16[64,4096]{1,0:T(8,128)(2,1)S(1)}, u32[]{:S(2)}, u32[]{:S(2)}) %collective-permute-start.14) | collective-permute-done | bytes 524320 | tf_op jit(solution)/shard_map/ppermute | solution.py:115
  194.7 5.6 %collective-permute-done.17 = bf16[64,4096]{1,0:T(8,128)(2,1)S(1)} collective-permute-done((bf16[64,4096]{1,0:T(8,128)(2,1)S(1)}, bf16[64,4096]{1,0:T(8,128)(2,1)S(1)}, u32[]{:S(2)}, u32[]{:S(2)}) %collective-permute-start.17) | collective-permute-done | bytes 524320 | tf_op jit(solution)/shard_map/ppermute | solution.py:115
  200.3 0.2 slice_add_fusion.3
  200.6 2.4 %maximum_add_fusion = f32[128,4096]{1,0:T(8,128)} fusion(f32[64,4096]{1,0:T(8,128)S(1)} %get-tuple-element.8, f32[64,4096]{1,0:T(8,128)S(1)} %get-tuple-element.7, bf16[704,4096]{1,0:T(8,128)(2,1)S(1)} %bitcast.29, f32[512,704]{0,1:T(8,128)S(1)} %maximum_multiply_fusion, f32[128]{0:T(128)S(1)} %get-tuple-element.23, s32[128]{0:T(128)S(1)} %copy-done.10), kind=kOutput, calls=%fused_computation.6 | convolution fusion | flops 739696640 | bytes 10322944 | tf_op jit(solution)/shard_map/dot_general | solution.py:120
  203.0 2.3 %convert_element_type.77 = f32[88,4096]{1,0:T(8,128)} convert(bf16[88,4096]{1,0:T(8,128)(2,1)} %reduce-scatter.2.cloned.1.call-done) | non-fusion elementwise | flops 360448 | bytes 2162688 | tf_op jit(solution)/shard_map/convert_element_type | solution.py:129
  (67 shorter events, 1.5 us)
Async XLA Ops:
  7.2 38.2 %copy-start.9 = (s32[128,8]{0,1:T(8,128)S(1)}, s32[128,8]{0,1:T(8,128)}, u32[]{:S(2)}) copy-start(s32[128,8]{0,1:T(8,128)} %param.7) | copy-start | bytes 12292
  7.2 85.6 %all-gather.4.cloned.1.call-start = ((), (), s32[]{:S(2)}) async-start(), calls=%async_computation.1 | async-start | bytes 6488064 | tf_op jit(solution)/shard_map/all_gather | solution.py:19
  7.9 195.1 %reduce-scatter.2.cloned.1.call-start = ((), (), s32[]{:S(2)}) async-start(), calls=%async_computation.2 | async-start | bytes 6488064 | tf_op jit(solution)/shard_map/reduce_scatter | solution.py:127
  8.8 6.4 %collective-permute-start.1 = (s32[64,8]{0,1:T(8,128)S(1)}, s32[64,8]{0,1:T(8,128)S(1)}, u32[]{:S(2)}, u32[]{:S(2)}) collective-permute-start(s32[64,8]{0,1:T(8,128)S(1)} %get-tuple-element.21), channel_id=1, source_target_pairs={{0,3},{1,0},{2,1},{3,2},{4,7},{5,4},{6,5},{7,6},{8,11},{9,8},{10,9... | collective-permute-start | bytes 6152 | tf_op jit(solution)/shard_map/ppermute | solution.py:30
  13.8 5.4 %collective-permute-start = (s32[64,8]{0,1:T(8,128)S(1)}, s32[64,8]{0,1:T(8,128)S(1)}, u32[]{:S(2)}, u32[]{:S(2)}) collective-permute-start(s32[64,8]{0,1:T(8,128)S(1)} %get-tuple-element.22), channel_id=1, source_target_pairs={{0,3},{1,0},{2,1},{3,2},{4,7},{5,4},{6,5},{7,6},{8,11},{9,8},{10,9... | collective-permute-start | bytes 6152 | tf_op jit(solution)/shard_map/ppermute | solution.py:30
  15.2 7.0 %collective-permute-start.3 = (s32[64,8]{0,1:T(8,128)S(1)}, s32[64,8]{0,1:T(8,128)S(1)}, u32[]{:S(2)}, u32[]{:S(2)}) collective-permute-start(s32[64,8]{0,1:T(8,128)S(1)} %collective-permute-done.1), channel_id=1, source_target_pairs={{0,3},{1,0},{2,1},{3,2},{4,7},{5,4},{6,5},{7,6},{8,11},{9,8},{10,9... | collective-permute-start | bytes 6152 | tf_op jit(solution)/shard_map/ppermute | solution.py:30
  19.2 7.2 %collective-permute-start.2 = (s32[64,8]{0,1:T(8,128)S(1)}, s32[64,8]{0,1:T(8,128)S(1)}, u32[]{:S(2)}, u32[]{:S(2)}) collective-permute-start(s32[64,8]{0,1:T(8,128)S(1)} %collective-permute-done), channel_id=1, source_target_pairs={{0,3},{1,0},{2,1},{3,2},{4,7},{5,4},{6,5},{7,6},{8,11},{9,8},{10,9... | collective-permute-start | bytes 6152 | tf_op jit(solution)/shard_map/ppermute | solution.py:30
  21.9 24.4 %collective-permute-start.6 = (bf16[64,4096]{1,0:T(8,128)(2,1)}, bf16[64,4096]{1,0:T(8,128)(2,1)S(1)}, u32[]{:S(2)}, u32[]{:S(2)}) collective-permute-start(bf16[64,4096]{1,0:T(8,128)(2,1)} %get-tuple-element.15), channel_id=1, source_target_pairs={{0,3},{1,0},{2,1},{3,2},{4,7},{5,4},{6,5},{7,6},{8,11},{9,8},{10,9... | collective-permute-start | bytes 1572872 | tf_op jit(solution)/shard_map/ppermute | solution.py:30
  21.9 70.9 %copy-start.1 = (bf16[128,4096]{1,0:T(8,128)(2,1)S(1)}, bf16[128,4096]{1,0:T(8,128)(2,1)}, u32[]{:S(2)}) copy-start(bf16[128,4096]{1,0:T(8,128)(2,1)} %param.4) | copy-start | bytes 3145732
  21.9 26.6 %collective-permute-start.7 = (bf16[64,4096]{1,0:T(8,128)(2,1)S(1)}, bf16[64,4096]{1,0:T(8,128)(2,1)S(1)}, u32[]{:S(2)}, u32[]{:S(2)}) collective-permute-start(bf16[64,4096]{1,0:T(8,128)(2,1)S(1)} %get-tuple-element.16), channel_id=1, source_target_pairs={{0,3},{1,0},{2,1},{3,2},{4,7},{5,4},{6,5},{7,6},{8,11},{9,8},{10,9... | collective-permute-start | bytes 1572872 | tf_op jit(solution)/shard_map/ppermute | solution.py:30
  22.2 23.1 %collective-permute-start.5 = (s32[64,8]{0,1:T(8,128)S(1)}, s32[64,8]{0,1:T(8,128)S(1)}, u32[]{:S(2)}, u32[]{:S(2)}) collective-permute-start(s32[64,8]{0,1:T(8,128)S(1)} %collective-permute-done.3), channel_id=1, source_target_pairs={{0,3},{1,0},{2,1},{3,2},{4,7},{5,4},{6,5},{7,6},{8,11},{9,8},{10,9... | collective-permute-start | bytes 6152 | tf_op jit(solution)/shard_map/ppermute | solution.py:30
  26.4 19.0 %collective-permute-start.4 = (s32[64,8]{0,1:T(8,128)S(1)}, s32[64,8]{0,1:T(8,128)S(1)}, u32[]{:S(2)}, u32[]{:S(2)}) collective-permute-start(s32[64,8]{0,1:T(8,128)S(1)} %collective-permute-done.2), channel_id=1, source_target_pairs={{0,3},{1,0},{2,1},{3,2},{4,7},{5,4},{6,5},{7,6},{8,11},{9,8},{10,9... | collective-permute-start | bytes 6152 | tf_op jit(solution)/shard_map/ppermute | solution.py:30
  46.3 14.9 %collective-permute-start.8 = (bf16[64,4096]{1,0:T(8,128)(2,1)S(1)}, bf16[64,4096]{1,0:T(8,128)(2,1)S(1)}, u32[]{:S(2)}, u32[]{:S(2)}) collective-permute-start(bf16[64,4096]{1,0:T(8,128)(2,1)S(1)} %collective-permute-done.6), channel_id=1, source_target_pairs={{0,3},{1,0},{2,1},{3,2},{4,7},{5,4},{6,5},{7,6},{8,11},{9,8},{10,9... | collective-permute-start | bytes 1572872 | tf_op jit(solution)/shard_map/ppermute | solution.py:30
  48.4 24.0 %collective-permute-start.9 = (bf16[64,4096]{1,0:T(8,128)(2,1)S(1)}, bf16[64,4096]{1,0:T(8,128)(2,1)S(1)}, u32[]{:S(2)}, u32[]{:S(2)}) collective-permute-start(bf16[64,4096]{1,0:T(8,128)(2,1)S(1)} %collective-permute-done.7), channel_id=1, source_target_pairs={{0,3},{1,0},{2,1},{3,2},{4,7},{5,4},{6,5},{7,6},{8,11},{9,8},{10,9... | collective-permute-start | bytes 1572872 | tf_op jit(solution)/shard_map/ppermute | solution.py:30
  61.2 22.5 %collective-permute-start.10 = (bf16[64,4096]{1,0:T(8,128)(2,1)S(1)}, bf16[64,4096]{1,0:T(8,128)(2,1)S(1)}, u32[]{:S(2)}, u32[]{:S(2)}) collective-permute-start(bf16[64,4096]{1,0:T(8,128)(2,1)S(1)} %collective-permute-done.8), channel_id=1, source_target_pairs={{0,3},{1,0},{2,1},{3,2},{4,7},{5,4},{6,5},{7,6},{8,11},{9,8},{10,9... | collective-permute-start | bytes 1572872 | tf_op jit(solution)/shard_map/ppermute | solution.py:30
  72.4 18.7 %collective-permute-start.11 = (bf16[64,4096]{1,0:T(8,128)(2,1)S(1)}, bf16[64,4096]{1,0:T(8,128)(2,1)S(1)}, u32[]{:S(2)}, u32[]{:S(2)}) collective-permute-start(bf16[64,4096]{1,0:T(8,128)(2,1)S(1)} %collective-permute-done.9), channel_id=1, source_target_pairs={{0,3},{1,0},{2,1},{3,2},{4,7},{5,4},{6,5},{7,6},{8,11},{9,8},{10,9... | collective-permute-start | bytes 1572872 | tf_op jit(solution)/shard_map/ppermute | solution.py:30
  83.7 7.5 %copy-start.4 = (bf16[64,4096]{1,0:T(8,128)(2,1)}, bf16[64,4096]{1,0:T(8,128)(2,1)S(1)}, u32[]{:S(2)}) copy-start(bf16[64,4096]{1,0:T(8,128)(2,1)S(1)} %collective-permute-done.10) | copy-start | bytes 1572868
  91.1 0.8 copy-start.6
  92.8 4.5 %copy-start = (bf16[704,4096]{1,0:T(8,128)(2,1)S(1)}, bf16[704,4096]{1,0:T(8,128)(2,1)}, u32[]{:S(2)}) copy-start(bf16[704,4096]{1,0:T(8,128)(2,1)} %all-gather.4.cloned.1.call-done) | copy-start | bytes 17301508
  98.9 1.7 copy-start.5
  98.9 1.7 copy-start.7
  102.3 3.2 %copy-start.10 = (s32[128]{0:T(128)S(1)}, s32[128]{0:T(128)}, u32[]{:S(2)}) copy-start(s32[128]{0:T(128)} %param.6) | copy-start | bytes 1540
  123.5 1.7 copy-start.2
  123.5 2.4 %copy-start.8 = (bf16[512,4096]{1,0:T(8,128)(2,1)S(1)}, bf16[512,4096]{1,0:T(8,128)(2,1)}, u32[]{:S(2)}) copy-start(bf16[512,4096]{1,0:T(8,128)(2,1)} %constant_dynamic-update-slice_fusion) | copy-start | bytes 12582916
  130.9 7.9 %slice-start = ((s8[5767168]{0:T(1024)(128)(4,1)}), s8[1572864]{0:T(1024)(128)(4,1)S(1)}, s32[]{:S(2)}) async-start(s8[5767168]{0:T(1024)(128)(4,1)} %bitcast.28), calls=%async_computation.3 | async-start | bytes 3145728
  130.9 7.9 %slice-start.1 = ((s8[5767168]{0:T(1024)(128)(4,1)}), s8[4194304]{0:T(1024)(128)(4,1)S(1)}, s32[]{:S(2)}) async-start(s8[5767168]{0:T(1024)(128)(4,1)} %bitcast.28), calls=%async_computation.4 | async-start | bytes 8388608
  131.0 7.9 %copy-start.3 = (bf16[512,704]{0,1:T(8,128)(2,1)S(1)}, bf16[512,704]{0,1:T(8,128)(2,1)}, u32[]{:S(2)}) copy-start(bf16[512,704]{0,1:T(8,128)(2,1)} %copy-done.2) | copy-start | bytes 2162692
  135.0 14.8 %collective-permute-start.12 = (bf16[64,4096]{1,0:T(8,128)(2,1)S(1)}, bf16[64,4096]{1,0:T(8,128)(2,1)S(1)}, u32[]{:S(2)}, u32[]{:S(2)}) collective-permute-start(bf16[64,4096]{1,0:T(8,128)(2,1)S(1)} %get-tuple-element.13), channel_id=1, source_target_pairs={{0,3},{1,0},{2,1},{3,2},{4,7},{5,4},{6,5},{7,6},{8,11},{9,8},{10,9... | collective-permute-start | bytes 1572872 | tf_op jit(solution)/shard_map/ppermute | solution.py:115
  138.8 18.8 %collective-permute-start.15 = (bf16[64,4096]{1,0:T(8,128)(2,1)S(1)}, bf16[64,4096]{1,0:T(8,128)(2,1)S(1)}, u32[]{:S(2)}, u32[]{:S(2)}) collective-permute-start(bf16[64,4096]{1,0:T(8,128)(2,1)S(1)} %get-tuple-element.14), channel_id=1, source_target_pairs={{0,3},{1,0},{2,1},{3,2},{4,7},{5,4},{6,5},{7,6},{8,11},{9,8},{10,9... | collective-permute-start | bytes 1572872 | tf_op jit(solution)/shard_map/ppermute | solution.py:115
  157.8 14.5 %collective-permute-start.13 = (bf16[64,4096]{1,0:T(8,128)(2,1)S(1)}, bf16[64,4096]{1,0:T(8,128)(2,1)S(1)}, u32[]{:S(2)}, u32[]{:S(2)}) collective-permute-start(bf16[64,4096]{1,0:T(8,128)(2,1)S(1)} %get-tuple-element.11), channel_id=1, source_target_pairs={{0,3},{1,0},{2,1},{3,2},{4,7},{5,4},{6,5},{7,6},{8,11},{9,8},{10,9... | collective-permute-start | bytes 1572872 | tf_op jit(solution)/shard_map/ppermute | solution.py:115
  162.1 18.8 %collective-permute-start.16 = (bf16[64,4096]{1,0:T(8,128)(2,1)S(1)}, bf16[64,4096]{1,0:T(8,128)(2,1)S(1)}, u32[]{:S(2)}, u32[]{:S(2)}) collective-permute-start(bf16[64,4096]{1,0:T(8,128)(2,1)S(1)} %get-tuple-element.12), channel_id=1, source_target_pairs={{0,3},{1,0},{2,1},{3,2},{4,7},{5,4},{6,5},{7,6},{8,11},{9,8},{10,9... | collective-permute-start | bytes 1572872 | tf_op jit(solution)/shard_map/ppermute | solution.py:115
  181.1 13.6 %collective-permute-start.14 = (bf16[64,4096]{1,0:T(8,128)(2,1)S(1)}, bf16[64,4096]{1,0:T(8,128)(2,1)S(1)}, u32[]{:S(2)}, u32[]{:S(2)}) collective-permute-start(bf16[64,4096]{1,0:T(8,128)(2,1)S(1)} %get-tuple-element.9), channel_id=1, source_target_pairs={{0,3},{1,0},{2,1},{3,2},{4,7},{5,4},{6,5},{7,6},{8,11},{9,8},{10,9... | collective-permute-start | bytes 1572872 | tf_op jit(solution)/shard_map/ppermute | solution.py:115
  185.4 14.9 %collective-permute-start.17 = (bf16[64,4096]{1,0:T(8,128)(2,1)S(1)}, bf16[64,4096]{1,0:T(8,128)(2,1)S(1)}, u32[]{:S(2)}, u32[]{:S(2)}) collective-permute-start(bf16[64,4096]{1,0:T(8,128)(2,1)S(1)} %get-tuple-element.10), channel_id=1, source_target_pairs={{0,3},{1,0},{2,1},{3,2},{4,7},{5,4},{6,5},{7,6},{8,11},{9,8},{10,9... | collective-permute-start | bytes 1572872 | tf_op jit(solution)/shard_map/ppermute | solution.py:115
Sparse Core Ops, SparseCore 0:
  9.9 46.0 all-gather.3
  131.1 60.4 reduce-scatter.1

commit v6 on v4

--- a/solution.py
+++ b/solution.py
@@ -20,11 +20,24 @@
     pool_size = pool.shape[0]
 
     ring_down = [(i, (i - 1) % slabs) for i in range(slabs)]
-    query_blocks = [queries]
-    id_blocks = [hard_ids]
-    for _ in range(slabs - 1):
-        query_blocks.append(lax.ppermute(query_blocks[-1], "slab", ring_down))
-        id_blocks.append(lax.ppermute(id_blocks[-1], "slab", ring_down))
+    ring_up = [(i, (i + 1) % slabs) for i in range(slabs)]
+    steps_down = slabs // 2
+    steps_up = slabs - 1 - steps_down
+
+    def ring_gather(x):
+        blocks = [x] * slabs
+        current = x
+        for step in range(1, steps_down + 1):
+            current = lax.ppermute(current, "slab", ring_down)
+            blocks[step] = current
+        current = x
+        for step in range(1, steps_up + 1):
+            current = lax.ppermute(current, "slab", ring_up)
+            blocks[slabs - step] = current
+        return blocks
+
+    query_blocks = ring_gather(queries)
+    id_blocks = ring_gather(hard_ids)
 
     def to_origin(x):
         doubled = jnp.concatenate([x, x], axis=0)
@@ -57,7 +70,15 @@
     pool_sum = jnp.sum(jnp.exp(pooled - pool_max[:, None]), axis=1)
     hard_origin = to_origin(hard_mine.reshape(slabs, query_rows_dev * hard_count))
     payload = jnp.concatenate([hard_origin.reshape(-1), pool_max, pool_sum])
-    gathered = lax.all_gather(payload, "slab", axis=0)
+    gathered = to_origin(
+        jnp.stack(
+            [payload]
+            + [
+                lax.ppermute(payload, "slab", [(i, (i - t) % slabs) for i in range(slabs)])
+                for t in range(1, slabs)
+            ]
+        )
+    )
     hard_split = column_rows * hard_count
     owner_origin = to_origin(owner_slab.reshape(slabs, query_rows_dev * hard_count))
     slab_iota = jnp.arange(slabs, dtype=jnp.int32)[:, None, None]
@@ -97,10 +118,20 @@
         rows = hard_matrix[block * query_rows_dev : (block + 1) * query_rows_dev]
         return jnp.dot(rows, pool, preferred_element_type=jnp.float32)
 
-    carried = grad_for(1)
-    for step in range(1, slabs):
-        carried = lax.ppermute(carried.astype(jnp.bfloat16), "slab", ring_down).astype(jnp.float32)
-        carried = carried + grad_for((step + 1) % slabs)
+    def hop(part, perm):
+        return lax.ppermute(part.astype(jnp.bfloat16), "slab", perm).astype(jnp.float32)
+
+    carried = grad_for(0)
+    if steps_down:
+        down = grad_for(slabs - steps_down)
+        for step in range(1, steps_down):
+            down = hop(down, ring_down) + grad_for(slabs - steps_down + step)
+        carried = carried + hop(down, ring_down)
+    if steps_up:
+        up = grad_for(steps_up)
+        for step in range(1, steps_up):
+            up = hop(up, ring_up) + grad_for(steps_up - step)
+        carried = carried + hop(up, ring_up)
     pool_grad = jnp.dot(coef_pool, pool, preferred_element_type=jnp.float32)
     query_grad = pool_grad + carried
 

time: 200 us -> 196 us (0.980)
  blocking collectives: 13.8 us -> 0 us
  waiting for transfers between devices: 104 us -> 117 us
  starting transfers between devices: 28.9 us -> 25.1 us
    all_gather x1 -> x0, blocking collectives: 13.8 us -> none  [per_device(): gathered = lax.all_gather(payload, 'slab', axis=0)]
    ppermute x9 -> x12, waiting for transfers between devices: 104 us -> 116 us  [the longest x3 57.8 us: hop(): lax.ppermute(part.astype(jnp.bfloat16), 'slab', perm).astype(jnp.float32)]
    ppermute x9 -> x12, starting transfers between devices: 28.8 us -> 25 us  [the longest x4 13.2 us: ring_gather(): current = lax.ppermute(current, 'slab', ring_down)]
  transfers between devices with their start and end apart: 11 -> 14, of which waited for: 7 -> 8; matrix products, arithmetic and copies ran while one was open for 9% -> 10% of each run, Pallas kernels for 0% -> 0%
where the time goes in v6:
time: 196 us
  waiting for transfers between devices  117 us (60%)
  matrix products  26.1 us (13%)
  starting transfers between devices  25.1 us (13%)
  between operations  14.4 us (7%)
  other arithmetic  9.3 us (5%)
  local copies, waits for them, and re-layouts  3.58 us (2%)
    ppermute x3, waiting for transfers between devices, hop(): lax.ppermute(part.astype(jnp.bfloat16), 'slab', perm).astype(jnp.float32)  57.8 us
    ppermute x4, waiting for transfers between devices, ring_gather(): current = lax.ppermute(current, 'slab', ring_down)  56.3 us
    ppermute x4, starting transfers between devices, ring_gather(): current = lax.ppermute(current, 'slab', ring_down)  13.2 us
    dot_general x4, matrix products, per_device(): lax.dot_general(block, pool, contract_rows, preferred_element_type=jnp.fl...  9.74 us
    dot_general x4, matrix products, grad_for(): return jnp.dot(rows, pool, preferred_element_type=jnp.float32)  8.61 us
    ppermute x3, starting transfers between devices, hop(): lax.ppermute(part.astype(jnp.bfloat16), 'slab', perm).astype(jnp.float32)  7.56 us
    dot_general x1, matrix products, per_device(): lax.dot_general(hard_matrix, column_queries, contract_cols, preferred_ele...  5.02 us
    ppermute x3, starting transfers between devices, per_device(): lax.ppermute(payload, 'slab', [(i, (i - t) % slabs) for i in range(slabs)])  4.24 us
  transfers between devices with their start and end apart: 14, of which 8 were waited for; matrix products, arithmetic and copies ran while one was open for 10% of the time, Pallas kernels for 0%

profile of v6, /device:TPU:0, one launch (start us, length us, event | category | flops | bytes accessed | tf_op | source)
XLA Modules:
  0.0 195.6 jit_solution(209371256898611236)
XLA Ops:
  7.2 0.0 all-gather.2.cloned.1.call-start
  7.2 0.7 all-gather.2.cloned.1.call-update
  7.9 0.0 reduce-scatter.2.cloned.1.call-start
  7.9 5.1 %collective-permute-start = (s32[128,8]{0,1:T(8,128)}, s32[128,8]{0,1:T(8,128)S(1)}, u32[]{:S(2)}, u32[]{:S(2)}) collective-permute-start(s32[128,8]{0,1:T(8,128)} %param.7), channel_id=1, source_target_pairs={{0,3},{1,0},{2,1},{3,2},{4,7},{5,4},{6,5},{7,6},{8,11},{9,8},{10,9... | collective-permute-start | bytes 12296 | tf_op jit(solution)/shard_map/ppermute | solution.py:31
  13.0 0.0 collective-permute-start.2
  13.0 0.0 collective-permute-start.5
  13.1 3.9 %collective-permute-start.3 = (bf16[128,4096]{1,0:T(8,128)(2,1)}, bf16[128,4096]{1,0:T(8,128)(2,1)S(1)}, u32[]{:S(2)}, u32[]{:S(2)}) collective-permute-start(bf16[128,4096]{1,0:T(8,128)(2,1)} %param.4), channel_id=1, source_target_pairs={{0,3},{1,0},{2,1},{3,2},{4,7},{5,4},{6,5},{7,6},{8,11},{9,8},{10,9... | collective-permute-start | bytes 3145736 | tf_op jit(solution)/shard_map/ppermute | solution.py:31
  16.9 0.7 constant_dynamic-update-slice_fusion.3
  17.6 2.0 %collective-permute-start.1 = (s32[128,8]{0,1:T(8,128)S(1)}, s32[128,8]{0,1:T(8,128)S(1)}, u32[]{:S(2)}, u32[]{:S(2)}) collective-permute-start(s32[128,8]{0,1:T(8,128)S(1)} %collective-permute-done), channel_id=1, source_target_pairs={{0,3},{1,0},{2,1},{3,2},{4,7},{5,4},{6,5},{7,6},{8,11},{9,8},{10,9... | collective-permute-start | bytes 12296 | tf_op jit(solution)/shard_map/ppermute | solution.py:31
  19.6 40.9 %collective-permute-done.1 = s32[128,8]{0,1:T(8,128)S(1)} collective-permute-done((s32[128,8]{0,1:T(8,128)S(1)}, s32[128,8]{0,1:T(8,128)S(1)}, u32[]{:S(2)}, u32[]{:S(2)}) %collective-permute-start.1) | collective-permute-done | bytes 4128 | tf_op jit(solution)/shard_map/ppermute | solution.py:31
  60.6 0.2 copy.19
  60.7 0.2 and.81
  61.0 0.1 copy.20
  61.1 0.2 div.35
  61.3 0.0 collective-permute-done.3
  61.3 2.3 %collective-permute-start.4 = (bf16[128,4096]{1,0:T(8,128)(2,1)S(1)}, bf16[128,4096]{1,0:T(8,128)(2,1)S(1)}, u32[]{:S(2)}, u32[]{:S(2)}) collective-permute-start(bf16[128,4096]{1,0:T(8,128)(2,1)S(1)} %collective-permute-done.3), channel_id=1, source_target_pairs={{0,3},{1,0},{2,1},{3,2},{4,7},{5,4},{6,5},{7,6},{8,11},{9,8},{10,9... | collective-permute-start | bytes 3145736 | tf_op jit(solution)/shard_map/ppermute | solution.py:31
  63.6 4.8 %fusion.37 = f32[128,704]{0,1:T(8,128)S(1)} fusion(bf16[128,4096]{1,0:T(8,128)(2,1)} %param.4, bf16[704,4096]{1,0:T(8,128)(2,1)} %all-gather.2.cloned.1.call-done), kind=kOutput, calls=%fused_computation.85 | convolution fusion | flops 738197504 | bytes 7176192 | tf_op jit(solution)/shard_map/dot_general | solution.py:52
  68.4 1.7 fusion.38
  70.0 0.0 copy-start.4
  70.0 1.7 fusion.40
  71.7 0.0 copy-start.10
  71.7 15.3 %collective-permute-done.4 = bf16[128,4096]{1,0:T(8,128)(2,1)S(1)} collective-permute-done((bf16[128,4096]{1,0:T(8,128)(2,1)S(1)}, bf16[128,4096]{1,0:T(8,128)(2,1)S(1)}, u32[]{:S(2)}, u32[]{:S(2)}) %collective-permute-start.4) | collective-permute-done | bytes 1048608 | tf_op jit(solution)/shard_map/ppermute | solution.py:31
  87.1 1.0 copy-done.8
  88.0 1.7 fusion.39
  89.7 0.0 copy-start.3
  89.7 0.1 maximum_multiply_fusion
  89.8 0.1 slice_reduce_fusion
  89.9 2.7 %select_reduce_fusion.1 = f32[512,8]{0,1:T(8,128)S(1)} fusion(f32[512,704]{0,1:T(8,128)S(1)} %maximum_multiply_fusion, s32[512,8]{0,1:T(8,128)S(1)} %get-tuple-element.8, pred[512,8]{0,1:T(8,128)(4,1)S(1)} %get-tuple-element.5), kind=kLoop, calls=%fused_computation.2 | loop fusion | flops 11530240 | bytes 1478656 | tf_op jit(solution)/shard_map/reduce_sum | solution.py:67
  92.6 0.1 copy.18
  92.7 0.2 reshape.312
  92.9 0.1 exponential_reduce_fusion
  93.1 1.8 collective-permute-start.8
  94.9 1.1 collective-permute-start.7
  96.0 1.3 collective-permute-start.6
  97.4 1.5 collective-permute-done.8
  98.9 0.6 collective-permute-done.7
  99.6 0.2 collective-permute-done.6
  99.8 0.2 concatenate.60
  100.0 0.1 fusion.16
  100.1 0.1 dynamic-slice
  100.3 0.2 reshape.315
  100.4 0.1 reduce_max.19
  100.6 0.2 exponential_reduce_fusion.1
  100.9 0.5 fusion.36
  101.4 2.8 %select_reduce_fusion = bf16[512,704]{0,1:T(8,128)(2,1)S(1)} fusion(f32[512,8]{0,1:T(8,128)S(1)} %fusion.29, s32[512,8]{0,1:T(8,128)S(1)} %get-tuple-element.8, pred[512,8]{0,1:T(8,128)(4,1)S(1)} %get-tuple-element.5), kind=kLoop, calls=%fused_computation.1 | loop fusion | flops 11173888 | bytes 757760 | tf_op jit(solution)/shard_map/reduce_sum | solution.py:113
  104.2 0.0 copy-start.5
  104.2 0.0 copy-start.9
  104.2 1.7 fusion.32
  105.9 0.1 copy-done.7
  106.0 0.3 copy-done.9
  106.3 5.0 %add_convert_fusion = bf16[704,4096]{1,0:T(8,128)(2,1)} fusion(f32[704,4096]{1,0:T(8,128)S(1)} %fusion.32, bf16[512,704]{0,1:T(8,128)(2,1)S(1)} %select_reduce_fusion, bf16[128,4096]{1,0:T(8,128)(2,1)S(1)} %copy-done.5, bf16[128,4096]{1,0:T(8,128)(2,1)S(1)} %copy-done.9, bf16[128,4096]{1,0:T(8,128)(2,1)S(1)} %copy-done.7, bf16[128,4096]{1,0:T(8,128)(2,1)S(1)} %copy-done.3), kind=kOutput, calls=%fused_computation | convolution fusion | flops 2975334400 | bytes 22216704 | tf_op jit(solution)/shard_map/dot_general | solution.py:141
  111.3 0.0 reduce-scatter.2.cloned.1.call-update
  111.4 3.9 %convolution_convert_fusion.1 = bf16[128,4096]{1,0:T(8,128)(2,1)S(1)} fusion(bf16[704,4096]{1,0:T(8,128)(2,1)} %all-gather.2.cloned.1.call-done, bf16[512,704]{0,1:T(8,128)(2,1)} %copy-done.1), kind=kOutput, calls=%fused_computation.6 | convolution fusion | flops 738721792 | bytes 6995968 | tf_op jit(solution)/shard_map/dot_general | solution.py:119
  115.3 3.2 %collective-permute-start.9 = (bf16[128,4096]{1,0:T(8,128)(2,1)S(1)}, bf16[128,4096]{1,0:T(8,128)(2,1)S(1)}, u32[]{:S(2)}, u32[]{:S(2)}) collective-permute-start(bf16[128,4096]{1,0:T(8,128)(2,1)S(1)} %convolution_convert_fusion.1), channel_id=1, source_target_pairs={{0,3},{1,0},{2,1},{3,2},{4,7},{5,4},{6,5},{7,6},{8,11},{9,8},{10,9... | collective-permute-start | bytes 3145736 | tf_op jit(solution)/shard_map/ppermute | solution.py:122
  118.5 1.0 convolution_convert_fusion
  119.5 0.1 collective-permute-start.11
  119.6 22.5 %collective-permute-done.9 = bf16[128,4096]{1,0:T(8,128)(2,1)S(1)} collective-permute-done((bf16[128,4096]{1,0:T(8,128)(2,1)S(1)}, bf16[128,4096]{1,0:T(8,128)(2,1)S(1)}, u32[]{:S(2)}, u32[]{:S(2)}) %collective-permute-start.9) | collective-permute-done | bytes 1048608 | tf_op jit(solution)/shard_map/ppermute | solution.py:122
  142.1 1.0 add_convert_fusion.1
  143.1 4.3 %collective-permute-start.10 = (bf16[128,4096]{1,0:T(8,128)(2,1)S(1)}, bf16[128,4096]{1,0:T(8,128)(2,1)S(1)}, u32[]{:S(2)}, u32[]{:S(2)}) collective-permute-start(bf16[128,4096]{1,0:T(8,128)(2,1)S(1)} %add_convert_fusion.1), channel_id=1, source_target_pairs={{0,3},{1,0},{2,1},{3,2},{4,7},{5,4},{6,5},{7,6},{8,11},{9,8},{10,9... | collective-permute-start | bytes 3145736 | tf_op jit(solution)/shard_map/ppermute | solution.py:122
  147.4 1.0 fusion.33
  148.5 16.7 %collective-permute-done.11 = bf16[128,4096]{1,0:T(8,128)(2,1)S(1)} collective-permute-done((bf16[128,4096]{1,0:T(8,128)(2,1)S(1)}, bf16[128,4096]{1,0:T(8,128)(2,1)S(1)}, u32[]{:S(2)}, u32[]{:S(2)}) %collective-permute-start.11) | collective-permute-done | bytes 1048608 | tf_op jit(solution)/shard_map/ppermute | solution.py:122
  165.2 18.6 %collective-permute-done.10 = bf16[128,4096]{1,0:T(8,128)(2,1)S(1)} collective-permute-done((bf16[128,4096]{1,0:T(8,128)(2,1)S(1)}, bf16[128,4096]{1,0:T(8,128)(2,1)S(1)}, u32[]{:S(2)}, u32[]{:S(2)}) %collective-permute-start.10) | collective-permute-done | bytes 1048608 | tf_op jit(solution)/shard_map/ppermute | solution.py:122
  183.7 2.7 %add_add_fusion = f32[128,4096]{1,0:T(8,128)} fusion(f32[128,4096]{1,0:T(8,128)S(1)} %fusion.33, bf16[128,4096]{1,0:T(8,128)(2,1)S(1)} %collective-permute-done.11, bf16[128,4096]{1,0:T(8,128)(2,1)S(1)} %collective-permute-done.10, bf16[704,4096]{1,0:T(8,128)(2,1)S(1)} %bitcast.28, bf16[512,704]{0,1:T(8,128)(2,1)S(1)} %copy-done.2), kind=kOutput, calls=%fused_computation.14 | convolution fusion | flops 740818944 | bytes 12238848 | tf_op jit(solution)/shard_map/dot_general | solution.py:119
  186.4 2.3 %convert_element_type.59 = f32[88,4096]{1,0:T(8,128)} convert(bf16[88,4096]{1,0:T(8,128)(2,1)} %reduce-scatter.2.cloned.1.call-done) | non-fusion elementwise | flops 360448 | bytes 2162688 | tf_op jit(solution)/shard_map/convert_element_type | solution.py:144
  (47 shorter events, 0.4 us)
Async XLA Ops:
  7.2 56.4 %all-gather.2.cloned.1.call-start = ((), (), s32[]{:S(2)}) async-start(), calls=%async_computation.1 | async-start | bytes 6488064 | tf_op jit(solution)/shard_map/all_gather | solution.py:19
  7.9 178.5 %reduce-scatter.2.cloned.1.call-start = ((), (), s32[]{:S(2)}) async-start(), calls=%async_computation.2 | async-start | bytes 6488064 | tf_op jit(solution)/shard_map/reduce_scatter | solution.py:142
  7.9 9.7 %collective-permute-start = (s32[128,8]{0,1:T(8,128)}, s32[128,8]{0,1:T(8,128)S(1)}, u32[]{:S(2)}, u32[]{:S(2)}) collective-permute-start(s32[128,8]{0,1:T(8,128)} %param.7), channel_id=1, source_target_pairs={{0,3},{1,0},{2,1},{3,2},{4,7},{5,4},{6,5},{7,6},{8,11},{9,8},{10,9... | collective-permute-start | bytes 12296 | tf_op jit(solution)/shard_map/ppermute | solution.py:31
  13.0 47.5 %collective-permute-start.2 = (s32[128,8]{0,1:T(8,128)}, s32[128,8]{0,1:T(8,128)S(1)}, u32[]{:S(2)}, u32[]{:S(2)}) collective-permute-start(s32[128,8]{0,1:T(8,128)} %param.7), channel_id=1, source_target_pairs={{0,1},{1,2},{2,3},{3,0},{4,5},{5,6},{6,7},{7,4},{8,9},{9,10},{10,1... | collective-permute-start | bytes 12296 | tf_op jit(solution)/shard_map/ppermute | solution.py:35
  13.0 57.0 %collective-permute-start.5 = (bf16[128,4096]{1,0:T(8,128)(2,1)}, bf16[128,4096]{1,0:T(8,128)(2,1)S(1)}, u32[]{:S(2)}, u32[]{:S(2)}) collective-permute-start(bf16[128,4096]{1,0:T(8,128)(2,1)} %param.4), channel_id=1, source_target_pairs={{0,1},{1,2},{2,3},{3,0},{4,5},{5,6},{6,7},{7,4},{8,9},{9,10},{10,1... | collective-permute-start | bytes 3145736 | tf_op jit(solution)/shard_map/ppermute | solution.py:35
  13.1 48.2 %collective-permute-start.3 = (bf16[128,4096]{1,0:T(8,128)(2,1)}, bf16[128,4096]{1,0:T(8,128)(2,1)S(1)}, u32[]{:S(2)}, u32[]{:S(2)}) collective-permute-start(bf16[128,4096]{1,0:T(8,128)(2,1)} %param.4), channel_id=1, source_target_pairs={{0,3},{1,0},{2,1},{3,2},{4,7},{5,4},{6,5},{7,6},{8,11},{9,8},{10,9... | collective-permute-start | bytes 3145736 | tf_op jit(solution)/shard_map/ppermute | solution.py:31
  17.6 42.9 %collective-permute-start.1 = (s32[128,8]{0,1:T(8,128)S(1)}, s32[128,8]{0,1:T(8,128)S(1)}, u32[]{:S(2)}, u32[]{:S(2)}) collective-permute-start(s32[128,8]{0,1:T(8,128)S(1)} %collective-permute-done), channel_id=1, source_target_pairs={{0,3},{1,0},{2,1},{3,2},{4,7},{5,4},{6,5},{7,6},{8,11},{9,8},{10,9... | collective-permute-start | bytes 12296 | tf_op jit(solution)/shard_map/ppermute | solution.py:31
  61.3 8.7 %copy-start.6 = (bf16[128,4096]{1,0:T(8,128)(2,1)}, bf16[128,4096]{1,0:T(8,128)(2,1)S(1)}, u32[]{:S(2)}) copy-start(bf16[128,4096]{1,0:T(8,128)(2,1)S(1)} %collective-permute-done.3) | copy-start | bytes 3145732
  61.3 25.7 %collective-permute-start.4 = (bf16[128,4096]{1,0:T(8,128)(2,1)S(1)}, bf16[128,4096]{1,0:T(8,128)(2,1)S(1)}, u32[]{:S(2)}, u32[]{:S(2)}) collective-permute-start(bf16[128,4096]{1,0:T(8,128)(2,1)S(1)} %collective-permute-done.3), channel_id=1, source_target_pairs={{0,3},{1,0},{2,1},{3,2},{4,7},{5,4},{6,5},{7,6},{8,11},{9,8},{10,9... | collective-permute-start | bytes 3145736 | tf_op jit(solution)/shard_map/ppermute | solution.py:31
  63.6 4.8 %copy-start = (bf16[704,4096]{1,0:T(8,128)(2,1)S(1)}, bf16[704,4096]{1,0:T(8,128)(2,1)}, u32[]{:S(2)}) copy-start(bf16[704,4096]{1,0:T(8,128)(2,1)} %all-gather.2.cloned.1.call-done) | copy-start | bytes 17301508
  70.0 17.0 %copy-start.4 = (bf16[128,4096]{1,0:T(8,128)(2,1)}, bf16[128,4096]{1,0:T(8,128)(2,1)S(1)}, u32[]{:S(2)}) copy-start(bf16[128,4096]{1,0:T(8,128)(2,1)S(1)} %collective-permute-done.5) | copy-start | bytes 3145732
  71.7 21.2 %copy-start.10 = (s32[128]{0:T(128)S(1)}, s32[128]{0:T(128)}, u32[]{:S(2)}) copy-start(s32[128]{0:T(128)} %param.6) | copy-start | bytes 1540
  87.1 1.0 copy-start.8
  89.7 14.5 %copy-start.3 = (bf16[128,4096]{1,0:T(8,128)(2,1)S(1)}, bf16[128,4096]{1,0:T(8,128)(2,1)}, u32[]{:S(2)}) copy-start(bf16[128,4096]{1,0:T(8,128)(2,1)} %param.4) | copy-start | bytes 3145732
  93.1 5.8 %collective-permute-start.8 = (f32[4352]{0:T(1024)S(1)}, f32[4352]{0:T(1024)S(1)}, u32[]{:S(2)}, u32[]{:S(2)}) collective-permute-start(f32[4352]{0:T(1024)S(1)} %pad_maximum_fusion), channel_id=1, source_target_pairs={{0,1},{1,2},{2,3},{3,0},{4,5},{5,6},{6,7},{7,4},{8,9},{9,10},{10,1... | collective-permute-start | bytes 52232 | tf_op jit(solution)/shard_map/ppermute | solution.py:77
  94.9 4.7 %collective-permute-start.7 = (f32[4352]{0:T(1024)S(1)}, f32[4352]{0:T(1024)S(1)}, u32[]{:S(2)}, u32[]{:S(2)}) collective-permute-start(f32[4352]{0:T(1024)S(1)} %pad_maximum_fusion), channel_id=1, source_target_pairs={{0,2},{1,3},{2,0},{3,1},{4,6},{5,7},{6,4},{7,5},{8,10},{9,11},{10,... | collective-permute-start | bytes 52232 | tf_op jit(solution)/shard_map/ppermute | solution.py:77
  96.0 3.8 %collective-permute-start.6 = (f32[4352]{0:T(1024)S(1)}, f32[4352]{0:T(1024)S(1)}, u32[]{:S(2)}, u32[]{:S(2)}) collective-permute-start(f32[4352]{0:T(1024)S(1)} %pad_maximum_fusion), channel_id=1, source_target_pairs={{0,3},{1,0},{2,1},{3,2},{4,7},{5,4},{6,5},{7,6},{8,11},{9,8},{10,9... | collective-permute-start | bytes 52232 | tf_op jit(solution)/shard_map/ppermute | solution.py:77
  104.2 1.7 copy-start.1
  104.2 1.7 copy-start.5
  104.2 1.8 copy-start.7
  104.2 2.1 %copy-start.9 = (bf16[128,4096]{1,0:T(8,128)(2,1)S(1)}, bf16[128,4096]{1,0:T(8,128)(2,1)}, u32[]{:S(2)}) copy-start(bf16[128,4096]{1,0:T(8,128)(2,1)} %copy-done.8) | copy-start | bytes 3145732
  111.3 7.1 %slice-start = ((s8[5767168]{0:T(1024)(128)(4,1)}), s8[1572864]{0:T(1024)(128)(4,1)S(1)}, s32[]{:S(2)}) async-start(s8[5767168]{0:T(1024)(128)(4,1)} %bitcast.27), calls=%async_computation.3 | async-start | bytes 3145728
  111.4 7.1 %slice-start.1 = ((s8[5767168]{0:T(1024)(128)(4,1)}), s8[4194304]{0:T(1024)(128)(4,1)S(1)}, s32[]{:S(2)}) async-start(s8[5767168]{0:T(1024)(128)(4,1)} %bitcast.27), calls=%async_computation.4 | async-start | bytes 8388608
  111.4 7.1 %copy-start.2 = (bf16[512,704]{0,1:T(8,128)(2,1)S(1)}, bf16[512,704]{0,1:T(8,128)(2,1)}, u32[]{:S(2)}) copy-start(bf16[512,704]{0,1:T(8,128)(2,1)} %copy-done.1) | copy-start | bytes 2162692
  115.3 26.8 %collective-permute-start.9 = (bf16[128,4096]{1,0:T(8,128)(2,1)S(1)}, bf16[128,4096]{1,0:T(8,128)(2,1)S(1)}, u32[]{:S(2)}, u32[]{:S(2)}) collective-permute-start(bf16[128,4096]{1,0:T(8,128)(2,1)S(1)} %convolution_convert_fusion.1), channel_id=1, source_target_pairs={{0,3},{1,0},{2,1},{3,2},{4,7},{5,4},{6,5},{7,6},{8,11},{9,8},{10,9... | collective-permute-start | bytes 3145736 | tf_op jit(solution)/shard_map/ppermute | solution.py:122
  119.5 45.7 %collective-permute-start.11 = (bf16[128,4096]{1,0:T(8,128)(2,1)S(1)}, bf16[128,4096]{1,0:T(8,128)(2,1)S(1)}, u32[]{:S(2)}, u32[]{:S(2)}) collective-permute-start(bf16[128,4096]{1,0:T(8,128)(2,1)S(1)} %convolution_convert_fusion), channel_id=1, source_target_pairs={{0,1},{1,2},{2,3},{3,0},{4,5},{5,6},{6,7},{7,4},{8,9},{9,10},{10,1... | collective-permute-start | bytes 3145736 | tf_op jit(solution)/shard_map/ppermute | solution.py:122
  143.1 40.6 %collective-permute-start.10 = (bf16[128,4096]{1,0:T(8,128)(2,1)S(1)}, bf16[128,4096]{1,0:T(8,128)(2,1)S(1)}, u32[]{:S(2)}, u32[]{:S(2)}) collective-permute-start(bf16[128,4096]{1,0:T(8,128)(2,1)S(1)} %add_convert_fusion.1), channel_id=1, source_target_pairs={{0,3},{1,0},{2,1},{3,2},{4,7},{5,4},{6,5},{7,6},{8,11},{9,8},{10,9... | collective-permute-start | bytes 3145736 | tf_op jit(solution)/shard_map/ppermute | solution.py:122
Sparse Core Ops, SparseCore 0:
  9.9 46.0 all-gather.1
  111.5 59.8 reduce-scatter.1

commit v7 on v6

--- a/solution.py
+++ b/solution.py
@@ -114,24 +114,46 @@
         jnp.where(hard_hit, coef_hard.astype(jnp.float32)[:, :, None], 0.0), axis=1
     ).astype(jnp.bfloat16)
 
-    def grad_for(block):
-        rows = hard_matrix[block * query_rows_dev : (block + 1) * query_rows_dev]
-        return jnp.dot(rows, pool, preferred_element_type=jnp.float32)
+    far_below = -1e30
+    local_max = jnp.max(jnp.where(mine, hard_mine, far_below), axis=1)
+    local_weight = jnp.where(mine, jnp.exp(hard_mine - local_max[:, None]), 0.0)
+    weight_matrix = jnp.sum(
+        jnp.where(hard_hit, local_weight.astype(jnp.bfloat16).astype(jnp.float32)[:, :, None], 0.0),
+        axis=1,
+    ).astype(jnp.bfloat16)
 
-    def hop(part, perm):
-        return lax.ppermute(part.astype(jnp.bfloat16), "slab", perm).astype(jnp.float32)
+    def rows_of(x, block):
+        return x[block * query_rows_dev : (block + 1) * query_rows_dev]
 
-    carried = grad_for(0)
+    def scaled_for(block):
+        part = jnp.dot(rows_of(weight_matrix, block), pool, preferred_element_type=jnp.float32)
+        return part, rows_of(local_max, block)
+
+    def merge(first, second):
+        (part_a, scale_a), (part_b, scale_b) = first, second
+        scale = jnp.maximum(scale_a, scale_b)
+        part = part_a * jnp.exp(scale_a - scale)[:, None] + part_b * jnp.exp(scale_b - scale)[:, None]
+        return part, scale
+
+    def hop(carried, perm):
+        part, scale = carried
+        part = lax.ppermute(part.astype(jnp.bfloat16), "slab", perm).astype(jnp.float32)
+        return part, lax.ppermute(scale, "slab", perm)
+
+    arrived = []
     if steps_down:
-        down = grad_for(slabs - steps_down)
+        down = scaled_for(slabs - steps_down)
         for step in range(1, steps_down):
-            down = hop(down, ring_down) + grad_for(slabs - steps_down + step)
-        carried = carried + hop(down, ring_down)
+            down = merge(hop(down, ring_down), scaled_for(slabs - steps_down + step))
+        arrived.append(hop(down, ring_down))
     if steps_up:
-        up = grad_for(steps_up)
+        up = scaled_for(steps_up)
         for step in range(1, steps_up):
-            up = hop(up, ring_up) + grad_for(steps_up - step)
-        carried = carried + hop(up, ring_up)
+            up = merge(hop(up, ring_up), scaled_for(steps_up - step))
+        arrived.append(hop(up, ring_up))
+    carried = jnp.dot(rows_of(hard_matrix, 0), pool, preferred_element_type=jnp.float32)
+    for part, scale in arrived:
+        carried = carried + part * jnp.exp(scale - row_lse)[:, None]
     pool_grad = jnp.dot(coef_pool, pool, preferred_element_type=jnp.float32)
     query_grad = pool_grad + carried
 

time: 196 us -> 203 us (1.036)
  matrix products: 26.1 us -> 29.5 us
  waiting for transfers between devices: 117 us -> 120 us
  other arithmetic: 9.3 us -> 11.7 us
    ppermute x3, starting transfers between devices: 7.56 us -> 1.96 us  [hop(): lax.ppermute(part.astype(jnp.bfloat16), 'slab', perm).astype(jnp.float32)]
    ppermute x0 -> x3, starting transfers between devices: none -> 4.42 us  [hop(): return (part, lax.ppermute(scale, 'slab', perm))]
    ppermute x0 -> x3, waiting for transfers between devices: none -> 3.07 us  [hop(): return (part, lax.ppermute(scale, 'slab', perm))]
    ppermute x3, waiting for transfers between devices: 2.37 us -> 0.16 us  [per_device(): lax.ppermute(payload, 'slab', [(i, (i - t) % slabs) for i in range(slabs)])]
  transfers between devices with their start and end apart: 14 -> 17, of which waited for: 8 -> 6; matrix products, arithmetic and copies ran while one was open for 10% -> 11% of each run, Pallas kernels for 0% -> 0%
where the time goes in v7:
time: 203 us
  waiting for transfers between devices  120 us (59%)
  matrix products  29.5 us (15%)
  starting transfers between devices  23.5 us (12%)
  between operations  14.4 us (7%)
  other arithmetic  11.7 us (6%)
  local copies, waits for them, and re-layouts  4.11 us (2%)
    ppermute x3, waiting for transfers between devices, hop(): lax.ppermute(part.astype(jnp.bfloat16), 'slab', perm).astype(jnp.float32)  59.6 us
    ppermute x4, waiting for transfers between devices, ring_gather(): current = lax.ppermute(current, 'slab', ring_down)  56.3 us
    ppermute x4, starting transfers between devices, ring_gather(): current = lax.ppermute(current, 'slab', ring_down)  13.2 us
    dot_general x4, matrix products, per_device(): lax.dot_general(block, pool, contract_rows, preferred_element_type=jnp.fl...  11 us
    dot_general x3, matrix products, scaled_for(): jnp.dot(rows_of(weight_matrix, block), pool, preferred_element_type=jnp.f...  6.12 us
    dot_general x1, matrix products, per_device(): lax.dot_general(hard_matrix, column_queries, contract_cols, preferred_ele...  6.04 us
    reduce_sum x1, other arithmetic, per_device(): jnp.sum(jnp.where(hard_hit, coef_hard.astype(jnp.float32)[:, :, None], 0....  4.55 us
    ppermute x3, starting transfers between devices, hop(): return (part, lax.ppermute(scale, 'slab', perm))  4.42 us
  transfers between devices with their start and end apart: 17, of which 6 were waited for; matrix products, arithmetic and copies ran while one was open for 11% of the time, Pallas kernels for 0%

profile of v7, /device:TPU:0, one launch (start us, length us, event | category | flops | bytes accessed | tf_op | source)
XLA Modules:
  0.0 203.1 jit_solution(12827283069999577197)
XLA Ops:
  7.2 0.0 all-gather.2.cloned.1.call-start
  7.2 0.7 all-gather.2.cloned.1.call-update
  7.9 0.0 reduce-scatter.2.cloned.1.call-start
  7.9 5.1 %collective-permute-start = (s32[128,8]{0,1:T(8,128)}, s32[128,8]{0,1:T(8,128)S(1)}, u32[]{:S(2)}, u32[]{:S(2)}) collective-permute-start(s32[128,8]{0,1:T(8,128)} %param.7), channel_id=1, source_target_pairs={{0,3},{1,0},{2,1},{3,2},{4,7},{5,4},{6,5},{7,6},{8,11},{9,8},{10,9... | collective-permute-start | bytes 12296 | tf_op jit(solution)/shard_map/ppermute | solution.py:31
  13.0 0.0 collective-permute-start.2
  13.0 0.0 collective-permute-start.5
  13.1 3.9 %collective-permute-start.3 = (bf16[128,4096]{1,0:T(8,128)(2,1)}, bf16[128,4096]{1,0:T(8,128)(2,1)S(1)}, u32[]{:S(2)}, u32[]{:S(2)}) collective-permute-start(bf16[128,4096]{1,0:T(8,128)(2,1)} %param.4), channel_id=1, source_target_pairs={{0,3},{1,0},{2,1},{3,2},{4,7},{5,4},{6,5},{7,6},{8,11},{9,8},{10,9... | collective-permute-start | bytes 3145736 | tf_op jit(solution)/shard_map/ppermute | solution.py:31
  16.9 0.7 constant_dynamic-update-slice_fusion.3
  17.6 2.0 collective-permute-start.1
  19.6 40.9 %collective-permute-done.1 = s32[128,8]{0,1:T(8,128)S(1)} collective-permute-done((s32[128,8]{0,1:T(8,128)S(1)}, s32[128,8]{0,1:T(8,128)S(1)}, u32[]{:S(2)}, u32[]{:S(2)}) %collective-permute-start.1) | collective-permute-done | bytes 4128 | tf_op jit(solution)/shard_map/ppermute | solution.py:31
  60.5 0.0 collective-permute-done.2
  60.5 0.6 fusion.19
  61.2 0.2 copy.21
  61.3 0.2 and.90
  61.6 0.1 copy.22
  61.7 0.2 div.38
  61.9 0.6 copy.27
  62.5 2.2 %collective-permute-start.4 = (bf16[128,4096]{1,0:T(8,128)(2,1)S(1)}, bf16[128,4096]{1,0:T(8,128)(2,1)}, u32[]{:S(2)}, u32[]{:S(2)}) collective-permute-start(bf16[128,4096]{1,0:T(8,128)(2,1)S(1)} %collective-permute-done.3), channel_id=1, source_target_pairs={{0,3},{1,0},{2,1},{3,2},{4,7},{5,4},{6,5},{7,6},{8,11},{9,8},{10,9... | collective-permute-start | bytes 3145736 | tf_op jit(solution)/shard_map/ppermute | solution.py:31
  64.7 4.8 %fusion.38 = f32[128,704]{0,1:T(8,128)S(1)} fusion(bf16[128,4096]{1,0:T(8,128)(2,1)} %param.4, bf16[704,4096]{1,0:T(8,128)(2,1)} %all-gather.2.cloned.1.call-done), kind=kOutput, calls=%fused_computation.94 | convolution fusion | flops 738197504 | bytes 7176192 | tf_op jit(solution)/shard_map/dot_general | solution.py:52
  69.5 1.7 fusion.39
  71.2 0.0 copy-start.4
  71.2 1.7 fusion.41
  72.9 0.0 copy-start.1
  72.9 15.4 %collective-permute-done.4 = bf16[128,4096]{1,0:T(8,128)(2,1)} collective-permute-done((bf16[128,4096]{1,0:T(8,128)(2,1)S(1)}, bf16[128,4096]{1,0:T(8,128)(2,1)}, u32[]{:S(2)}, u32[]{:S(2)}) %collective-permute-start.4) | collective-permute-done | bytes 1048608 | tf_op jit(solution)/shard_map/ppermute | solution.py:31
  88.3 2.9 %fusion.40 = f32[128,704]{0,1:T(8,128)S(1)} fusion(bf16[128,4096]{1,0:T(8,128)(2,1)} %collective-permute-done.4, bf16[704,4096]{1,0:T(8,128)(2,1)S(1)} %copy-done), kind=kOutput, calls=%fused_computation.96 | convolution fusion | flops 738197504 | bytes 7176192 | tf_op jit(solution)/shard_map/dot_general | solution.py:52
  91.2 0.1 maximum_multiply_fusion
  91.4 0.1 slice_reduce_fusion
  91.5 2.7 %select_reduce_fusion.2 = f32[512,8]{0,1:T(8,128)S(1)} fusion(f32[512,704]{0,1:T(8,128)S(1)} %maximum_multiply_fusion, s32[512,8]{0,1:T(8,128)S(1)} %get-tuple-element.12, pred[512,8]{0,1:T(8,128)(4,1)S(1)} %copy-done.8), kind=kLoop, calls=%fused_computation.3 | loop fusion | flops 11530240 | bytes 1478656 | tf_op jit(solution)/shard_map/reduce_sum | solution.py:67
  94.2 0.1 copy.20
  94.3 2.3 %collective-permute-start.10 = (f32[128]{0:T(128)S(1)}, f32[128]{0:T(128)S(1)}, u32[]{:S(2)}, u32[]{:S(2)}) collective-permute-start(f32[128]{0:T(128)S(1)} %slice.47), channel_id=1, source_target_pairs={{0,3},{1,0},{2,1},{3,2},{4,7},{5,4},{6,5},{7,6},{8,11},{9,8},{10,9... | collective-permute-start | bytes 1544 | tf_op jit(solution)/shard_map/ppermute | solution.py:141
  96.7 0.2 reshape.378
  96.9 0.1 exponential_reduce_fusion
  97.0 0.1 collective-permute-start.8
  97.1 1.0 collective-permute-start.7
  98.1 2.8 %collective-permute-start.6 = (f32[4352]{0:T(1024)S(1)}, f32[4352]{0:T(1024)S(1)}, u32[]{:S(2)}, u32[]{:S(2)}) collective-permute-start(f32[4352]{0:T(1024)S(1)} %pad_maximum_fusion), channel_id=1, source_target_pairs={{0,3},{1,0},{2,1},{3,2},{4,7},{5,4},{6,5},{7,6},{8,11},{9,8},{10,9... | collective-permute-start | bytes 52232 | tf_op jit(solution)/shard_map/ppermute | solution.py:77
  100.9 1.1 collective-permute-start.12
  102.1 0.9 collective-permute-start.14
  103.1 0.2 collective-permute-done.6
  103.2 0.2 concatenate.67
  103.5 0.1 fusion.16
  103.5 0.1 dynamic-slice
  103.7 0.2 reshape.381
  103.9 0.1 reduce_max.28
  104.1 0.2 exponential_reduce_fusion.1
  104.3 3.1 %collective-permute-done.14 = f32[128]{0:T(128)S(1)} collective-permute-done((f32[128]{0:T(128)S(1)}, f32[128]{0:T(128)S(1)}, u32[]{:S(2)}, u32[]{:S(2)}) %collective-permute-start.14) | collective-permute-done | bytes 544 | tf_op jit(solution)/shard_map/ppermute | solution.py:141
  107.4 0.5 subtract_exponential_fusion.1
  107.9 1.7 fusion.33
  109.6 4.5 %select_reduce_fusion.1 = (bf16[512,704]{0,1:T(8,128)(2,1)S(1)}, bf16[512,704]{0,1:T(8,128)(2,1)}) fusion(f32[512,8]{0,1:T(8,128)S(1)} %fusion.29, s32[512,8]{0,1:T(8,128)S(1)} %get-tuple-element.12, pred[512,8]{0,1:T(8,128)(4,1)S(1)} %copy-done.9, f32[512,8]{0,1:T(8,128)S(1)} %fusion.30), kind=kLoop, calls=%fused_computation.2 | loop fusion | flops 16580608 | bytes 1495040 | tf_op jit(solution)/shard_map/reduce_sum | solution.py:113
  114.1 0.8 copy-done.3
  115.0 6.0 %add_convert_fusion = bf16[704,4096]{1,0:T(8,128)(2,1)} fusion(f32[704,4096]{1,0:T(8,128)S(1)} %fusion.33, bf16[512,704]{0,1:T(8,128)(2,1)S(1)} %get-tuple-element.5, bf16[128,4096]{1,0:T(8,128)(2,1)S(1)} %copy-done.5, bf16[128,4096]{1,0:T(8,128)(2,1)} %collective-permute-done.4, bf16[128,4096]{1,0:T(8,128)(2,1)S(1)} %copy-done.7, ...), kind=kOutput, calls=%fused_computation | convolution fusion | flops 2975334400 | bytes 22216704 | tf_op jit(solution)/shard_map/dot_general | solution.py:163
  121.0 0.0 reduce-scatter.2.cloned.1.call-update
  121.1 3.9 %convolution_convert_fusion.1 = bf16[128,4096]{1,0:T(8,128)(2,1)S(1)} fusion(bf16[704,4096]{1,0:T(8,128)(2,1)} %all-gather.2.cloned.1.call-done, bf16[512,704]{0,1:T(8,128)(2,1)} %get-tuple-element.6), kind=kOutput, calls=%fused_computation.7 | convolution fusion | flops 738721792 | bytes 6995968 | tf_op jit(solution)/shard_map/dot_general | solution.py:129
  125.0 0.7 collective-permute-start.9
  125.6 0.3 slice-done.1
  125.9 0.1 copy-done.2
  126.1 1.0 convolution_convert_fusion
  127.1 1.0 collective-permute-start.13
  128.1 42.0 %collective-permute-done.9 = bf16[128,4096]{1,0:T(8,128)(2,1)S(1)} collective-permute-done((bf16[128,4096]{1,0:T(8,128)(2,1)S(1)}, bf16[128,4096]{1,0:T(8,128)(2,1)S(1)}, u32[]{:S(2)}, u32[]{:S(2)}) %collective-permute-start.9) | collective-permute-done | bytes 1048608 | tf_op jit(solution)/shard_map/ppermute | solution.py:140
  170.1 1.2 add_convert_fusion.1
  171.4 0.3 collective-permute-start.11
  171.7 1.9 fusion.14
  173.6 17.6 %collective-permute-done.11 = bf16[128,4096]{1,0:T(8,128)(2,1)S(1)} collective-permute-done((bf16[128,4096]{1,0:T(8,128)(2,1)S(1)}, bf16[128,4096]{1,0:T(8,128)(2,1)S(1)}, u32[]{:S(2)}, u32[]{:S(2)}) %collective-permute-start.11) | collective-permute-done | bytes 1048608 | tf_op jit(solution)/shard_map/ppermute | solution.py:140
  191.2 2.8 %add_add_fusion = f32[128,4096]{1,0:T(8,128)} fusion(bf16[128,4096]{1,0:T(8,128)(2,1)S(1)} %collective-permute-done.13, f32[128,4096]{1,0:T(8,128)S(1)} %fusion.14, bf16[128,4096]{1,0:T(8,128)(2,1)S(1)} %collective-permute-done.11, f32[128]{0:T(128)S(1)} %get-tuple-element.17, f32[128]{0:T(128)S(1)} %get-tuple-element.15, ...), kind=kOutput, calls=%fused_computation.15 | convolution fusion | flops 742318080 | bytes 12421120 | tf_op jit(solution)/shard_map/dot_general | solution.py:157
  194.0 2.3 %convert_element_type.79 = f32[88,4096]{1,0:T(8,128)} convert(bf16[88,4096]{1,0:T(8,128)(2,1)} %reduce-scatter.2.cloned.1.call-done) | non-fusion elementwise | flops 360448 | bytes 2162688 | tf_op jit(solution)/shard_map/convert_element_type | solution.py:166
  (60 shorter events, 0.4 us)
Async XLA Ops:
  7.2 57.6 %all-gather.2.cloned.1.call-start = ((), (), s32[]{:S(2)}) async-start(), calls=%async_computation.1 | async-start | bytes 6488064 | tf_op jit(solution)/shard_map/all_gather | solution.py:19
  7.9 186.1 %reduce-scatter.2.cloned.1.call-start = ((), (), s32[]{:S(2)}) async-start(), calls=%async_computation.2 | async-start | bytes 6488064 | tf_op jit(solution)/shard_map/reduce_scatter | solution.py:164
  7.9 9.7 %collective-permute-start = (s32[128,8]{0,1:T(8,128)}, s32[128,8]{0,1:T(8,128)S(1)}, u32[]{:S(2)}, u32[]{:S(2)}) collective-permute-start(s32[128,8]{0,1:T(8,128)} %param.7), channel_id=1, source_target_pairs={{0,3},{1,0},{2,1},{3,2},{4,7},{5,4},{6,5},{7,6},{8,11},{9,8},{10,9... | collective-permute-start | bytes 12296 | tf_op jit(solution)/shard_map/ppermute | solution.py:31
  13.0 47.5 %collective-permute-start.2 = (s32[128,8]{0,1:T(8,128)}, s32[128,8]{0,1:T(8,128)S(1)}, u32[]{:S(2)}, u32[]{:S(2)}) collective-permute-start(s32[128,8]{0,1:T(8,128)} %param.7), channel_id=1, source_target_pairs={{0,1},{1,2},{2,3},{3,0},{4,5},{5,6},{6,7},{7,4},{8,9},{9,10},{10,1... | collective-permute-start | bytes 12296 | tf_op jit(solution)/shard_map/ppermute | solution.py:35
  13.0 58.2 %collective-permute-start.5 = (bf16[128,4096]{1,0:T(8,128)(2,1)}, bf16[128,4096]{1,0:T(8,128)(2,1)S(1)}, u32[]{:S(2)}, u32[]{:S(2)}) collective-permute-start(bf16[128,4096]{1,0:T(8,128)(2,1)} %param.4), channel_id=1, source_target_pairs={{0,1},{1,2},{2,3},{3,0},{4,5},{5,6},{6,7},{7,4},{8,9},{9,10},{10,1... | collective-permute-start | bytes 3145736 | tf_op jit(solution)/shard_map/ppermute | solution.py:35
  13.1 49.5 %collective-permute-start.3 = (bf16[128,4096]{1,0:T(8,128)(2,1)}, bf16[128,4096]{1,0:T(8,128)(2,1)S(1)}, u32[]{:S(2)}, u32[]{:S(2)}) collective-permute-start(bf16[128,4096]{1,0:T(8,128)(2,1)} %param.4), channel_id=1, source_target_pairs={{0,3},{1,0},{2,1},{3,2},{4,7},{5,4},{6,5},{7,6},{8,11},{9,8},{10,9... | collective-permute-start | bytes 3145736 | tf_op jit(solution)/shard_map/ppermute | solution.py:31
  17.6 42.9 %collective-permute-start.1 = (s32[128,8]{0,1:T(8,128)S(1)}, s32[128,8]{0,1:T(8,128)S(1)}, u32[]{:S(2)}, u32[]{:S(2)}) collective-permute-start(s32[128,8]{0,1:T(8,128)S(1)} %collective-permute-done), channel_id=1, source_target_pairs={{0,3},{1,0},{2,1},{3,2},{4,7},{5,4},{6,5},{7,6},{8,11},{9,8},{10,9... | collective-permute-start | bytes 12296 | tf_op jit(solution)/shard_map/ppermute | solution.py:31
  62.5 8.7 %copy-start.6 = (bf16[128,4096]{1,0:T(8,128)(2,1)}, bf16[128,4096]{1,0:T(8,128)(2,1)S(1)}, u32[]{:S(2)}) copy-start(bf16[128,4096]{1,0:T(8,128)(2,1)S(1)} %collective-permute-done.3) | copy-start | bytes 3145732
  62.5 25.8 %collective-permute-start.4 = (bf16[128,4096]{1,0:T(8,128)(2,1)S(1)}, bf16[128,4096]{1,0:T(8,128)(2,1)}, u32[]{:S(2)}, u32[]{:S(2)}) collective-permute-start(bf16[128,4096]{1,0:T(8,128)(2,1)S(1)} %collective-permute-done.3), channel_id=1, source_target_pairs={{0,3},{1,0},{2,1},{3,2},{4,7},{5,4},{6,5},{7,6},{8,11},{9,8},{10,9... | collective-permute-start | bytes 3145736 | tf_op jit(solution)/shard_map/ppermute | solution.py:31
  64.7 4.8 %copy-start = (bf16[704,4096]{1,0:T(8,128)(2,1)S(1)}, bf16[704,4096]{1,0:T(8,128)(2,1)}, u32[]{:S(2)}) copy-start(bf16[704,4096]{1,0:T(8,128)(2,1)} %all-gather.2.cloned.1.call-done) | copy-start | bytes 17301508
  71.2 17.1 %copy-start.4 = (bf16[128,4096]{1,0:T(8,128)(2,1)}, bf16[128,4096]{1,0:T(8,128)(2,1)S(1)}, u32[]{:S(2)}) copy-start(bf16[128,4096]{1,0:T(8,128)(2,1)S(1)} %collective-permute-done.5) | copy-start | bytes 3145732
  72.9 18.6 %copy-start.8 = (pred[512,8]{0,1:T(8,128)(4,1)S(1)}, pred[512,8]{0,1:T(8,128)(4,1)}, u32[]{:S(2)}) copy-start(pred[512,8]{0,1:T(8,128)(4,1)} %get-tuple-element.9) | copy-start | bytes 12292
  72.9 35.0 %copy-start.1 = (bf16[128,4096]{1,0:T(8,128)(2,1)S(1)}, bf16[128,4096]{1,0:T(8,128)(2,1)}, u32[]{:S(2)}) copy-start(bf16[128,4096]{1,0:T(8,128)(2,1)} %param.4) | copy-start | bytes 3145732
  88.3 8.5 %copy-start.11 = (s32[128]{0:T(128)S(1)}, s32[128]{0:T(128)}, u32[]{:S(2)}) copy-start(s32[128]{0:T(128)} %param.6) | copy-start | bytes 1540
  88.3 15.1 %copy-start.10 = (s32[1,8,4,128]{3,1,2,0:T(8,128)S(1)}, s32[1,8,4,128]{3,1,2,0:T(8,128)}, u32[]{:S(2)}) copy-start(s32[1,8,4,128]{3,1,2,0:T(8,128)} %copy.27) | copy-start | bytes 49156
  88.3 16.0 %copy-start.9 = (pred[512,8]{0,1:T(8,128)(4,1)S(1)}, pred[512,8]{0,1:T(8,128)(4,1)}, u32[]{:S(2)}) copy-start(pred[512,8]{0,1:T(8,128)(4,1)} %get-tuple-element.9) | copy-start | bytes 12292
  94.3 6.6 %collective-permute-start.10 = (f32[128]{0:T(128)S(1)}, f32[128]{0:T(128)S(1)}, u32[]{:S(2)}, u32[]{:S(2)}) collective-permute-start(f32[128]{0:T(128)S(1)} %slice.47), channel_id=1, source_target_pairs={{0,3},{1,0},{2,1},{3,2},{4,7},{5,4},{6,5},{7,6},{8,11},{9,8},{10,9... | collective-permute-start | bytes 1544 | tf_op jit(solution)/shard_map/ppermute | solution.py:141
  97.0 6.0 %collective-permute-start.8 = (f32[4352]{0:T(1024)S(1)}, f32[4352]{0:T(1024)S(1)}, u32[]{:S(2)}, u32[]{:S(2)}) collective-permute-start(f32[4352]{0:T(1024)S(1)} %pad_maximum_fusion), channel_id=1, source_target_pairs={{0,1},{1,2},{2,3},{3,0},{4,5},{5,6},{6,7},{7,4},{8,9},{9,10},{10,1... | collective-permute-start | bytes 52232 | tf_op jit(solution)/shard_map/ppermute | solution.py:77
  97.1 5.9 %collective-permute-start.7 = (f32[4352]{0:T(1024)S(1)}, f32[4352]{0:T(1024)S(1)}, u32[]{:S(2)}, u32[]{:S(2)}) collective-permute-start(f32[4352]{0:T(1024)S(1)} %pad_maximum_fusion), channel_id=1, source_target_pairs={{0,2},{1,3},{2,0},{3,1},{4,6},{5,7},{6,4},{7,5},{8,10},{9,11},{10,... | collective-permute-start | bytes 52232 | tf_op jit(solution)/shard_map/ppermute | solution.py:77
  98.1 5.2 %collective-permute-start.6 = (f32[4352]{0:T(1024)S(1)}, f32[4352]{0:T(1024)S(1)}, u32[]{:S(2)}, u32[]{:S(2)}) collective-permute-start(f32[4352]{0:T(1024)S(1)} %pad_maximum_fusion), channel_id=1, source_target_pairs={{0,3},{1,0},{2,1},{3,2},{4,7},{5,4},{6,5},{7,6},{8,11},{9,8},{10,9... | collective-permute-start | bytes 52232 | tf_op jit(solution)/shard_map/ppermute | solution.py:77
  100.9 6.5 %collective-permute-start.12 = (f32[128]{0:T(128)S(1)}, f32[128]{0:T(128)S(1)}, u32[]{:S(2)}, u32[]{:S(2)}) collective-permute-start(f32[128]{0:T(128)S(1)} %get-tuple-element.8), channel_id=1, source_target_pairs={{0,3},{1,0},{2,1},{3,2},{4,7},{5,4},{6,5},{7,6},{8,11},{9,8},{10,9... | collective-permute-start | bytes 1544 | tf_op jit(solution)/shard_map/ppermute | solution.py:141
  102.1 5.3 %collective-permute-start.14 = (f32[128]{0:T(128)S(1)}, f32[128]{0:T(128)S(1)}, u32[]{:S(2)}, u32[]{:S(2)}) collective-permute-start(f32[128]{0:T(128)S(1)} %get-tuple-element.19), channel_id=1, source_target_pairs={{0,1},{1,2},{2,3},{3,0},{4,5},{5,6},{6,7},{7,4},{8,9},{9,10},{10,1... | collective-permute-start | bytes 1544 | tf_op jit(solution)/shard_map/ppermute | solution.py:141
  107.9 7.1 %copy-start.5 = (bf16[128,4096]{1,0:T(8,128)(2,1)S(1)}, bf16[128,4096]{1,0:T(8,128)(2,1)}, u32[]{:S(2)}) copy-start(bf16[128,4096]{1,0:T(8,128)(2,1)} %copy-done.4) | copy-start | bytes 3145732
  107.9 7.1 %copy-start.7 = (bf16[128,4096]{1,0:T(8,128)(2,1)S(1)}, bf16[128,4096]{1,0:T(8,128)(2,1)}, u32[]{:S(2)}) copy-start(bf16[128,4096]{1,0:T(8,128)(2,1)} %copy-done.6) | copy-start | bytes 3145732
  114.1 0.8 copy-start.3
  121.0 4.6 %slice-start = ((s8[5767168]{0:T(1024)(128)(4,1)}), s8[1572864]{0:T(1024)(128)(4,1)S(1)}, s32[]{:S(2)}) async-start(s8[5767168]{0:T(1024)(128)(4,1)} %bitcast.27), calls=%async_computation.3 | async-start | bytes 3145728
  121.1 4.9 %slice-start.1 = ((s8[5767168]{0:T(1024)(128)(4,1)}), s8[4194304]{0:T(1024)(128)(4,1)S(1)}, s32[]{:S(2)}) async-start(s8[5767168]{0:T(1024)(128)(4,1)} %bitcast.27), calls=%async_computation.4 | async-start | bytes 8388608
  121.1 5.0 %copy-start.2 = (bf16[512,704]{0,1:T(8,128)(2,1)S(1)}, bf16[512,704]{0,1:T(8,128)(2,1)}, u32[]{:S(2)}) copy-start(bf16[512,704]{0,1:T(8,128)(2,1)} %get-tuple-element.6) | copy-start | bytes 2162692
  125.0 45.2 %collective-permute-start.9 = (bf16[128,4096]{1,0:T(8,128)(2,1)S(1)}, bf16[128,4096]{1,0:T(8,128)(2,1)S(1)}, u32[]{:S(2)}, u32[]{:S(2)}) collective-permute-start(bf16[128,4096]{1,0:T(8,128)(2,1)S(1)} %convolution_convert_fusion.1), channel_id=1, source_target_pairs={{0,3},{1,0},{2,1},{3,2},{4,7},{5,4},{6,5},{7,6},{8,11},{9,8},{10,9... | collective-permute-start | bytes 3145736 | tf_op jit(solution)/shard_map/ppermute | solution.py:140
  127.1 46.5 %collective-permute-start.13 = (bf16[128,4096]{1,0:T(8,128)(2,1)S(1)}, bf16[128,4096]{1,0:T(8,128)(2,1)S(1)}, u32[]{:S(2)}, u32[]{:S(2)}) collective-permute-start(bf16[128,4096]{1,0:T(8,128)(2,1)S(1)} %convolution_convert_fusion), channel_id=1, source_target_pairs={{0,1},{1,2},{2,3},{3,0},{4,5},{5,6},{6,7},{7,4},{8,9},{9,10},{10,1... | collective-permute-start | bytes 3145736 | tf_op jit(solution)/shard_map/ppermute | solution.py:140
  171.4 19.8 %collective-permute-start.11 = (bf16[128,4096]{1,0:T(8,128)(2,1)S(1)}, bf16[128,4096]{1,0:T(8,128)(2,1)S(1)}, u32[]{:S(2)}, u32[]{:S(2)}) collective-permute-start(bf16[128,4096]{1,0:T(8,128)(2,1)S(1)} %add_convert_fusion.1), channel_id=1, source_target_pairs={{0,3},{1,0},{2,1},{3,2},{4,7},{5,4},{6,5},{7,6},{8,11},{9,8},{10,9... | collective-permute-start | bytes 3145736 | tf_op jit(solution)/shard_map/ppermute | solution.py:140
Sparse Core Ops, SparseCore 0:
  9.9 46.0 all-gather.1
  121.2 57.3 reduce-scatter.1

commit v8 on v6

--- a/solution.py
+++ b/solution.py
@@ -70,15 +70,41 @@
     pool_sum = jnp.sum(jnp.exp(pooled - pool_max[:, None]), axis=1)
     hard_origin = to_origin(hard_mine.reshape(slabs, query_rows_dev * hard_count))
     payload = jnp.concatenate([hard_origin.reshape(-1), pool_max, pool_sum])
-    gathered = to_origin(
-        jnp.stack(
-            [payload]
-            + [
-                lax.ppermute(payload, "slab", [(i, (i - t) % slabs) for i in range(slabs)])
-                for t in range(1, slabs)
-            ]
-        )
-    )
+    far_below = -1e30
+    local_max = jnp.max(jnp.where(mine, hard_mine, far_below), axis=1)
+    local_max = local_max.astype(jnp.bfloat16).astype(jnp.float32)
+    local_weight = jnp.where(mine, jnp.exp(hard_mine - local_max[:, None]), 0.0)
+    weight_matrix = jnp.sum(
+        jnp.where(hard_hit, local_weight.astype(jnp.bfloat16).astype(jnp.float32)[:, :, None], 0.0),
+        axis=1,
+    ).astype(jnp.bfloat16)
+
+    def rows_of(x, block):
+        return x[block * query_rows_dev : (block + 1) * query_rows_dev]
+
+    def scaled_for(block):
+        part = jnp.dot(rows_of(weight_matrix, block), pool, preferred_element_type=jnp.float32)
+        return part, rows_of(local_max, block)
+
+    def merge(first, second):
+        (part_a, scale_a), (part_b, scale_b) = first, second
+        scale = jnp.maximum(scale_a, scale_b)
+        part = part_a * jnp.exp(scale_a - scale)[:, None] + part_b * jnp.exp(scale_b - scale)[:, None]
+        return part, scale
+
+    def hop(carried, perm):
+        part, scale = carried
+        scale_row = jnp.zeros((1, model_width), jnp.bfloat16)
+        scale_row = lax.dynamic_update_slice(scale_row, scale.astype(jnp.bfloat16)[None], (0, 0))
+        sent = lax.ppermute(
+            jnp.concatenate([part.astype(jnp.bfloat16), scale_row], axis=0), "slab", perm
+        ).astype(jnp.float32)
+        return sent[:query_rows_dev], sent[query_rows_dev, :query_rows_dev]
+
+    first_down = scaled_for(slabs - steps_down) if steps_down else None
+    first_up = scaled_for(steps_up) if steps_up else None
+    (first_down, first_up), payload = lax.optimization_barrier(((first_down, first_up), payload))
+    gathered = lax.all_gather(payload, "slab", axis=0)
     hard_split = column_rows * hard_count
     owner_origin = to_origin(owner_slab.reshape(slabs, query_rows_dev * hard_count))
     slab_iota = jnp.arange(slabs, dtype=jnp.int32)[:, None, None]
@@ -114,24 +140,20 @@
         jnp.where(hard_hit, coef_hard.astype(jnp.float32)[:, :, None], 0.0), axis=1
     ).astype(jnp.bfloat16)
 
-    def grad_for(block):
-        rows = hard_matrix[block * query_rows_dev : (block + 1) * query_rows_dev]
-        return jnp.dot(rows, pool, preferred_element_type=jnp.float32)
-
-    def hop(part, perm):
-        return lax.ppermute(part.astype(jnp.bfloat16), "slab", perm).astype(jnp.float32)
-
-    carried = grad_for(0)
+    arrived = []
     if steps_down:
-        down = grad_for(slabs - steps_down)
+        down = first_down
         for step in range(1, steps_down):
-            down = hop(down, ring_down) + grad_for(slabs - steps_down + step)
-        carried = carried + hop(down, ring_down)
+            down = merge(hop(down, ring_down), scaled_for(slabs - steps_down + step))
+        arrived.append(hop(down, ring_down))
     if steps_up:
-        up = grad_for(steps_up)
+        up = first_up
         for step in range(1, steps_up):
-            up = hop(up, ring_up) + grad_for(steps_up - step)
-        carried = carried + hop(up, ring_up)
+            up = merge(hop(up, ring_up), scaled_for(steps_up - step))
+        arrived.append(hop(up, ring_up))
+    carried = jnp.dot(rows_of(hard_matrix, 0), pool, preferred_element_type=jnp.float32)
+    for part, scale in arrived:
+        carried = carried + part * jnp.exp(scale - row_lse)[:, None]
     pool_grad = jnp.dot(coef_pool, pool, preferred_element_type=jnp.float32)
     query_grad = pool_grad + carried
 

time: 196 us -> 266 us (1.36)
  blocking collectives: 0 us -> 31.4 us
  waiting for transfers between devices: 117 us -> 139 us
  other arithmetic: 9.3 us -> 21.3 us
  matrix products: 26.1 us -> 35.5 us
  starting transfers between devices: 25.1 us -> 19.4 us
    reduce_scatter x1, waiting for transfers between devices: 0.01 us -> 47.6 us  [per_device(): lax.psum_scatter(partial.astype(jnp.bfloat16), 'blk', scatter_dimension=0...]
    all_gather x0 -> x1, blocking collectives: none -> 31.4 us  [per_device(): gathered = lax.all_gather(payload, 'slab', axis=0)]
    ppermute x6 -> x3, waiting for transfers between devices: 60.1 us -> 33.8 us  [hop(): lax.ppermute(jnp.concatenate([part.astype(jnp.bfloat16), scale_row], axis...]
    ppermute x6 -> x3, starting transfers between devices: 11.8 us -> 6.1 us  [hop(): lax.ppermute(jnp.concatenate([part.astype(jnp.bfloat16), scale_row], axis...]
    dot_general x4, matrix products: 8.61 us -> 13.4 us  [the longest x3 9.75 us: scaled_for(): jnp.dot(rows_of(weight_matrix, block), pool, preferred_element_type=jnp.f...]
    concatenate x0 -> x3, other arithmetic: none -> 4.53 us  [hop(): jnp.concatenate([part.astype(jnp.bfloat16), scale_row], axis=0)]
    convert_element_type x0 -> x5, other arithmetic: none -> 4.44 us  [the longest x3 4.43 us: hop(): sent = lax.ppermute(jnp.concatenate([part.astype(jnp.bfloat16), scale_row...]
    reduce_sum x0 -> x1, other arithmetic: none -> 2.96 us  [per_device(): jnp.sum(jnp.where(hard_hit, local_weight.astype(jnp.bfloat16).astype(jnp....]
  transfers between devices with their start and end apart: 14 -> 11, of which waited for: 8 -> 5; matrix products, arithmetic and copies ran while one was open for 10% -> 11% of each run, Pallas kernels for 0% -> 0%
where the time goes in v8:
time: 266 us
  waiting for transfers between devices  139 us (52%)
  matrix products  35.5 us (13%)
  blocking collectives  31.4 us (12%)
  other arithmetic  21.3 us (8%)
  starting transfers between devices  19.4 us (7%)
  between operations  14.5 us (5%)
  local copies, waits for them, and re-layouts  5.05 us (2%)
    ppermute x4, waiting for transfers between devices, ring_gather(): current = lax.ppermute(current, 'slab', ring_down)  56.7 us
    reduce_scatter x1, waiting for transfers between devices, per_device(): lax.psum_scatter(partial.astype(jnp.bfloat16), 'blk', scatter_dimension=0...  47.6 us
    ppermute x3, waiting for transfers between devices, hop(): lax.ppermute(jnp.concatenate([part.astype(jnp.bfloat16), scale_row], axis...  33.8 us
    all_gather x1, blocking collectives, per_device(): gathered = lax.all_gather(payload, 'slab', axis=0)  31.4 us
    ppermute x4, starting transfers between devices, ring_gather(): current = lax.ppermute(current, 'slab', ring_down)  13.2 us
    dot_general x4, matrix products, per_device(): lax.dot_general(block, pool, contract_rows, preferred_element_type=jnp.fl...  10.7 us
    dot_general x3, matrix products, scaled_for(): jnp.dot(rows_of(weight_matrix, block), pool, preferred_element_type=jnp.f...  9.75 us
    ppermute x3, starting transfers between devices, hop(): lax.ppermute(jnp.concatenate([part.astype(jnp.bfloat16), scale_row], axis...  6.1 us
  transfers between devices with their start and end apart: 11, of which 5 were waited for; matrix products, arithmetic and copies ran while one was open for 11% of the time, Pallas kernels for 0%

profile of v8, /device:TPU:0, one launch (start us, length us, event | category | flops | bytes accessed | tf_op | source)
XLA Modules:
  0.0 266.0 jit_solution(13512675791804893511)
XLA Ops:
  7.2 0.0 all-gather.4.cloned.1.call-start
  7.2 0.7 all-gather.4.cloned.1.call-update
  7.9 0.0 reduce-scatter.2.cloned.1.call-start
  8.0 5.1 %collective-permute-start = (s32[128,8]{0,1:T(8,128)}, s32[128,8]{0,1:T(8,128)S(1)}, u32[]{:S(2)}, u32[]{:S(2)}) collective-permute-start(s32[128,8]{0,1:T(8,128)} %param.7), channel_id=1, source_target_pairs={{0,3},{1,0},{2,1},{3,2},{4,7},{5,4},{6,5},{7,6},{8,11},{9,8},{10,9... | collective-permute-start | bytes 12296 | tf_op jit(solution)/shard_map/ppermute | solution.py:31
  13.1 0.0 collective-permute-start.2
  13.1 0.0 collective-permute-start.5
  13.1 3.9 %collective-permute-start.3 = (bf16[128,4096]{1,0:T(8,128)(2,1)}, bf16[128,4096]{1,0:T(8,128)(2,1)S(1)}, u32[]{:S(2)}, u32[]{:S(2)}) collective-permute-start(bf16[128,4096]{1,0:T(8,128)(2,1)} %param.4), channel_id=1, source_target_pairs={{0,3},{1,0},{2,1},{3,2},{4,7},{5,4},{6,5},{7,6},{8,11},{9,8},{10,9... | collective-permute-start | bytes 3145736 | tf_op jit(solution)/shard_map/ppermute | solution.py:31
  16.9 0.7 constant_dynamic-update-slice_fusion.3
  17.6 2.0 collective-permute-start.1
  19.6 40.9 %collective-permute-done.1 = s32[128,8]{0,1:T(8,128)S(1)} collective-permute-done((s32[128,8]{0,1:T(8,128)S(1)}, s32[128,8]{0,1:T(8,128)S(1)}, u32[]{:S(2)}, u32[]{:S(2)}) %collective-permute-start.1) | collective-permute-done | bytes 4128 | tf_op jit(solution)/shard_map/ppermute | solution.py:31
  60.5 0.0 collective-permute-done.2
  60.6 0.2 copy.29
  60.8 0.2 and.89
  60.9 0.1 copy.30
  61.1 0.2 div.38
  61.3 2.3 collective-permute-start.4
  63.6 4.4 %fusion.55 = f32[128,704]{0,1:T(8,128)S(1)} fusion(bf16[128,4096]{1,0:T(8,128)(2,1)S(1)} %copy-done.5, bf16[704,4096]{1,0:T(8,128)(2,1)} %all-gather.4.cloned.1.call-done), kind=kOutput, calls=%fused_computation.117 | convolution fusion | flops 738197504 | bytes 7176192 | tf_op jit(solution)/shard_map/dot_general | solution.py:52
  68.1 1.7 fusion.56
  69.7 0.0 collective-permute-done.5
  69.8 1.7 fusion.58
  71.4 15.7 %collective-permute-done.4 = bf16[128,4096]{1,0:T(8,128)(2,1)} collective-permute-done((bf16[128,4096]{1,0:T(8,128)(2,1)S(1)}, bf16[128,4096]{1,0:T(8,128)(2,1)}, u32[]{:S(2)}, u32[]{:S(2)}) %collective-permute-start.4) | collective-permute-done | bytes 1048608 | tf_op jit(solution)/shard_map/ppermute | solution.py:31
  87.2 2.9 %fusion.57 = f32[128,704]{0,1:T(8,128)S(1)} fusion(bf16[128,4096]{1,0:T(8,128)(2,1)} %collective-permute-done.4, bf16[704,4096]{1,0:T(8,128)(2,1)S(1)} %copy-done), kind=kOutput, calls=%fused_computation.119 | convolution fusion | flops 738197504 | bytes 7176192 | tf_op jit(solution)/shard_map/dot_general | solution.py:52
  90.1 0.1 maximum_multiply_fusion
  90.2 0.0 copy-start.12
  90.2 0.1 slice_reduce_fusion
  90.3 2.7 %select_reduce_fusion.2 = f32[512,8]{0,1:T(8,128)S(1)} fusion(f32[512,704]{0,1:T(8,128)S(1)} %maximum_multiply_fusion, s32[512,8]{0,1:T(8,128)S(1)} %get-tuple-element.15, pred[512,8]{0,1:T(8,128)(4,1)S(1)} %fusion.31), kind=kLoop, calls=%fused_computation.3 | loop fusion | flops 11530240 | bytes 1478656 | tf_op jit(solution)/shard_map/reduce_sum | solution.py:67
  93.0 0.1 copy.28
  93.2 0.2 reshape.381
  93.4 0.0 slice-start
  93.4 3.0 %select_reduce_fusion.1 = bf16[512,704]{0,1:T(8,128)(2,1)S(1)} fusion(f32[512,8]{0,1:T(8,128)S(1)} %fusion.40, s32[512,8]{0,1:T(8,128)S(1)} %get-tuple-element.15, pred[512,8]{0,1:T(8,128)(4,1)S(1)} %fusion.31), kind=kLoop, calls=%fused_computation.2 | loop fusion | flops 11173888 | bytes 757760 | tf_op jit(solution)/shard_map/reduce_sum | solution.py:77
  96.4 0.1 exponential_reduce_fusion
  96.5 0.0 slice-start.1
  96.5 4.8 %fusion.24 = bf16[128,4096]{1,0:T(8,128)(2,1)} fusion(bf16[704,4096]{1,0:T(8,128)(2,1)} %all-gather.4.cloned.1.call-done, bf16[512,704]{0,1:T(8,128)(2,1)S(1)} %select_reduce_fusion.1), kind=kOutput, calls=%fused_computation.39 | convolution fusion | flops 738197504 | bytes 6995968 | tf_op jit(solution)/shard_map/dot_general | solution.py:86
  101.3 1.0 fusion.26
  102.4 1.1 fusion.16
  103.5 2.3 collective-permute-start.6
  105.8 31.4 %all-gather.1 = f32[4,1,4352]{2,1,0:T(1,128)S(1)} all-gather(f32[1,1,4352]{2,1,0:T(1,128)S(1)} %reshape.386), channel_id=2, replica_groups=mesh['blk'=8,'slab'=4] {'slab'}, dimensions={0}, use_global_device_ids=true | all-gather | bytes 87040 | tf_op jit(solution)/shard_map/all_gather | solution.py:107
  137.3 0.1 fusion.28
  137.3 2.3 fusion.18
  139.7 0.7 collective-permute-start.8
  140.4 1.5 convert_element_type.99
  142.0 3.9 %fusion.15 = bf16[128,4096]{1,0:T(8,128)(2,1)S(1)} fusion(f32[129,4096]{1,0:T(8,128)S(1)} %convert_element_type.99, f32[128]{0:T(128)S(1)} %get-tuple-element.18, bf16[704,4096]{1,0:T(8,128)(2,1)} %all-gather.4.cloned.1.call-done, f32[128]{0:T(128)S(1)} %get-tuple-element.17, bf16[512,704]{0,1:T(8,128)(2,1)} %copy-done.6), kind=kOutput, calls=%fused_computation.25 | convolution fusion | flops 740294656 | bytes 9094144 | tf_op jit(solution)/shard_map/dot_general | solution.py:86
  145.9 1.1 fusion.17
  147.0 3.1 %collective-permute-start.7 = (bf16[129,4096]{1,0:T(8,128)(2,1)}, bf16[129,4096]{1,0:T(8,128)(2,1)}, u32[]{:S(2)}, u32[]{:S(2)}) collective-permute-start(bf16[129,4096]{1,0:T(8,128)(2,1)} %fusion.17), channel_id=1, source_target_pairs={{0,3},{1,0},{2,1},{3,2},{4,7},{5,4},{6,5},{7,6},{8,11},{9,8},{10,9... | collective-permute-start | bytes 3170312 | tf_op jit(solution)/shard_map/ppermute | solution.py:99
  150.1 0.2 reshape.384
  150.3 0.1 reduce_max.29
  150.4 0.2 exponential_reduce_fusion.1
  150.7 2.8 %select_reduce_fusion = bf16[512,704]{0,1:T(8,128)(2,1)S(1)} fusion(f32[512,8]{0,1:T(8,128)S(1)} %fusion.42, s32[512,8]{0,1:T(8,128)S(1)} %get-tuple-element.15, pred[512,8]{0,1:T(8,128)(4,1)S(1)} %fusion.31), kind=kLoop, calls=%fused_computation.1 | loop fusion | flops 11173888 | bytes 757760 | tf_op jit(solution)/shard_map/reduce_sum | solution.py:139
  153.5 15.8 %collective-permute-done.8 = bf16[129,4096]{1,0:T(8,128)(2,1)} collective-permute-done((bf16[129,4096]{1,0:T(8,128)(2,1)}, bf16[129,4096]{1,0:T(8,128)(2,1)}, u32[]{:S(2)}, u32[]{:S(2)}) %collective-permute-start.8) | collective-permute-done | bytes 1056800 | tf_op jit(solution)/shard_map/ppermute | solution.py:99
  169.3 1.5 convert_element_type.105
  170.8 18.0 %collective-permute-done.7 = bf16[129,4096]{1,0:T(8,128)(2,1)} collective-permute-done((bf16[129,4096]{1,0:T(8,128)(2,1)}, bf16[129,4096]{1,0:T(8,128)(2,1)}, u32[]{:S(2)}, u32[]{:S(2)}) %collective-permute-start.7) | collective-permute-done | bytes 1056800 | tf_op jit(solution)/shard_map/ppermute | solution.py:99
  188.8 1.5 convert_element_type.102
  190.3 0.6 fusion.47
  190.9 0.8 copy-done.3
  191.7 1.7 fusion.50
  193.3 6.0 %add_convert_fusion = bf16[704,4096]{1,0:T(8,128)(2,1)} fusion(f32[704,4096]{1,0:T(8,128)S(1)} %fusion.50, bf16[512,704]{0,1:T(8,128)(2,1)S(1)} %select_reduce_fusion, bf16[128,4096]{1,0:T(8,128)(2,1)S(1)} %copy-done.9, bf16[128,4096]{1,0:T(8,128)(2,1)} %collective-permute-done.4, bf16[128,4096]{1,0:T(8,128)(2,1)S(1)} %copy-done.11, ...), kind=kOutput, calls=%fused_computation | convolution fusion | flops 2975334400 | bytes 22216704 | tf_op jit(solution)/shard_map/dot_general | solution.py:163
  199.3 0.0 reduce-scatter.2.cloned.1.call-update
  199.4 3.8 %fusion.51 = f32[128,4096]{1,0:T(8,128)S(1)} fusion(bf16[704,4096]{1,0:T(8,128)(2,1)} %all-gather.4.cloned.1.call-done, f32[512,704]{0,1:T(8,128)S(1)} %maximum_multiply_fusion, f32[128]{0:T(128)S(1)} %get-tuple-element.25, s32[128]{0:T(128)S(1)} %copy-done.12), kind=kOutput, calls=%fused_computation.114 | convolution fusion | flops 738648064 | bytes 8225792 | tf_op jit(solution)/shard_map/dot_general | solution.py:157
  203.2 0.9 slice-done.3
  204.1 0.7 copy-done.2
  204.8 0.7 copy-done.4
  205.5 3.6 %fusion.12 = f32[128,4096]{1,0:T(8,128)} fusion(f32[128,4096]{1,0:T(8,128)S(1)} %fusion.51, f32[129,4096]{1,0:T(8,128)S(1)} %copy-done.2, f32[129,4096]{1,0:T(8,128)S(1)} %copy-done.4, f32[128]{0:T(128)S(1)} %get-tuple-element.24, f32[128]{0:T(128)S(1)} %get-tuple-element.22, bf16[704,4096]{1,0:T(8,128)(2,1)S(1)} %bitcast.65, bf16[512,704]{0,1:T(8,128)(2,1)} %copy-done.7), kind=kOutput, calls=%fused_computation.20 | convolution fusion | flops 740818944 | bytes 14337024 | tf_op jit(solution)/shard_map/dot_general | solution.py:154
  209.2 47.6 %reduce-scatter.2.cloned.1.call-done = bf16[88,4096]{1,0:T(8,128)(2,1)} async-done(((bf16[704,4096]{1,0:T(8,128)(2,1)}), bf16[88,4096]{1,0:T(8,128)(2,1)}) %reduce-scatter.2.cloned.1.call-update) | async-done | bytes 720912 | tf_op jit(solution)/shard_map/reduce_scatter | solution.py:164
  256.8 2.3 convert_element_type.107
  (61 shorter events, 0.4 us)
Async XLA Ops:
  7.2 56.4 %copy-start.5 = (bf16[128,4096]{1,0:T(8,128)(2,1)S(1)}, bf16[128,4096]{1,0:T(8,128)(2,1)}, u32[]{:S(2)}) copy-start(bf16[128,4096]{1,0:T(8,128)(2,1)} %param.4) | copy-start | bytes 3145732
  7.2 56.4 %all-gather.4.cloned.1.call-start = ((), (), s32[]{:S(2)}) async-start(), calls=%async_computation.1 | async-start | bytes 6488064 | tf_op jit(solution)/shard_map/all_gather | solution.py:19
  7.9 248.9 %reduce-scatter.2.cloned.1.call-start = ((), (), s32[]{:S(2)}) async-start(), calls=%async_computation.2 | async-start | bytes 6488064 | tf_op jit(solution)/shard_map/reduce_scatter | solution.py:164
  8.0 9.7 %collective-permute-start = (s32[128,8]{0,1:T(8,128)}, s32[128,8]{0,1:T(8,128)S(1)}, u32[]{:S(2)}, u32[]{:S(2)}) collective-permute-start(s32[128,8]{0,1:T(8,128)} %param.7), channel_id=1, source_target_pairs={{0,3},{1,0},{2,1},{3,2},{4,7},{5,4},{6,5},{7,6},{8,11},{9,8},{10,9... | collective-permute-start | bytes 12296 | tf_op jit(solution)/shard_map/ppermute | solution.py:31
  13.1 47.5 %collective-permute-start.2 = (s32[128,8]{0,1:T(8,128)}, s32[128,8]{0,1:T(8,128)S(1)}, u32[]{:S(2)}, u32[]{:S(2)}) collective-permute-start(s32[128,8]{0,1:T(8,128)} %param.7), channel_id=1, source_target_pairs={{0,1},{1,2},{2,3},{3,0},{4,5},{5,6},{6,7},{7,4},{8,9},{9,10},{10,1... | collective-permute-start | bytes 12296 | tf_op jit(solution)/shard_map/ppermute | solution.py:35
  13.1 56.7 %collective-permute-start.5 = (bf16[128,4096]{1,0:T(8,128)(2,1)}, bf16[128,4096]{1,0:T(8,128)(2,1)S(1)}, u32[]{:S(2)}, u32[]{:S(2)}) collective-permute-start(bf16[128,4096]{1,0:T(8,128)(2,1)} %param.4), channel_id=1, source_target_pairs={{0,1},{1,2},{2,3},{3,0},{4,5},{5,6},{6,7},{7,4},{8,9},{9,10},{10,1... | collective-permute-start | bytes 3145736 | tf_op jit(solution)/shard_map/ppermute | solution.py:35
  13.1 48.2 %collective-permute-start.3 = (bf16[128,4096]{1,0:T(8,128)(2,1)}, bf16[128,4096]{1,0:T(8,128)(2,1)S(1)}, u32[]{:S(2)}, u32[]{:S(2)}) collective-permute-start(bf16[128,4096]{1,0:T(8,128)(2,1)} %param.4), channel_id=1, source_target_pairs={{0,3},{1,0},{2,1},{3,2},{4,7},{5,4},{6,5},{7,6},{8,11},{9,8},{10,9... | collective-permute-start | bytes 3145736 | tf_op jit(solution)/shard_map/ppermute | solution.py:31
  17.6 42.9 %collective-permute-start.1 = (s32[128,8]{0,1:T(8,128)S(1)}, s32[128,8]{0,1:T(8,128)S(1)}, u32[]{:S(2)}, u32[]{:S(2)}) collective-permute-start(s32[128,8]{0,1:T(8,128)S(1)} %collective-permute-done), channel_id=1, source_target_pairs={{0,3},{1,0},{2,1},{3,2},{4,7},{5,4},{6,5},{7,6},{8,11},{9,8},{10,9... | collective-permute-start | bytes 12296 | tf_op jit(solution)/shard_map/ppermute | solution.py:31
  61.3 6.7 %copy-start.10 = (bf16[128,4096]{1,0:T(8,128)(2,1)}, bf16[128,4096]{1,0:T(8,128)(2,1)S(1)}, u32[]{:S(2)}) copy-start(bf16[128,4096]{1,0:T(8,128)(2,1)S(1)} %collective-permute-done.3) | copy-start | bytes 3145732
  61.3 25.9 %collective-permute-start.4 = (bf16[128,4096]{1,0:T(8,128)(2,1)S(1)}, bf16[128,4096]{1,0:T(8,128)(2,1)}, u32[]{:S(2)}, u32[]{:S(2)}) collective-permute-start(bf16[128,4096]{1,0:T(8,128)(2,1)S(1)} %collective-permute-done.3), channel_id=1, source_target_pairs={{0,3},{1,0},{2,1},{3,2},{4,7},{5,4},{6,5},{7,6},{8,11},{9,8},{10,9... | collective-permute-start | bytes 3145736 | tf_op jit(solution)/shard_map/ppermute | solution.py:31
  63.6 4.5 %copy-start = (bf16[704,4096]{1,0:T(8,128)(2,1)S(1)}, bf16[704,4096]{1,0:T(8,128)(2,1)}, u32[]{:S(2)}) copy-start(bf16[704,4096]{1,0:T(8,128)(2,1)} %all-gather.4.cloned.1.call-done) | copy-start | bytes 17301508
  69.8 1.7 copy-start.8
  90.2 6.2 %copy-start.12 = (s32[128]{0:T(128)S(1)}, s32[128]{0:T(128)}, u32[]{:S(2)}) copy-start(s32[128]{0:T(128)} %param.6) | copy-start | bytes 1540
  93.4 8.0 %slice-start = ((s8[5767168]{0:T(1024)(128)(4,1)}), s8[1572864]{0:T(1024)(128)(4,1)S(1)}, s32[]{:S(2)}) async-start(s8[5767168]{0:T(1024)(128)(4,1)} %bitcast.62), calls=%async_computation.3 | async-start | bytes 3145728
  96.3 5.0 %copy-start.6 = (bf16[512,704]{0,1:T(8,128)(2,1)}, bf16[512,704]{0,1:T(8,128)(2,1)S(1)}, u32[]{:S(2)}) copy-start(bf16[512,704]{0,1:T(8,128)(2,1)S(1)} %select_reduce_fusion.1) | copy-start | bytes 2162692
  96.5 4.8 %slice-start.1 = ((s8[5767168]{0:T(1024)(128)(4,1)}), s8[4194304]{0:T(1024)(128)(4,1)S(1)}, s32[]{:S(2)}) async-start(s8[5767168]{0:T(1024)(128)(4,1)} %bitcast.62), calls=%async_computation.4 | async-start | bytes 8388608
  103.5 37.0 %collective-permute-start.6 = (bf16[129,4096]{1,0:T(8,128)(2,1)}, bf16[129,4096]{1,0:T(8,128)(2,1)}, u32[]{:S(2)}, u32[]{:S(2)}) collective-permute-start(bf16[129,4096]{1,0:T(8,128)(2,1)} %fusion.16), channel_id=1, source_target_pairs={{0,3},{1,0},{2,1},{3,2},{4,7},{5,4},{6,5},{7,6},{8,11},{9,8},{10,9... | collective-permute-start | bytes 3170312 | tf_op jit(solution)/shard_map/ppermute | solution.py:99
  139.7 29.7 %collective-permute-start.8 = (bf16[129,4096]{1,0:T(8,128)(2,1)}, bf16[129,4096]{1,0:T(8,128)(2,1)}, u32[]{:S(2)}, u32[]{:S(2)}) collective-permute-start(bf16[129,4096]{1,0:T(8,128)(2,1)} %fusion.18), channel_id=1, source_target_pairs={{0,1},{1,2},{2,3},{3,0},{4,5},{5,6},{6,7},{7,4},{8,9},{9,10},{10,1... | collective-permute-start | bytes 3170312 | tf_op jit(solution)/shard_map/ppermute | solution.py:99
  147.0 41.8 %collective-permute-start.7 = (bf16[129,4096]{1,0:T(8,128)(2,1)}, bf16[129,4096]{1,0:T(8,128)(2,1)}, u32[]{:S(2)}, u32[]{:S(2)}) collective-permute-start(bf16[129,4096]{1,0:T(8,128)(2,1)} %fusion.17), channel_id=1, source_target_pairs={{0,3},{1,0},{2,1},{3,2},{4,7},{5,4},{6,5},{7,6},{8,11},{9,8},{10,9... | collective-permute-start | bytes 3170312 | tf_op jit(solution)/shard_map/ppermute | solution.py:99
  153.5 39.8 %copy-start.7 = (bf16[512,704]{0,1:T(8,128)(2,1)}, bf16[512,704]{0,1:T(8,128)(2,1)S(1)}, u32[]{:S(2)}) copy-start(bf16[512,704]{0,1:T(8,128)(2,1)S(1)} %select_reduce_fusion) | copy-start | bytes 2162692
  170.8 20.0 %copy-start.1 = (f32[129,4096]{1,0:T(8,128)}, f32[129,4096]{1,0:T(8,128)S(1)}, u32[]{:S(2)}) copy-start(f32[129,4096]{1,0:T(8,128)S(1)} %convert_element_type.105) | copy-start | bytes 6340612
  190.3 1.4 copy-start.3
  191.7 1.7 copy-start.9
  191.7 1.7 copy-start.11
  199.3 3.9 %slice-start.2 = ((s8[5767168]{0:T(1024)(128)(4,1)}), s8[1572864]{0:T(1024)(128)(4,1)S(1)}, s32[]{:S(2)}) async-start(s8[5767168]{0:T(1024)(128)(4,1)} %bitcast.64), calls=%async_computation.5 | async-start | bytes 3145728
  199.3 4.8 %slice-start.3 = ((s8[5767168]{0:T(1024)(128)(4,1)}), s8[4194304]{0:T(1024)(128)(4,1)S(1)}, s32[]{:S(2)}) async-start(s8[5767168]{0:T(1024)(128)(4,1)} %bitcast.64), calls=%async_computation.6 | async-start | bytes 8388608
  199.3 5.5 %copy-start.2 = (f32[129,4096]{1,0:T(8,128)S(1)}, f32[129,4096]{1,0:T(8,128)}, u32[]{:S(2)}) copy-start(f32[129,4096]{1,0:T(8,128)} %copy-done.1) | copy-start | bytes 6340612
  199.3 6.2 %copy-start.4 = (f32[129,4096]{1,0:T(8,128)S(1)}, f32[129,4096]{1,0:T(8,128)}, u32[]{:S(2)}) copy-start(f32[129,4096]{1,0:T(8,128)} %copy-done.3) | copy-start | bytes 6340612
Sparse Core Ops, SparseCore 0:
  9.9 46.0 all-gather.3
  199.4 57.2 reduce-scatter.1

commit v9 on v6

--- a/solution.py
+++ b/solution.py
@@ -16,7 +16,10 @@
     contract_rows = (((1,), (1,)), ((), ()))
     contract_cols = (((0,), (0,)), ((), ()))
 
-    pool = lax.all_gather(passages, "blk", axis=0, tiled=True)
+    blocks = lax.axis_size("blk")
+    pool = lax.all_to_all(
+        jnp.broadcast_to(passages[None], (blocks,) + passages.shape), "blk", 0, 0, tiled=True
+    ).reshape(blocks * passages.shape[0], passages.shape[1])
     pool_size = pool.shape[0]
 
     ring_down = [(i, (i - 1) % slabs) for i in range(slabs)]
@@ -139,9 +142,16 @@
     partial = lax.dot_general(
         coef_pool, queries, contract_cols, preferred_element_type=jnp.float32
     ) + lax.dot_general(hard_matrix, column_queries, contract_cols, preferred_element_type=jnp.float32)
-    passage_grad = lax.psum_scatter(
-        partial.astype(jnp.bfloat16), "blk", scatter_dimension=0, tiled=True
-    ).astype(jnp.float32)
+    passage_grad = jnp.sum(
+        lax.all_to_all(
+            partial.astype(jnp.bfloat16).reshape(blocks, passage_rows_dev, model_width),
+            "blk",
+            0,
+            0,
+            tiled=True,
+        ).astype(jnp.float32),
+        axis=0,
+    )
     return (query_loss, query_grad, passage_grad)
 
 

time: 196 us -> 210 us (1.071)
  matrix products: 26.1 us -> 46 us
  between operations: 14.4 us -> 0.97 us
  starting transfers between devices: 25.1 us -> 36.9 us
  waiting for transfers between devices: 117 us -> 108 us
  other arithmetic: 9.3 us -> 11.9 us
  local copies, waits for them, and re-layouts: 3.58 us -> 5.88 us
    ppermute x4, waiting for transfers between devices: 56.3 us -> 42 us  [ring_gather(): current = lax.ppermute(current, 'slab', ring_down)]
    all_to_all x0 -> x2, waiting for transfers between devices: none -> 10.6 us  [the longest x1 10.6 us: per_device(): lax.all_to_all(jnp.broadcast_to(passages[None], (blocks,) + passages.shap...]
    all_to_all x0 -> x2, starting transfers between devices: none -> 10 us  [the longest x1 5.3 us: per_device(): lax.all_to_all(jnp.broadcast_to(passages[None], (blocks,) + passages.shap...]
    dot_general x4, matrix products: 9.74 us -> 18.2 us  [per_device(): lax.dot_general(block, pool, contract_rows, preferred_element_type=jnp.fl...]
    dot_general x4, matrix products: 8.61 us -> 16.2 us  [grad_for(): return jnp.dot(rows, pool, preferred_element_type=jnp.float32)]
    reduce_sum x0 -> x1, other arithmetic: none -> 4.89 us  [per_device(): jnp.sum(lax.all_to_all(partial.astype(jnp.bfloat16).reshape(blocks, passa...]
    ppermute x3, waiting for transfers between devices: 57.8 us -> 53 us  [hop(): lax.ppermute(part.astype(jnp.bfloat16), 'slab', perm).astype(jnp.float32)]
    broadcast_in_dim x0 -> x1, local copies, waits for them, and re-layouts: none -> 4.38 us  [per_device(): jnp.broadcast_to(passages[None], (blocks,) + passages.shape)]
  transfers between devices with their start and end apart: 14 -> 14, of which waited for: 8 -> 7; matrix products, arithmetic and copies ran while one was open for 10% -> 16% of each run, Pallas kernels for 0% -> 0%
where the time goes in v9:
time: 210 us
  waiting for transfers between devices  108 us (51%)
  matrix products  46 us (22%)
  starting transfers between devices  36.9 us (18%)
  other arithmetic  11.9 us (6%)
  local copies, waits for them, and re-layouts  5.88 us (3%)
    ppermute x3, waiting for transfers between devices, hop(): lax.ppermute(part.astype(jnp.bfloat16), 'slab', perm).astype(jnp.float32)  53 us
    ppermute x4, waiting for transfers between devices, ring_gather(): current = lax.ppermute(current, 'slab', ring_down)  42 us
    dot_general x4, matrix products, per_device(): lax.dot_general(block, pool, contract_rows, preferred_element_type=jnp.fl...  18.2 us
    dot_general x4, matrix products, grad_for(): return jnp.dot(rows, pool, preferred_element_type=jnp.float32)  16.2 us
    ppermute x4, starting transfers between devices, ring_gather(): current = lax.ppermute(current, 'slab', ring_down)  12.7 us
    all_to_all x1, waiting for transfers between devices, per_device(): lax.all_to_all(jnp.broadcast_to(passages[None], (blocks,) + passages.shap...  10.6 us
    ppermute x3, starting transfers between devices, hop(): lax.ppermute(part.astype(jnp.bfloat16), 'slab', perm).astype(jnp.float32)  7.82 us
    ppermute x3, starting transfers between devices, per_device(): lax.ppermute(payload, 'slab', [(i, (i - t) % slabs) for i in range(slabs)])  6.34 us
  transfers between devices with their start and end apart: 14, of which 7 were waited for; matrix products, arithmetic and copies ran while one was open for 16% of the time, Pallas kernels for 0%

profile of v9, /device:TPU:0, one launch (start us, length us, event | category | flops | bytes accessed | tf_op | source)
XLA Modules:
  0.0 209.6 jit_solution(8817996272969860229)
XLA Ops:
  0.6 4.4 %broadcast_in_dim.28 = bf16[8,88,4096]{2,1,0:T(8,128)(2,1)} broadcast(bf16[88,4096]{1,0:T(8,128)(2,1)} %param.5), dimensions={1,2} | broadcast | bytes 6488064 | tf_op jit(solution)/shard_map/broadcast_in_dim | solution.py:21
  5.0 5.3 %all-to-all-start = ((bf16[8,88,4096]{2,1,0:T(8,128)(2,1)}), bf16[8,88,4096]{2,1,0:T(8,128)(2,1)}, u32[]{:S(2)}, u32[]{:S(2)}) async-start(bf16[8,88,4096]{2,1,0:T(8,128)(2,1)} %broadcast_in_dim.28), calls=%async_computation | async-start | bytes 11534336 | tf_op jit(solution)/shard_map/all_to_all | solution.py:20
  10.3 0.0 copy-done.4
  10.3 4.6 %collective-permute-start = (s32[128,8]{0,1:T(8,128)S(1)}, s32[128,8]{0,1:T(8,128)S(1)}, u32[]{:S(2)}, u32[]{:S(2)}) collective-permute-start(s32[128,8]{0,1:T(8,128)S(1)} %copy-done.4), channel_id=1, source_target_pairs={{0,3},{1,0},{2,1},{3,2},{4,7},{5,4},{6,5},{7,6},{8,11},{9,8},{10,9... | collective-permute-start | bytes 12296 | tf_op jit(solution)/shard_map/ppermute | solution.py:34
  15.0 0.0 collective-permute-start.2
  15.0 0.0 copy-done
  15.0 0.0 collective-permute-start.5
  15.0 3.8 %collective-permute-start.3 = (bf16[128,4096]{1,0:T(8,128)(2,1)S(1)}, bf16[128,4096]{1,0:T(8,128)(2,1)}, u32[]{:S(2)}, u32[]{:S(2)}) collective-permute-start(bf16[128,4096]{1,0:T(8,128)(2,1)S(1)} %copy-done), channel_id=1, source_target_pairs={{0,3},{1,0},{2,1},{3,2},{4,7},{5,4},{6,5},{7,6},{8,11},{9,8},{10,9... | collective-permute-start | bytes 3145736 | tf_op jit(solution)/shard_map/ppermute | solution.py:34
  18.8 0.0 collective-permute-done
  18.8 2.0 collective-permute-start.1
  20.8 42.0 %collective-permute-done.1 = s32[128,8]{0,1:T(8,128)S(1)} collective-permute-done((s32[128,8]{0,1:T(8,128)S(1)}, s32[128,8]{0,1:T(8,128)S(1)}, u32[]{:S(2)}, u32[]{:S(2)}) %collective-permute-start.1) | collective-permute-done | bytes 4128 | tf_op jit(solution)/shard_map/ppermute | solution.py:34
  62.8 0.0 collective-permute-done.2
  62.9 0.2 copy.19
  63.0 0.2 and.81
  63.3 0.1 copy.20
  63.4 0.2 div.35
  63.6 0.0 collective-permute-done.3
  63.6 2.3 %collective-permute-start.4 = (bf16[128,4096]{1,0:T(8,128)(2,1)}, bf16[128,4096]{1,0:T(8,128)(2,1)}, u32[]{:S(2)}, u32[]{:S(2)}) collective-permute-start(bf16[128,4096]{1,0:T(8,128)(2,1)} %collective-permute-done.3), channel_id=1, source_target_pairs={{0,3},{1,0},{2,1},{3,2},{4,7},{5,4},{6,5},{7,6},{8,11},{9,8},{10,9... | collective-permute-start | bytes 3145736 | tf_op jit(solution)/shard_map/ppermute | solution.py:34
  65.9 10.6 %all-to-all-done = bf16[8,88,4096]{2,1,0:T(8,128)(2,1)} async-done(((bf16[8,88,4096]{2,1,0:T(8,128)(2,1)}), bf16[8,88,4096]{2,1,0:T(8,128)(2,1)}, u32[]{:S(2)}, u32[]{:S(2)}) %all-to-all-start) | async-done | bytes 5767200 | tf_op jit(solution)/shard_map/all_to_all | solution.py:20
  76.5 4.3 %fusion.37 = f32[128,704]{0,1:T(8,128)S(1)} fusion(bf16[128,4096]{1,0:T(8,128)(2,1)S(1)} %copy-done, bf16[704,4096]{1,0:T(8,128)(2,1)} %bitcast), kind=kOutput, calls=%fused_computation.86 | convolution fusion | flops 738197504 | bytes 7176192 | tf_op jit(solution)/shard_map/dot_general | solution.py:55
  80.8 4.6 %fusion.38 = f32[128,704]{0,1:T(8,128)S(1)} fusion(bf16[128,4096]{1,0:T(8,128)(2,1)} %collective-permute-done.3, bf16[704,4096]{1,0:T(8,128)(2,1)} %bitcast), kind=kOutput, calls=%fused_computation.87 | convolution fusion | flops 738197504 | bytes 7176192 | tf_op jit(solution)/shard_map/dot_general | solution.py:55
  85.4 0.0 collective-permute-done.5
  85.4 0.0 copy-start.1
  85.4 4.7 %fusion.40 = f32[128,704]{0,1:T(8,128)S(1)} fusion(bf16[128,4096]{1,0:T(8,128)(2,1)S(1)} %collective-permute-done.5, bf16[704,4096]{1,0:T(8,128)(2,1)} %bitcast), kind=kOutput, calls=%fused_computation.89 | convolution fusion | flops 738197504 | bytes 7176192 | tf_op jit(solution)/shard_map/dot_general | solution.py:55
  90.1 0.0 copy-start.3
  90.1 0.0 collective-permute-done.4
  90.2 4.6 %fusion.39 = f32[128,704]{0,1:T(8,128)S(1)} fusion(bf16[128,4096]{1,0:T(8,128)(2,1)} %collective-permute-done.4, bf16[704,4096]{1,0:T(8,128)(2,1)} %bitcast), kind=kOutput, calls=%fused_computation.88 | convolution fusion | flops 738197504 | bytes 7176192 | tf_op jit(solution)/shard_map/dot_general | solution.py:55
  94.8 0.1 maximum_multiply_fusion
  94.9 0.1 slice_reduce_fusion
  95.0 2.7 %select_reduce_fusion.1 = f32[512,8]{0,1:T(8,128)S(1)} fusion(f32[512,704]{0,1:T(8,128)S(1)} %maximum_multiply_fusion, s32[512,8]{0,1:T(8,128)S(1)} %get-tuple-element.8, pred[512,8]{0,1:T(8,128)(4,1)S(1)} %get-tuple-element.5), kind=kLoop, calls=%fused_computation.3 | loop fusion | flops 11530240 | bytes 1478656 | tf_op jit(solution)/shard_map/reduce_sum | solution.py:70
  97.7 0.1 copy.18
  97.8 0.2 reshape.320
  98.0 0.1 exponential_reduce_fusion
  98.2 2.4 %collective-permute-start.8 = (f32[4352]{0:T(1024)S(1)}, f32[4352]{0:T(1024)S(1)}, u32[]{:S(2)}, u32[]{:S(2)}) collective-permute-start(f32[4352]{0:T(1024)S(1)} %pad_maximum_fusion), channel_id=1, source_target_pairs={{0,1},{1,2},{2,3},{3,0},{4,5},{5,6},{6,7},{7,4},{8,9},{9,10},{10,1... | collective-permute-start | bytes 52232 | tf_op jit(solution)/shard_map/ppermute | solution.py:80
  100.5 2.6 %collective-permute-start.7 = (f32[4352]{0:T(1024)S(1)}, f32[4352]{0:T(1024)S(1)}, u32[]{:S(2)}, u32[]{:S(2)}) collective-permute-start(f32[4352]{0:T(1024)S(1)} %pad_maximum_fusion), channel_id=1, source_target_pairs={{0,2},{1,3},{2,0},{3,1},{4,6},{5,7},{6,4},{7,5},{8,10},{9,11},{10,... | collective-permute-start | bytes 52232 | tf_op jit(solution)/shard_map/ppermute | solution.py:80
  103.1 1.3 collective-permute-start.6
  104.5 0.0 collective-permute-done.8
  104.6 0.6 collective-permute-done.7
  105.2 1.7 collective-permute-done.6
  106.9 0.2 concatenate.60
  107.2 0.1 fusion.16
  107.2 0.1 dynamic-slice
  107.4 0.2 reshape.323
  107.6 0.1 reduce_max.19
  107.7 0.2 exponential_reduce_fusion.1
  108.0 0.5 fusion.36
  108.5 2.8 %select_reduce_fusion = bf16[512,704]{0,1:T(8,128)(2,1)S(1)} fusion(f32[512,8]{0,1:T(8,128)S(1)} %fusion.29, s32[512,8]{0,1:T(8,128)S(1)} %get-tuple-element.8, pred[512,8]{0,1:T(8,128)(4,1)S(1)} %get-tuple-element.5), kind=kLoop, calls=%fused_computation.2 | loop fusion | flops 11173888 | bytes 757760 | tf_op jit(solution)/shard_map/reduce_sum | solution.py:116
  111.3 0.0 copy-start.2
  111.3 1.7 fusion.32
  113.0 6.2 %add_convert_fusion = bf16[704,4096]{1,0:T(8,128)(2,1)} fusion(f32[704,4096]{1,0:T(8,128)S(1)} %fusion.32, bf16[512,704]{0,1:T(8,128)(2,1)S(1)} %select_reduce_fusion, bf16[128,4096]{1,0:T(8,128)(2,1)S(1)} %copy-done.2, bf16[128,4096]{1,0:T(8,128)(2,1)} %collective-permute-done.4, bf16[128,4096]{1,0:T(8,128)(2,1)} %collective-permute-done.3, ...), kind=kOutput, calls=%fused_computation.1 | convolution fusion | flops 2975334400 | bytes 22216704 | tf_op jit(solution)/shard_map/dot_general | solution.py:144
  119.3 4.7 %all-to-all-start.1 = ((bf16[8,88,4096]{2,1,0:T(8,128)(2,1)}), bf16[8,88,4096]{2,1,0:T(8,128)(2,1)}, u32[]{:S(2)}, u32[]{:S(2)}) async-start(bf16[8,88,4096]{2,1,0:T(8,128)(2,1)} %bitcast.29), calls=%async_computation.1 | async-start | bytes 11534336 | tf_op jit(solution)/shard_map/all_to_all | solution.py:146
  124.0 3.7 %convolution_convert_fusion.1 = bf16[128,4096]{1,0:T(8,128)(2,1)S(1)} fusion(bf16[704,4096]{1,0:T(8,128)(2,1)} %bitcast, bf16[512,704]{0,1:T(8,128)(2,1)S(1)} %select_reduce_fusion), kind=kOutput, calls=%fused_computation.7 | convolution fusion | flops 738721792 | bytes 6995968 | tf_op jit(solution)/shard_map/dot_general | solution.py:122
  127.6 3.2 %collective-permute-start.9 = (bf16[128,4096]{1,0:T(8,128)(2,1)S(1)}, bf16[128,4096]{1,0:T(8,128)(2,1)S(1)}, u32[]{:S(2)}, u32[]{:S(2)}) collective-permute-start(bf16[128,4096]{1,0:T(8,128)(2,1)S(1)} %convolution_convert_fusion.1), channel_id=1, source_target_pairs={{0,3},{1,0},{2,1},{3,2},{4,7},{5,4},{6,5},{7,6},{8,11},{9,8},{10,9... | collective-permute-start | bytes 3145736 | tf_op jit(solution)/shard_map/ppermute | solution.py:125
  130.8 3.6 %convolution_convert_fusion = bf16[128,4096]{1,0:T(8,128)(2,1)S(1)} fusion(bf16[704,4096]{1,0:T(8,128)(2,1)} %bitcast, bf16[512,704]{0,1:T(8,128)(2,1)S(1)} %select_reduce_fusion), kind=kOutput, calls=%fused_computation.6 | convolution fusion | flops 738721792 | bytes 6995968 | tf_op jit(solution)/shard_map/dot_general | solution.py:122
  134.5 0.1 collective-permute-start.11
  134.6 19.8 %collective-permute-done.9 = bf16[128,4096]{1,0:T(8,128)(2,1)S(1)} collective-permute-done((bf16[128,4096]{1,0:T(8,128)(2,1)S(1)}, bf16[128,4096]{1,0:T(8,128)(2,1)S(1)}, u32[]{:S(2)}, u32[]{:S(2)}) %collective-permute-start.9) | collective-permute-done | bytes 1048608 | tf_op jit(solution)/shard_map/ppermute | solution.py:125
  154.4 3.7 %add_convert_fusion.1 = bf16[128,4096]{1,0:T(8,128)(2,1)S(1)} fusion(bf16[128,4096]{1,0:T(8,128)(2,1)S(1)} %collective-permute-done.9, bf16[704,4096]{1,0:T(8,128)(2,1)} %bitcast, bf16[512,704]{0,1:T(8,128)(2,1)S(1)} %select_reduce_fusion), kind=kOutput, calls=%fused_computation.16 | convolution fusion | flops 739770368 | bytes 8044544 | tf_op jit(solution)/shard_map/dot_general | solution.py:122
  158.1 4.6 %collective-permute-start.10 = (bf16[128,4096]{1,0:T(8,128)(2,1)S(1)}, bf16[128,4096]{1,0:T(8,128)(2,1)S(1)}, u32[]{:S(2)}, u32[]{:S(2)}) collective-permute-start(bf16[128,4096]{1,0:T(8,128)(2,1)S(1)} %add_convert_fusion.1), channel_id=1, source_target_pairs={{0,3},{1,0},{2,1},{3,2},{4,7},{5,4},{6,5},{7,6},{8,11},{9,8},{10,9... | collective-permute-start | bytes 3145736 | tf_op jit(solution)/shard_map/ppermute | solution.py:125
  162.6 3.7 %fusion.33 = f32[128,4096]{1,0:T(8,128)S(1)} fusion(bf16[704,4096]{1,0:T(8,128)(2,1)} %bitcast, f32[512,704]{0,1:T(8,128)S(1)} %maximum_multiply_fusion, f32[128]{0:T(128)S(1)} %get-tuple-element.11, s32[128]{0:T(128)S(1)} %copy-done.3), kind=kOutput, calls=%fused_computation.83 | convolution fusion | flops 738648064 | bytes 8225792 | tf_op jit(solution)/shard_map/dot_general | solution.py:138
  166.3 11.0 %collective-permute-done.11 = bf16[128,4096]{1,0:T(8,128)(2,1)S(1)} collective-permute-done((bf16[128,4096]{1,0:T(8,128)(2,1)S(1)}, bf16[128,4096]{1,0:T(8,128)(2,1)S(1)}, u32[]{:S(2)}, u32[]{:S(2)}) %collective-permute-start.11) | collective-permute-done | bytes 1048608 | tf_op jit(solution)/shard_map/ppermute | solution.py:125
  177.3 22.1 %collective-permute-done.10 = bf16[128,4096]{1,0:T(8,128)(2,1)S(1)} collective-permute-done((bf16[128,4096]{1,0:T(8,128)(2,1)S(1)}, bf16[128,4096]{1,0:T(8,128)(2,1)S(1)}, u32[]{:S(2)}, u32[]{:S(2)}) %collective-permute-start.10) | collective-permute-done | bytes 1048608 | tf_op jit(solution)/shard_map/ppermute | solution.py:125
  199.5 5.3 %add_add_fusion = f32[128,4096]{1,0:T(8,128)} fusion(f32[128,4096]{1,0:T(8,128)S(1)} %fusion.33, bf16[128,4096]{1,0:T(8,128)(2,1)S(1)} %collective-permute-done.11, bf16[128,4096]{1,0:T(8,128)(2,1)S(1)} %collective-permute-done.10, bf16[704,4096]{1,0:T(8,128)(2,1)} %bitcast, bf16[512,704]{0,1:T(8,128)(2,1)S(1)} %select_reduce_fusion), kind=kOutput, calls=%fused_computation.15 | convolution fusion | flops 740818944 | bytes 12238848 | tf_op jit(solution)/shard_map/dot_general | solution.py:122
  204.7 0.0 all-to-all-done.1
  204.7 4.9 %convert_reduce_fusion = f32[88,4096]{1,0:T(8,128)} fusion(bf16[8,88,4096]{2,1,0:T(8,128)(2,1)} %all-to-all-done.1), kind=kLoop, calls=%fused_computation | loop fusion | flops 5406720 | bytes 7208960 | tf_op jit(solution)/shard_map/reduce_sum | solution.py:145
  (29 shorter events, 0.3 us)
Async XLA Ops:
  5.0 5.3 %copy-start.4 = (s32[128,8]{0,1:T(8,128)S(1)}, s32[128,8]{0,1:T(8,128)}, u32[]{:S(2)}) copy-start(s32[128,8]{0,1:T(8,128)} %param.7) | copy-start | bytes 12292
  5.0 9.9 %copy-start = (bf16[128,4096]{1,0:T(8,128)(2,1)S(1)}, bf16[128,4096]{1,0:T(8,128)(2,1)}, u32[]{:S(2)}) copy-start(bf16[128,4096]{1,0:T(8,128)(2,1)} %param.4) | copy-start | bytes 3145732
  5.0 71.5 %all-to-all-start = ((bf16[8,88,4096]{2,1,0:T(8,128)(2,1)}), bf16[8,88,4096]{2,1,0:T(8,128)(2,1)}, u32[]{:S(2)}, u32[]{:S(2)}) async-start(bf16[8,88,4096]{2,1,0:T(8,128)(2,1)} %broadcast_in_dim.28), calls=%async_computation | async-start | bytes 11534336 | tf_op jit(solution)/shard_map/all_to_all | solution.py:20
  10.3 8.5 %collective-permute-start = (s32[128,8]{0,1:T(8,128)S(1)}, s32[128,8]{0,1:T(8,128)S(1)}, u32[]{:S(2)}, u32[]{:S(2)}) collective-permute-start(s32[128,8]{0,1:T(8,128)S(1)} %copy-done.4), channel_id=1, source_target_pairs={{0,3},{1,0},{2,1},{3,2},{4,7},{5,4},{6,5},{7,6},{8,11},{9,8},{10,9... | collective-permute-start | bytes 12296 | tf_op jit(solution)/shard_map/ppermute | solution.py:34
  15.0 47.9 %collective-permute-start.2 = (s32[128,8]{0,1:T(8,128)S(1)}, s32[128,8]{0,1:T(8,128)S(1)}, u32[]{:S(2)}, u32[]{:S(2)}) collective-permute-start(s32[128,8]{0,1:T(8,128)S(1)} %copy-done.4), channel_id=1, source_target_pairs={{0,1},{1,2},{2,3},{3,0},{4,5},{5,6},{6,7},{7,4},{8,9},{9,10},{10,1... | collective-permute-start | bytes 12296 | tf_op jit(solution)/shard_map/ppermute | solution.py:38
  15.0 70.5 %collective-permute-start.5 = (bf16[128,4096]{1,0:T(8,128)(2,1)S(1)}, bf16[128,4096]{1,0:T(8,128)(2,1)S(1)}, u32[]{:S(2)}, u32[]{:S(2)}) collective-permute-start(bf16[128,4096]{1,0:T(8,128)(2,1)S(1)} %copy-done), channel_id=1, source_target_pairs={{0,1},{1,2},{2,3},{3,0},{4,5},{5,6},{6,7},{7,4},{8,9},{9,10},{10,1... | collective-permute-start | bytes 3145736 | tf_op jit(solution)/shard_map/ppermute | solution.py:38
  15.0 48.6 %collective-permute-start.3 = (bf16[128,4096]{1,0:T(8,128)(2,1)S(1)}, bf16[128,4096]{1,0:T(8,128)(2,1)}, u32[]{:S(2)}, u32[]{:S(2)}) collective-permute-start(bf16[128,4096]{1,0:T(8,128)(2,1)S(1)} %copy-done), channel_id=1, source_target_pairs={{0,3},{1,0},{2,1},{3,2},{4,7},{5,4},{6,5},{7,6},{8,11},{9,8},{10,9... | collective-permute-start | bytes 3145736 | tf_op jit(solution)/shard_map/ppermute | solution.py:34
  18.8 44.0 %collective-permute-start.1 = (s32[128,8]{0,1:T(8,128)S(1)}, s32[128,8]{0,1:T(8,128)S(1)}, u32[]{:S(2)}, u32[]{:S(2)}) collective-permute-start(s32[128,8]{0,1:T(8,128)S(1)} %collective-permute-done), channel_id=1, source_target_pairs={{0,3},{1,0},{2,1},{3,2},{4,7},{5,4},{6,5},{7,6},{8,11},{9,8},{10,9... | collective-permute-start | bytes 12296 | tf_op jit(solution)/shard_map/ppermute | solution.py:34
  63.6 26.5 %collective-permute-start.4 = (bf16[128,4096]{1,0:T(8,128)(2,1)}, bf16[128,4096]{1,0:T(8,128)(2,1)}, u32[]{:S(2)}, u32[]{:S(2)}) collective-permute-start(bf16[128,4096]{1,0:T(8,128)(2,1)} %collective-permute-done.3), channel_id=1, source_target_pairs={{0,3},{1,0},{2,1},{3,2},{4,7},{5,4},{6,5},{7,6},{8,11},{9,8},{10,9... | collective-permute-start | bytes 3145736 | tf_op jit(solution)/shard_map/ppermute | solution.py:34
  85.4 4.7 %copy-start.1 = (bf16[128,4096]{1,0:T(8,128)(2,1)}, bf16[128,4096]{1,0:T(8,128)(2,1)S(1)}, u32[]{:S(2)}) copy-start(bf16[128,4096]{1,0:T(8,128)(2,1)S(1)} %collective-permute-done.5) | copy-start | bytes 3145732
  90.1 7.9 %copy-start.3 = (s32[128]{0:T(128)S(1)}, s32[128]{0:T(128)}, u32[]{:S(2)}) copy-start(s32[128]{0:T(128)} %param.6) | copy-start | bytes 1540
  98.2 6.4 %collective-permute-start.8 = (f32[4352]{0:T(1024)S(1)}, f32[4352]{0:T(1024)S(1)}, u32[]{:S(2)}, u32[]{:S(2)}) collective-permute-start(f32[4352]{0:T(1024)S(1)} %pad_maximum_fusion), channel_id=1, source_target_pairs={{0,1},{1,2},{2,3},{3,0},{4,5},{5,6},{6,7},{7,4},{8,9},{9,10},{10,1... | collective-permute-start | bytes 52232 | tf_op jit(solution)/shard_map/ppermute | solution.py:80
  100.5 4.7 %collective-permute-start.7 = (f32[4352]{0:T(1024)S(1)}, f32[4352]{0:T(1024)S(1)}, u32[]{:S(2)}, u32[]{:S(2)}) collective-permute-start(f32[4352]{0:T(1024)S(1)} %pad_maximum_fusion), channel_id=1, source_target_pairs={{0,2},{1,3},{2,0},{3,1},{4,6},{5,7},{6,4},{7,5},{8,10},{9,11},{10,... | collective-permute-start | bytes 52232 | tf_op jit(solution)/shard_map/ppermute | solution.py:80
  103.1 3.8 %collective-permute-start.6 = (f32[4352]{0:T(1024)S(1)}, f32[4352]{0:T(1024)S(1)}, u32[]{:S(2)}, u32[]{:S(2)}) collective-permute-start(f32[4352]{0:T(1024)S(1)} %pad_maximum_fusion), channel_id=1, source_target_pairs={{0,3},{1,0},{2,1},{3,2},{4,7},{5,4},{6,5},{7,6},{8,11},{9,8},{10,9... | collective-permute-start | bytes 52232 | tf_op jit(solution)/shard_map/ppermute | solution.py:80
  111.3 1.7 copy-start.2
  119.3 85.5 %all-to-all-start.1 = ((bf16[8,88,4096]{2,1,0:T(8,128)(2,1)}), bf16[8,88,4096]{2,1,0:T(8,128)(2,1)}, u32[]{:S(2)}, u32[]{:S(2)}) async-start(bf16[8,88,4096]{2,1,0:T(8,128)(2,1)} %bitcast.29), calls=%async_computation.1 | async-start | bytes 11534336 | tf_op jit(solution)/shard_map/all_to_all | solution.py:146
  127.6 26.8 %collective-permute-start.9 = (bf16[128,4096]{1,0:T(8,128)(2,1)S(1)}, bf16[128,4096]{1,0:T(8,128)(2,1)S(1)}, u32[]{:S(2)}, u32[]{:S(2)}) collective-permute-start(bf16[128,4096]{1,0:T(8,128)(2,1)S(1)} %convolution_convert_fusion.1), channel_id=1, source_target_pairs={{0,3},{1,0},{2,1},{3,2},{4,7},{5,4},{6,5},{7,6},{8,11},{9,8},{10,9... | collective-permute-start | bytes 3145736 | tf_op jit(solution)/shard_map/ppermute | solution.py:125
  134.5 42.9 %collective-permute-start.11 = (bf16[128,4096]{1,0:T(8,128)(2,1)S(1)}, bf16[128,4096]{1,0:T(8,128)(2,1)S(1)}, u32[]{:S(2)}, u32[]{:S(2)}) collective-permute-start(bf16[128,4096]{1,0:T(8,128)(2,1)S(1)} %convolution_convert_fusion), channel_id=1, source_target_pairs={{0,1},{1,2},{2,3},{3,0},{4,5},{5,6},{6,7},{7,4},{8,9},{9,10},{10,1... | collective-permute-start | bytes 3145736 | tf_op jit(solution)/shard_map/ppermute | solution.py:125
  158.1 41.4 %collective-permute-start.10 = (bf16[128,4096]{1,0:T(8,128)(2,1)S(1)}, bf16[128,4096]{1,0:T(8,128)(2,1)S(1)}, u32[]{:S(2)}, u32[]{:S(2)}) collective-permute-start(bf16[128,4096]{1,0:T(8,128)(2,1)S(1)} %add_convert_fusion.1), channel_id=1, source_target_pairs={{0,3},{1,0},{2,1},{3,2},{4,7},{5,4},{6,5},{7,6},{8,11},{9,8},{10,9... | collective-permute-start | bytes 3145736 | tf_op jit(solution)/shard_map/ppermute | solution.py:125

commit v10 on v6

--- a/solution.py
+++ b/solution.py
@@ -47,16 +47,13 @@
         doubled = jnp.concatenate([x, x], axis=0)
         return lax.dynamic_slice_in_dim(doubled, my_slab, slabs, axis=0)
 
-    scores = jnp.concatenate(
-        [
-            lax.dot_general(block, pool, contract_rows, preferred_element_type=jnp.float32)
-            for block in query_blocks
-        ],
-        axis=0,
-    ) * logit_scale
+    score_blocks = [
+        lax.dot_general(block, pool, contract_rows, preferred_element_type=jnp.float32) * logit_scale
+        for block in query_blocks
+    ]
     column_ids = jnp.concatenate(id_blocks, axis=0)
     column_rows = column_ids.shape[0]
-    pooled = scores[:query_rows_dev]
+    pooled = score_blocks[0]
 
     owner_dev = column_ids // passage_rows_dev
     owner_slab = owner_dev % slabs
@@ -64,7 +61,20 @@
     mine = owner_slab == my_slab
     pool_iota = jnp.arange(pool_size, dtype=jnp.int32)[None, None, :]
     hard_hit = (hard_pos[:, :, None] == pool_iota) & mine[:, :, None]
-    hard_mine = jnp.sum(jnp.where(hard_hit, scores[:, None, :], 0.0), axis=2)
+    hard_mine = jnp.concatenate(
+        [
+            jnp.sum(
+                jnp.where(
+                    hard_hit[t * query_rows_dev : (t + 1) * query_rows_dev],
+                    block_scores[:, None, :],
+                    0.0,
+                ),
+                axis=2,
+            )
+            for t, block_scores in enumerate(score_blocks)
+        ],
+        axis=0,
+    )
 
     pool_max = jnp.max(pooled, axis=1)
     pool_sum = jnp.sum(jnp.exp(pooled - pool_max[:, None]), axis=1)

time: 196 us -> 199 us (1.015)
  other arithmetic: 9.3 us -> 11.6 us
  matrix products: 26.1 us -> 28.1 us
    and x0 -> x1, other arithmetic: none -> 3.66 us  [per_device(): hard_hit = (hard_pos[:, :, None] == pool_iota) & mine[:, :, None]]
  transfers between devices with their start and end apart: 14 -> 14, of which waited for: 8 -> 8; matrix products, arithmetic and copies ran while one was open for 10% -> 11% of each run, Pallas kernels for 0% -> 0%
where the time goes in v10:
time: 199 us
  waiting for transfers between devices  116 us (58%)
  matrix products  28.1 us (14%)
  starting transfers between devices  25.3 us (13%)
  between operations  14.4 us (7%)
  other arithmetic  11.6 us (6%)
  local copies, waits for them, and re-layouts  3.17 us (2%)
    ppermute x3, waiting for transfers between devices, hop(): lax.ppermute(part.astype(jnp.bfloat16), 'slab', perm).astype(jnp.float32)  57.8 us
    ppermute x4, waiting for transfers between devices, ring_gather(): current = lax.ppermute(current, 'slab', ring_down)  55.4 us
    ppermute x4, starting transfers between devices, ring_gather(): current = lax.ppermute(current, 'slab', ring_down)  13.2 us
    dot_general x4, matrix products, per_device(): lax.dot_general(block, pool, contract_rows, preferred_element_type=jnp.fl...  11 us
    dot_general x4, matrix products, grad_for(): return jnp.dot(rows, pool, preferred_element_type=jnp.float32)  8.48 us
    ppermute x3, starting transfers between devices, hop(): lax.ppermute(part.astype(jnp.bfloat16), 'slab', perm).astype(jnp.float32)  7.57 us
    dot_general x1, matrix products, per_device(): lax.dot_general(hard_matrix, column_queries, contract_cols, preferred_ele...  5.97 us
    ppermute x3, starting transfers between devices, per_device(): lax.ppermute(payload, 'slab', [(i, (i - t) % slabs) for i in range(slabs)])  4.41 us
  transfers between devices with their start and end apart: 14, of which 8 were waited for; matrix products, arithmetic and copies ran while one was open for 11% of the time, Pallas kernels for 0%

profile of v10, /device:TPU:0, one launch (start us, length us, event | category | flops | bytes accessed | tf_op | source)
XLA Modules:
  0.0 198.8 jit_solution(3151914899568250768)
XLA Ops:
  7.2 0.0 all-gather.2.cloned.1.call-start
  7.2 0.7 all-gather.2.cloned.1.call-update
  7.9 0.0 reduce-scatter.2.cloned.1.call-start
  7.9 5.1 %collective-permute-start = (s32[128,8]{0,1:T(8,128)}, s32[128,8]{0,1:T(8,128)S(1)}, u32[]{:S(2)}, u32[]{:S(2)}) collective-permute-start(s32[128,8]{0,1:T(8,128)} %param.7), channel_id=1, source_target_pairs={{0,3},{1,0},{2,1},{3,2},{4,7},{5,4},{6,5},{7,6},{8,11},{9,8},{10,9... | collective-permute-start | bytes 12296 | tf_op jit(solution)/shard_map/ppermute | solution.py:31
  13.0 0.0 collective-permute-start.2
  13.1 3.9 %collective-permute-start.3 = (bf16[128,4096]{1,0:T(8,128)(2,1)}, bf16[128,4096]{1,0:T(8,128)(2,1)S(1)}, u32[]{:S(2)}, u32[]{:S(2)}) collective-permute-start(bf16[128,4096]{1,0:T(8,128)(2,1)} %param.4), channel_id=1, source_target_pairs={{0,3},{1,0},{2,1},{3,2},{4,7},{5,4},{6,5},{7,6},{8,11},{9,8},{10,9... | collective-permute-start | bytes 3145736 | tf_op jit(solution)/shard_map/ppermute | solution.py:31
  16.9 0.7 constant_dynamic-update-slice_fusion.3
  17.6 2.0 %collective-permute-start.1 = (s32[128,8]{0,1:T(8,128)S(1)}, s32[128,8]{0,1:T(8,128)S(1)}, u32[]{:S(2)}, u32[]{:S(2)}) collective-permute-start(s32[128,8]{0,1:T(8,128)S(1)} %collective-permute-done), channel_id=1, source_target_pairs={{0,3},{1,0},{2,1},{3,2},{4,7},{5,4},{6,5},{7,6},{8,11},{9,8},{10,9... | collective-permute-start | bytes 12296 | tf_op jit(solution)/shard_map/ppermute | solution.py:31
  19.6 40.9 %collective-permute-done.1 = s32[128,8]{0,1:T(8,128)S(1)} collective-permute-done((s32[128,8]{0,1:T(8,128)S(1)}, s32[128,8]{0,1:T(8,128)S(1)}, u32[]{:S(2)}, u32[]{:S(2)}) %collective-permute-start.1) | collective-permute-done | bytes 4128 | tf_op jit(solution)/shard_map/ppermute | solution.py:31
  60.5 0.0 collective-permute-done.2
  60.6 0.2 copy.25
  60.7 0.2 and.81
  61.0 0.1 copy.26
  61.1 0.2 div.35
  61.3 3.7 %fusion = pred[512,8,704]{0,2,1:T(8,128)(4,1)} fusion(s32[512,8]{0,1:T(8,128)S(1)} %get-tuple-element.12, pred[512,8]{0,1:T(8,128)(4,1)S(1)} %get-tuple-element.9), kind=kLoop, calls=%fused_computation.3 | loop fusion | flops 5767168 | bytes 2904064 | tf_op jit(solution)/shard_map/and | solution.py:63
  64.9 0.0 collective-permute-done.3
  64.9 0.0 copy-start.5
  65.0 2.3 %collective-permute-start.4 = (bf16[128,4096]{1,0:T(8,128)(2,1)S(1)}, bf16[128,4096]{1,0:T(8,128)(2,1)}, u32[]{:S(2)}, u32[]{:S(2)}) collective-permute-start(bf16[128,4096]{1,0:T(8,128)(2,1)S(1)} %collective-permute-done.3), channel_id=1, source_target_pairs={{0,3},{1,0},{2,1},{3,2},{4,7},{5,4},{6,5},{7,6},{8,11},{9,8},{10,9... | collective-permute-start | bytes 3145736 | tf_op jit(solution)/shard_map/ppermute | solution.py:31
  67.2 4.8 %fusion.37 = (f32[128]{0:T(128)S(1)}, f32[128,704]{0,1:T(8,128)S(1)}) fusion(bf16[128,4096]{1,0:T(8,128)(2,1)} %param.4, bf16[704,4096]{1,0:T(8,128)(2,1)} %all-gather.2.cloned.1.call-done), kind=kOutput, calls=%fused_computation.91 | convolution fusion | flops 738377600 | bytes 7176704 | tf_op jit(solution)/shard_map/dot_general | solution.py:51
  72.0 1.7 convolution_multiply_fusion.2
  73.7 0.0 collective-permute-done.5
  73.7 0.0 copy-start.3
  73.7 1.0 copy-done.3
  74.7 1.7 convolution_multiply_fusion
  76.4 0.0 copy-start.7
  76.4 0.0 copy-start.2
  76.4 14.4 %collective-permute-done.4 = bf16[128,4096]{1,0:T(8,128)(2,1)} collective-permute-done((bf16[128,4096]{1,0:T(8,128)(2,1)S(1)}, bf16[128,4096]{1,0:T(8,128)(2,1)}, u32[]{:S(2)}, u32[]{:S(2)}) %collective-permute-start.4) | collective-permute-done | bytes 1048608 | tf_op jit(solution)/shard_map/ppermute | solution.py:31
  90.8 2.9 %convolution_multiply_fusion.1 = f32[128,704]{0,1:T(8,128)S(1)} fusion(bf16[128,4096]{1,0:T(8,128)(2,1)} %collective-permute-done.4, bf16[704,4096]{1,0:T(8,128)(2,1)S(1)} %copy-done), kind=kOutput, calls=%fused_computation.20 | convolution fusion | flops 738287616 | bytes 7176192 | tf_op jit(solution)/shard_map/dot_general | solution.py:51
  93.7 1.5 select_reduce_fusion.4
  95.3 0.1 copy.24
  95.4 0.2 reshape.313
  95.6 0.1 exponential_reduce_fusion
  95.7 2.0 collective-permute-start.8
  97.7 1.1 collective-permute-start.7
  98.8 1.3 collective-permute-start.6
  100.2 1.5 collective-permute-done.8
  101.8 0.6 collective-permute-done.7
  102.4 0.2 collective-permute-done.6
  102.6 0.2 concatenate.60
  102.9 0.1 fusion.16
  102.9 0.1 dynamic-slice
  103.1 0.2 reshape.316
  103.3 0.1 reduce_max.19
  103.4 0.2 exponential_reduce_fusion.1
  103.7 0.5 fusion.36
  104.2 2.8 %select_reduce_fusion = bf16[512,704]{0,1:T(8,128)(2,1)S(1)} fusion(f32[512,8]{0,1:T(8,128)S(1)} %fusion.29, pred[512,8]{0,1:T(8,128)(4,1)S(1)} %get-tuple-element.9, s32[512,8]{0,1:T(8,128)S(1)} %get-tuple-element.12), kind=kLoop, calls=%fused_computation.1 | loop fusion | flops 11173888 | bytes 757760 | tf_op jit(solution)/shard_map/reduce_sum | solution.py:123
  107.0 0.0 copy-start.4
  107.0 0.0 copy-start.6
  107.1 1.7 fusion.30
  108.7 6.0 %add_convert_fusion = bf16[704,4096]{1,0:T(8,128)(2,1)} fusion(f32[704,4096]{1,0:T(8,128)S(1)} %fusion.30, bf16[512,704]{0,1:T(8,128)(2,1)S(1)} %select_reduce_fusion, bf16[128,4096]{1,0:T(8,128)(2,1)S(1)} %copy-done.4, bf16[128,4096]{1,0:T(8,128)(2,1)} %collective-permute-done.4, bf16[128,4096]{1,0:T(8,128)(2,1)S(1)} %copy-done.6, ...), kind=kOutput, calls=%fused_computation | convolution fusion | flops 2975334400 | bytes 22216704 | tf_op jit(solution)/shard_map/dot_general | solution.py:151
  114.7 0.0 reduce-scatter.2.cloned.1.call-update
  114.7 0.0 slice-start.1
  114.7 3.8 %convolution_convert_fusion.1 = bf16[128,4096]{1,0:T(8,128)(2,1)S(1)} fusion(bf16[704,4096]{1,0:T(8,128)(2,1)} %all-gather.2.cloned.1.call-done, bf16[512,704]{0,1:T(8,128)(2,1)S(1)} %select_reduce_fusion), kind=kOutput, calls=%fused_computation.5 | convolution fusion | flops 738721792 | bytes 6995968 | tf_op jit(solution)/shard_map/dot_general | solution.py:129
  118.5 3.2 %collective-permute-start.9 = (bf16[128,4096]{1,0:T(8,128)(2,1)S(1)}, bf16[128,4096]{1,0:T(8,128)(2,1)S(1)}, u32[]{:S(2)}, u32[]{:S(2)}) collective-permute-start(bf16[128,4096]{1,0:T(8,128)(2,1)S(1)} %convolution_convert_fusion.1), channel_id=1, source_target_pairs={{0,3},{1,0},{2,1},{3,2},{4,7},{5,4},{6,5},{7,6},{8,11},{9,8},{10,9... | collective-permute-start | bytes 3145736 | tf_op jit(solution)/shard_map/ppermute | solution.py:132
  121.7 1.0 convolution_convert_fusion
  122.8 0.1 collective-permute-start.11
  122.8 22.5 %collective-permute-done.9 = bf16[128,4096]{1,0:T(8,128)(2,1)S(1)} collective-permute-done((bf16[128,4096]{1,0:T(8,128)(2,1)S(1)}, bf16[128,4096]{1,0:T(8,128)(2,1)S(1)}, u32[]{:S(2)}, u32[]{:S(2)}) %collective-permute-start.9) | collective-permute-done | bytes 1048608 | tf_op jit(solution)/shard_map/ppermute | solution.py:132
  145.3 1.0 add_convert_fusion.1
  146.4 4.3 %collective-permute-start.10 = (bf16[128,4096]{1,0:T(8,128)(2,1)S(1)}, bf16[128,4096]{1,0:T(8,128)(2,1)S(1)}, u32[]{:S(2)}, u32[]{:S(2)}) collective-permute-start(bf16[128,4096]{1,0:T(8,128)(2,1)S(1)} %add_convert_fusion.1), channel_id=1, source_target_pairs={{0,3},{1,0},{2,1},{3,2},{4,7},{5,4},{6,5},{7,6},{8,11},{9,8},{10,9... | collective-permute-start | bytes 3145736 | tf_op jit(solution)/shard_map/ppermute | solution.py:132
  150.7 1.0 fusion.31
  151.8 16.7 %collective-permute-done.11 = bf16[128,4096]{1,0:T(8,128)(2,1)S(1)} collective-permute-done((bf16[128,4096]{1,0:T(8,128)(2,1)S(1)}, bf16[128,4096]{1,0:T(8,128)(2,1)S(1)}, u32[]{:S(2)}, u32[]{:S(2)}) %collective-permute-start.11) | collective-permute-done | bytes 1048608 | tf_op jit(solution)/shard_map/ppermute | solution.py:132
  168.5 18.6 %collective-permute-done.10 = bf16[128,4096]{1,0:T(8,128)(2,1)S(1)} collective-permute-done((bf16[128,4096]{1,0:T(8,128)(2,1)S(1)}, bf16[128,4096]{1,0:T(8,128)(2,1)S(1)}, u32[]{:S(2)}, u32[]{:S(2)}) %collective-permute-start.10) | collective-permute-done | bytes 1048608 | tf_op jit(solution)/shard_map/ppermute | solution.py:132
  187.0 2.6 %add_add_fusion = f32[128,4096]{1,0:T(8,128)} fusion(f32[128,4096]{1,0:T(8,128)S(1)} %fusion.31, bf16[128,4096]{1,0:T(8,128)(2,1)S(1)} %collective-permute-done.11, bf16[128,4096]{1,0:T(8,128)(2,1)S(1)} %collective-permute-done.10, bf16[704,4096]{1,0:T(8,128)(2,1)S(1)} %bitcast.28, bf16[512,704]{0,1:T(8,128)(2,1)S(1)} %select_reduce_fusion), kind=kOutput, calls=%fused_computation.17 | convolution fusion | flops 740818944 | bytes 12238848 | tf_op jit(solution)/shard_map/dot_general | solution.py:129
  189.7 2.3 %convert_element_type.59 = f32[88,4096]{1,0:T(8,128)} convert(bf16[88,4096]{1,0:T(8,128)(2,1)} %reduce-scatter.2.cloned.1.call-done) | non-fusion elementwise | flops 360448 | bytes 2162688 | tf_op jit(solution)/shard_map/convert_element_type | solution.py:154
  (41 shorter events, 0.4 us)
Async XLA Ops:
  7.2 60.1 %all-gather.2.cloned.1.call-start = ((), (), s32[]{:S(2)}) async-start(), calls=%async_computation.1 | async-start | bytes 6488064 | tf_op jit(solution)/shard_map/all_gather | solution.py:19
  7.9 181.8 %reduce-scatter.2.cloned.1.call-start = ((), (), s32[]{:S(2)}) async-start(), calls=%async_computation.2 | async-start | bytes 6488064 | tf_op jit(solution)/shard_map/reduce_scatter | solution.py:152
  7.9 9.7 %collective-permute-start = (s32[128,8]{0,1:T(8,128)}, s32[128,8]{0,1:T(8,128)S(1)}, u32[]{:S(2)}, u32[]{:S(2)}) collective-permute-start(s32[128,8]{0,1:T(8,128)} %param.7), channel_id=1, source_target_pairs={{0,3},{1,0},{2,1},{3,2},{4,7},{5,4},{6,5},{7,6},{8,11},{9,8},{10,9... | collective-permute-start | bytes 12296 | tf_op jit(solution)/shard_map/ppermute | solution.py:31
  13.0 47.5 %collective-permute-start.2 = (s32[128,8]{0,1:T(8,128)}, s32[128,8]{0,1:T(8,128)S(1)}, u32[]{:S(2)}, u32[]{:S(2)}) collective-permute-start(s32[128,8]{0,1:T(8,128)} %param.7), channel_id=1, source_target_pairs={{0,1},{1,2},{2,3},{3,0},{4,5},{5,6},{6,7},{7,4},{8,9},{9,10},{10,1... | collective-permute-start | bytes 12296 | tf_op jit(solution)/shard_map/ppermute | solution.py:35
  13.0 60.7 %collective-permute-start.5 = (bf16[128,4096]{1,0:T(8,128)(2,1)}, bf16[128,4096]{1,0:T(8,128)(2,1)S(1)}, u32[]{:S(2)}, u32[]{:S(2)}) collective-permute-start(bf16[128,4096]{1,0:T(8,128)(2,1)} %param.4), channel_id=1, source_target_pairs={{0,1},{1,2},{2,3},{3,0},{4,5},{5,6},{6,7},{7,4},{8,9},{9,10},{10,1... | collective-permute-start | bytes 3145736 | tf_op jit(solution)/shard_map/ppermute | solution.py:35
  13.1 51.9 %collective-permute-start.3 = (bf16[128,4096]{1,0:T(8,128)(2,1)}, bf16[128,4096]{1,0:T(8,128)(2,1)S(1)}, u32[]{:S(2)}, u32[]{:S(2)}) collective-permute-start(bf16[128,4096]{1,0:T(8,128)(2,1)} %param.4), channel_id=1, source_target_pairs={{0,3},{1,0},{2,1},{3,2},{4,7},{5,4},{6,5},{7,6},{8,11},{9,8},{10,9... | collective-permute-start | bytes 3145736 | tf_op jit(solution)/shard_map/ppermute | solution.py:31
  17.6 42.9 %collective-permute-start.1 = (s32[128,8]{0,1:T(8,128)S(1)}, s32[128,8]{0,1:T(8,128)S(1)}, u32[]{:S(2)}, u32[]{:S(2)}) collective-permute-start(s32[128,8]{0,1:T(8,128)S(1)} %collective-permute-done), channel_id=1, source_target_pairs={{0,3},{1,0},{2,1},{3,2},{4,7},{5,4},{6,5},{7,6},{8,11},{9,8},{10,9... | collective-permute-start | bytes 12296 | tf_op jit(solution)/shard_map/ppermute | solution.py:31
  64.9 8.7 %copy-start.5 = (bf16[128,4096]{1,0:T(8,128)(2,1)}, bf16[128,4096]{1,0:T(8,128)(2,1)S(1)}, u32[]{:S(2)}) copy-start(bf16[128,4096]{1,0:T(8,128)(2,1)S(1)} %collective-permute-done.3) | copy-start | bytes 3145732
  65.0 25.9 %collective-permute-start.4 = (bf16[128,4096]{1,0:T(8,128)(2,1)S(1)}, bf16[128,4096]{1,0:T(8,128)(2,1)}, u32[]{:S(2)}, u32[]{:S(2)}) collective-permute-start(bf16[128,4096]{1,0:T(8,128)(2,1)S(1)} %collective-permute-done.3), channel_id=1, source_target_pairs={{0,3},{1,0},{2,1},{3,2},{4,7},{5,4},{6,5},{7,6},{8,11},{9,8},{10,9... | collective-permute-start | bytes 3145736 | tf_op jit(solution)/shard_map/ppermute | solution.py:31
  67.2 4.8 %copy-start = (bf16[704,4096]{1,0:T(8,128)(2,1)S(1)}, bf16[704,4096]{1,0:T(8,128)(2,1)}, u32[]{:S(2)}) copy-start(bf16[704,4096]{1,0:T(8,128)(2,1)} %all-gather.2.cloned.1.call-done) | copy-start | bytes 17301508
  73.7 20.0 %copy-start.1 = (pred[512,8,704]{0,2,1:T(8,128)(4,1)S(1)}, pred[512,8,704]{0,2,1:T(8,128)(4,1)}, u32[]{:S(2)}) copy-start(pred[512,8,704]{0,2,1:T(8,128)(4,1)} %fusion) | copy-start | bytes 8650756
  73.7 1.0 copy-start.3
  76.4 19.2 %copy-start.7 = (s32[128]{0:T(128)S(1)}, s32[128]{0:T(128)}, u32[]{:S(2)}) copy-start(s32[128]{0:T(128)} %param.6) | copy-start | bytes 1540
  76.4 30.7 %copy-start.2 = (bf16[128,4096]{1,0:T(8,128)(2,1)S(1)}, bf16[128,4096]{1,0:T(8,128)(2,1)}, u32[]{:S(2)}) copy-start(bf16[128,4096]{1,0:T(8,128)(2,1)} %param.4) | copy-start | bytes 3145732
  95.7 6.0 %collective-permute-start.8 = (f32[4352]{0:T(1024)S(1)}, f32[4352]{0:T(1024)S(1)}, u32[]{:S(2)}, u32[]{:S(2)}) collective-permute-start(f32[4352]{0:T(1024)S(1)} %pad_maximum_fusion), channel_id=1, source_target_pairs={{0,1},{1,2},{2,3},{3,0},{4,5},{5,6},{6,7},{7,4},{8,9},{9,10},{10,1... | collective-permute-start | bytes 52232 | tf_op jit(solution)/shard_map/ppermute | solution.py:87
  97.7 4.7 %collective-permute-start.7 = (f32[4352]{0:T(1024)S(1)}, f32[4352]{0:T(1024)S(1)}, u32[]{:S(2)}, u32[]{:S(2)}) collective-permute-start(f32[4352]{0:T(1024)S(1)} %pad_maximum_fusion), channel_id=1, source_target_pairs={{0,2},{1,3},{2,0},{3,1},{4,6},{5,7},{6,4},{7,5},{8,10},{9,11},{10,... | collective-permute-start | bytes 52232 | tf_op jit(solution)/shard_map/ppermute | solution.py:87
  98.8 3.8 %collective-permute-start.6 = (f32[4352]{0:T(1024)S(1)}, f32[4352]{0:T(1024)S(1)}, u32[]{:S(2)}, u32[]{:S(2)}) collective-permute-start(f32[4352]{0:T(1024)S(1)} %pad_maximum_fusion), channel_id=1, source_target_pairs={{0,3},{1,0},{2,1},{3,2},{4,7},{5,4},{6,5},{7,6},{8,11},{9,8},{10,9... | collective-permute-start | bytes 52232 | tf_op jit(solution)/shard_map/ppermute | solution.py:87
  107.0 1.7 copy-start.4
  107.0 1.7 copy-start.6
  114.7 7.0 %slice-start = ((s8[5767168]{0:T(1024)(128)(4,1)}), s8[1572864]{0:T(1024)(128)(4,1)S(1)}, s32[]{:S(2)}) async-start(s8[5767168]{0:T(1024)(128)(4,1)} %bitcast.27), calls=%async_computation.3 | async-start | bytes 3145728
  114.7 7.0 %slice-start.1 = ((s8[5767168]{0:T(1024)(128)(4,1)}), s8[4194304]{0:T(1024)(128)(4,1)S(1)}, s32[]{:S(2)}) async-start(s8[5767168]{0:T(1024)(128)(4,1)} %bitcast.27), calls=%async_computation.4 | async-start | bytes 8388608
  118.5 26.8 %collective-permute-start.9 = (bf16[128,4096]{1,0:T(8,128)(2,1)S(1)}, bf16[128,4096]{1,0:T(8,128)(2,1)S(1)}, u32[]{:S(2)}, u32[]{:S(2)}) collective-permute-start(bf16[128,4096]{1,0:T(8,128)(2,1)S(1)} %convolution_convert_fusion.1), channel_id=1, source_target_pairs={{0,3},{1,0},{2,1},{3,2},{4,7},{5,4},{6,5},{7,6},{8,11},{9,8},{10,9... | collective-permute-start | bytes 3145736 | tf_op jit(solution)/shard_map/ppermute | solution.py:132
  122.8 45.7 %collective-permute-start.11 = (bf16[128,4096]{1,0:T(8,128)(2,1)S(1)}, bf16[128,4096]{1,0:T(8,128)(2,1)S(1)}, u32[]{:S(2)}, u32[]{:S(2)}) collective-permute-start(bf16[128,4096]{1,0:T(8,128)(2,1)S(1)} %convolution_convert_fusion), channel_id=1, source_target_pairs={{0,1},{1,2},{2,3},{3,0},{4,5},{5,6},{6,7},{7,4},{8,9},{9,10},{10,1... | collective-permute-start | bytes 3145736 | tf_op jit(solution)/shard_map/ppermute | solution.py:132
  146.4 40.7 %collective-permute-start.10 = (bf16[128,4096]{1,0:T(8,128)(2,1)S(1)}, bf16[128,4096]{1,0:T(8,128)(2,1)S(1)}, u32[]{:S(2)}, u32[]{:S(2)}) collective-permute-start(bf16[128,4096]{1,0:T(8,128)(2,1)S(1)} %add_convert_fusion.1), channel_id=1, source_target_pairs={{0,3},{1,0},{2,1},{3,2},{4,7},{5,4},{6,5},{7,6},{8,11},{9,8},{10,9... | collective-permute-start | bytes 3145736 | tf_op jit(solution)/shard_map/ppermute | solution.py:132
Sparse Core Ops, SparseCore 0:
  9.9 46.0 all-gather.1
  114.9 59.8 reduce-scatter.1

commit v11 on v6

--- a/solution.py
+++ b/solution.py
@@ -135,13 +135,15 @@
     pool_grad = jnp.dot(coef_pool, pool, preferred_element_type=jnp.float32)
     query_grad = pool_grad + carried
 
-    column_queries = jnp.concatenate(query_blocks, axis=0)
     partial = lax.dot_general(
-        coef_pool, queries, contract_cols, preferred_element_type=jnp.float32
-    ) + lax.dot_general(hard_matrix, column_queries, contract_cols, preferred_element_type=jnp.float32)
-    passage_grad = lax.psum_scatter(
-        partial.astype(jnp.bfloat16), "blk", scatter_dimension=0, tiled=True
-    ).astype(jnp.float32)
+        jnp.concatenate([coef_pool, hard_matrix], axis=0),
+        jnp.concatenate([queries] + query_blocks, axis=0),
+        contract_cols,
+        preferred_element_type=jnp.float32,
+    ).astype(jnp.bfloat16)
+    passage_grad = lax.psum_scatter(partial, "blk", scatter_dimension=0, tiled=True).astype(
+        jnp.float32
+    )
     return (query_loss, query_grad, passage_grad)
 
 

time: 196 us -> 207 us (1.056)
  local copies, waits for them, and re-layouts: 3.58 us -> 12.1 us
  matrix products: 26.1 us -> 29.2 us
    unnamed x31 -> x23, local copies, waits for them, and re-layouts: 2.12 us -> 9.55 us
    ppermute x3, starting transfers between devices: 7.56 us -> 2.19 us  [hop(): lax.ppermute(part.astype(jnp.bfloat16), 'slab', perm).astype(jnp.float32)]
    ppermute x4, starting transfers between devices: 13.2 us -> 17 us  [ring_gather(): current = lax.ppermute(current, 'slab', ring_down)]
    ppermute x4, waiting for transfers between devices: 56.3 us -> 53.1 us  [ring_gather(): current = lax.ppermute(current, 'slab', ring_down)]
    ppermute x3, waiting for transfers between devices: 57.8 us -> 60.3 us  [hop(): lax.ppermute(part.astype(jnp.bfloat16), 'slab', perm).astype(jnp.float32)]
    dot_general x2 -> x1, matrix products: 6.68 us -> 9.07 us  [per_device(): lax.dot_general(jnp.concatenate([coef_pool, hard_matrix], axis=0), jnp.co...]
  transfers between devices with their start and end apart: 14 -> 14, of which waited for: 8 -> 8; matrix products, arithmetic and copies ran while one was open for 10% -> 15% of each run, Pallas kernels for 0% -> 0%
where the time goes in v11:
time: 207 us
  waiting for transfers between devices  117 us (57%)
  matrix products  29.2 us (14%)
  starting transfers between devices  24.2 us (12%)
  between operations  14.4 us (7%)
  local copies, waits for them, and re-layouts  12.1 us (6%)
  other arithmetic  10 us (5%)
    ppermute x3, waiting for transfers between devices, hop(): lax.ppermute(part.astype(jnp.bfloat16), 'slab', perm).astype(jnp.float32)  60.3 us
    ppermute x4, waiting for transfers between devices, ring_gather(): current = lax.ppermute(current, 'slab', ring_down)  53.1 us
    ppermute x4, starting transfers between devices, ring_gather(): current = lax.ppermute(current, 'slab', ring_down)  17 us
    dot_general x4, matrix products, per_device(): lax.dot_general(block, pool, contract_rows, preferred_element_type=jnp.fl...  10.7 us
    unnamed x23, local copies, waits for them, and re-layouts  9.55 us
    dot_general x1, matrix products, per_device(): lax.dot_general(jnp.concatenate([coef_pool, hard_matrix], axis=0), jnp.co...  9.07 us
    dot_general x4, matrix products, grad_for(): return jnp.dot(rows, pool, preferred_element_type=jnp.float32)  8.47 us
    ppermute x3, starting transfers between devices, per_device(): lax.ppermute(payload, 'slab', [(i, (i - t) % slabs) for i in range(slabs)])  4.99 us
  transfers between devices with their start and end apart: 14, of which 8 were waited for; matrix products, arithmetic and copies ran while one was open for 15% of the time, Pallas kernels for 0%

profile of v11, /device:TPU:0, one launch (start us, length us, event | category | flops | bytes accessed | tf_op | source)
XLA Modules:
  0.0 206.6 jit_solution(9442113093963996559)
XLA Ops:
  7.2 0.0 copy-start.1
  7.2 0.0 all-gather.2.cloned.1.call-start
  7.2 0.7 all-gather.2.cloned.1.call-update
  7.9 0.0 reduce-scatter.2.cloned.1.call-start
  8.0 5.1 %collective-permute-start = (s32[128,8]{0,1:T(8,128)}, s32[128,8]{0,1:T(8,128)S(1)}, u32[]{:S(2)}, u32[]{:S(2)}) collective-permute-start(s32[128,8]{0,1:T(8,128)} %param.7), channel_id=1, source_target_pairs={{0,3},{1,0},{2,1},{3,2},{4,7},{5,4},{6,5},{7,6},{8,11},{9,8},{10,9... | collective-permute-start | bytes 12296 | tf_op jit(solution)/shard_map/ppermute | solution.py:31
  13.1 3.8 %collective-permute-start.3 = (bf16[128,4096]{1,0:T(8,128)(2,1)}, bf16[128,4096]{1,0:T(8,128)(2,1)S(1)}, u32[]{:S(2)}, u32[]{:S(2)}) collective-permute-start(bf16[128,4096]{1,0:T(8,128)(2,1)} %param.4), channel_id=1, source_target_pairs={{0,3},{1,0},{2,1},{3,2},{4,7},{5,4},{6,5},{7,6},{8,11},{9,8},{10,9... | collective-permute-start | bytes 3145736 | tf_op jit(solution)/shard_map/ppermute | solution.py:31
  16.9 2.4 %constant_dynamic-update-slice_fusion.8 = bf16[640,4096]{1,0:T(8,128)(2,1)} fusion(bf16[128,4096]{1,0:T(8,128)(2,1)} %param.4), kind=kLoop, calls=%fused_computation.54 | loop fusion | bytes 2097152
  19.3 2.5 %constant_dynamic-update-slice_fusion.7 = bf16[640,4096]{1,0:T(8,128)(2,1)} fusion(bf16[640,4096]{1,0:T(8,128)(2,1)} %constant_dynamic-update-slice_fusion.8, bf16[128,4096]{1,0:T(8,128)(2,1)} %param.4), kind=kLoop, calls=%fused_computation.53 | loop fusion | bytes 2097152
  21.7 0.7 constant_dynamic-update-slice_fusion.3
  22.4 3.8 %collective-permute-start.1 = (s32[128,8]{0,1:T(8,128)S(1)}, s32[128,8]{0,1:T(8,128)S(1)}, u32[]{:S(2)}, u32[]{:S(2)}) collective-permute-start(s32[128,8]{0,1:T(8,128)S(1)} %collective-permute-done), channel_id=1, source_target_pairs={{0,3},{1,0},{2,1},{3,2},{4,7},{5,4},{6,5},{7,6},{8,11},{9,8},{10,9... | collective-permute-start | bytes 12296 | tf_op jit(solution)/shard_map/ppermute | solution.py:31
  26.2 35.4 %collective-permute-done.1 = s32[128,8]{0,1:T(8,128)S(1)} collective-permute-done((s32[128,8]{0,1:T(8,128)S(1)}, s32[128,8]{0,1:T(8,128)S(1)}, u32[]{:S(2)}, u32[]{:S(2)}) %collective-permute-start.1) | collective-permute-done | bytes 4128 | tf_op jit(solution)/shard_map/ppermute | solution.py:31
  61.6 4.3 %collective-permute-start.4 = (bf16[128,4096]{1,0:T(8,128)(2,1)S(1)}, bf16[128,4096]{1,0:T(8,128)(2,1)}, u32[]{:S(2)}, u32[]{:S(2)}) collective-permute-start(bf16[128,4096]{1,0:T(8,128)(2,1)S(1)} %collective-permute-done.3), channel_id=1, source_target_pairs={{0,3},{1,0},{2,1},{3,2},{4,7},{5,4},{6,5},{7,6},{8,11},{9,8},{10,9... | collective-permute-start | bytes 3145736 | tf_op jit(solution)/shard_map/ppermute | solution.py:31
  65.9 0.6 fusion.15
  66.5 0.2 copy.21
  66.7 0.2 and.81
  66.9 0.1 copy.22
  67.0 0.2 div.35
  67.3 0.6 copy.27
  67.9 1.1 constant_dynamic-update-slice_fusion.6
  68.9 17.7 %collective-permute-done.4 = bf16[128,4096]{1,0:T(8,128)(2,1)} collective-permute-done((bf16[128,4096]{1,0:T(8,128)(2,1)S(1)}, bf16[128,4096]{1,0:T(8,128)(2,1)}, u32[]{:S(2)}, u32[]{:S(2)}) %collective-permute-start.4) | collective-permute-done | bytes 1048608 | tf_op jit(solution)/shard_map/ppermute | solution.py:31
  86.6 2.3 %constant_dynamic-update-slice_fusion.5 = bf16[640,4096]{1,0:T(8,128)(2,1)} fusion(bf16[640,4096]{1,0:T(8,128)(2,1)} %constant_dynamic-update-slice_fusion.6, bf16[128,4096]{1,0:T(8,128)(2,1)} %collective-permute-done.4), kind=kLoop, calls=%fused_computation.51 | loop fusion | bytes 2097152
  88.9 4.4 %fusion.31 = f32[128,704]{0,1:T(8,128)S(1)} fusion(bf16[128,4096]{1,0:T(8,128)(2,1)S(1)} %copy-done.1, bf16[704,4096]{1,0:T(8,128)(2,1)} %all-gather.2.cloned.1.call-done), kind=kOutput, calls=%fused_computation.84 | convolution fusion | flops 738197504 | bytes 7176192 | tf_op jit(solution)/shard_map/dot_general | solution.py:52
  93.4 1.7 fusion.32
  95.0 2.9 %fusion.33 = f32[128,704]{0,1:T(8,128)S(1)} fusion(bf16[128,4096]{1,0:T(8,128)(2,1)} %collective-permute-done.4, bf16[704,4096]{1,0:T(8,128)(2,1)S(1)} %copy-done), kind=kOutput, calls=%fused_computation.86 | convolution fusion | flops 738197504 | bytes 7176192 | tf_op jit(solution)/shard_map/dot_general | solution.py:52
  97.9 0.0 copy-start.2
  98.0 0.0 copy-start.4
  98.0 1.7 fusion.34
  99.6 0.0 copy-start.3
  99.7 0.1 maximum_multiply_fusion
  99.8 0.1 slice_reduce_fusion
  99.9 2.7 %select_reduce_fusion.1 = f32[512,8]{0,1:T(8,128)S(1)} fusion(f32[512,704]{0,1:T(8,128)S(1)} %maximum_multiply_fusion, s32[512,8]{0,1:T(8,128)S(1)} %get-tuple-element.8, pred[512,8]{0,1:T(8,128)(4,1)S(1)} %copy-done.2), kind=kLoop, calls=%fused_computation.1 | loop fusion | flops 11530240 | bytes 1478656 | tf_op jit(solution)/shard_map/reduce_sum | solution.py:67
  102.5 0.1 copy.20
  102.7 0.2 reshape.312
  102.9 0.1 exponential_reduce_fusion
  103.0 0.1 collective-permute-start.8
  103.1 4.9 %collective-permute-start.7 = (f32[4352]{0:T(1024)S(1)}, f32[4352]{0:T(1024)S(1)}, u32[]{:S(2)}, u32[]{:S(2)}) collective-permute-start(f32[4352]{0:T(1024)S(1)} %pad_maximum_fusion), channel_id=1, source_target_pairs={{0,2},{1,3},{2,0},{3,1},{4,6},{5,7},{6,4},{7,5},{8,10},{9,11},{10,... | collective-permute-start | bytes 52232 | tf_op jit(solution)/shard_map/ppermute | solution.py:77
  108.0 0.0 collective-permute-start.6
  108.0 1.1 constant_dynamic-update-slice_fusion.4
  109.1 0.1 collective-permute-done.8
  109.2 0.5 collective-permute-done.7
  109.8 2.0 collective-permute-done.6
  111.8 0.2 concatenate.63
  112.0 0.1 fusion.12
  112.1 0.1 dynamic-slice
  112.3 0.2 reshape.315
  112.5 0.1 reduce_max.19
  112.6 0.2 exponential_reduce_fusion.1
  112.9 0.5 fusion.30
  113.4 0.1 subtract_convert_fusion
  113.5 2.8 %select_reduce_fusion = bf16[512,704]{0,1:T(8,128)(2,1)S(1)} fusion(f32[512,8]{0,1:T(8,128)S(1)} %fusion.25, s32[512,8]{0,1:T(8,128)S(1)} %get-tuple-element.8, pred[512,8]{0,1:T(8,128)(4,1)S(1)} %copy-done.2), kind=kLoop, calls=%fused_computation | loop fusion | flops 11173888 | bytes 757760 | tf_op jit(solution)/shard_map/reduce_sum | solution.py:113
  116.3 9.1 %convolution_convert_fusion = bf16[704,4096]{1,0:T(8,128)(2,1)} fusion(bf16[640,4096]{1,0:T(8,128)(2,1)} %constant_dynamic-update-slice_fusion.4, bf16[512,704]{0,1:T(8,128)(2,1)S(1)} %select_reduce_fusion, bf16[128,704]{0,1:T(8,128)(2,1)S(1)} %subtract_convert_fusion), kind=kOutput, calls=%fused_computation.4 | convolution fusion | flops 3695673344 | bytes 11911168 | tf_op jit(solution)/shard_map/dot_general | solution.py:138
  125.4 0.0 reduce-scatter.2.cloned.1.call-update
  125.4 3.8 %convolution_convert_fusion.2 = bf16[128,4096]{1,0:T(8,128)(2,1)S(1)} fusion(bf16[704,4096]{1,0:T(8,128)(2,1)} %all-gather.2.cloned.1.call-done, bf16[512,704]{0,1:T(8,128)(2,1)S(1)} %select_reduce_fusion), kind=kOutput, calls=%fused_computation.6 | convolution fusion | flops 738721792 | bytes 6995968 | tf_op jit(solution)/shard_map/dot_general | solution.py:119
  129.2 2.1 %collective-permute-start.9 = (bf16[128,4096]{1,0:T(8,128)(2,1)S(1)}, bf16[128,4096]{1,0:T(8,128)(2,1)S(1)}, u32[]{:S(2)}, u32[]{:S(2)}) collective-permute-start(bf16[128,4096]{1,0:T(8,128)(2,1)S(1)} %convolution_convert_fusion.2), channel_id=1, source_target_pairs={{0,3},{1,0},{2,1},{3,2},{4,7},{5,4},{6,5},{7,6},{8,11},{9,8},{10,9... | collective-permute-start | bytes 3145736 | tf_op jit(solution)/shard_map/ppermute | solution.py:122
  131.3 1.0 convolution_convert_fusion.1
  132.3 0.1 collective-permute-start.11
  132.4 40.0 %collective-permute-done.9 = bf16[128,4096]{1,0:T(8,128)(2,1)S(1)} collective-permute-done((bf16[128,4096]{1,0:T(8,128)(2,1)S(1)}, bf16[128,4096]{1,0:T(8,128)(2,1)S(1)}, u32[]{:S(2)}, u32[]{:S(2)}) %collective-permute-start.9) | collective-permute-done | bytes 1048608 | tf_op jit(solution)/shard_map/ppermute | solution.py:122
  172.4 1.0 add_convert_fusion
  173.4 0.1 collective-permute-start.10
  173.5 1.0 fusion.35
  174.5 3.8 %collective-permute-done.11 = bf16[128,4096]{1,0:T(8,128)(2,1)S(1)} collective-permute-done((bf16[128,4096]{1,0:T(8,128)(2,1)S(1)}, bf16[128,4096]{1,0:T(8,128)(2,1)S(1)}, u32[]{:S(2)}, u32[]{:S(2)}) %collective-permute-start.11) | collective-permute-done | bytes 1048608 | tf_op jit(solution)/shard_map/ppermute | solution.py:122
  178.3 16.5 %collective-permute-done.10 = bf16[128,4096]{1,0:T(8,128)(2,1)S(1)} collective-permute-done((bf16[128,4096]{1,0:T(8,128)(2,1)S(1)}, bf16[128,4096]{1,0:T(8,128)(2,1)S(1)}, u32[]{:S(2)}, u32[]{:S(2)}) %collective-permute-start.10) | collective-permute-done | bytes 1048608 | tf_op jit(solution)/shard_map/ppermute | solution.py:122
  194.8 2.6 %add_add_fusion = f32[128,4096]{1,0:T(8,128)} fusion(f32[128,4096]{1,0:T(8,128)S(1)} %fusion.35, bf16[128,4096]{1,0:T(8,128)(2,1)S(1)} %collective-permute-done.11, bf16[128,4096]{1,0:T(8,128)(2,1)S(1)} %collective-permute-done.10, bf16[704,4096]{1,0:T(8,128)(2,1)S(1)} %bitcast.28, bf16[512,704]{0,1:T(8,128)(2,1)S(1)} %select_reduce_fusion), kind=kOutput, calls=%fused_computation.7 | convolution fusion | flops 740818944 | bytes 12238848 | tf_op jit(solution)/shard_map/dot_general | solution.py:119
  197.4 2.3 %convert_element_type.59 = f32[88,4096]{1,0:T(8,128)} convert(bf16[88,4096]{1,0:T(8,128)(2,1)} %reduce-scatter.2.cloned.1.call-done) | non-fusion elementwise | flops 360448 | bytes 2162688 | tf_op jit(solution)/shard_map/convert_element_type | solution.py:144
  (40 shorter events, 0.3 us)
Async XLA Ops:
  7.2 81.8 %copy-start.1 = (bf16[128,4096]{1,0:T(8,128)(2,1)S(1)}, bf16[128,4096]{1,0:T(8,128)(2,1)}, u32[]{:S(2)}) copy-start(bf16[128,4096]{1,0:T(8,128)(2,1)} %param.4) | copy-start | bytes 3145732
  7.2 81.7 %all-gather.2.cloned.1.call-start = ((), (), s32[]{:S(2)}) async-start(), calls=%async_computation.1 | async-start | bytes 6488064 | tf_op jit(solution)/shard_map/all_gather | solution.py:19
  7.9 189.5 %reduce-scatter.2.cloned.1.call-start = ((), (), s32[]{:S(2)}) async-start(), calls=%async_computation.2 | async-start | bytes 6488064 | tf_op jit(solution)/shard_map/reduce_scatter | solution.py:144
  8.0 14.5 %collective-permute-start = (s32[128,8]{0,1:T(8,128)}, s32[128,8]{0,1:T(8,128)S(1)}, u32[]{:S(2)}, u32[]{:S(2)}) collective-permute-start(s32[128,8]{0,1:T(8,128)} %param.7), channel_id=1, source_target_pairs={{0,3},{1,0},{2,1},{3,2},{4,7},{5,4},{6,5},{7,6},{8,11},{9,8},{10,9... | collective-permute-start | bytes 12296 | tf_op jit(solution)/shard_map/ppermute | solution.py:31
  13.1 48.6 %collective-permute-start.2 = (s32[128,8]{0,1:T(8,128)}, s32[128,8]{0,1:T(8,128)S(1)}, u32[]{:S(2)}, u32[]{:S(2)}) collective-permute-start(s32[128,8]{0,1:T(8,128)} %param.7), channel_id=1, source_target_pairs={{0,1},{1,2},{2,3},{3,0},{4,5},{5,6},{6,7},{7,4},{8,9},{9,10},{10,1... | collective-permute-start | bytes 12296 | tf_op jit(solution)/shard_map/ppermute | solution.py:35
  13.1 48.6 %collective-permute-start.3 = (bf16[128,4096]{1,0:T(8,128)(2,1)}, bf16[128,4096]{1,0:T(8,128)(2,1)S(1)}, u32[]{:S(2)}, u32[]{:S(2)}) collective-permute-start(bf16[128,4096]{1,0:T(8,128)(2,1)} %param.4), channel_id=1, source_target_pairs={{0,3},{1,0},{2,1},{3,2},{4,7},{5,4},{6,5},{7,6},{8,11},{9,8},{10,9... | collective-permute-start | bytes 3145736 | tf_op jit(solution)/shard_map/ppermute | solution.py:31
  16.9 81.1 %collective-permute-start.5 = (bf16[128,4096]{1,0:T(8,128)(2,1)}, bf16[128,4096]{1,0:T(8,128)(2,1)S(1)}, u32[]{:S(2)}, u32[]{:S(2)}) collective-permute-start(bf16[128,4096]{1,0:T(8,128)(2,1)} %param.4), channel_id=1, source_target_pairs={{0,1},{1,2},{2,3},{3,0},{4,5},{5,6},{6,7},{7,4},{8,9},{9,10},{10,1... | collective-permute-start | bytes 3145736 | tf_op jit(solution)/shard_map/ppermute | solution.py:35
  22.4 39.2 %collective-permute-start.1 = (s32[128,8]{0,1:T(8,128)S(1)}, s32[128,8]{0,1:T(8,128)S(1)}, u32[]{:S(2)}, u32[]{:S(2)}) collective-permute-start(s32[128,8]{0,1:T(8,128)S(1)} %collective-permute-done), channel_id=1, source_target_pairs={{0,3},{1,0},{2,1},{3,2},{4,7},{5,4},{6,5},{7,6},{8,11},{9,8},{10,9... | collective-permute-start | bytes 12296 | tf_op jit(solution)/shard_map/ppermute | solution.py:31
  61.6 25.0 %collective-permute-start.4 = (bf16[128,4096]{1,0:T(8,128)(2,1)S(1)}, bf16[128,4096]{1,0:T(8,128)(2,1)}, u32[]{:S(2)}, u32[]{:S(2)}) collective-permute-start(bf16[128,4096]{1,0:T(8,128)(2,1)S(1)} %collective-permute-done.3), channel_id=1, source_target_pairs={{0,3},{1,0},{2,1},{3,2},{4,7},{5,4},{6,5},{7,6},{8,11},{9,8},{10,9... | collective-permute-start | bytes 3145736 | tf_op jit(solution)/shard_map/ppermute | solution.py:31
  88.9 4.5 %copy-start = (bf16[704,4096]{1,0:T(8,128)(2,1)S(1)}, bf16[704,4096]{1,0:T(8,128)(2,1)}, u32[]{:S(2)}) copy-start(bf16[704,4096]{1,0:T(8,128)(2,1)} %all-gather.2.cloned.1.call-done) | copy-start | bytes 17301508
  97.9 1.9 copy-start.2
  98.0 4.9 %copy-start.4 = (s32[128]{0:T(128)S(1)}, s32[128]{0:T(128)}, u32[]{:S(2)}) copy-start(s32[128]{0:T(128)} %param.6) | copy-start | bytes 1540
  99.6 12.4 %copy-start.3 = (s32[1,8,4,128]{3,1,2,0:T(8,128)S(1)}, s32[1,8,4,128]{3,1,2,0:T(8,128)}, u32[]{:S(2)}) copy-start(s32[1,8,4,128]{3,1,2,0:T(8,128)} %copy.27) | copy-start | bytes 49156
  103.0 6.2 %collective-permute-start.8 = (f32[4352]{0:T(1024)S(1)}, f32[4352]{0:T(1024)S(1)}, u32[]{:S(2)}, u32[]{:S(2)}) collective-permute-start(f32[4352]{0:T(1024)S(1)} %pad_maximum_fusion), channel_id=1, source_target_pairs={{0,1},{1,2},{2,3},{3,0},{4,5},{5,6},{6,7},{7,4},{8,9},{9,10},{10,1... | collective-permute-start | bytes 52232 | tf_op jit(solution)/shard_map/ppermute | solution.py:77
  103.1 6.7 %collective-permute-start.7 = (f32[4352]{0:T(1024)S(1)}, f32[4352]{0:T(1024)S(1)}, u32[]{:S(2)}, u32[]{:S(2)}) collective-permute-start(f32[4352]{0:T(1024)S(1)} %pad_maximum_fusion), channel_id=1, source_target_pairs={{0,2},{1,3},{2,0},{3,1},{4,6},{5,7},{6,4},{7,5},{8,10},{9,11},{10,... | collective-permute-start | bytes 52232 | tf_op jit(solution)/shard_map/ppermute | solution.py:77
  108.0 3.8 %collective-permute-start.6 = (f32[4352]{0:T(1024)S(1)}, f32[4352]{0:T(1024)S(1)}, u32[]{:S(2)}, u32[]{:S(2)}) collective-permute-start(f32[4352]{0:T(1024)S(1)} %pad_maximum_fusion), channel_id=1, source_target_pairs={{0,3},{1,0},{2,1},{3,2},{4,7},{5,4},{6,5},{7,6},{8,11},{9,8},{10,9... | collective-permute-start | bytes 52232 | tf_op jit(solution)/shard_map/ppermute | solution.py:77
  125.4 5.9 %slice-start = ((s8[5767168]{0:T(1024)(128)(4,1)}), s8[1572864]{0:T(1024)(128)(4,1)S(1)}, s32[]{:S(2)}) async-start(s8[5767168]{0:T(1024)(128)(4,1)} %bitcast.27), calls=%async_computation.3 | async-start | bytes 3145728
  125.4 5.9 %slice-start.1 = ((s8[5767168]{0:T(1024)(128)(4,1)}), s8[4194304]{0:T(1024)(128)(4,1)S(1)}, s32[]{:S(2)}) async-start(s8[5767168]{0:T(1024)(128)(4,1)} %bitcast.27), calls=%async_computation.4 | async-start | bytes 8388608
  129.2 43.2 %collective-permute-start.9 = (bf16[128,4096]{1,0:T(8,128)(2,1)S(1)}, bf16[128,4096]{1,0:T(8,128)(2,1)S(1)}, u32[]{:S(2)}, u32[]{:S(2)}) collective-permute-start(bf16[128,4096]{1,0:T(8,128)(2,1)S(1)} %convolution_convert_fusion.2), channel_id=1, source_target_pairs={{0,3},{1,0},{2,1},{3,2},{4,7},{5,4},{6,5},{7,6},{8,11},{9,8},{10,9... | collective-permute-start | bytes 3145736 | tf_op jit(solution)/shard_map/ppermute | solution.py:122
  132.3 45.9 %collective-permute-start.11 = (bf16[128,4096]{1,0:T(8,128)(2,1)S(1)}, bf16[128,4096]{1,0:T(8,128)(2,1)S(1)}, u32[]{:S(2)}, u32[]{:S(2)}) collective-permute-start(bf16[128,4096]{1,0:T(8,128)(2,1)S(1)} %convolution_convert_fusion.1), channel_id=1, source_target_pairs={{0,1},{1,2},{2,3},{3,0},{4,5},{5,6},{6,7},{7,4},{8,9},{9,10},{10,1... | collective-permute-start | bytes 3145736 | tf_op jit(solution)/shard_map/ppermute | solution.py:122
  173.4 21.3 %collective-permute-start.10 = (bf16[128,4096]{1,0:T(8,128)(2,1)S(1)}, bf16[128,4096]{1,0:T(8,128)(2,1)S(1)}, u32[]{:S(2)}, u32[]{:S(2)}) collective-permute-start(bf16[128,4096]{1,0:T(8,128)(2,1)S(1)} %add_convert_fusion), channel_id=1, source_target_pairs={{0,3},{1,0},{2,1},{3,2},{4,7},{5,4},{6,5},{7,6},{8,11},{9,8},{10,9... | collective-permute-start | bytes 3145736 | tf_op jit(solution)/shard_map/ppermute | solution.py:122
Sparse Core Ops, SparseCore 0:
  9.9 46.0 all-gather.1
  125.5 58.7 reduce-scatter.1

commit v12 on v6

--- a/solution.py
+++ b/solution.py
@@ -63,13 +63,26 @@
     hard_pos = (owner_dev // slabs) * passage_rows_dev + column_ids % passage_rows_dev
     mine = owner_slab == my_slab
     pool_iota = jnp.arange(pool_size, dtype=jnp.int32)[None, None, :]
-    hard_hit = (hard_pos[:, :, None] == pool_iota) & mine[:, :, None]
-    hard_mine = jnp.sum(jnp.where(hard_hit, scores[:, None, :], 0.0), axis=2)
+    hit_count = jnp.sum(
+        ((hard_pos[:, :, None] == pool_iota) & mine[:, :, None]).astype(jnp.float32), axis=1
+    )
+    is_hard = hit_count > 0
+    far_below = -1e30
+    hard_max = jnp.max(jnp.where(is_hard, scores, far_below), axis=1)
+    hard_sum = jnp.sum(
+        jnp.where(is_hard, hit_count * jnp.exp(scores - hard_max[:, None]), 0.0), axis=1
+    )
 
     pool_max = jnp.max(pooled, axis=1)
     pool_sum = jnp.sum(jnp.exp(pooled - pool_max[:, None]), axis=1)
-    hard_origin = to_origin(hard_mine.reshape(slabs, query_rows_dev * hard_count))
-    payload = jnp.concatenate([hard_origin.reshape(-1), pool_max, pool_sum])
+    payload = jnp.concatenate(
+        [
+            to_origin(hard_max.reshape(slabs, query_rows_dev)).reshape(-1),
+            to_origin(hard_sum.reshape(slabs, query_rows_dev)).reshape(-1),
+            pool_max,
+            pool_sum,
+        ]
+    )
     gathered = to_origin(
         jnp.stack(
             [payload]
@@ -79,27 +92,17 @@
             ]
         )
     )
-    hard_split = column_rows * hard_count
-    owner_origin = to_origin(owner_slab.reshape(slabs, query_rows_dev * hard_count))
-    slab_iota = jnp.arange(slabs, dtype=jnp.int32)[:, None, None]
-    hard_all = jnp.sum(
-        jnp.where(
-            owner_origin[None] == slab_iota,
-            gathered[:, :hard_split].reshape(slabs, slabs, query_rows_dev * hard_count),
-            0.0,
-        ),
-        axis=0,
+    split = column_rows
+    max_by_owner = gathered[:, :split].reshape(slabs, slabs, query_rows_dev)
+    sum_by_owner = gathered[:, split : 2 * split].reshape(slabs, slabs, query_rows_dev)
+    max_pool = gathered[:, 2 * split : 2 * split + query_rows_dev]
+    sum_pool = gathered[:, 2 * split + query_rows_dev :]
+
+    row_top = jnp.maximum(max_pool, jnp.max(max_by_owner, axis=0))
+    row_total = sum_pool * jnp.exp(max_pool - row_top) + jnp.sum(
+        sum_by_owner * jnp.exp(max_by_owner - row_top[None]), axis=0
     )
-    hard_all = to_ring(hard_all).reshape(column_rows, hard_count)
-    stats = to_ring(gathered[:, hard_split:].reshape(slabs, 2, query_rows_dev))
-    max_all = stats[:, 0].reshape(column_rows)
-    sum_all = stats[:, 1].reshape(column_rows)
-
-    row_top = jnp.maximum(max_all, jnp.max(hard_all, axis=1))
-    row_total = sum_all * jnp.exp(max_all - row_top) + jnp.sum(
-        jnp.exp(hard_all - row_top[:, None]), axis=1
-    )
-    lse_all = row_top + jnp.log(row_total)
+    lse_all = to_ring(row_top + jnp.log(row_total)).reshape(column_rows)
     row_lse = lse_all[:query_rows_dev]
 
     onehot = (jnp.arange(pool_size, dtype=jnp.int32)[None, :] == positive[:, None]).astype(
@@ -107,11 +110,8 @@
     )
     query_loss = row_lse - jnp.sum(onehot * pooled, axis=1)
     coef_pool = (jnp.exp(pooled - row_lse[:, None]) - onehot).astype(jnp.bfloat16)
-    coef_hard = jnp.where(
-        mine, jnp.exp(hard_mine - lse_all[:, None]).astype(jnp.bfloat16), jnp.zeros((), jnp.bfloat16)
-    )
-    hard_matrix = jnp.sum(
-        jnp.where(hard_hit, coef_hard.astype(jnp.float32)[:, :, None], 0.0), axis=1
+    hard_matrix = jnp.where(
+        is_hard, hit_count * jnp.exp(scores - lse_all[:, None]), 0.0
     ).astype(jnp.bfloat16)
 
     def grad_for(block):

time: 196 us -> 195 us (level)
  matrix products: 26.1 us -> 31 us
  local copies, waits for them, and re-layouts: 3.58 us -> 0.95 us
  waiting for transfers between devices: 117 us -> 115 us
    dot_general x4, matrix products: 9.74 us -> 13.2 us  [per_device(): lax.dot_general(block, pool, contract_rows, preferred_element_type=jnp.fl...]
    reduce_sum x4 -> x3, other arithmetic: 5.75 us -> 3.15 us  [the longest x1 2.64 us: per_device(): jnp.sum(((hard_pos[:, :, None] == pool_iota) & mine[:, :, None]).astype(j...]
  transfers between devices with their start and end apart: 14 -> 14, of which waited for: 8 -> 8; matrix products, arithmetic and copies ran while one was open for 10% -> 12% of each run, Pallas kernels for 0% -> 0%
where the time goes in v12:
time: 195 us
  waiting for transfers between devices  115 us (59%)
  matrix products  31 us (16%)
  starting transfers between devices  25.1 us (13%)
  between operations  14.3 us (7%)
  other arithmetic  8.41 us (4%)
    ppermute x3, waiting for transfers between devices, hop(): lax.ppermute(part.astype(jnp.bfloat16), 'slab', perm).astype(jnp.float32)  57.3 us
    ppermute x4, waiting for transfers between devices, ring_gather(): current = lax.ppermute(current, 'slab', ring_down)  54.4 us
    dot_general x4, matrix products, per_device(): lax.dot_general(block, pool, contract_rows, preferred_element_type=jnp.fl...  13.2 us
    ppermute x4, starting transfers between devices, ring_gather(): current = lax.ppermute(current, 'slab', ring_down)  13.2 us
    dot_general x4, matrix products, grad_for(): return jnp.dot(rows, pool, preferred_element_type=jnp.float32)  8.62 us
    ppermute x3, starting transfers between devices, hop(): lax.ppermute(part.astype(jnp.bfloat16), 'slab', perm).astype(jnp.float32)  7.56 us
    dot_general x1, matrix products, per_device(): lax.dot_general(hard_matrix, column_queries, contract_cols, preferred_ele...  6.45 us
    ppermute x3, starting transfers between devices, per_device(): lax.ppermute(payload, 'slab', [(i, (i - t) % slabs) for i in range(slabs)])  4.23 us
  transfers between devices with their start and end apart: 14, of which 8 were waited for; matrix products, arithmetic and copies ran while one was open for 12% of the time, Pallas kernels for 0%

profile of v12, /device:TPU:0, one launch (start us, length us, event | category | flops | bytes accessed | tf_op | source)
XLA Modules:
  0.0 194.5 jit_solution(5122026864357573218)
XLA Ops:
  7.2 0.0 copy-start.6
  7.2 0.0 all-gather.2.cloned.1.call-start
  7.2 0.7 all-gather.2.cloned.1.call-update
  7.9 0.0 reduce-scatter.2.cloned.1.call-start
  8.0 5.1 %collective-permute-start = (s32[128,8]{0,1:T(8,128)}, s32[128,8]{0,1:T(8,128)S(1)}, u32[]{:S(2)}, u32[]{:S(2)}) collective-permute-start(s32[128,8]{0,1:T(8,128)} %param.7), channel_id=1, source_target_pairs={{0,3},{1,0},{2,1},{3,2},{4,7},{5,4},{6,5},{7,6},{8,11},{9,8},{10,9... | collective-permute-start | bytes 12296 | tf_op jit(solution)/shard_map/ppermute | solution.py:31
  13.1 0.0 collective-permute-start.2
  13.1 0.0 collective-permute-start.5
  13.1 3.9 %collective-permute-start.3 = (bf16[128,4096]{1,0:T(8,128)(2,1)}, bf16[128,4096]{1,0:T(8,128)(2,1)}, u32[]{:S(2)}, u32[]{:S(2)}) collective-permute-start(bf16[128,4096]{1,0:T(8,128)(2,1)} %param.4), channel_id=1, source_target_pairs={{0,3},{1,0},{2,1},{3,2},{4,7},{5,4},{6,5},{7,6},{8,11},{9,8},{10,9... | collective-permute-start | bytes 3145736 | tf_op jit(solution)/shard_map/ppermute | solution.py:31
  16.9 0.7 constant_dynamic-update-slice_fusion.3
  17.6 0.0 collective-permute-done
  17.6 2.0 %collective-permute-start.1 = (s32[128,8]{0,1:T(8,128)S(1)}, s32[128,8]{0,1:T(8,128)S(1)}, u32[]{:S(2)}, u32[]{:S(2)}) collective-permute-start(s32[128,8]{0,1:T(8,128)S(1)} %collective-permute-done), channel_id=1, source_target_pairs={{0,3},{1,0},{2,1},{3,2},{4,7},{5,4},{6,5},{7,6},{8,11},{9,8},{10,9... | collective-permute-start | bytes 12296 | tf_op jit(solution)/shard_map/ppermute | solution.py:31
  19.6 41.0 %collective-permute-done.1 = s32[128,8]{0,1:T(8,128)S(1)} collective-permute-done((s32[128,8]{0,1:T(8,128)S(1)}, s32[128,8]{0,1:T(8,128)S(1)}, u32[]{:S(2)}, u32[]{:S(2)}) %collective-permute-start.1) | collective-permute-done | bytes 4128 | tf_op jit(solution)/shard_map/ppermute | solution.py:31
  60.6 0.0 collective-permute-done.2
  60.7 2.6 %convert_reduce_fusion = f32[512,704]{0,1:T(8,128)S(1)} fusion(s32[512,8]{0,1:T(8,128)S(1)} %fusion.17, pred[512,8]{0,1:T(8,128)(4,1)S(1)} %fusion.18), kind=kLoop, calls=%fused_computation.1 | loop fusion | flops 11173888 | bytes 1462272 | tf_op jit(solution)/shard_map/reduce_sum | solution.py:66
  63.3 0.0 collective-permute-done.3
  63.3 2.3 %collective-permute-start.4 = (bf16[128,4096]{1,0:T(8,128)(2,1)}, bf16[128,4096]{1,0:T(8,128)(2,1)}, u32[]{:S(2)}, u32[]{:S(2)}) collective-permute-start(bf16[128,4096]{1,0:T(8,128)(2,1)} %collective-permute-done.3), channel_id=1, source_target_pairs={{0,3},{1,0},{2,1},{3,2},{4,7},{5,4},{6,5},{7,6},{8,11},{9,8},{10,9... | collective-permute-start | bytes 3145736 | tf_op jit(solution)/shard_map/ppermute | solution.py:31
  65.6 0.0 copy-done.6
  65.6 4.4 %fusion.31 = f32[128,704]{0,1:T(8,128)S(1)} fusion(bf16[128,4096]{1,0:T(8,128)(2,1)S(1)} %copy-done.6, bf16[704,4096]{1,0:T(8,128)(2,1)} %all-gather.2.cloned.1.call-done), kind=kOutput, calls=%fused_computation.72 | convolution fusion | flops 738197504 | bytes 7176192 | tf_op jit(solution)/shard_map/dot_general | solution.py:52
  70.1 0.0 copy-done
  70.1 2.9 %fusion.32 = f32[128,704]{0,1:T(8,128)S(1)} fusion(bf16[128,4096]{1,0:T(8,128)(2,1)} %collective-permute-done.3, bf16[704,4096]{1,0:T(8,128)(2,1)S(1)} %copy-done), kind=kOutput, calls=%fused_computation.73 | convolution fusion | flops 738197504 | bytes 7176192 | tf_op jit(solution)/shard_map/dot_general | solution.py:52
  73.0 0.0 copy-start.1
  73.0 0.0 collective-permute-done.5
  73.0 3.0 %fusion.34 = f32[128,704]{0,1:T(8,128)S(1)} fusion(bf16[128,4096]{1,0:T(8,128)(2,1)} %collective-permute-done.5, bf16[704,4096]{1,0:T(8,128)(2,1)S(1)} %copy-done), kind=kOutput, calls=%fused_computation.75 | convolution fusion | flops 738197504 | bytes 7176192 | tf_op jit(solution)/shard_map/dot_general | solution.py:52
  76.0 0.0 copy-start.2
  76.0 13.4 %collective-permute-done.4 = bf16[128,4096]{1,0:T(8,128)(2,1)} collective-permute-done((bf16[128,4096]{1,0:T(8,128)(2,1)}, bf16[128,4096]{1,0:T(8,128)(2,1)}, u32[]{:S(2)}, u32[]{:S(2)}) %collective-permute-start.4) | collective-permute-done | bytes 1048608 | tf_op jit(solution)/shard_map/ppermute | solution.py:31
  89.4 2.9 %fusion.33 = f32[128,704]{0,1:T(8,128)S(1)} fusion(bf16[128,4096]{1,0:T(8,128)(2,1)} %collective-permute-done.4, bf16[704,4096]{1,0:T(8,128)(2,1)S(1)} %copy-done), kind=kOutput, calls=%fused_computation.74 | convolution fusion | flops 738197504 | bytes 7176192 | tf_op jit(solution)/shard_map/dot_general | solution.py:52
  92.3 0.0 copy-start.3
  92.3 0.3 select_reduce_fusion.1
  92.7 0.0 copy-done.1
  92.7 0.4 select_reduce_fusion
  93.1 0.1 slice_reduce_fusion
  93.3 0.1 copy-done.8
  93.3 0.1 exponential_reduce_fusion
  93.5 1.8 collective-permute-start.8
  95.3 1.1 collective-permute-start.7
  96.4 1.3 collective-permute-start.6
  97.7 1.3 collective-permute-done.8
  99.1 0.7 collective-permute-done.7
  99.8 0.2 collective-permute-done.6
  100.0 0.1 concatenate.47
  100.1 0.0 copy-start.7
  100.2 0.1 fusion.26
  100.2 0.1 fusion.22
  100.3 0.1 fusion.25
  100.5 1.6 select_convert_fusion
  102.0 0.0 copy-start.4
  102.1 1.7 fusion.29
  103.7 6.5 %add_convert_fusion = bf16[704,4096]{1,0:T(8,128)(2,1)} fusion(f32[704,4096]{1,0:T(8,128)S(1)} %fusion.29, bf16[512,704]{0,1:T(8,128)(2,1)S(1)} %select_convert_fusion, bf16[128,4096]{1,0:T(8,128)(2,1)} %collective-permute-done.5, bf16[128,4096]{1,0:T(8,128)(2,1)} %collective-permute-done.4, bf16[128,4096]{1,0:T(8,128)(2,1)} %collective-permute-done.3, ...), kind=kOutput, calls=%fused_computation | convolution fusion | flops 2975334400 | bytes 22216704 | tf_op jit(solution)/shard_map/dot_general | solution.py:141
  110.2 0.0 reduce-scatter.2.cloned.1.call-update
  110.2 0.0 slice-start.1
  110.2 0.0 copy-start.5
  110.2 3.9 %convolution_convert_fusion.1 = bf16[128,4096]{1,0:T(8,128)(2,1)S(1)} fusion(bf16[704,4096]{1,0:T(8,128)(2,1)} %all-gather.2.cloned.1.call-done, bf16[512,704]{0,1:T(8,128)(2,1)} %copy-done.4), kind=kOutput, calls=%fused_computation.5 | convolution fusion | flops 738721792 | bytes 6995968 | tf_op jit(solution)/shard_map/dot_general | solution.py:119
  114.1 3.2 %collective-permute-start.9 = (bf16[128,4096]{1,0:T(8,128)(2,1)S(1)}, bf16[128,4096]{1,0:T(8,128)(2,1)S(1)}, u32[]{:S(2)}, u32[]{:S(2)}) collective-permute-start(bf16[128,4096]{1,0:T(8,128)(2,1)S(1)} %convolution_convert_fusion.1), channel_id=1, source_target_pairs={{0,3},{1,0},{2,1},{3,2},{4,7},{5,4},{6,5},{7,6},{8,11},{9,8},{10,9... | collective-permute-start | bytes 3145736 | tf_op jit(solution)/shard_map/ppermute | solution.py:122
  117.3 1.0 convolution_convert_fusion
  118.4 0.1 collective-permute-start.11
  118.4 22.5 %collective-permute-done.9 = bf16[128,4096]{1,0:T(8,128)(2,1)S(1)} collective-permute-done((bf16[128,4096]{1,0:T(8,128)(2,1)S(1)}, bf16[128,4096]{1,0:T(8,128)(2,1)S(1)}, u32[]{:S(2)}, u32[]{:S(2)}) %collective-permute-start.9) | collective-permute-done | bytes 1048608 | tf_op jit(solution)/shard_map/ppermute | solution.py:122
  140.9 1.0 add_convert_fusion.1
  142.0 4.3 %collective-permute-start.10 = (bf16[128,4096]{1,0:T(8,128)(2,1)S(1)}, bf16[128,4096]{1,0:T(8,128)(2,1)S(1)}, u32[]{:S(2)}, u32[]{:S(2)}) collective-permute-start(bf16[128,4096]{1,0:T(8,128)(2,1)S(1)} %add_convert_fusion.1), channel_id=1, source_target_pairs={{0,3},{1,0},{2,1},{3,2},{4,7},{5,4},{6,5},{7,6},{8,11},{9,8},{10,9... | collective-permute-start | bytes 3145736 | tf_op jit(solution)/shard_map/ppermute | solution.py:122
  146.3 0.5 fusion.28
  146.8 1.0 fusion.30
  147.9 16.2 %collective-permute-done.11 = bf16[128,4096]{1,0:T(8,128)(2,1)S(1)} collective-permute-done((bf16[128,4096]{1,0:T(8,128)(2,1)S(1)}, bf16[128,4096]{1,0:T(8,128)(2,1)S(1)}, u32[]{:S(2)}, u32[]{:S(2)}) %collective-permute-start.11) | collective-permute-done | bytes 1048608 | tf_op jit(solution)/shard_map/ppermute | solution.py:122
  164.1 18.6 %collective-permute-done.10 = bf16[128,4096]{1,0:T(8,128)(2,1)S(1)} collective-permute-done((bf16[128,4096]{1,0:T(8,128)(2,1)S(1)}, bf16[128,4096]{1,0:T(8,128)(2,1)S(1)}, u32[]{:S(2)}, u32[]{:S(2)}) %collective-permute-start.10) | collective-permute-done | bytes 1048608 | tf_op jit(solution)/shard_map/ppermute | solution.py:122
  182.7 2.7 %add_add_fusion = f32[128,4096]{1,0:T(8,128)} fusion(f32[128,4096]{1,0:T(8,128)S(1)} %fusion.30, bf16[128,4096]{1,0:T(8,128)(2,1)S(1)} %collective-permute-done.11, bf16[128,4096]{1,0:T(8,128)(2,1)S(1)} %collective-permute-done.10, bf16[704,4096]{1,0:T(8,128)(2,1)S(1)} %bitcast.38, bf16[512,704]{0,1:T(8,128)(2,1)S(1)} %copy-done.5), kind=kOutput, calls=%fused_computation.13 | convolution fusion | flops 740818944 | bytes 12238848 | tf_op jit(solution)/shard_map/dot_general | solution.py:119
  185.3 2.3 %convert_element_type.47 = f32[88,4096]{1,0:T(8,128)} convert(bf16[88,4096]{1,0:T(8,128)(2,1)} %reduce-scatter.2.cloned.1.call-done) | non-fusion elementwise | flops 360448 | bytes 2162688 | tf_op jit(solution)/shard_map/convert_element_type | solution.py:144
  (31 shorter events, 0.2 us)
Async XLA Ops:
  7.2 58.4 %copy-start.6 = (bf16[128,4096]{1,0:T(8,128)(2,1)S(1)}, bf16[128,4096]{1,0:T(8,128)(2,1)}, u32[]{:S(2)}) copy-start(bf16[128,4096]{1,0:T(8,128)(2,1)} %param.4) | copy-start | bytes 3145732
  7.2 58.4 %all-gather.2.cloned.1.call-start = ((), (), s32[]{:S(2)}) async-start(), calls=%async_computation.1 | async-start | bytes 6488064 | tf_op jit(solution)/shard_map/all_gather | solution.py:19
  7.9 177.4 %reduce-scatter.2.cloned.1.call-start = ((), (), s32[]{:S(2)}) async-start(), calls=%async_computation.2 | async-start | bytes 6488064 | tf_op jit(solution)/shard_map/reduce_scatter | solution.py:142
  8.0 9.7 %collective-permute-start = (s32[128,8]{0,1:T(8,128)}, s32[128,8]{0,1:T(8,128)S(1)}, u32[]{:S(2)}, u32[]{:S(2)}) collective-permute-start(s32[128,8]{0,1:T(8,128)} %param.7), channel_id=1, source_target_pairs={{0,3},{1,0},{2,1},{3,2},{4,7},{5,4},{6,5},{7,6},{8,11},{9,8},{10,9... | collective-permute-start | bytes 12296 | tf_op jit(solution)/shard_map/ppermute | solution.py:31
  13.1 47.5 %collective-permute-start.2 = (s32[128,8]{0,1:T(8,128)}, s32[128,8]{0,1:T(8,128)S(1)}, u32[]{:S(2)}, u32[]{:S(2)}) collective-permute-start(s32[128,8]{0,1:T(8,128)} %param.7), channel_id=1, source_target_pairs={{0,1},{1,2},{2,3},{3,0},{4,5},{5,6},{6,7},{7,4},{8,9},{9,10},{10,1... | collective-permute-start | bytes 12296 | tf_op jit(solution)/shard_map/ppermute | solution.py:35
  13.1 59.9 %collective-permute-start.5 = (bf16[128,4096]{1,0:T(8,128)(2,1)}, bf16[128,4096]{1,0:T(8,128)(2,1)}, u32[]{:S(2)}, u32[]{:S(2)}) collective-permute-start(bf16[128,4096]{1,0:T(8,128)(2,1)} %param.4), channel_id=1, source_target_pairs={{0,1},{1,2},{2,3},{3,0},{4,5},{5,6},{6,7},{7,4},{8,9},{9,10},{10,1... | collective-permute-start | bytes 3145736 | tf_op jit(solution)/shard_map/ppermute | solution.py:35
  13.1 50.3 %collective-permute-start.3 = (bf16[128,4096]{1,0:T(8,128)(2,1)}, bf16[128,4096]{1,0:T(8,128)(2,1)}, u32[]{:S(2)}, u32[]{:S(2)}) collective-permute-start(bf16[128,4096]{1,0:T(8,128)(2,1)} %param.4), channel_id=1, source_target_pairs={{0,3},{1,0},{2,1},{3,2},{4,7},{5,4},{6,5},{7,6},{8,11},{9,8},{10,9... | collective-permute-start | bytes 3145736 | tf_op jit(solution)/shard_map/ppermute | solution.py:31
  17.6 43.0 %collective-permute-start.1 = (s32[128,8]{0,1:T(8,128)S(1)}, s32[128,8]{0,1:T(8,128)S(1)}, u32[]{:S(2)}, u32[]{:S(2)}) collective-permute-start(s32[128,8]{0,1:T(8,128)S(1)} %collective-permute-done), channel_id=1, source_target_pairs={{0,3},{1,0},{2,1},{3,2},{4,7},{5,4},{6,5},{7,6},{8,11},{9,8},{10,9... | collective-permute-start | bytes 12296 | tf_op jit(solution)/shard_map/ppermute | solution.py:31
  63.3 26.1 %collective-permute-start.4 = (bf16[128,4096]{1,0:T(8,128)(2,1)}, bf16[128,4096]{1,0:T(8,128)(2,1)}, u32[]{:S(2)}, u32[]{:S(2)}) collective-permute-start(bf16[128,4096]{1,0:T(8,128)(2,1)} %collective-permute-done.3), channel_id=1, source_target_pairs={{0,3},{1,0},{2,1},{3,2},{4,7},{5,4},{6,5},{7,6},{8,11},{9,8},{10,9... | collective-permute-start | bytes 3145736 | tf_op jit(solution)/shard_map/ppermute | solution.py:31
  65.6 4.5 %copy-start = (bf16[704,4096]{1,0:T(8,128)(2,1)S(1)}, bf16[704,4096]{1,0:T(8,128)(2,1)}, u32[]{:S(2)}) copy-start(bf16[704,4096]{1,0:T(8,128)(2,1)} %all-gather.2.cloned.1.call-done) | copy-start | bytes 17301508
  73.0 19.7 %copy-start.1 = (f32[128,704]{0,1:T(8,128)}, f32[128,704]{0,1:T(8,128)S(1)}, u32[]{:S(2)}) copy-start(f32[128,704]{0,1:T(8,128)S(1)} %fusion.32) | copy-start | bytes 1081348
  76.0 17.1 %copy-start.2 = (f32[128,704]{0,1:T(8,128)}, f32[128,704]{0,1:T(8,128)S(1)}, u32[]{:S(2)}) copy-start(f32[128,704]{0,1:T(8,128)S(1)} %fusion.34) | copy-start | bytes 1081348
  92.3 0.8 copy-start.3
  92.7 0.7 copy-start.8
  93.5 5.6 %collective-permute-start.8 = (f32[1280]{0:T(1024)S(1)}, f32[1280]{0:T(1024)S(1)}, u32[]{:S(2)}, u32[]{:S(2)}) collective-permute-start(f32[1280]{0:T(1024)S(1)} %pad_maximum_fusion), channel_id=1, source_target_pairs={{0,1},{1,2},{2,3},{3,0},{4,5},{5,6},{6,7},{7,4},{8,9},{9,10},{10,1... | collective-permute-start | bytes 15368 | tf_op jit(solution)/shard_map/ppermute | solution.py:90
  95.3 4.5 %collective-permute-start.7 = (f32[1280]{0:T(1024)S(1)}, f32[1280]{0:T(1024)S(1)}, u32[]{:S(2)}, u32[]{:S(2)}) collective-permute-start(f32[1280]{0:T(1024)S(1)} %pad_maximum_fusion), channel_id=1, source_target_pairs={{0,2},{1,3},{2,0},{3,1},{4,6},{5,7},{6,4},{7,5},{8,10},{9,11},{10,... | collective-permute-start | bytes 15368 | tf_op jit(solution)/shard_map/ppermute | solution.py:90
  96.4 3.7 %collective-permute-start.6 = (f32[1280]{0:T(1024)S(1)}, f32[1280]{0:T(1024)S(1)}, u32[]{:S(2)}, u32[]{:S(2)}) collective-permute-start(f32[1280]{0:T(1024)S(1)} %pad_maximum_fusion), channel_id=1, source_target_pairs={{0,3},{1,0},{2,1},{3,2},{4,7},{5,4},{6,5},{7,6},{8,11},{9,8},{10,9... | collective-permute-start | bytes 15368 | tf_op jit(solution)/shard_map/ppermute | solution.py:90
  100.1 1.9 copy-start.7
  102.0 1.7 copy-start.4
  110.2 7.1 %slice-start = ((s8[5767168]{0:T(1024)(128)(4,1)}), s8[1572864]{0:T(1024)(128)(4,1)S(1)}, s32[]{:S(2)}) async-start(s8[5767168]{0:T(1024)(128)(4,1)} %bitcast.37), calls=%async_computation.3 | async-start | bytes 3145728
  110.2 7.1 %slice-start.1 = ((s8[5767168]{0:T(1024)(128)(4,1)}), s8[4194304]{0:T(1024)(128)(4,1)S(1)}, s32[]{:S(2)}) async-start(s8[5767168]{0:T(1024)(128)(4,1)} %bitcast.37), calls=%async_computation.4 | async-start | bytes 8388608
  110.2 7.1 %copy-start.5 = (bf16[512,704]{0,1:T(8,128)(2,1)S(1)}, bf16[512,704]{0,1:T(8,128)(2,1)}, u32[]{:S(2)}) copy-start(bf16[512,704]{0,1:T(8,128)(2,1)} %copy-done.4) | copy-start | bytes 2162692
  114.1 26.8 %collective-permute-start.9 = (bf16[128,4096]{1,0:T(8,128)(2,1)S(1)}, bf16[128,4096]{1,0:T(8,128)(2,1)S(1)}, u32[]{:S(2)}, u32[]{:S(2)}) collective-permute-start(bf16[128,4096]{1,0:T(8,128)(2,1)S(1)} %convolution_convert_fusion.1), channel_id=1, source_target_pairs={{0,3},{1,0},{2,1},{3,2},{4,7},{5,4},{6,5},{7,6},{8,11},{9,8},{10,9... | collective-permute-start | bytes 3145736 | tf_op jit(solution)/shard_map/ppermute | solution.py:122
  118.4 45.7 %collective-permute-start.11 = (bf16[128,4096]{1,0:T(8,128)(2,1)S(1)}, bf16[128,4096]{1,0:T(8,128)(2,1)S(1)}, u32[]{:S(2)}, u32[]{:S(2)}) collective-permute-start(bf16[128,4096]{1,0:T(8,128)(2,1)S(1)} %convolution_convert_fusion), channel_id=1, source_target_pairs={{0,1},{1,2},{2,3},{3,0},{4,5},{5,6},{6,7},{7,4},{8,9},{9,10},{10,1... | collective-permute-start | bytes 3145736 | tf_op jit(solution)/shard_map/ppermute | solution.py:122
  142.0 40.7 %collective-permute-start.10 = (bf16[128,4096]{1,0:T(8,128)(2,1)S(1)}, bf16[128,4096]{1,0:T(8,128)(2,1)S(1)}, u32[]{:S(2)}, u32[]{:S(2)}) collective-permute-start(bf16[128,4096]{1,0:T(8,128)(2,1)S(1)} %add_convert_fusion.1), channel_id=1, source_target_pairs={{0,3},{1,0},{2,1},{3,2},{4,7},{5,4},{6,5},{7,6},{8,11},{9,8},{10,9... | collective-permute-start | bytes 3145736 | tf_op jit(solution)/shard_map/ppermute | solution.py:122
Sparse Core Ops, SparseCore 0:
  9.9 46.0 all-gather.1
  110.3 59.8 reduce-scatter.1

commit v13 on v12

--- a/solution.py
+++ b/solution.py
@@ -127,14 +127,6 @@
         for step in range(1, steps_down):
             down = hop(down, ring_down) + grad_for(slabs - steps_down + step)
         carried = carried + hop(down, ring_down)
-    if steps_up:
-        up = grad_for(steps_up)
-        for step in range(1, steps_up):
-            up = hop(up, ring_up) + grad_for(steps_up - step)
-        carried = carried + hop(up, ring_up)
-    pool_grad = jnp.dot(coef_pool, pool, preferred_element_type=jnp.float32)
-    query_grad = pool_grad + carried
-
     column_queries = jnp.concatenate(query_blocks, axis=0)
     partial = lax.dot_general(
         coef_pool, queries, contract_cols, preferred_element_type=jnp.float32
@@ -142,6 +134,16 @@
     passage_grad = lax.psum_scatter(
         partial.astype(jnp.bfloat16), "blk", scatter_dimension=0, tiled=True
     ).astype(jnp.float32)
+    if steps_up:
+        up = grad_for(steps_up)
+        for step in range(1, steps_up):
+            up = hop(up, ring_up) + grad_for(steps_up - step)
+        up = hop(up, ring_up)
+        up, passage_grad = lax.optimization_barrier((up, passage_grad))
+        carried = carried + up
+    pool_grad = jnp.dot(coef_pool, pool, preferred_element_type=jnp.float32)
+    query_grad = pool_grad + carried
+
     return (query_loss, query_grad, passage_grad)
 
 

time: 195 us -> 194 us (level)
  waiting for transfers between devices: 115 us -> 105 us
  matrix products: 31 us -> 36.4 us
  other arithmetic: 8.41 us -> 13.4 us
  starting transfers between devices: 25.1 us -> 22.9 us
    ppermute x3, waiting for transfers between devices: 57.3 us -> 47.8 us  [hop(): lax.ppermute(part.astype(jnp.bfloat16), 'slab', perm).astype(jnp.float32)]
    ppermute x3, starting transfers between devices: 7.56 us -> 2.15 us  [hop(): lax.ppermute(part.astype(jnp.bfloat16), 'slab', perm).astype(jnp.float32)]
    ppermute x4, waiting for transfers between devices: 54.4 us -> 50.8 us  [ring_gather(): current = lax.ppermute(current, 'slab', ring_down)]
    add x0 -> x1, other arithmetic: none -> 3.66 us  [per_device(): query_grad = pool_grad + carried]
    dot_general x4, matrix products: 8.62 us -> 12.1 us  [grad_for(): return jnp.dot(rows, pool, preferred_element_type=jnp.float32)]
    ppermute x3, waiting for transfers between devices: 2.31 us -> 4.79 us  [per_device(): lax.ppermute(payload, 'slab', [(i, (i - t) % slabs) for i in range(slabs)])]
  transfers between devices with their start and end apart: 14 -> 14, of which waited for: 8 -> 9; matrix products, arithmetic and copies ran while one was open for 12% -> 16% of each run, Pallas kernels for 0% -> 0%
where the time goes in v13:
time: 194 us
  waiting for transfers between devices  105 us (54%)
  matrix products  36.4 us (19%)
  starting transfers between devices  22.9 us (12%)
  between operations  14.3 us (7%)
  other arithmetic  13.4 us (7%)
    ppermute x4, waiting for transfers between devices, ring_gather(): current = lax.ppermute(current, 'slab', ring_down)  50.8 us
    ppermute x3, waiting for transfers between devices, hop(): lax.ppermute(part.astype(jnp.bfloat16), 'slab', perm).astype(jnp.float32)  47.8 us
    ppermute x4, starting transfers between devices, ring_gather(): current = lax.ppermute(current, 'slab', ring_down)  14.1 us
    dot_general x4, matrix products, per_device(): lax.dot_general(block, pool, contract_rows, preferred_element_type=jnp.fl...  12.3 us
    dot_general x4, matrix products, grad_for(): return jnp.dot(rows, pool, preferred_element_type=jnp.float32)  12.1 us
    dot_general x1, matrix products, per_device(): lax.dot_general(hard_matrix, column_queries, contract_cols, preferred_ele...  6.69 us
    ppermute x3, starting transfers between devices, per_device(): lax.ppermute(payload, 'slab', [(i, (i - t) % slabs) for i in range(slabs)])  4.98 us
    ppermute x3, waiting for transfers between devices, per_device(): lax.ppermute(payload, 'slab', [(i, (i - t) % slabs) for i in range(slabs)])  4.79 us
  transfers between devices with their start and end apart: 14, of which 9 were waited for; matrix products, arithmetic and copies ran while one was open for 16% of the time, Pallas kernels for 0%

profile of v13, /device:TPU:0, one launch (start us, length us, event | category | flops | bytes accessed | tf_op | source)
XLA Modules:
  0.0 193.7 jit_solution(17121568354440774278)
XLA Ops:
  7.2 0.0 all-gather.2.cloned.1.call-start
  7.2 0.7 all-gather.2.cloned.1.call-update
  7.9 0.0 reduce-scatter.2.cloned.1.call-start
  7.9 5.1 %collective-permute-start.3 = (bf16[128,4096]{1,0:T(8,128)(2,1)}, bf16[128,4096]{1,0:T(8,128)(2,1)}, u32[]{:S(2)}, u32[]{:S(2)}) collective-permute-start(bf16[128,4096]{1,0:T(8,128)(2,1)} %param.4), channel_id=1, source_target_pairs={{0,3},{1,0},{2,1},{3,2},{4,7},{5,4},{6,5},{7,6},{8,11},{9,8},{10,9... | collective-permute-start | bytes 3145736 | tf_op jit(solution)/shard_map/ppermute | solution.py:31
  13.0 0.4 collective-permute-start
  13.5 1.6 collective-permute-start.2
  15.1 0.0 collective-permute-start.5
  15.1 0.7 constant_dynamic-update-slice_fusion.3
  15.8 21.2 %collective-permute-done = s32[128,8]{0,1:T(8,128)S(1)} collective-permute-done((s32[128,8]{0,1:T(8,128)}, s32[128,8]{0,1:T(8,128)S(1)}, u32[]{:S(2)}, u32[]{:S(2)}) %collective-permute-start) | collective-permute-done | bytes 4128 | tf_op jit(solution)/shard_map/ppermute | solution.py:31
  37.0 4.3 %collective-permute-start.1 = (s32[128,8]{0,1:T(8,128)S(1)}, s32[128,8]{0,1:T(8,128)S(1)}, u32[]{:S(2)}, u32[]{:S(2)}) collective-permute-start(s32[128,8]{0,1:T(8,128)S(1)} %collective-permute-done), channel_id=1, source_target_pairs={{0,3},{1,0},{2,1},{3,2},{4,7},{5,4},{6,5},{7,6},{8,11},{9,8},{10,9... | collective-permute-start | bytes 12296 | tf_op jit(solution)/shard_map/ppermute | solution.py:31
  41.3 17.3 %collective-permute-done.1 = s32[128,8]{0,1:T(8,128)S(1)} collective-permute-done((s32[128,8]{0,1:T(8,128)S(1)}, s32[128,8]{0,1:T(8,128)S(1)}, u32[]{:S(2)}, u32[]{:S(2)}) %collective-permute-start.1) | collective-permute-done | bytes 4128 | tf_op jit(solution)/shard_map/ppermute | solution.py:31
  58.5 0.0 collective-permute-done.2
  58.6 0.0 collective-permute-done.3
  58.6 4.3 %collective-permute-start.4 = (bf16[128,4096]{1,0:T(8,128)(2,1)}, bf16[128,4096]{1,0:T(8,128)(2,1)}, u32[]{:S(2)}, u32[]{:S(2)}) collective-permute-start(bf16[128,4096]{1,0:T(8,128)(2,1)} %collective-permute-done.3), channel_id=1, source_target_pairs={{0,3},{1,0},{2,1},{3,2},{4,7},{5,4},{6,5},{7,6},{8,11},{9,8},{10,9... | collective-permute-start | bytes 3145736 | tf_op jit(solution)/shard_map/ppermute | solution.py:31
  62.9 2.6 %convert_reduce_fusion = f32[512,704]{0,1:T(8,128)S(1)} fusion(s32[512,8]{0,1:T(8,128)S(1)} %fusion.17, pred[512,8]{0,1:T(8,128)(4,1)S(1)} %fusion.18), kind=kLoop, calls=%fused_computation.1 | loop fusion | flops 11173888 | bytes 1462272 | tf_op jit(solution)/shard_map/reduce_sum | solution.py:66
  65.5 0.0 copy-start.9
  65.5 0.0 all-gather.2.cloned.1.call-done
  65.6 4.8 %fusion.32 = f32[128,704]{0,1:T(8,128)S(1)} fusion(bf16[128,4096]{1,0:T(8,128)(2,1)} %collective-permute-done.3, bf16[704,4096]{1,0:T(8,128)(2,1)} %all-gather.2.cloned.1.call-done), kind=kOutput, calls=%fused_computation.73 | convolution fusion | flops 738197504 | bytes 7176192 | tf_op jit(solution)/shard_map/dot_general | solution.py:52
  70.3 0.1 copy-done
  70.5 1.7 fusion.31
  72.1 12.3 %collective-permute-done.4 = bf16[128,4096]{1,0:T(8,128)(2,1)} collective-permute-done((bf16[128,4096]{1,0:T(8,128)(2,1)}, bf16[128,4096]{1,0:T(8,128)(2,1)}, u32[]{:S(2)}, u32[]{:S(2)}) %collective-permute-start.4) | collective-permute-done | bytes 1048608 | tf_op jit(solution)/shard_map/ppermute | solution.py:31
  84.4 2.9 %fusion.33 = f32[128,704]{0,1:T(8,128)S(1)} fusion(bf16[128,4096]{1,0:T(8,128)(2,1)} %collective-permute-done.4, bf16[704,4096]{1,0:T(8,128)(2,1)S(1)} %copy-done), kind=kOutput, calls=%fused_computation.74 | convolution fusion | flops 738197504 | bytes 7176192 | tf_op jit(solution)/shard_map/dot_general | solution.py:52
  87.3 0.0 copy-start.5
  87.3 0.0 collective-permute-done.5
  87.4 3.0 %fusion.34 = f32[128,704]{0,1:T(8,128)S(1)} fusion(bf16[128,4096]{1,0:T(8,128)(2,1)} %collective-permute-done.5, bf16[704,4096]{1,0:T(8,128)(2,1)S(1)} %copy-done), kind=kOutput, calls=%fused_computation.75 | convolution fusion | flops 738197504 | bytes 7176192 | tf_op jit(solution)/shard_map/dot_general | solution.py:52
  90.4 0.0 copy-start.7
  90.4 0.3 select_reduce_fusion.1
  90.7 0.0 copy-start.11
  90.8 0.4 select_reduce_fusion
  91.2 0.1 slice_reduce_fusion
  91.3 0.1 copy-done.11
  91.4 0.1 exponential_reduce_fusion
  91.5 4.3 %collective-permute-start.6 = (f32[1280]{0:T(1024)S(1)}, f32[1280]{0:T(1024)S(1)}, u32[]{:S(2)}, u32[]{:S(2)}) collective-permute-start(f32[1280]{0:T(1024)S(1)} %pad_maximum_fusion), channel_id=1, source_target_pairs={{0,3},{1,0},{2,1},{3,2},{4,7},{5,4},{6,5},{7,6},{8,11},{9,8},{10,9... | collective-permute-start | bytes 15368 | tf_op jit(solution)/shard_map/ppermute | solution.py:90
  95.9 0.6 collective-permute-start.8
  96.5 0.7 collective-permute-done.6
  97.3 3.2 %collective-permute-done.7 = f32[1280]{0:T(1024)S(1)} collective-permute-done((f32[1280]{0:T(1024)S(1)}, f32[1280]{0:T(1024)S(1)}, u32[]{:S(2)}, u32[]{:S(2)}) %collective-permute-start.7) | collective-permute-done | bytes 5152 | tf_op jit(solution)/shard_map/ppermute | solution.py:90
  100.4 0.9 collective-permute-done.8
  101.3 0.1 concatenate.47
  101.4 0.1 fusion.26
  101.5 0.1 fusion.22
  101.6 0.1 fusion.25
  101.8 0.0 copy-start.6
  101.8 0.0 copy-start.8
  101.8 3.0 %fusion.29 = f32[704,4096]{1,0:T(8,128)S(1)} fusion(bf16[128,4096]{1,0:T(8,128)(2,1)} %param.4, f32[512,704]{0,1:T(8,128)S(1)} %get-tuple-element.10, f32[128]{0:T(128)S(1)} %slice_bitcast_fusion, s32[128]{0:T(128)S(1)} %copy-done.11), kind=kOutput, calls=%fused_computation.70 | convolution fusion | flops 738648064 | bytes 12944384 | tf_op jit(solution)/shard_map/dot_general | solution.py:131
  104.8 0.0 copy-start.10
  104.8 1.2 select_convert_fusion
  106.0 6.7 %add_convert_fusion = bf16[704,4096]{1,0:T(8,128)(2,1)} fusion(f32[704,4096]{1,0:T(8,128)S(1)} %fusion.29, bf16[512,704]{0,1:T(8,128)(2,1)} %select_convert_fusion, bf16[128,4096]{1,0:T(8,128)(2,1)} %collective-permute-done.5, bf16[128,4096]{1,0:T(8,128)(2,1)} %collective-permute-done.4, bf16[128,4096]{1,0:T(8,128)(2,1)} %collective-permute-done.3, ...), kind=kOutput, calls=%fused_computation | convolution fusion | flops 2975334400 | bytes 22216704 | tf_op jit(solution)/shard_map/dot_general | solution.py:133
  112.7 0.0 reduce-scatter.2.cloned.1.call-update
  112.8 0.0 slice-start.1
  112.8 3.9 %convolution_convert_fusion.1 = bf16[128,4096]{1,0:T(8,128)(2,1)S(1)} fusion(bf16[704,4096]{1,0:T(8,128)(2,1)} %all-gather.2.cloned.1.call-done, bf16[512,704]{0,1:T(8,128)(2,1)} %select_convert_fusion), kind=kOutput, calls=%fused_computation.5 | convolution fusion | flops 738721792 | bytes 6995968 | tf_op jit(solution)/shard_map/dot_general | solution.py:119
  116.7 0.6 collective-permute-start.9
  117.3 1.9 %convolution_convert_fusion = bf16[128,4096]{1,0:T(8,128)(2,1)S(1)} fusion(bf16[704,4096]{1,0:T(8,128)(2,1)S(1)} %bitcast.38, bf16[512,704]{0,1:T(8,128)(2,1)} %select_convert_fusion), kind=kOutput, calls=%fused_computation.4 | convolution fusion | flops 738721792 | bytes 6995968 | tf_op jit(solution)/shard_map/dot_general | solution.py:119
  119.2 1.5 collective-permute-start.11
  120.8 37.9 %collective-permute-done.9 = bf16[128,4096]{1,0:T(8,128)(2,1)S(1)} collective-permute-done((bf16[128,4096]{1,0:T(8,128)(2,1)S(1)}, bf16[128,4096]{1,0:T(8,128)(2,1)S(1)}, u32[]{:S(2)}, u32[]{:S(2)}) %collective-permute-start.9) | collective-permute-done | bytes 1048608 | tf_op jit(solution)/shard_map/ppermute | solution.py:122
  158.7 3.0 %add_convert_fusion.1 = bf16[128,4096]{1,0:T(8,128)(2,1)} fusion(bf16[128,4096]{1,0:T(8,128)(2,1)S(1)} %collective-permute-done.9, bf16[704,4096]{1,0:T(8,128)(2,1)S(1)} %bitcast.38, bf16[512,704]{0,1:T(8,128)(2,1)} %select_convert_fusion), kind=kOutput, calls=%fused_computation.14 | convolution fusion | flops 739770368 | bytes 8044544 | tf_op jit(solution)/shard_map/dot_general | solution.py:119
  161.7 0.0 collective-permute-start.10
  161.7 0.5 fusion.28
  162.2 3.3 %fusion.14 = f32[128,4096]{1,0:T(8,128)} fusion(bf16[704,4096]{1,0:T(8,128)(2,1)S(1)} %bitcast.38, bf16[512,704]{0,1:T(8,128)(2,1)} %select_convert_fusion), kind=kOutput, calls=%fused_computation.29 | convolution fusion | flops 738197504 | bytes 8044544 | tf_op jit(solution)/shard_map/dot_general | solution.py:119
  165.4 2.4 %fusion.30 = f32[128,4096]{1,0:T(8,128)} fusion(bf16[704,4096]{1,0:T(8,128)(2,1)S(1)} %bitcast.38, f32[512,704]{0,1:T(8,128)S(1)} %get-tuple-element.10, f32[128]{0:T(128)S(1)} %slice_bitcast_fusion, s32[128]{0:T(128)S(1)} %copy-done.11), kind=kOutput, calls=%fused_computation.71 | convolution fusion | flops 738648064 | bytes 8225792 | tf_op jit(solution)/shard_map/dot_general | solution.py:144
  167.8 1.5 convert_element_type.45
  169.4 1.4 reduce-scatter.2.cloned.1.call-done
  170.8 2.5 %convert_element_type.47 = f32[88,4096]{1,0:T(8,128)} convert(bf16[88,4096]{1,0:T(8,128)(2,1)} %reduce-scatter.2.cloned.1.call-done) | non-fusion elementwise | flops 360448 | bytes 2162688 | tf_op jit(solution)/shard_map/convert_element_type | solution.py:136
  173.2 9.9 %collective-permute-done.10 = bf16[128,4096]{1,0:T(8,128)(2,1)} collective-permute-done((bf16[128,4096]{1,0:T(8,128)(2,1)}, bf16[128,4096]{1,0:T(8,128)(2,1)}, u32[]{:S(2)}, u32[]{:S(2)}) %collective-permute-start.10) | collective-permute-done | bytes 1048608 | tf_op jit(solution)/shard_map/ppermute | solution.py:122
  183.1 3.7 %add_add_fusion = f32[128,4096]{1,0:T(8,128)} fusion(f32[128,4096]{1,0:T(8,128)} %fusion.30, f32[128,4096]{1,0:T(8,128)S(1)} %copy-done.2, f32[128,4096]{1,0:T(8,128)S(1)} %copy-done.1, bf16[128,4096]{1,0:T(8,128)(2,1)} %collective-permute-done.10), kind=kLoop, calls=%fused_computation.13 | loop fusion | flops 2097152 | bytes 9437184 | tf_op jit(solution)/shard_map/add | solution.py:145
  (39 shorter events, 0.2 us)
Async XLA Ops:
  7.2 58.4 %all-gather.2.cloned.1.call-start = ((), (), s32[]{:S(2)}) async-start(), calls=%async_computation.1 | async-start | bytes 6488064 | tf_op jit(solution)/shard_map/all_gather | solution.py:19
  7.9 162.9 %reduce-scatter.2.cloned.1.call-start = ((), (), s32[]{:S(2)}) async-start(), calls=%async_computation.2 | async-start | bytes 6488064 | tf_op jit(solution)/shard_map/reduce_scatter | solution.py:134
  7.9 50.6 %collective-permute-start.3 = (bf16[128,4096]{1,0:T(8,128)(2,1)}, bf16[128,4096]{1,0:T(8,128)(2,1)}, u32[]{:S(2)}, u32[]{:S(2)}) collective-permute-start(bf16[128,4096]{1,0:T(8,128)(2,1)} %param.4), channel_id=1, source_target_pairs={{0,3},{1,0},{2,1},{3,2},{4,7},{5,4},{6,5},{7,6},{8,11},{9,8},{10,9... | collective-permute-start | bytes 3145736 | tf_op jit(solution)/shard_map/ppermute | solution.py:31
  13.0 23.9 %collective-permute-start = (s32[128,8]{0,1:T(8,128)}, s32[128,8]{0,1:T(8,128)S(1)}, u32[]{:S(2)}, u32[]{:S(2)}) collective-permute-start(s32[128,8]{0,1:T(8,128)} %param.7), channel_id=1, source_target_pairs={{0,3},{1,0},{2,1},{3,2},{4,7},{5,4},{6,5},{7,6},{8,11},{9,8},{10,9... | collective-permute-start | bytes 12296 | tf_op jit(solution)/shard_map/ppermute | solution.py:31
  13.5 45.0 %collective-permute-start.2 = (s32[128,8]{0,1:T(8,128)}, s32[128,8]{0,1:T(8,128)S(1)}, u32[]{:S(2)}, u32[]{:S(2)}) collective-permute-start(s32[128,8]{0,1:T(8,128)} %param.7), channel_id=1, source_target_pairs={{0,1},{1,2},{2,3},{3,0},{4,5},{5,6},{6,7},{7,4},{8,9},{9,10},{10,1... | collective-permute-start | bytes 12296 | tf_op jit(solution)/shard_map/ppermute | solution.py:35
  15.1 72.3 %collective-permute-start.5 = (bf16[128,4096]{1,0:T(8,128)(2,1)}, bf16[128,4096]{1,0:T(8,128)(2,1)}, u32[]{:S(2)}, u32[]{:S(2)}) collective-permute-start(bf16[128,4096]{1,0:T(8,128)(2,1)} %param.4), channel_id=1, source_target_pairs={{0,1},{1,2},{2,3},{3,0},{4,5},{5,6},{6,7},{7,4},{8,9},{9,10},{10,1... | collective-permute-start | bytes 3145736 | tf_op jit(solution)/shard_map/ppermute | solution.py:35
  37.0 21.5 %collective-permute-start.1 = (s32[128,8]{0,1:T(8,128)S(1)}, s32[128,8]{0,1:T(8,128)S(1)}, u32[]{:S(2)}, u32[]{:S(2)}) collective-permute-start(s32[128,8]{0,1:T(8,128)S(1)} %collective-permute-done), channel_id=1, source_target_pairs={{0,3},{1,0},{2,1},{3,2},{4,7},{5,4},{6,5},{7,6},{8,11},{9,8},{10,9... | collective-permute-start | bytes 12296 | tf_op jit(solution)/shard_map/ppermute | solution.py:31
  58.6 25.8 %collective-permute-start.4 = (bf16[128,4096]{1,0:T(8,128)(2,1)}, bf16[128,4096]{1,0:T(8,128)(2,1)}, u32[]{:S(2)}, u32[]{:S(2)}) collective-permute-start(bf16[128,4096]{1,0:T(8,128)(2,1)} %collective-permute-done.3), channel_id=1, source_target_pairs={{0,3},{1,0},{2,1},{3,2},{4,7},{5,4},{6,5},{7,6},{8,11},{9,8},{10,9... | collective-permute-start | bytes 3145736 | tf_op jit(solution)/shard_map/ppermute | solution.py:31
  65.5 4.8 %copy-start.9 = (bf16[128,4096]{1,0:T(8,128)(2,1)S(1)}, bf16[128,4096]{1,0:T(8,128)(2,1)}, u32[]{:S(2)}) copy-start(bf16[128,4096]{1,0:T(8,128)(2,1)} %param.4) | copy-start | bytes 3145732
  65.6 4.9 %copy-start = (bf16[704,4096]{1,0:T(8,128)(2,1)S(1)}, bf16[704,4096]{1,0:T(8,128)(2,1)}, u32[]{:S(2)}) copy-start(bf16[704,4096]{1,0:T(8,128)(2,1)} %all-gather.2.cloned.1.call-done) | copy-start | bytes 17301508
  72.1 18.6 %copy-start.3 = (f32[128,704]{0,1:T(8,128)}, f32[128,704]{0,1:T(8,128)S(1)}, u32[]{:S(2)}) copy-start(f32[128,704]{0,1:T(8,128)S(1)} %fusion.31) | copy-start | bytes 1081348
  87.3 3.4 %copy-start.5 = (f32[128,704]{0,1:T(8,128)}, f32[128,704]{0,1:T(8,128)S(1)}, u32[]{:S(2)}) copy-start(f32[128,704]{0,1:T(8,128)S(1)} %fusion.33) | copy-start | bytes 1081348
  90.4 0.8 copy-start.7
  90.7 0.7 copy-start.11
  91.5 5.7 %collective-permute-start.6 = (f32[1280]{0:T(1024)S(1)}, f32[1280]{0:T(1024)S(1)}, u32[]{:S(2)}, u32[]{:S(2)}) collective-permute-start(f32[1280]{0:T(1024)S(1)} %pad_maximum_fusion), channel_id=1, source_target_pairs={{0,3},{1,0},{2,1},{3,2},{4,7},{5,4},{6,5},{7,6},{8,11},{9,8},{10,9... | collective-permute-start | bytes 15368 | tf_op jit(solution)/shard_map/ppermute | solution.py:90
  95.9 4.5 %collective-permute-start.7 = (f32[1280]{0:T(1024)S(1)}, f32[1280]{0:T(1024)S(1)}, u32[]{:S(2)}, u32[]{:S(2)}) collective-permute-start(f32[1280]{0:T(1024)S(1)} %pad_maximum_fusion), channel_id=1, source_target_pairs={{0,2},{1,3},{2,0},{3,1},{4,6},{5,7},{6,4},{7,5},{8,10},{9,11},{10,... | collective-permute-start | bytes 15368 | tf_op jit(solution)/shard_map/ppermute | solution.py:90
  95.9 5.4 %collective-permute-start.8 = (f32[1280]{0:T(1024)S(1)}, f32[1280]{0:T(1024)S(1)}, u32[]{:S(2)}, u32[]{:S(2)}) collective-permute-start(f32[1280]{0:T(1024)S(1)} %pad_maximum_fusion), channel_id=1, source_target_pairs={{0,1},{1,2},{2,3},{3,0},{4,5},{5,6},{6,7},{7,4},{8,9},{9,10},{10,1... | collective-permute-start | bytes 15368 | tf_op jit(solution)/shard_map/ppermute | solution.py:90
  101.8 3.0 %copy-start.4 = (f32[128,704]{0,1:T(8,128)S(1)}, f32[128,704]{0,1:T(8,128)}, u32[]{:S(2)}) copy-start(f32[128,704]{0,1:T(8,128)} %copy-done.3) | copy-start | bytes 1081348
  101.8 3.0 %copy-start.6 = (f32[128,704]{0,1:T(8,128)S(1)}, f32[128,704]{0,1:T(8,128)}, u32[]{:S(2)}) copy-start(f32[128,704]{0,1:T(8,128)} %copy-done.5) | copy-start | bytes 1081348
  101.8 3.0 %copy-start.8 = (f32[128,704]{0,1:T(8,128)S(1)}, f32[128,704]{0,1:T(8,128)}, u32[]{:S(2)}) copy-start(f32[128,704]{0,1:T(8,128)} %copy-done.7) | copy-start | bytes 1081348
  104.8 1.2 copy-start.10
  112.7 4.6 %slice-start = ((s8[5767168]{0:T(1024)(128)(4,1)}), s8[1572864]{0:T(1024)(128)(4,1)S(1)}, s32[]{:S(2)}) async-start(s8[5767168]{0:T(1024)(128)(4,1)} %bitcast.37), calls=%async_computation.3 | async-start | bytes 3145728
  112.8 4.5 %slice-start.1 = ((s8[5767168]{0:T(1024)(128)(4,1)}), s8[4194304]{0:T(1024)(128)(4,1)S(1)}, s32[]{:S(2)}) async-start(s8[5767168]{0:T(1024)(128)(4,1)} %bitcast.37), calls=%async_computation.4 | async-start | bytes 8388608
  116.7 42.0 %collective-permute-start.9 = (bf16[128,4096]{1,0:T(8,128)(2,1)S(1)}, bf16[128,4096]{1,0:T(8,128)(2,1)S(1)}, u32[]{:S(2)}, u32[]{:S(2)}) collective-permute-start(bf16[128,4096]{1,0:T(8,128)(2,1)S(1)} %convolution_convert_fusion.1), channel_id=1, source_target_pairs={{0,3},{1,0},{2,1},{3,2},{4,7},{5,4},{6,5},{7,6},{8,11},{9,8},{10,9... | collective-permute-start | bytes 3145736 | tf_op jit(solution)/shard_map/ppermute | solution.py:122
  119.2 48.6 %collective-permute-start.11 = (bf16[128,4096]{1,0:T(8,128)(2,1)S(1)}, bf16[128,4096]{1,0:T(8,128)(2,1)S(1)}, u32[]{:S(2)}, u32[]{:S(2)}) collective-permute-start(bf16[128,4096]{1,0:T(8,128)(2,1)S(1)} %convolution_convert_fusion), channel_id=1, source_target_pairs={{0,1},{1,2},{2,3},{3,0},{4,5},{5,6},{6,7},{7,4},{8,9},{9,10},{10,1... | collective-permute-start | bytes 3145736 | tf_op jit(solution)/shard_map/ppermute | solution.py:122
  161.7 21.5 %collective-permute-start.10 = (bf16[128,4096]{1,0:T(8,128)(2,1)}, bf16[128,4096]{1,0:T(8,128)(2,1)}, u32[]{:S(2)}, u32[]{:S(2)}) collective-permute-start(bf16[128,4096]{1,0:T(8,128)(2,1)} %add_convert_fusion.1), channel_id=1, source_target_pairs={{0,3},{1,0},{2,1},{3,2},{4,7},{5,4},{6,5},{7,6},{8,11},{9,8},{10,9... | collective-permute-start | bytes 3145736 | tf_op jit(solution)/shard_map/ppermute | solution.py:122
  167.8 15.3 %copy-start.1 = (f32[128,4096]{1,0:T(8,128)S(1)}, f32[128,4096]{1,0:T(8,128)}, u32[]{:S(2)}) copy-start(f32[128,4096]{1,0:T(8,128)} %fusion.14) | copy-start | bytes 6291460
  170.8 12.4 %copy-start.2 = (f32[128,4096]{1,0:T(8,128)S(1)}, f32[128,4096]{1,0:T(8,128)}, u32[]{:S(2)}) copy-start(f32[128,4096]{1,0:T(8,128)} %convert_element_type.45) | copy-start | bytes 6291460
Sparse Core Ops, SparseCore 0:
  9.9 46.0 all-gather.1
  112.9 57.8 reduce-scatter.1

commit v14 on v13

--- a/solution.py
+++ b/solution.py
@@ -121,7 +121,10 @@
     def hop(part, perm):
         return lax.ppermute(part.astype(jnp.bfloat16), "slab", perm).astype(jnp.float32)
 
-    carried = grad_for(0)
+    own_coef = (
+        coef_pool.astype(jnp.float32) + hard_matrix[:query_rows_dev].astype(jnp.float32)
+    ).astype(jnp.bfloat16)
+    carried = jnp.dot(own_coef, pool, preferred_element_type=jnp.float32)
     if steps_down:
         down = grad_for(slabs - steps_down)
         for step in range(1, steps_down):
@@ -129,8 +132,11 @@
         carried = carried + hop(down, ring_down)
     column_queries = jnp.concatenate(query_blocks, axis=0)
     partial = lax.dot_general(
-        coef_pool, queries, contract_cols, preferred_element_type=jnp.float32
-    ) + lax.dot_general(hard_matrix, column_queries, contract_cols, preferred_element_type=jnp.float32)
+        jnp.concatenate([own_coef, hard_matrix[query_rows_dev:]], axis=0),
+        column_queries,
+        contract_cols,
+        preferred_element_type=jnp.float32,
+    )
     passage_grad = lax.psum_scatter(
         partial.astype(jnp.bfloat16), "blk", scatter_dimension=0, tiled=True
     ).astype(jnp.float32)
@@ -141,8 +147,7 @@
         up = hop(up, ring_up)
         up, passage_grad = lax.optimization_barrier((up, passage_grad))
         carried = carried + up
-    pool_grad = jnp.dot(coef_pool, pool, preferred_element_type=jnp.float32)
-    query_grad = pool_grad + carried
+    query_grad = carried
 
     return (query_loss, query_grad, passage_grad)
 

time: 194 us -> 190 us (0.979)
  matrix products: 36.4 us -> 29.9 us
  waiting for transfers between devices: 105 us -> 108 us
    dot_general x4 -> x3, matrix products: 12.1 us -> 6.84 us  [grad_for(): return jnp.dot(rows, pool, preferred_element_type=jnp.float32)]
    reduce_scatter x1, waiting for transfers between devices: 1.4 us -> 4.39 us  [per_device(): lax.psum_scatter(partial.astype(jnp.bfloat16), 'blk', scatter_dimension=0...]
    dot_general x3 -> x2, matrix products: 12 us -> 9.96 us  [the longest x1 7.59 us: per_device(): lax.dot_general(jnp.concatenate([own_coef, hard_matrix[query_rows_dev:]],...]
    add x1, other arithmetic: 3.66 us -> 1.72 us  [per_device(): carried = carried + up]
  transfers between devices with their start and end apart: 14 -> 14, of which waited for: 9 -> 10; matrix products, arithmetic and copies ran while one was open for 16% -> 14% of each run, Pallas kernels for 0% -> 0%
where the time goes in v14:
time: 190 us
  waiting for transfers between devices  108 us (57%)
  matrix products  29.9 us (16%)
  starting transfers between devices  22.8 us (12%)
  between operations  14.3 us (8%)
  other arithmetic  12.8 us (7%)
    ppermute x4, waiting for transfers between devices, ring_gather(): current = lax.ppermute(current, 'slab', ring_down)  50 us
    ppermute x3, waiting for transfers between devices, hop(): lax.ppermute(part.astype(jnp.bfloat16), 'slab', perm).astype(jnp.float32)  49.6 us
    ppermute x4, starting transfers between devices, ring_gather(): current = lax.ppermute(current, 'slab', ring_down)  14.1 us
    dot_general x4, matrix products, per_device(): lax.dot_general(block, pool, contract_rows, preferred_element_type=jnp.fl...  13.1 us
    dot_general x1, matrix products, per_device(): lax.dot_general(jnp.concatenate([own_coef, hard_matrix[query_rows_dev:]],...  7.59 us
    dot_general x3, matrix products, grad_for(): return jnp.dot(rows, pool, preferred_element_type=jnp.float32)  6.84 us
    ppermute x3, starting transfers between devices, per_device(): lax.ppermute(payload, 'slab', [(i, (i - t) % slabs) for i in range(slabs)])  4.89 us
    reduce_scatter x1, waiting for transfers between devices, per_device(): lax.psum_scatter(partial.astype(jnp.bfloat16), 'blk', scatter_dimension=0...  4.39 us
  transfers between devices with their start and end apart: 14, of which 10 were waited for; matrix products, arithmetic and copies ran while one was open for 14% of the time, Pallas kernels for 0%

profile of v14, /device:TPU:0, one launch (start us, length us, event | category | flops | bytes accessed | tf_op | source)
XLA Modules:
  0.0 190.0 jit_solution(7943355008856122946)
XLA Ops:
  7.2 0.0 copy-start.5
  7.2 0.0 all-gather.2.cloned.1.call-start
  7.2 0.7 all-gather.2.cloned.1.call-update
  7.9 0.0 reduce-scatter.2.cloned.1.call-start
  8.0 5.1 %collective-permute-start.3 = (bf16[128,4096]{1,0:T(8,128)(2,1)}, bf16[128,4096]{1,0:T(8,128)(2,1)}, u32[]{:S(2)}, u32[]{:S(2)}) collective-permute-start(bf16[128,4096]{1,0:T(8,128)(2,1)} %param.4), channel_id=1, source_target_pairs={{0,3},{1,0},{2,1},{3,2},{4,7},{5,4},{6,5},{7,6},{8,11},{9,8},{10,9... | collective-permute-start | bytes 3145736 | tf_op jit(solution)/shard_map/ppermute | solution.py:31
  13.1 0.4 collective-permute-start
  13.5 1.6 collective-permute-start.2
  15.1 0.0 collective-permute-start.5
  15.1 0.7 constant_dynamic-update-slice_fusion.3
  15.8 21.2 %collective-permute-done = s32[128,8]{0,1:T(8,128)S(1)} collective-permute-done((s32[128,8]{0,1:T(8,128)}, s32[128,8]{0,1:T(8,128)S(1)}, u32[]{:S(2)}, u32[]{:S(2)}) %collective-permute-start) | collective-permute-done | bytes 4128 | tf_op jit(solution)/shard_map/ppermute | solution.py:31
  37.0 4.3 %collective-permute-start.1 = (s32[128,8]{0,1:T(8,128)S(1)}, s32[128,8]{0,1:T(8,128)S(1)}, u32[]{:S(2)}, u32[]{:S(2)}) collective-permute-start(s32[128,8]{0,1:T(8,128)S(1)} %collective-permute-done), channel_id=1, source_target_pairs={{0,3},{1,0},{2,1},{3,2},{4,7},{5,4},{6,5},{7,6},{8,11},{9,8},{10,9... | collective-permute-start | bytes 12296 | tf_op jit(solution)/shard_map/ppermute | solution.py:31
  41.3 17.3 %collective-permute-done.1 = s32[128,8]{0,1:T(8,128)S(1)} collective-permute-done((s32[128,8]{0,1:T(8,128)S(1)}, s32[128,8]{0,1:T(8,128)S(1)}, u32[]{:S(2)}, u32[]{:S(2)}) %collective-permute-start.1) | collective-permute-done | bytes 4128 | tf_op jit(solution)/shard_map/ppermute | solution.py:31
  58.5 0.0 collective-permute-done.2
  58.6 0.0 collective-permute-done.3
  58.6 4.3 %collective-permute-start.4 = (bf16[128,4096]{1,0:T(8,128)(2,1)}, bf16[128,4096]{1,0:T(8,128)(2,1)}, u32[]{:S(2)}, u32[]{:S(2)}) collective-permute-start(bf16[128,4096]{1,0:T(8,128)(2,1)} %collective-permute-done.3), channel_id=1, source_target_pairs={{0,3},{1,0},{2,1},{3,2},{4,7},{5,4},{6,5},{7,6},{8,11},{9,8},{10,9... | collective-permute-start | bytes 3145736 | tf_op jit(solution)/shard_map/ppermute | solution.py:31
  62.9 2.6 %convert_reduce_fusion = f32[512,704]{0,1:T(8,128)S(1)} fusion(s32[512,8]{0,1:T(8,128)S(1)} %fusion.18, pred[512,8]{0,1:T(8,128)(4,1)S(1)} %fusion.19), kind=kLoop, calls=%fused_computation | loop fusion | flops 11173888 | bytes 1462272 | tf_op jit(solution)/shard_map/reduce_sum | solution.py:66
  65.5 0.0 all-gather.2.cloned.1.call-done
  65.6 4.4 %fusion.30 = f32[128,704]{0,1:T(8,128)S(1)} fusion(bf16[128,4096]{1,0:T(8,128)(2,1)S(1)} %copy-done.5, bf16[704,4096]{1,0:T(8,128)(2,1)} %all-gather.2.cloned.1.call-done), kind=kOutput, calls=%fused_computation.72 | convolution fusion | flops 738197504 | bytes 7176192 | tf_op jit(solution)/shard_map/dot_general | solution.py:52
  70.0 2.9 %fusion.31 = f32[128,704]{0,1:T(8,128)S(1)} fusion(bf16[128,4096]{1,0:T(8,128)(2,1)} %collective-permute-done.3, bf16[704,4096]{1,0:T(8,128)(2,1)S(1)} %copy-done), kind=kOutput, calls=%fused_computation.73 | convolution fusion | flops 738197504 | bytes 7176192 | tf_op jit(solution)/shard_map/dot_general | solution.py:52
  72.9 11.5 %collective-permute-done.4 = bf16[128,4096]{1,0:T(8,128)(2,1)} collective-permute-done((bf16[128,4096]{1,0:T(8,128)(2,1)}, bf16[128,4096]{1,0:T(8,128)(2,1)}, u32[]{:S(2)}, u32[]{:S(2)}) %collective-permute-start.4) | collective-permute-done | bytes 1048608 | tf_op jit(solution)/shard_map/ppermute | solution.py:31
  84.5 2.9 %fusion.32 = f32[128,704]{0,1:T(8,128)S(1)} fusion(bf16[128,4096]{1,0:T(8,128)(2,1)} %collective-permute-done.4, bf16[704,4096]{1,0:T(8,128)(2,1)S(1)} %copy-done), kind=kOutput, calls=%fused_computation.74 | convolution fusion | flops 738197504 | bytes 7176192 | tf_op jit(solution)/shard_map/dot_general | solution.py:52
  87.3 0.0 collective-permute-done.5
  87.4 2.9 %fusion.33 = f32[128,704]{0,1:T(8,128)S(1)} fusion(bf16[128,4096]{1,0:T(8,128)(2,1)} %collective-permute-done.5, bf16[704,4096]{1,0:T(8,128)(2,1)S(1)} %copy-done), kind=kOutput, calls=%fused_computation.75 | convolution fusion | flops 738197504 | bytes 7176192 | tf_op jit(solution)/shard_map/dot_general | solution.py:52
  90.2 0.0 copy-start.3
  90.3 0.3 select_reduce_fusion.1
  90.6 0.4 select_reduce_fusion
  91.0 0.0 copy-start.4
  91.0 0.1 slice_reduce_fusion
  91.1 1.0 copy-done.4
  92.1 0.0 copy-done.7
  92.1 0.1 exponential_reduce_fusion
  92.2 0.1 collective-permute-start.8
  92.3 4.8 %collective-permute-start.7 = (f32[1280]{0:T(1024)S(1)}, f32[1280]{0:T(1024)S(1)}, u32[]{:S(2)}, u32[]{:S(2)}) collective-permute-start(f32[1280]{0:T(1024)S(1)} %pad_maximum_fusion), channel_id=1, source_target_pairs={{0,2},{1,3},{2,0},{3,1},{4,6},{5,7},{6,4},{7,5},{8,10},{9,11},{10,... | collective-permute-start | bytes 15368 | tf_op jit(solution)/shard_map/ppermute | solution.py:90
  97.1 0.0 collective-permute-start.6
  97.1 1.1 collective-permute-done.8
  98.2 0.6 collective-permute-done.7
  98.8 2.0 %collective-permute-done.6 = f32[1280]{0:T(1024)S(1)} collective-permute-done((f32[1280]{0:T(1024)S(1)}, f32[1280]{0:T(1024)S(1)}, u32[]{:S(2)}, u32[]{:S(2)}) %collective-permute-start.6) | collective-permute-done | bytes 5152 | tf_op jit(solution)/shard_map/ppermute | solution.py:90
  100.8 0.1 concatenate.50
  100.9 0.1 fusion.27
  101.0 0.1 fusion.23
  101.1 0.1 fusion.26
  101.2 0.0 copy-start.6
  101.2 1.4 select_convert_fusion
  102.7 0.1 slice.53
  102.7 1.1 add_convert_fusion.1
  103.8 7.6 %convolution_convert_fusion = bf16[704,4096]{1,0:T(8,128)(2,1)} fusion(bf16[128,4096]{1,0:T(8,128)(2,1)} %collective-permute-done.5, bf16[128,4096]{1,0:T(8,128)(2,1)} %collective-permute-done.4, bf16[128,4096]{1,0:T(8,128)(2,1)} %collective-permute-done.3, bf16[128,4096]{1,0:T(8,128)(2,1)S(1)} %copy-done.6, bf16[384,704]{0,1:T(8,128)(2,1)S(1)} %slice.53, ...), kind=kOutput, calls=%fused_computation.3 | convolution fusion | flops 2973892608 | bytes 10682368 | tf_op jit(solution)/shard_map/dot_general | solution.py:134
  111.4 0.0 reduce-scatter.2.cloned.1.call-update
  111.5 0.0 slice-start.1
  111.5 3.8 %convolution_convert_fusion.2 = bf16[128,4096]{1,0:T(8,128)(2,1)S(1)} fusion(bf16[704,4096]{1,0:T(8,128)(2,1)} %all-gather.2.cloned.1.call-done, bf16[512,704]{0,1:T(8,128)(2,1)S(1)} %select_convert_fusion), kind=kOutput, calls=%fused_computation.5 | convolution fusion | flops 738721792 | bytes 6995968 | tf_op jit(solution)/shard_map/dot_general | solution.py:119
  115.3 1.9 %collective-permute-start.9 = (bf16[128,4096]{1,0:T(8,128)(2,1)S(1)}, bf16[128,4096]{1,0:T(8,128)(2,1)S(1)}, u32[]{:S(2)}, u32[]{:S(2)}) collective-permute-start(bf16[128,4096]{1,0:T(8,128)(2,1)S(1)} %convolution_convert_fusion.2), channel_id=1, source_target_pairs={{0,3},{1,0},{2,1},{3,2},{4,7},{5,4},{6,5},{7,6},{8,11},{9,8},{10,9... | collective-permute-start | bytes 3145736 | tf_op jit(solution)/shard_map/ppermute | solution.py:122
  117.2 0.0 slice-done
  117.2 1.0 convolution_convert_fusion.1
  118.2 0.2 collective-permute-start.11
  118.5 39.0 %collective-permute-done.9 = bf16[128,4096]{1,0:T(8,128)(2,1)S(1)} collective-permute-done((bf16[128,4096]{1,0:T(8,128)(2,1)S(1)}, bf16[128,4096]{1,0:T(8,128)(2,1)S(1)}, u32[]{:S(2)}, u32[]{:S(2)}) %collective-permute-start.9) | collective-permute-done | bytes 1048608 | tf_op jit(solution)/shard_map/ppermute | solution.py:122
  157.4 2.0 %add_convert_fusion = bf16[128,4096]{1,0:T(8,128)(2,1)} fusion(bf16[128,4096]{1,0:T(8,128)(2,1)S(1)} %collective-permute-done.9, bf16[704,4096]{1,0:T(8,128)(2,1)S(1)} %bitcast.36, bf16[512,704]{0,1:T(8,128)(2,1)S(1)} %select_convert_fusion), kind=kOutput, calls=%fused_computation.14 | convolution fusion | flops 739770368 | bytes 8044544 | tf_op jit(solution)/shard_map/dot_general | solution.py:119
  159.5 0.0 collective-permute-start.10
  159.5 0.5 fusion.29
  160.0 2.4 %fusion.34 = f32[128,4096]{1,0:T(8,128)} fusion(bf16[128,704]{0,1:T(8,128)(2,1)S(1)} %add_convert_fusion.1, bf16[704,4096]{1,0:T(8,128)(2,1)S(1)} %bitcast.36), kind=kOutput, calls=%fused_computation.76 | convolution fusion | flops 738197504 | bytes 8044544 | tf_op jit(solution)/shard_map/dot_general | solution.py:127
  162.4 1.9 %collective-permute-done.11 = bf16[128,4096]{1,0:T(8,128)(2,1)S(1)} collective-permute-done((bf16[128,4096]{1,0:T(8,128)(2,1)S(1)}, bf16[128,4096]{1,0:T(8,128)(2,1)S(1)}, u32[]{:S(2)}, u32[]{:S(2)}) %collective-permute-start.11) | collective-permute-done | bytes 1048608 | tf_op jit(solution)/shard_map/ppermute | solution.py:122
  164.3 1.5 convert_element_type.57
  165.8 4.4 %reduce-scatter.2.cloned.1.call-done = bf16[88,4096]{1,0:T(8,128)(2,1)} async-done(((bf16[704,4096]{1,0:T(8,128)(2,1)}), bf16[88,4096]{1,0:T(8,128)(2,1)}) %reduce-scatter.2.cloned.1.call-update) | async-done | bytes 720912 | tf_op jit(solution)/shard_map/reduce_scatter | solution.py:140
  170.2 2.5 %convert_element_type.59 = f32[88,4096]{1,0:T(8,128)} convert(bf16[88,4096]{1,0:T(8,128)(2,1)} %reduce-scatter.2.cloned.1.call-done) | non-fusion elementwise | flops 360448 | bytes 2162688 | tf_op jit(solution)/shard_map/convert_element_type | solution.py:142
  172.7 8.7 %collective-permute-done.10 = bf16[128,4096]{1,0:T(8,128)(2,1)S(1)} collective-permute-done((bf16[128,4096]{1,0:T(8,128)(2,1)}, bf16[128,4096]{1,0:T(8,128)(2,1)S(1)}, u32[]{:S(2)}, u32[]{:S(2)}) %collective-permute-start.10) | collective-permute-done | bytes 1048608 | tf_op jit(solution)/shard_map/ppermute | solution.py:122
  181.4 1.7 add_add_fusion
  (31 shorter events, 0.2 us)
Async XLA Ops:
  7.2 58.4 %copy-start.5 = (bf16[128,4096]{1,0:T(8,128)(2,1)S(1)}, bf16[128,4096]{1,0:T(8,128)(2,1)}, u32[]{:S(2)}) copy-start(bf16[128,4096]{1,0:T(8,128)(2,1)} %param.4) | copy-start | bytes 3145732
  7.2 58.4 %all-gather.2.cloned.1.call-start = ((), (), s32[]{:S(2)}) async-start(), calls=%async_computation.1 | async-start | bytes 6488064 | tf_op jit(solution)/shard_map/all_gather | solution.py:19
  7.9 162.3 %reduce-scatter.2.cloned.1.call-start = ((), (), s32[]{:S(2)}) async-start(), calls=%async_computation.2 | async-start | bytes 6488064 | tf_op jit(solution)/shard_map/reduce_scatter | solution.py:140
  8.0 50.6 %collective-permute-start.3 = (bf16[128,4096]{1,0:T(8,128)(2,1)}, bf16[128,4096]{1,0:T(8,128)(2,1)}, u32[]{:S(2)}, u32[]{:S(2)}) collective-permute-start(bf16[128,4096]{1,0:T(8,128)(2,1)} %param.4), channel_id=1, source_target_pairs={{0,3},{1,0},{2,1},{3,2},{4,7},{5,4},{6,5},{7,6},{8,11},{9,8},{10,9... | collective-permute-start | bytes 3145736 | tf_op jit(solution)/shard_map/ppermute | solution.py:31
  13.1 23.9 %collective-permute-start = (s32[128,8]{0,1:T(8,128)}, s32[128,8]{0,1:T(8,128)S(1)}, u32[]{:S(2)}, u32[]{:S(2)}) collective-permute-start(s32[128,8]{0,1:T(8,128)} %param.7), channel_id=1, source_target_pairs={{0,3},{1,0},{2,1},{3,2},{4,7},{5,4},{6,5},{7,6},{8,11},{9,8},{10,9... | collective-permute-start | bytes 12296 | tf_op jit(solution)/shard_map/ppermute | solution.py:31
  13.5 45.0 %collective-permute-start.2 = (s32[128,8]{0,1:T(8,128)}, s32[128,8]{0,1:T(8,128)S(1)}, u32[]{:S(2)}, u32[]{:S(2)}) collective-permute-start(s32[128,8]{0,1:T(8,128)} %param.7), channel_id=1, source_target_pairs={{0,1},{1,2},{2,3},{3,0},{4,5},{5,6},{6,7},{7,4},{8,9},{9,10},{10,1... | collective-permute-start | bytes 12296 | tf_op jit(solution)/shard_map/ppermute | solution.py:35
  15.1 72.3 %collective-permute-start.5 = (bf16[128,4096]{1,0:T(8,128)(2,1)}, bf16[128,4096]{1,0:T(8,128)(2,1)}, u32[]{:S(2)}, u32[]{:S(2)}) collective-permute-start(bf16[128,4096]{1,0:T(8,128)(2,1)} %param.4), channel_id=1, source_target_pairs={{0,1},{1,2},{2,3},{3,0},{4,5},{5,6},{6,7},{7,4},{8,9},{9,10},{10,1... | collective-permute-start | bytes 3145736 | tf_op jit(solution)/shard_map/ppermute | solution.py:35
  37.0 21.5 %collective-permute-start.1 = (s32[128,8]{0,1:T(8,128)S(1)}, s32[128,8]{0,1:T(8,128)S(1)}, u32[]{:S(2)}, u32[]{:S(2)}) collective-permute-start(s32[128,8]{0,1:T(8,128)S(1)} %collective-permute-done), channel_id=1, source_target_pairs={{0,3},{1,0},{2,1},{3,2},{4,7},{5,4},{6,5},{7,6},{8,11},{9,8},{10,9... | collective-permute-start | bytes 12296 | tf_op jit(solution)/shard_map/ppermute | solution.py:31
  58.6 25.8 %collective-permute-start.4 = (bf16[128,4096]{1,0:T(8,128)(2,1)}, bf16[128,4096]{1,0:T(8,128)(2,1)}, u32[]{:S(2)}, u32[]{:S(2)}) collective-permute-start(bf16[128,4096]{1,0:T(8,128)(2,1)} %collective-permute-done.3), channel_id=1, source_target_pairs={{0,3},{1,0},{2,1},{3,2},{4,7},{5,4},{6,5},{7,6},{8,11},{9,8},{10,9... | collective-permute-start | bytes 3145736 | tf_op jit(solution)/shard_map/ppermute | solution.py:31
  65.6 4.5 %copy-start = (bf16[704,4096]{1,0:T(8,128)(2,1)S(1)}, bf16[704,4096]{1,0:T(8,128)(2,1)}, u32[]{:S(2)}) copy-start(bf16[704,4096]{1,0:T(8,128)(2,1)} %all-gather.2.cloned.1.call-done) | copy-start | bytes 17301508
  90.2 0.7 copy-start.3
  90.6 1.5 copy-start.7
  91.0 1.1 copy-start.4
  92.2 6.0 %collective-permute-start.8 = (f32[1280]{0:T(1024)S(1)}, f32[1280]{0:T(1024)S(1)}, u32[]{:S(2)}, u32[]{:S(2)}) collective-permute-start(f32[1280]{0:T(1024)S(1)} %pad_maximum_fusion), channel_id=1, source_target_pairs={{0,1},{1,2},{2,3},{3,0},{4,5},{5,6},{6,7},{7,4},{8,9},{9,10},{10,1... | collective-permute-start | bytes 15368 | tf_op jit(solution)/shard_map/ppermute | solution.py:90
  92.3 6.5 %collective-permute-start.7 = (f32[1280]{0:T(1024)S(1)}, f32[1280]{0:T(1024)S(1)}, u32[]{:S(2)}, u32[]{:S(2)}) collective-permute-start(f32[1280]{0:T(1024)S(1)} %pad_maximum_fusion), channel_id=1, source_target_pairs={{0,2},{1,3},{2,0},{3,1},{4,6},{5,7},{6,4},{7,5},{8,10},{9,11},{10,... | collective-permute-start | bytes 15368 | tf_op jit(solution)/shard_map/ppermute | solution.py:90
  97.1 3.7 %collective-permute-start.6 = (f32[1280]{0:T(1024)S(1)}, f32[1280]{0:T(1024)S(1)}, u32[]{:S(2)}, u32[]{:S(2)}) collective-permute-start(f32[1280]{0:T(1024)S(1)} %pad_maximum_fusion), channel_id=1, source_target_pairs={{0,3},{1,0},{2,1},{3,2},{4,7},{5,4},{6,5},{7,6},{8,11},{9,8},{10,9... | collective-permute-start | bytes 15368 | tf_op jit(solution)/shard_map/ppermute | solution.py:90
  101.2 2.6 %copy-start.6 = (bf16[128,4096]{1,0:T(8,128)(2,1)S(1)}, bf16[128,4096]{1,0:T(8,128)(2,1)}, u32[]{:S(2)}) copy-start(bf16[128,4096]{1,0:T(8,128)(2,1)} %param.4) | copy-start | bytes 3145732
  111.4 5.8 %slice-start = ((s8[5767168]{0:T(1024)(128)(4,1)}), s8[1572864]{0:T(1024)(128)(4,1)S(1)}, s32[]{:S(2)}) async-start(s8[5767168]{0:T(1024)(128)(4,1)} %bitcast.35), calls=%async_computation.3 | async-start | bytes 3145728
  111.5 5.8 %slice-start.1 = ((s8[5767168]{0:T(1024)(128)(4,1)}), s8[4194304]{0:T(1024)(128)(4,1)S(1)}, s32[]{:S(2)}) async-start(s8[5767168]{0:T(1024)(128)(4,1)} %bitcast.35), calls=%async_computation.4 | async-start | bytes 8388608
  115.3 42.2 %collective-permute-start.9 = (bf16[128,4096]{1,0:T(8,128)(2,1)S(1)}, bf16[128,4096]{1,0:T(8,128)(2,1)S(1)}, u32[]{:S(2)}, u32[]{:S(2)}) collective-permute-start(bf16[128,4096]{1,0:T(8,128)(2,1)S(1)} %convolution_convert_fusion.2), channel_id=1, source_target_pairs={{0,3},{1,0},{2,1},{3,2},{4,7},{5,4},{6,5},{7,6},{8,11},{9,8},{10,9... | collective-permute-start | bytes 3145736 | tf_op jit(solution)/shard_map/ppermute | solution.py:122
  118.2 46.1 %collective-permute-start.11 = (bf16[128,4096]{1,0:T(8,128)(2,1)S(1)}, bf16[128,4096]{1,0:T(8,128)(2,1)S(1)}, u32[]{:S(2)}, u32[]{:S(2)}) collective-permute-start(bf16[128,4096]{1,0:T(8,128)(2,1)S(1)} %convolution_convert_fusion.1), channel_id=1, source_target_pairs={{0,1},{1,2},{2,3},{3,0},{4,5},{5,6},{6,7},{7,4},{8,9},{9,10},{10,1... | collective-permute-start | bytes 3145736 | tf_op jit(solution)/shard_map/ppermute | solution.py:122
  159.5 21.9 %collective-permute-start.10 = (bf16[128,4096]{1,0:T(8,128)(2,1)}, bf16[128,4096]{1,0:T(8,128)(2,1)S(1)}, u32[]{:S(2)}, u32[]{:S(2)}) collective-permute-start(bf16[128,4096]{1,0:T(8,128)(2,1)} %add_convert_fusion), channel_id=1, source_target_pairs={{0,3},{1,0},{2,1},{3,2},{4,7},{5,4},{6,5},{7,6},{8,11},{9,8},{10,9... | collective-permute-start | bytes 3145736 | tf_op jit(solution)/shard_map/ppermute | solution.py:122
  162.4 19.0 %copy-start.1 = (f32[128,4096]{1,0:T(8,128)S(1)}, f32[128,4096]{1,0:T(8,128)}, u32[]{:S(2)}) copy-start(f32[128,4096]{1,0:T(8,128)} %fusion.34) | copy-start | bytes 6291460
  170.2 11.2 %copy-start.2 = (f32[128,4096]{1,0:T(8,128)S(1)}, f32[128,4096]{1,0:T(8,128)}, u32[]{:S(2)}) copy-start(f32[128,4096]{1,0:T(8,128)} %convert_element_type.57) | copy-start | bytes 6291460
Sparse Core Ops, SparseCore 0:
  9.9 46.0 all-gather.1
  111.6 58.6 reduce-scatter.1

commit v15 on v14

--- a/solution.py
+++ b/solution.py
@@ -63,15 +63,27 @@
     hard_pos = (owner_dev // slabs) * passage_rows_dev + column_ids % passage_rows_dev
     mine = owner_slab == my_slab
     pool_iota = jnp.arange(pool_size, dtype=jnp.int32)[None, None, :]
-    hit_count = jnp.sum(
-        ((hard_pos[:, :, None] == pool_iota) & mine[:, :, None]).astype(jnp.float32), axis=1
-    )
+    far_below = -1e30
+    counts, maxes, sums = [], [], []
+    for t in range(slabs):
+        rows = slice(t * query_rows_dev, (t + 1) * query_rows_dev)
+        block_scores = scores[rows]
+        count = jnp.sum(
+            ((hard_pos[rows][:, :, None] == pool_iota) & mine[rows][:, :, None]).astype(
+                jnp.float32
+            ),
+            axis=1,
+        )
+        top = jnp.max(jnp.where(count > 0, block_scores, far_below), axis=1)
+        counts.append(count)
+        maxes.append(top)
+        sums.append(
+            jnp.sum(jnp.where(count > 0, count * jnp.exp(block_scores - top[:, None]), 0.0), axis=1)
+        )
+    hit_count = jnp.concatenate(counts, axis=0)
     is_hard = hit_count > 0
-    far_below = -1e30
-    hard_max = jnp.max(jnp.where(is_hard, scores, far_below), axis=1)
-    hard_sum = jnp.sum(
-        jnp.where(is_hard, hit_count * jnp.exp(scores - hard_max[:, None]), 0.0), axis=1
-    )
+    hard_max = jnp.concatenate(maxes)
+    hard_sum = jnp.concatenate(sums)
 
     pool_max = jnp.max(pooled, axis=1)
     pool_sum = jnp.sum(jnp.exp(pooled - pool_max[:, None]), axis=1)

time: 190 us -> 193 us (1.016)
  waiting for transfers between devices: 108 us -> 110 us
    ppermute x4, starting transfers between devices: 14.1 us -> 17 us  [ring_gather(): current = lax.ppermute(current, 'slab', ring_down)]
    ppermute x4, waiting for transfers between devices: 50 us -> 52.4 us  [ring_gather(): current = lax.ppermute(current, 'slab', ring_down)]
  transfers between devices with their start and end apart: 14 -> 14, of which waited for: 10 -> 9; matrix products, arithmetic and copies ran while one was open for 14% -> 14% of each run, Pallas kernels for 0% -> 0%
where the time goes in v15:
time: 193 us; the launch traced here: 192 us
  waiting for transfers between devices  110 us (57%)
  matrix products  30.2 us (16%)
  starting transfers between devices  24.1 us (12%)
  between operations  14.4 us (7%)
  other arithmetic  11.9 us (6%)
    ppermute x4, waiting for transfers between devices, ring_gather(): current = lax.ppermute(current, 'slab', ring_down)  52.4 us
    ppermute x3, waiting for transfers between devices, hop(): lax.ppermute(part.astype(jnp.bfloat16), 'slab', perm).astype(jnp.float32)  49 us
    ppermute x4, starting transfers between devices, ring_gather(): current = lax.ppermute(current, 'slab', ring_down)  17 us
    dot_general x4, matrix products, per_device(): lax.dot_general(block, pool, contract_rows, preferred_element_type=jnp.fl...  13.4 us
    dot_general x1, matrix products, per_device(): lax.dot_general(jnp.concatenate([own_coef, hard_matrix[query_rows_dev:]],...  7.63 us
    dot_general x3, matrix products, grad_for(): return jnp.dot(rows, pool, preferred_element_type=jnp.float32)  6.81 us
    ppermute x3, starting transfers between devices, per_device(): lax.ppermute(payload, 'slab', [(i, (i - t) % slabs) for i in range(slabs)])  4.9 us
    reduce_scatter x1, waiting for transfers between devices, per_device(): lax.psum_scatter(partial.astype(jnp.bfloat16), 'blk', scatter_dimension=0...  4.4 us
  transfers between devices with their start and end apart: 14, of which 9 were waited for; matrix products, arithmetic and copies ran while one was open for 14% of the time, Pallas kernels for 0%

profile of v15, /device:TPU:0, one launch (start us, length us, event | category | flops | bytes accessed | tf_op | source)
XLA Modules:
  0.0 192.2 jit_solution(5535799875439689784)
XLA Ops:
  7.2 0.0 copy-start.8
  7.2 0.0 all-gather.2.cloned.1.call-start
  7.2 0.7 all-gather.2.cloned.1.call-update
  7.9 0.0 reduce-scatter.2.cloned.1.call-start
  8.0 5.1 %collective-permute-start = (s32[128,8]{0,1:T(8,128)}, s32[128,8]{0,1:T(8,128)S(1)}, u32[]{:S(2)}, u32[]{:S(2)}) collective-permute-start(s32[128,8]{0,1:T(8,128)} %param.7), channel_id=1, source_target_pairs={{0,3},{1,0},{2,1},{3,2},{4,7},{5,4},{6,5},{7,6},{8,11},{9,8},{10,9... | collective-permute-start | bytes 12296 | tf_op jit(solution)/shard_map/ppermute | solution.py:31
  13.1 0.0 collective-permute-start.2
  13.1 3.8 %collective-permute-start.3 = (bf16[128,4096]{1,0:T(8,128)(2,1)}, bf16[128,4096]{1,0:T(8,128)(2,1)}, u32[]{:S(2)}, u32[]{:S(2)}) collective-permute-start(bf16[128,4096]{1,0:T(8,128)(2,1)} %param.4), channel_id=1, source_target_pairs={{0,3},{1,0},{2,1},{3,2},{4,7},{5,4},{6,5},{7,6},{8,11},{9,8},{10,9... | collective-permute-start | bytes 3145736 | tf_op jit(solution)/shard_map/ppermute | solution.py:31
  16.9 0.0 collective-permute-start.5
  16.9 0.7 constant_dynamic-update-slice_fusion.3
  17.6 0.0 collective-permute-done
  17.6 3.8 %collective-permute-start.1 = (s32[128,8]{0,1:T(8,128)S(1)}, s32[128,8]{0,1:T(8,128)S(1)}, u32[]{:S(2)}, u32[]{:S(2)}) collective-permute-start(s32[128,8]{0,1:T(8,128)S(1)} %collective-permute-done), channel_id=1, source_target_pairs={{0,3},{1,0},{2,1},{3,2},{4,7},{5,4},{6,5},{7,6},{8,11},{9,8},{10,9... | collective-permute-start | bytes 12296 | tf_op jit(solution)/shard_map/ppermute | solution.py:31
  21.4 40.2 %collective-permute-done.1 = s32[128,8]{0,1:T(8,128)S(1)} collective-permute-done((s32[128,8]{0,1:T(8,128)S(1)}, s32[128,8]{0,1:T(8,128)S(1)}, u32[]{:S(2)}, u32[]{:S(2)}) %collective-permute-start.1) | collective-permute-done | bytes 4128 | tf_op jit(solution)/shard_map/ppermute | solution.py:31
  61.6 0.0 collective-permute-done.2
  61.7 1.2 convert_reduce_fusion.2
  63.0 0.0 collective-permute-done.3
  63.0 4.3 %collective-permute-start.4 = (bf16[128,4096]{1,0:T(8,128)(2,1)}, bf16[128,4096]{1,0:T(8,128)(2,1)}, u32[]{:S(2)}, u32[]{:S(2)}) collective-permute-start(bf16[128,4096]{1,0:T(8,128)(2,1)} %collective-permute-done.3), channel_id=1, source_target_pairs={{0,3},{1,0},{2,1},{3,2},{4,7},{5,4},{6,5},{7,6},{8,11},{9,8},{10,9... | collective-permute-start | bytes 3145736 | tf_op jit(solution)/shard_map/ppermute | solution.py:31
  67.2 1.2 convert_reduce_fusion
  68.5 0.0 copy-start.3
  68.5 0.0 all-gather.2.cloned.1.call-done
  68.5 4.4 %fusion.35 = f32[128,704]{0,1:T(8,128)S(1)} fusion(bf16[128,4096]{1,0:T(8,128)(2,1)S(1)} %copy-done.8, bf16[704,4096]{1,0:T(8,128)(2,1)} %all-gather.2.cloned.1.call-done), kind=kOutput, calls=%fused_computation.95 | convolution fusion | flops 738197504 | bytes 7176192 | tf_op jit(solution)/shard_map/dot_general | solution.py:52
  73.0 3.0 %fusion.36 = f32[128,704]{0,1:T(8,128)S(1)} fusion(bf16[128,4096]{1,0:T(8,128)(2,1)} %collective-permute-done.3, bf16[704,4096]{1,0:T(8,128)(2,1)S(1)} %copy-done), kind=kOutput, calls=%fused_computation.96 | convolution fusion | flops 738197504 | bytes 7176192 | tf_op jit(solution)/shard_map/dot_general | solution.py:52
  76.0 12.2 %collective-permute-done.4 = bf16[128,4096]{1,0:T(8,128)(2,1)} collective-permute-done((bf16[128,4096]{1,0:T(8,128)(2,1)}, bf16[128,4096]{1,0:T(8,128)(2,1)}, u32[]{:S(2)}, u32[]{:S(2)}) %collective-permute-start.4) | collective-permute-done | bytes 1048608 | tf_op jit(solution)/shard_map/ppermute | solution.py:31
  88.2 2.9 %fusion.37 = f32[128,704]{0,1:T(8,128)S(1)} fusion(bf16[128,4096]{1,0:T(8,128)(2,1)} %collective-permute-done.4, bf16[704,4096]{1,0:T(8,128)(2,1)S(1)} %copy-done), kind=kOutput, calls=%fused_computation.97 | convolution fusion | flops 738197504 | bytes 7176192 | tf_op jit(solution)/shard_map/dot_general | solution.py:52
  91.1 0.0 collective-permute-done.5
  91.2 3.0 %fusion.38 = f32[128,704]{0,1:T(8,128)S(1)} fusion(bf16[128,4096]{1,0:T(8,128)(2,1)} %collective-permute-done.5, bf16[704,4096]{1,0:T(8,128)(2,1)S(1)} %copy-done), kind=kOutput, calls=%fused_computation.98 | convolution fusion | flops 738197504 | bytes 7176192 | tf_op jit(solution)/shard_map/dot_general | solution.py:52
  94.2 0.0 copy-start.7
  94.2 0.1 maximum_multiply_fusion
  94.3 0.0 copy-start.10
  94.3 0.2 select_reduce_fusion.8
  94.5 0.4 copy-done.7
  95.0 0.1 copy-done.10
  95.0 0.4 select_reduce_fusion.4
  95.4 0.1 exponential_reduce_fusion
  95.6 0.1 collective-permute-start.8
  95.7 4.8 %collective-permute-start.7 = (f32[1280]{0:T(1024)S(1)}, f32[1280]{0:T(1024)S(1)}, u32[]{:S(2)}, u32[]{:S(2)}) collective-permute-start(f32[1280]{0:T(1024)S(1)} %pad_maximum_fusion.1), channel_id=1, source_target_pairs={{0,2},{1,3},{2,0},{3,1},{4,6},{5,7},{6,4},{7,5},{8,10},{9,11},{10,... | collective-permute-start | bytes 15368 | tf_op jit(solution)/shard_map/ppermute | solution.py:102
  100.5 0.0 collective-permute-start.6
  100.5 1.1 collective-permute-done.8
  101.6 0.6 collective-permute-done.7
  102.1 2.0 %collective-permute-done.6 = f32[1280]{0:T(1024)S(1)} collective-permute-done((f32[1280]{0:T(1024)S(1)}, f32[1280]{0:T(1024)S(1)}, u32[]{:S(2)}, u32[]{:S(2)}) %collective-permute-start.6) | collective-permute-done | bytes 5152 | tf_op jit(solution)/shard_map/ppermute | solution.py:102
  104.2 0.1 concatenate.44
  104.3 0.1 fusion.30
  104.4 0.1 fusion.26
  104.4 0.1 fusion.29
  104.6 0.0 copy-start.9
  104.6 1.9 select_convert_fusion
  106.5 0.1 slice.109
  106.5 0.1 add_convert_fusion.1
  106.7 7.6 %convolution_convert_fusion = bf16[704,4096]{1,0:T(8,128)(2,1)} fusion(bf16[128,4096]{1,0:T(8,128)(2,1)} %collective-permute-done.5, bf16[128,4096]{1,0:T(8,128)(2,1)} %collective-permute-done.4, bf16[128,4096]{1,0:T(8,128)(2,1)} %collective-permute-done.3, bf16[128,4096]{1,0:T(8,128)(2,1)S(1)} %copy-done.9, bf16[384,704]{0,1:T(8,128)(2,1)S(1)} %slice.109, ...), kind=kOutput, calls=%fused_computation | convolution fusion | flops 2973892608 | bytes 10682368 | tf_op jit(solution)/shard_map/dot_general | solution.py:146
  114.3 0.0 reduce-scatter.2.cloned.1.call-update
  114.3 0.0 slice-start.1
  114.3 3.8 %convolution_convert_fusion.2 = bf16[128,4096]{1,0:T(8,128)(2,1)S(1)} fusion(bf16[704,4096]{1,0:T(8,128)(2,1)} %all-gather.2.cloned.1.call-done, bf16[512,704]{0,1:T(8,128)(2,1)S(1)} %select_convert_fusion), kind=kOutput, calls=%fused_computation.2 | convolution fusion | flops 738721792 | bytes 6995968 | tf_op jit(solution)/shard_map/dot_general | solution.py:131
  118.1 1.9 %collective-permute-start.9 = (bf16[128,4096]{1,0:T(8,128)(2,1)S(1)}, bf16[128,4096]{1,0:T(8,128)(2,1)S(1)}, u32[]{:S(2)}, u32[]{:S(2)}) collective-permute-start(bf16[128,4096]{1,0:T(8,128)(2,1)S(1)} %convolution_convert_fusion.2), channel_id=1, source_target_pairs={{0,3},{1,0},{2,1},{3,2},{4,7},{5,4},{6,5},{7,6},{8,11},{9,8},{10,9... | collective-permute-start | bytes 3145736 | tf_op jit(solution)/shard_map/ppermute | solution.py:134
  120.1 1.0 convolution_convert_fusion.1
  121.1 0.2 collective-permute-start.11
  121.3 39.0 %collective-permute-done.9 = bf16[128,4096]{1,0:T(8,128)(2,1)S(1)} collective-permute-done((bf16[128,4096]{1,0:T(8,128)(2,1)S(1)}, bf16[128,4096]{1,0:T(8,128)(2,1)S(1)}, u32[]{:S(2)}, u32[]{:S(2)}) %collective-permute-start.9) | collective-permute-done | bytes 1048608 | tf_op jit(solution)/shard_map/ppermute | solution.py:134
  160.3 2.0 %add_convert_fusion = bf16[128,4096]{1,0:T(8,128)(2,1)} fusion(bf16[128,4096]{1,0:T(8,128)(2,1)S(1)} %collective-permute-done.9, bf16[704,4096]{1,0:T(8,128)(2,1)S(1)} %bitcast.38, bf16[512,704]{0,1:T(8,128)(2,1)S(1)} %select_convert_fusion), kind=kOutput, calls=%fused_computation.23 | convolution fusion | flops 739770368 | bytes 8044544 | tf_op jit(solution)/shard_map/dot_general | solution.py:131
  162.3 0.5 fusion.32
  162.8 2.4 %fusion.39 = f32[128,4096]{1,0:T(8,128)} fusion(bf16[128,704]{0,1:T(8,128)(2,1)S(1)} %add_convert_fusion.1, bf16[704,4096]{1,0:T(8,128)(2,1)S(1)} %bitcast.38), kind=kOutput, calls=%fused_computation.99 | convolution fusion | flops 738197504 | bytes 8044544 | tf_op jit(solution)/shard_map/dot_general | solution.py:139
  165.2 2.0 %collective-permute-done.11 = bf16[128,4096]{1,0:T(8,128)(2,1)S(1)} collective-permute-done((bf16[128,4096]{1,0:T(8,128)(2,1)S(1)}, bf16[128,4096]{1,0:T(8,128)(2,1)S(1)}, u32[]{:S(2)}, u32[]{:S(2)}) %collective-permute-start.11) | collective-permute-done | bytes 1048608 | tf_op jit(solution)/shard_map/ppermute | solution.py:134
  167.2 1.5 convert_element_type.69
  168.7 4.4 %reduce-scatter.2.cloned.1.call-done = bf16[88,4096]{1,0:T(8,128)(2,1)} async-done(((bf16[704,4096]{1,0:T(8,128)(2,1)}), bf16[88,4096]{1,0:T(8,128)(2,1)}) %reduce-scatter.2.cloned.1.call-update) | async-done | bytes 720912 | tf_op jit(solution)/shard_map/reduce_scatter | solution.py:152
  173.1 2.5 %convert_element_type.71 = f32[88,4096]{1,0:T(8,128)} convert(bf16[88,4096]{1,0:T(8,128)(2,1)} %reduce-scatter.2.cloned.1.call-done) | non-fusion elementwise | flops 360448 | bytes 2162688 | tf_op jit(solution)/shard_map/convert_element_type | solution.py:154
  175.6 8.1 %collective-permute-done.10 = bf16[128,4096]{1,0:T(8,128)(2,1)S(1)} collective-permute-done((bf16[128,4096]{1,0:T(8,128)(2,1)}, bf16[128,4096]{1,0:T(8,128)(2,1)S(1)}, u32[]{:S(2)}, u32[]{:S(2)}) %collective-permute-start.10) | collective-permute-done | bytes 1048608 | tf_op jit(solution)/shard_map/ppermute | solution.py:134
  183.7 1.7 add_add_fusion
  (43 shorter events, 0.3 us)
Async XLA Ops:
  7.2 61.4 %copy-start.8 = (bf16[128,4096]{1,0:T(8,128)(2,1)S(1)}, bf16[128,4096]{1,0:T(8,128)(2,1)}, u32[]{:S(2)}) copy-start(bf16[128,4096]{1,0:T(8,128)(2,1)} %param.4) | copy-start | bytes 3145732
  7.2 61.3 %all-gather.2.cloned.1.call-start = ((), (), s32[]{:S(2)}) async-start(), calls=%async_computation.1 | async-start | bytes 6488064 | tf_op jit(solution)/shard_map/all_gather | solution.py:19
  7.9 165.2 %reduce-scatter.2.cloned.1.call-start = ((), (), s32[]{:S(2)}) async-start(), calls=%async_computation.2 | async-start | bytes 6488064 | tf_op jit(solution)/shard_map/reduce_scatter | solution.py:152
  8.0 9.6 %collective-permute-start = (s32[128,8]{0,1:T(8,128)}, s32[128,8]{0,1:T(8,128)S(1)}, u32[]{:S(2)}, u32[]{:S(2)}) collective-permute-start(s32[128,8]{0,1:T(8,128)} %param.7), channel_id=1, source_target_pairs={{0,3},{1,0},{2,1},{3,2},{4,7},{5,4},{6,5},{7,6},{8,11},{9,8},{10,9... | collective-permute-start | bytes 12296 | tf_op jit(solution)/shard_map/ppermute | solution.py:31
  13.1 48.6 %collective-permute-start.2 = (s32[128,8]{0,1:T(8,128)}, s32[128,8]{0,1:T(8,128)S(1)}, u32[]{:S(2)}, u32[]{:S(2)}) collective-permute-start(s32[128,8]{0,1:T(8,128)} %param.7), channel_id=1, source_target_pairs={{0,1},{1,2},{2,3},{3,0},{4,5},{5,6},{6,7},{7,4},{8,9},{9,10},{10,1... | collective-permute-start | bytes 12296 | tf_op jit(solution)/shard_map/ppermute | solution.py:35
  13.1 49.9 %collective-permute-start.3 = (bf16[128,4096]{1,0:T(8,128)(2,1)}, bf16[128,4096]{1,0:T(8,128)(2,1)}, u32[]{:S(2)}, u32[]{:S(2)}) collective-permute-start(bf16[128,4096]{1,0:T(8,128)(2,1)} %param.4), channel_id=1, source_target_pairs={{0,3},{1,0},{2,1},{3,2},{4,7},{5,4},{6,5},{7,6},{8,11},{9,8},{10,9... | collective-permute-start | bytes 3145736 | tf_op jit(solution)/shard_map/ppermute | solution.py:31
  16.9 74.3 %collective-permute-start.5 = (bf16[128,4096]{1,0:T(8,128)(2,1)}, bf16[128,4096]{1,0:T(8,128)(2,1)}, u32[]{:S(2)}, u32[]{:S(2)}) collective-permute-start(bf16[128,4096]{1,0:T(8,128)(2,1)} %param.4), channel_id=1, source_target_pairs={{0,1},{1,2},{2,3},{3,0},{4,5},{5,6},{6,7},{7,4},{8,9},{9,10},{10,1... | collective-permute-start | bytes 3145736 | tf_op jit(solution)/shard_map/ppermute | solution.py:35
  17.6 44.0 %collective-permute-start.1 = (s32[128,8]{0,1:T(8,128)S(1)}, s32[128,8]{0,1:T(8,128)S(1)}, u32[]{:S(2)}, u32[]{:S(2)}) collective-permute-start(s32[128,8]{0,1:T(8,128)S(1)} %collective-permute-done), channel_id=1, source_target_pairs={{0,3},{1,0},{2,1},{3,2},{4,7},{5,4},{6,5},{7,6},{8,11},{9,8},{10,9... | collective-permute-start | bytes 12296 | tf_op jit(solution)/shard_map/ppermute | solution.py:31
  63.0 25.3 %collective-permute-start.4 = (bf16[128,4096]{1,0:T(8,128)(2,1)}, bf16[128,4096]{1,0:T(8,128)(2,1)}, u32[]{:S(2)}, u32[]{:S(2)}) collective-permute-start(bf16[128,4096]{1,0:T(8,128)(2,1)} %collective-permute-done.3), channel_id=1, source_target_pairs={{0,3},{1,0},{2,1},{3,2},{4,7},{5,4},{6,5},{7,6},{8,11},{9,8},{10,9... | collective-permute-start | bytes 3145736 | tf_op jit(solution)/shard_map/ppermute | solution.py:31
  68.5 26.5 %copy-start.3 = (f32[128,704]{0,1:T(8,128)}, f32[128,704]{0,1:T(8,128)S(1)}, u32[]{:S(2)}) copy-start(f32[128,704]{0,1:T(8,128)S(1)} %get-tuple-element.26) | copy-start | bytes 1081348
  68.5 4.5 %copy-start = (bf16[704,4096]{1,0:T(8,128)(2,1)S(1)}, bf16[704,4096]{1,0:T(8,128)(2,1)}, u32[]{:S(2)}) copy-start(bf16[704,4096]{1,0:T(8,128)(2,1)} %all-gather.2.cloned.1.call-done) | copy-start | bytes 17301508
  73.0 21.2 %copy-start.4 = (f32[128,704]{0,1:T(8,128)}, f32[128,704]{0,1:T(8,128)S(1)}, u32[]{:S(2)}) copy-start(f32[128,704]{0,1:T(8,128)S(1)} %fusion.35) | copy-start | bytes 1081348
  76.0 18.2 %copy-start.5 = (f32[128,704]{0,1:T(8,128)}, f32[128,704]{0,1:T(8,128)S(1)}, u32[]{:S(2)}) copy-start(f32[128,704]{0,1:T(8,128)S(1)} %fusion.36) | copy-start | bytes 1081348
  91.1 3.1 %copy-start.6 = (f32[128,704]{0,1:T(8,128)}, f32[128,704]{0,1:T(8,128)S(1)}, u32[]{:S(2)}) copy-start(f32[128,704]{0,1:T(8,128)S(1)} %fusion.37) | copy-start | bytes 1081348
  94.2 0.7 copy-start.7
  94.3 0.7 copy-start.10
  95.6 6.0 %collective-permute-start.8 = (f32[1280]{0:T(1024)S(1)}, f32[1280]{0:T(1024)S(1)}, u32[]{:S(2)}, u32[]{:S(2)}) collective-permute-start(f32[1280]{0:T(1024)S(1)} %pad_maximum_fusion.1), channel_id=1, source_target_pairs={{0,1},{1,2},{2,3},{3,0},{4,5},{5,6},{6,7},{7,4},{8,9},{9,10},{10,1... | collective-permute-start | bytes 15368 | tf_op jit(solution)/shard_map/ppermute | solution.py:102
  95.7 6.5 %collective-permute-start.7 = (f32[1280]{0:T(1024)S(1)}, f32[1280]{0:T(1024)S(1)}, u32[]{:S(2)}, u32[]{:S(2)}) collective-permute-start(f32[1280]{0:T(1024)S(1)} %pad_maximum_fusion.1), channel_id=1, source_target_pairs={{0,2},{1,3},{2,0},{3,1},{4,6},{5,7},{6,4},{7,5},{8,10},{9,11},{10,... | collective-permute-start | bytes 15368 | tf_op jit(solution)/shard_map/ppermute | solution.py:102
  100.5 3.7 %collective-permute-start.6 = (f32[1280]{0:T(1024)S(1)}, f32[1280]{0:T(1024)S(1)}, u32[]{:S(2)}, u32[]{:S(2)}) collective-permute-start(f32[1280]{0:T(1024)S(1)} %pad_maximum_fusion.1), channel_id=1, source_target_pairs={{0,3},{1,0},{2,1},{3,2},{4,7},{5,4},{6,5},{7,6},{8,11},{9,8},{10,9... | collective-permute-start | bytes 15368 | tf_op jit(solution)/shard_map/ppermute | solution.py:102
  104.6 2.1 %copy-start.9 = (bf16[128,4096]{1,0:T(8,128)(2,1)S(1)}, bf16[128,4096]{1,0:T(8,128)(2,1)}, u32[]{:S(2)}) copy-start(bf16[128,4096]{1,0:T(8,128)(2,1)} %param.4) | copy-start | bytes 3145732
  114.3 5.8 %slice-start = ((s8[5767168]{0:T(1024)(128)(4,1)}), s8[1572864]{0:T(1024)(128)(4,1)S(1)}, s32[]{:S(2)}) async-start(s8[5767168]{0:T(1024)(128)(4,1)} %bitcast.37), calls=%async_computation.3 | async-start | bytes 3145728
  114.3 5.8 %slice-start.1 = ((s8[5767168]{0:T(1024)(128)(4,1)}), s8[4194304]{0:T(1024)(128)(4,1)S(1)}, s32[]{:S(2)}) async-start(s8[5767168]{0:T(1024)(128)(4,1)} %bitcast.37), calls=%async_computation.4 | async-start | bytes 8388608
  118.1 42.2 %collective-permute-start.9 = (bf16[128,4096]{1,0:T(8,128)(2,1)S(1)}, bf16[128,4096]{1,0:T(8,128)(2,1)S(1)}, u32[]{:S(2)}, u32[]{:S(2)}) collective-permute-start(bf16[128,4096]{1,0:T(8,128)(2,1)S(1)} %convolution_convert_fusion.2), channel_id=1, source_target_pairs={{0,3},{1,0},{2,1},{3,2},{4,7},{5,4},{6,5},{7,6},{8,11},{9,8},{10,9... | collective-permute-start | bytes 3145736 | tf_op jit(solution)/shard_map/ppermute | solution.py:134
  121.1 46.1 %collective-permute-start.11 = (bf16[128,4096]{1,0:T(8,128)(2,1)S(1)}, bf16[128,4096]{1,0:T(8,128)(2,1)S(1)}, u32[]{:S(2)}, u32[]{:S(2)}) collective-permute-start(bf16[128,4096]{1,0:T(8,128)(2,1)S(1)} %convolution_convert_fusion.1), channel_id=1, source_target_pairs={{0,1},{1,2},{2,3},{3,0},{4,5},{5,6},{6,7},{7,4},{8,9},{9,10},{10,1... | collective-permute-start | bytes 3145736 | tf_op jit(solution)/shard_map/ppermute | solution.py:134
  162.3 21.3 %collective-permute-start.10 = (bf16[128,4096]{1,0:T(8,128)(2,1)}, bf16[128,4096]{1,0:T(8,128)(2,1)S(1)}, u32[]{:S(2)}, u32[]{:S(2)}) collective-permute-start(bf16[128,4096]{1,0:T(8,128)(2,1)} %add_convert_fusion), channel_id=1, source_target_pairs={{0,3},{1,0},{2,1},{3,2},{4,7},{5,4},{6,5},{7,6},{8,11},{9,8},{10,9... | collective-permute-start | bytes 3145736 | tf_op jit(solution)/shard_map/ppermute | solution.py:134
  165.2 18.5 %copy-start.1 = (f32[128,4096]{1,0:T(8,128)S(1)}, f32[128,4096]{1,0:T(8,128)}, u32[]{:S(2)}) copy-start(f32[128,4096]{1,0:T(8,128)} %fusion.39) | copy-start | bytes 6291460
  173.1 10.6 %copy-start.2 = (f32[128,4096]{1,0:T(8,128)S(1)}, f32[128,4096]{1,0:T(8,128)}, u32[]{:S(2)}) copy-start(f32[128,4096]{1,0:T(8,128)} %convert_element_type.69) | copy-start | bytes 6291460
Sparse Core Ops, SparseCore 0:
  9.9 46.0 all-gather.1
  114.5 58.6 reduce-scatter.1

commit v16 on v14

--- a/solution.py
+++ b/solution.py
@@ -24,20 +24,24 @@
     steps_down = slabs // 2
     steps_up = slabs - 1 - steps_down
 
-    def ring_gather(x):
+    def ring_gather(x, gates=None):
         blocks = [x] * slabs
         current = x
         for step in range(1, steps_down + 1):
+            if gates is not None:
+                current, _ = lax.optimization_barrier((current, gates[step]))
             current = lax.ppermute(current, "slab", ring_down)
             blocks[step] = current
         current = x
         for step in range(1, steps_up + 1):
+            if gates is not None:
+                current, _ = lax.optimization_barrier((current, gates[slabs - step]))
             current = lax.ppermute(current, "slab", ring_up)
             blocks[slabs - step] = current
         return blocks
 
-    query_blocks = ring_gather(queries)
     id_blocks = ring_gather(hard_ids)
+    query_blocks = ring_gather(queries, id_blocks)
 
     def to_origin(x):
         doubled = jnp.concatenate([x, x], axis=0)

time: 190 us -> 193 us (1.016)
  waiting for transfers between devices: 108 us -> 115 us
  starting transfers between devices: 22.8 us -> 18.6 us
    ppermute x4, waiting for transfers between devices: 50 us -> 54.4 us  [ring_gather(): current = lax.ppermute(current, 'slab', ring_down)]
    ppermute x2, waiting for transfers between devices: 0.01 us -> 4.08 us  [ring_gather(): current = lax.ppermute(current, 'slab', ring_up)]
    ppermute x4, starting transfers between devices: 14.1 us -> 11.1 us  [ring_gather(): current = lax.ppermute(current, 'slab', ring_down)]
  transfers between devices with their start and end apart: 14 -> 14, of which waited for: 10 -> 11; matrix products, arithmetic and copies ran while one was open for 14% -> 14% of each run, Pallas kernels for 0% -> 0%
where the time goes in v16:
time: 193 us; the launch traced here: 192 us
  waiting for transfers between devices  115 us (60%)
  matrix products  29.9 us (15%)
  starting transfers between devices  18.6 us (10%)
  between operations  14.3 us (7%)
  other arithmetic  12.8 us (7%)
  local copies, waits for them, and re-layouts  1.94 us (1%)
    ppermute x4, waiting for transfers between devices, ring_gather(): current = lax.ppermute(current, 'slab', ring_down)  54.4 us
    ppermute x3, waiting for transfers between devices, hop(): lax.ppermute(part.astype(jnp.bfloat16), 'slab', perm).astype(jnp.float32)  47.8 us
    dot_general x4, matrix products, per_device(): lax.dot_general(block, pool, contract_rows, preferred_element_type=jnp.fl...  13.1 us
    ppermute x4, starting transfers between devices, ring_gather(): current = lax.ppermute(current, 'slab', ring_down)  11.1 us
    dot_general x1, matrix products, per_device(): lax.dot_general(jnp.concatenate([own_coef, hard_matrix[query_rows_dev:]],...  7.59 us
    dot_general x3, matrix products, grad_for(): return jnp.dot(rows, pool, preferred_element_type=jnp.float32)  6.84 us
    reduce_scatter x1, waiting for transfers between devices, per_device(): lax.psum_scatter(partial.astype(jnp.bfloat16), 'blk', scatter_dimension=0...  4.87 us
    ppermute x3, starting transfers between devices, per_device(): lax.ppermute(payload, 'slab', [(i, (i - t) % slabs) for i in range(slabs)])  4.82 us
  transfers between devices with their start and end apart: 14, of which 11 were waited for; matrix products, arithmetic and copies ran while one was open for 14% of the time, Pallas kernels for 0%

profile of v16, /device:TPU:0, one launch (start us, length us, event | category | flops | bytes accessed | tf_op | source)
XLA Modules:
  0.0 192.3 jit_solution(10486634707144138910)
XLA Ops:
  7.2 0.0 copy-start.5
  7.2 0.0 all-gather.2.cloned.1.call-start
  7.2 0.7 all-gather.2.cloned.1.call-update
  7.9 0.0 reduce-scatter.2.cloned.1.call-start
  8.0 5.1 %collective-permute-start = (s32[128,8]{0,1:T(8,128)}, s32[128,8]{0,1:T(8,128)S(1)}, u32[]{:S(2)}, u32[]{:S(2)}) collective-permute-start(s32[128,8]{0,1:T(8,128)} %param.7), channel_id=1, source_target_pairs={{0,3},{1,0},{2,1},{3,2},{4,7},{5,4},{6,5},{7,6},{8,11},{9,8},{10,9... | collective-permute-start | bytes 12296 | tf_op jit(solution)/shard_map/ppermute | solution.py:33
  13.1 0.0 collective-permute-start.2
  13.1 0.8 constant_dynamic-update-slice_fusion.3
  13.8 0.8 collective-permute-done
  14.6 4.1 %collective-permute-done.2 = s32[128,8]{0,1:T(8,128)S(1)} collective-permute-done((s32[128,8]{0,1:T(8,128)}, s32[128,8]{0,1:T(8,128)S(1)}, u32[]{:S(2)}, u32[]{:S(2)}) %collective-permute-start.2) | collective-permute-done | bytes 4128 | tf_op jit(solution)/shard_map/ppermute | solution.py:39
  18.7 0.0 collective-permute-start.5
  18.7 3.8 %collective-permute-start.3 = (bf16[128,4096]{1,0:T(8,128)(2,1)}, bf16[128,4096]{1,0:T(8,128)(2,1)}, u32[]{:S(2)}, u32[]{:S(2)}) collective-permute-start(bf16[128,4096]{1,0:T(8,128)(2,1)} %param.4), channel_id=1, source_target_pairs={{0,3},{1,0},{2,1},{3,2},{4,7},{5,4},{6,5},{7,6},{8,11},{9,8},{10,9... | collective-permute-start | bytes 3145736 | tf_op jit(solution)/shard_map/ppermute | solution.py:33
  22.5 0.0 collective-permute-start.1
  22.5 42.4 %collective-permute-done.1 = s32[128,8]{0,1:T(8,128)S(1)} collective-permute-done((s32[128,8]{0,1:T(8,128)S(1)}, s32[128,8]{0,1:T(8,128)S(1)}, u32[]{:S(2)}, u32[]{:S(2)}) %collective-permute-start.1) | collective-permute-done | bytes 4128 | tf_op jit(solution)/shard_map/ppermute | solution.py:33
  65.1 2.6 %convert_reduce_fusion = f32[512,704]{0,1:T(8,128)S(1)} fusion(s32[512,8]{0,1:T(8,128)S(1)} %fusion.18, pred[512,8]{0,1:T(8,128)(4,1)S(1)} %fusion.19), kind=kLoop, calls=%fused_computation | loop fusion | flops 11173888 | bytes 1462272 | tf_op jit(solution)/shard_map/reduce_sum | solution.py:70
  67.7 0.0 collective-permute-done.3
  67.7 2.1 %collective-permute-start.4 = (bf16[128,4096]{1,0:T(8,128)(2,1)}, bf16[128,4096]{1,0:T(8,128)(2,1)}, u32[]{:S(2)}, u32[]{:S(2)}) collective-permute-start(bf16[128,4096]{1,0:T(8,128)(2,1)} %collective-permute-done.3), channel_id=1, source_target_pairs={{0,3},{1,0},{2,1},{3,2},{4,7},{5,4},{6,5},{7,6},{8,11},{9,8},{10,9... | collective-permute-start | bytes 3145736 | tf_op jit(solution)/shard_map/ppermute | solution.py:33
  69.8 0.0 copy-done.5
  69.8 4.4 %fusion.30 = f32[128,704]{0,1:T(8,128)S(1)} fusion(bf16[128,4096]{1,0:T(8,128)(2,1)S(1)} %copy-done.5, bf16[704,4096]{1,0:T(8,128)(2,1)} %all-gather.2.cloned.1.call-done), kind=kOutput, calls=%fused_computation.72 | convolution fusion | flops 738197504 | bytes 7176192 | tf_op jit(solution)/shard_map/dot_general | solution.py:56
  74.3 0.0 copy-done
  74.3 2.9 %fusion.31 = f32[128,704]{0,1:T(8,128)S(1)} fusion(bf16[128,4096]{1,0:T(8,128)(2,1)} %collective-permute-done.3, bf16[704,4096]{1,0:T(8,128)(2,1)S(1)} %copy-done), kind=kOutput, calls=%fused_computation.73 | convolution fusion | flops 738197504 | bytes 7176192 | tf_op jit(solution)/shard_map/dot_general | solution.py:56
  77.2 0.0 collective-permute-done.5
  77.2 2.9 %fusion.33 = f32[128,704]{0,1:T(8,128)S(1)} fusion(bf16[128,4096]{1,0:T(8,128)(2,1)} %collective-permute-done.5, bf16[704,4096]{1,0:T(8,128)(2,1)S(1)} %copy-done), kind=kOutput, calls=%fused_computation.75 | convolution fusion | flops 738197504 | bytes 7176192 | tf_op jit(solution)/shard_map/dot_general | solution.py:56
  80.1 11.2 %collective-permute-done.4 = bf16[128,4096]{1,0:T(8,128)(2,1)} collective-permute-done((bf16[128,4096]{1,0:T(8,128)(2,1)}, bf16[128,4096]{1,0:T(8,128)(2,1)}, u32[]{:S(2)}, u32[]{:S(2)}) %collective-permute-start.4) | collective-permute-done | bytes 1048608 | tf_op jit(solution)/shard_map/ppermute | solution.py:33
  91.3 2.9 %fusion.32 = f32[128,704]{0,1:T(8,128)S(1)} fusion(bf16[128,4096]{1,0:T(8,128)(2,1)} %collective-permute-done.4, bf16[704,4096]{1,0:T(8,128)(2,1)S(1)} %copy-done), kind=kOutput, calls=%fused_computation.74 | convolution fusion | flops 738197504 | bytes 7176192 | tf_op jit(solution)/shard_map/dot_general | solution.py:56
  94.2 0.0 copy-start.3
  94.2 0.3 select_reduce_fusion.1
  94.5 0.4 select_reduce_fusion
  94.9 0.0 copy-done.3
  94.9 0.0 copy-start.4
  94.9 0.1 slice_reduce_fusion
  95.1 1.0 copy-done.4
  96.0 0.1 exponential_reduce_fusion
  96.2 0.7 collective-permute-start.8
  96.9 3.4 %collective-permute-start.7 = (f32[1280]{0:T(1024)S(1)}, f32[1280]{0:T(1024)S(1)}, u32[]{:S(2)}, u32[]{:S(2)}) collective-permute-start(f32[1280]{0:T(1024)S(1)} %pad_maximum_fusion), channel_id=1, source_target_pairs={{0,2},{1,3},{2,0},{3,1},{4,6},{5,7},{6,4},{7,5},{8,10},{9,11},{10,... | collective-permute-start | bytes 15368 | tf_op jit(solution)/shard_map/ppermute | solution.py:94
  100.3 0.7 collective-permute-start.6
  101.0 0.7 collective-permute-done.8
  101.7 0.3 collective-permute-done.7
  102.0 2.0 %collective-permute-done.6 = f32[1280]{0:T(1024)S(1)} collective-permute-done((f32[1280]{0:T(1024)S(1)}, f32[1280]{0:T(1024)S(1)}, u32[]{:S(2)}, u32[]{:S(2)}) %collective-permute-start.6) | collective-permute-done | bytes 5152 | tf_op jit(solution)/shard_map/ppermute | solution.py:94
  104.0 0.1 concatenate.50
  104.1 0.1 fusion.27
  104.2 0.1 fusion.23
  104.3 0.1 fusion.26
  104.4 0.0 copy-start.6
  104.4 1.4 select_convert_fusion
  105.8 0.1 slice.53
  105.9 1.1 add_convert_fusion.1
  107.0 7.6 %convolution_convert_fusion = bf16[704,4096]{1,0:T(8,128)(2,1)} fusion(bf16[128,4096]{1,0:T(8,128)(2,1)} %collective-permute-done.5, bf16[128,4096]{1,0:T(8,128)(2,1)} %collective-permute-done.4, bf16[128,4096]{1,0:T(8,128)(2,1)} %collective-permute-done.3, bf16[128,4096]{1,0:T(8,128)(2,1)S(1)} %copy-done.6, bf16[384,704]{0,1:T(8,128)(2,1)S(1)} %slice.53, ...), kind=kOutput, calls=%fused_computation.3 | convolution fusion | flops 2973892608 | bytes 10682368 | tf_op jit(solution)/shard_map/dot_general | solution.py:138
  114.6 0.0 reduce-scatter.2.cloned.1.call-update
  114.7 0.0 slice-start.1
  114.7 3.8 %convolution_convert_fusion.2 = bf16[128,4096]{1,0:T(8,128)(2,1)S(1)} fusion(bf16[704,4096]{1,0:T(8,128)(2,1)} %all-gather.2.cloned.1.call-done, bf16[512,704]{0,1:T(8,128)(2,1)S(1)} %select_convert_fusion), kind=kOutput, calls=%fused_computation.5 | convolution fusion | flops 738721792 | bytes 6995968 | tf_op jit(solution)/shard_map/dot_general | solution.py:123
  118.5 2.5 %collective-permute-start.9 = (bf16[128,4096]{1,0:T(8,128)(2,1)S(1)}, bf16[128,4096]{1,0:T(8,128)(2,1)S(1)}, u32[]{:S(2)}, u32[]{:S(2)}) collective-permute-start(bf16[128,4096]{1,0:T(8,128)(2,1)S(1)} %convolution_convert_fusion.2), channel_id=1, source_target_pairs={{0,3},{1,0},{2,1},{3,2},{4,7},{5,4},{6,5},{7,6},{8,11},{9,8},{10,9... | collective-permute-start | bytes 3145736 | tf_op jit(solution)/shard_map/ppermute | solution.py:126
  121.0 1.0 convolution_convert_fusion.1
  122.0 0.1 collective-permute-start.11
  122.1 38.6 %collective-permute-done.9 = bf16[128,4096]{1,0:T(8,128)(2,1)S(1)} collective-permute-done((bf16[128,4096]{1,0:T(8,128)(2,1)S(1)}, bf16[128,4096]{1,0:T(8,128)(2,1)S(1)}, u32[]{:S(2)}, u32[]{:S(2)}) %collective-permute-start.9) | collective-permute-done | bytes 1048608 | tf_op jit(solution)/shard_map/ppermute | solution.py:126
  160.7 2.0 %add_convert_fusion = bf16[128,4096]{1,0:T(8,128)(2,1)} fusion(bf16[128,4096]{1,0:T(8,128)(2,1)S(1)} %collective-permute-done.9, bf16[704,4096]{1,0:T(8,128)(2,1)S(1)} %bitcast.36, bf16[512,704]{0,1:T(8,128)(2,1)S(1)} %select_convert_fusion), kind=kOutput, calls=%fused_computation.14 | convolution fusion | flops 739770368 | bytes 8044544 | tf_op jit(solution)/shard_map/dot_general | solution.py:123
  162.7 0.0 collective-permute-start.10
  162.7 0.5 fusion.29
  163.2 2.4 %fusion.34 = f32[128,4096]{1,0:T(8,128)} fusion(bf16[128,704]{0,1:T(8,128)(2,1)S(1)} %add_convert_fusion.1, bf16[704,4096]{1,0:T(8,128)(2,1)S(1)} %bitcast.36), kind=kOutput, calls=%fused_computation.76 | convolution fusion | flops 738197504 | bytes 8044544 | tf_op jit(solution)/shard_map/dot_general | solution.py:131
  165.6 2.0 %collective-permute-done.11 = bf16[128,4096]{1,0:T(8,128)(2,1)S(1)} collective-permute-done((bf16[128,4096]{1,0:T(8,128)(2,1)S(1)}, bf16[128,4096]{1,0:T(8,128)(2,1)S(1)}, u32[]{:S(2)}, u32[]{:S(2)}) %collective-permute-start.11) | collective-permute-done | bytes 1048608 | tf_op jit(solution)/shard_map/ppermute | solution.py:126
  167.6 1.5 convert_element_type.57
  169.1 4.9 %reduce-scatter.2.cloned.1.call-done = bf16[88,4096]{1,0:T(8,128)(2,1)} async-done(((bf16[704,4096]{1,0:T(8,128)(2,1)}), bf16[88,4096]{1,0:T(8,128)(2,1)}) %reduce-scatter.2.cloned.1.call-update) | async-done | bytes 720912 | tf_op jit(solution)/shard_map/reduce_scatter | solution.py:144
  174.0 2.5 %convert_element_type.59 = f32[88,4096]{1,0:T(8,128)} convert(bf16[88,4096]{1,0:T(8,128)(2,1)} %reduce-scatter.2.cloned.1.call-done) | non-fusion elementwise | flops 360448 | bytes 2162688 | tf_op jit(solution)/shard_map/convert_element_type | solution.py:146
  176.5 7.2 %collective-permute-done.10 = bf16[128,4096]{1,0:T(8,128)(2,1)S(1)} collective-permute-done((bf16[128,4096]{1,0:T(8,128)(2,1)}, bf16[128,4096]{1,0:T(8,128)(2,1)S(1)}, u32[]{:S(2)}, u32[]{:S(2)}) %collective-permute-start.10) | collective-permute-done | bytes 1048608 | tf_op jit(solution)/shard_map/ppermute | solution.py:126
  183.7 1.7 add_add_fusion
  (31 shorter events, 0.2 us)
Async XLA Ops:
  7.2 62.7 %copy-start.5 = (bf16[128,4096]{1,0:T(8,128)(2,1)S(1)}, bf16[128,4096]{1,0:T(8,128)(2,1)}, u32[]{:S(2)}) copy-start(bf16[128,4096]{1,0:T(8,128)(2,1)} %param.4) | copy-start | bytes 3145732
  7.2 62.7 %all-gather.2.cloned.1.call-start = ((), (), s32[]{:S(2)}) async-start(), calls=%async_computation.1 | async-start | bytes 6488064 | tf_op jit(solution)/shard_map/all_gather | solution.py:19
  7.9 166.1 %reduce-scatter.2.cloned.1.call-start = ((), (), s32[]{:S(2)}) async-start(), calls=%async_computation.2 | async-start | bytes 6488064 | tf_op jit(solution)/shard_map/reduce_scatter | solution.py:144
  8.0 6.6 %collective-permute-start = (s32[128,8]{0,1:T(8,128)}, s32[128,8]{0,1:T(8,128)S(1)}, u32[]{:S(2)}, u32[]{:S(2)}) collective-permute-start(s32[128,8]{0,1:T(8,128)} %param.7), channel_id=1, source_target_pairs={{0,3},{1,0},{2,1},{3,2},{4,7},{5,4},{6,5},{7,6},{8,11},{9,8},{10,9... | collective-permute-start | bytes 12296 | tf_op jit(solution)/shard_map/ppermute | solution.py:33
  13.1 5.6 %collective-permute-start.2 = (s32[128,8]{0,1:T(8,128)}, s32[128,8]{0,1:T(8,128)S(1)}, u32[]{:S(2)}, u32[]{:S(2)}) collective-permute-start(s32[128,8]{0,1:T(8,128)} %param.7), channel_id=1, source_target_pairs={{0,1},{1,2},{2,3},{3,0},{4,5},{5,6},{6,7},{7,4},{8,9},{9,10},{10,1... | collective-permute-start | bytes 12296 | tf_op jit(solution)/shard_map/ppermute | solution.py:39
  18.7 58.5 %collective-permute-start.5 = (bf16[128,4096]{1,0:T(8,128)(2,1)}, bf16[128,4096]{1,0:T(8,128)(2,1)}, u32[]{:S(2)}, u32[]{:S(2)}) collective-permute-start(bf16[128,4096]{1,0:T(8,128)(2,1)} %param.4), channel_id=1, source_target_pairs={{0,1},{1,2},{2,3},{3,0},{4,5},{5,6},{6,7},{7,4},{8,9},{9,10},{10,1... | collective-permute-start | bytes 3145736 | tf_op jit(solution)/shard_map/ppermute | solution.py:39
  18.7 49.0 %collective-permute-start.3 = (bf16[128,4096]{1,0:T(8,128)(2,1)}, bf16[128,4096]{1,0:T(8,128)(2,1)}, u32[]{:S(2)}, u32[]{:S(2)}) collective-permute-start(bf16[128,4096]{1,0:T(8,128)(2,1)} %param.4), channel_id=1, source_target_pairs={{0,3},{1,0},{2,1},{3,2},{4,7},{5,4},{6,5},{7,6},{8,11},{9,8},{10,9... | collective-permute-start | bytes 3145736 | tf_op jit(solution)/shard_map/ppermute | solution.py:33
  22.5 42.5 %collective-permute-start.1 = (s32[128,8]{0,1:T(8,128)S(1)}, s32[128,8]{0,1:T(8,128)S(1)}, u32[]{:S(2)}, u32[]{:S(2)}) collective-permute-start(s32[128,8]{0,1:T(8,128)S(1)} %collective-permute-done), channel_id=1, source_target_pairs={{0,3},{1,0},{2,1},{3,2},{4,7},{5,4},{6,5},{7,6},{8,11},{9,8},{10,9... | collective-permute-start | bytes 12296 | tf_op jit(solution)/shard_map/ppermute | solution.py:33
  67.7 23.6 %collective-permute-start.4 = (bf16[128,4096]{1,0:T(8,128)(2,1)}, bf16[128,4096]{1,0:T(8,128)(2,1)}, u32[]{:S(2)}, u32[]{:S(2)}) collective-permute-start(bf16[128,4096]{1,0:T(8,128)(2,1)} %collective-permute-done.3), channel_id=1, source_target_pairs={{0,3},{1,0},{2,1},{3,2},{4,7},{5,4},{6,5},{7,6},{8,11},{9,8},{10,9... | collective-permute-start | bytes 3145736 | tf_op jit(solution)/shard_map/ppermute | solution.py:33
  69.8 4.5 %copy-start = (bf16[704,4096]{1,0:T(8,128)(2,1)S(1)}, bf16[704,4096]{1,0:T(8,128)(2,1)}, u32[]{:S(2)}) copy-start(bf16[704,4096]{1,0:T(8,128)(2,1)} %all-gather.2.cloned.1.call-done) | copy-start | bytes 17301508
  94.2 0.7 copy-start.3
  94.5 1.5 copy-start.7
  94.9 1.1 copy-start.4
  96.2 5.5 %collective-permute-start.8 = (f32[1280]{0:T(1024)S(1)}, f32[1280]{0:T(1024)S(1)}, u32[]{:S(2)}, u32[]{:S(2)}) collective-permute-start(f32[1280]{0:T(1024)S(1)} %pad_maximum_fusion), channel_id=1, source_target_pairs={{0,1},{1,2},{2,3},{3,0},{4,5},{5,6},{6,7},{7,4},{8,9},{9,10},{10,1... | collective-permute-start | bytes 15368 | tf_op jit(solution)/shard_map/ppermute | solution.py:94
  96.9 5.1 %collective-permute-start.7 = (f32[1280]{0:T(1024)S(1)}, f32[1280]{0:T(1024)S(1)}, u32[]{:S(2)}, u32[]{:S(2)}) collective-permute-start(f32[1280]{0:T(1024)S(1)} %pad_maximum_fusion), channel_id=1, source_target_pairs={{0,2},{1,3},{2,0},{3,1},{4,6},{5,7},{6,4},{7,5},{8,10},{9,11},{10,... | collective-permute-start | bytes 15368 | tf_op jit(solution)/shard_map/ppermute | solution.py:94
  100.3 3.7 %collective-permute-start.6 = (f32[1280]{0:T(1024)S(1)}, f32[1280]{0:T(1024)S(1)}, u32[]{:S(2)}, u32[]{:S(2)}) collective-permute-start(f32[1280]{0:T(1024)S(1)} %pad_maximum_fusion), channel_id=1, source_target_pairs={{0,3},{1,0},{2,1},{3,2},{4,7},{5,4},{6,5},{7,6},{8,11},{9,8},{10,9... | collective-permute-start | bytes 15368 | tf_op jit(solution)/shard_map/ppermute | solution.py:94
  104.4 2.6 %copy-start.6 = (bf16[128,4096]{1,0:T(8,128)(2,1)S(1)}, bf16[128,4096]{1,0:T(8,128)(2,1)}, u32[]{:S(2)}) copy-start(bf16[128,4096]{1,0:T(8,128)(2,1)} %param.4) | copy-start | bytes 3145732
  114.6 6.4 %slice-start = ((s8[5767168]{0:T(1024)(128)(4,1)}), s8[1572864]{0:T(1024)(128)(4,1)S(1)}, s32[]{:S(2)}) async-start(s8[5767168]{0:T(1024)(128)(4,1)} %bitcast.35), calls=%async_computation.3 | async-start | bytes 3145728
  114.7 6.3 %slice-start.1 = ((s8[5767168]{0:T(1024)(128)(4,1)}), s8[4194304]{0:T(1024)(128)(4,1)S(1)}, s32[]{:S(2)}) async-start(s8[5767168]{0:T(1024)(128)(4,1)} %bitcast.35), calls=%async_computation.4 | async-start | bytes 8388608
  118.5 42.2 %collective-permute-start.9 = (bf16[128,4096]{1,0:T(8,128)(2,1)S(1)}, bf16[128,4096]{1,0:T(8,128)(2,1)S(1)}, u32[]{:S(2)}, u32[]{:S(2)}) collective-permute-start(bf16[128,4096]{1,0:T(8,128)(2,1)S(1)} %convolution_convert_fusion.2), channel_id=1, source_target_pairs={{0,3},{1,0},{2,1},{3,2},{4,7},{5,4},{6,5},{7,6},{8,11},{9,8},{10,9... | collective-permute-start | bytes 3145736 | tf_op jit(solution)/shard_map/ppermute | solution.py:126
  122.0 45.6 %collective-permute-start.11 = (bf16[128,4096]{1,0:T(8,128)(2,1)S(1)}, bf16[128,4096]{1,0:T(8,128)(2,1)S(1)}, u32[]{:S(2)}, u32[]{:S(2)}) collective-permute-start(bf16[128,4096]{1,0:T(8,128)(2,1)S(1)} %convolution_convert_fusion.1), channel_id=1, source_target_pairs={{0,1},{1,2},{2,3},{3,0},{4,5},{5,6},{6,7},{7,4},{8,9},{9,10},{10,1... | collective-permute-start | bytes 3145736 | tf_op jit(solution)/shard_map/ppermute | solution.py:126
  162.7 21.0 %collective-permute-start.10 = (bf16[128,4096]{1,0:T(8,128)(2,1)}, bf16[128,4096]{1,0:T(8,128)(2,1)S(1)}, u32[]{:S(2)}, u32[]{:S(2)}) collective-permute-start(bf16[128,4096]{1,0:T(8,128)(2,1)} %add_convert_fusion), channel_id=1, source_target_pairs={{0,3},{1,0},{2,1},{3,2},{4,7},{5,4},{6,5},{7,6},{8,11},{9,8},{10,9... | collective-permute-start | bytes 3145736 | tf_op jit(solution)/shard_map/ppermute | solution.py:126
  165.6 18.1 %copy-start.1 = (f32[128,4096]{1,0:T(8,128)S(1)}, f32[128,4096]{1,0:T(8,128)}, u32[]{:S(2)}) copy-start(f32[128,4096]{1,0:T(8,128)} %fusion.34) | copy-start | bytes 6291460
  174.0 9.7 %copy-start.2 = (f32[128,4096]{1,0:T(8,128)S(1)}, f32[128,4096]{1,0:T(8,128)}, u32[]{:S(2)}) copy-start(f32[128,4096]{1,0:T(8,128)} %convert_element_type.57) | copy-start | bytes 6291460
Sparse Core Ops, SparseCore 0:
  9.9 46.0 all-gather.1
  114.8 59.1 reduce-scatter.1

commit v17 on v14

--- a/solution.py
+++ b/solution.py
@@ -125,8 +125,22 @@
         coef_pool.astype(jnp.float32) + hard_matrix[:query_rows_dev].astype(jnp.float32)
     ).astype(jnp.bfloat16)
     carried = jnp.dot(own_coef, pool, preferred_element_type=jnp.float32)
+    first_blocks = [slabs - steps_down] if steps_down else []
+    first_blocks += [steps_up] if steps_up else []
+    first_parts = jnp.dot(
+        jnp.concatenate(
+            [hard_matrix[b * query_rows_dev : (b + 1) * query_rows_dev] for b in first_blocks],
+            axis=0,
+        ),
+        pool,
+        preferred_element_type=jnp.float32,
+    )
+    first = {
+        b: first_parts[k * query_rows_dev : (k + 1) * query_rows_dev]
+        for k, b in enumerate(first_blocks)
+    }
     if steps_down:
-        down = grad_for(slabs - steps_down)
+        down = first[slabs - steps_down]
         for step in range(1, steps_down):
             down = hop(down, ring_down) + grad_for(slabs - steps_down + step)
         carried = carried + hop(down, ring_down)
@@ -141,7 +155,7 @@
         partial.astype(jnp.bfloat16), "blk", scatter_dimension=0, tiled=True
     ).astype(jnp.float32)
     if steps_up:
-        up = grad_for(steps_up)
+        up = first[steps_up]
         for step in range(1, steps_up):
             up = hop(up, ring_up) + grad_for(steps_up - step)
         up = hop(up, ring_up)

time: 190 us -> 191 us (level)
    dot_general x3 -> x1, matrix products: 6.84 us -> 2.01 us  [grad_for(): return jnp.dot(rows, pool, preferred_element_type=jnp.float32)]
    dot_general x0 -> x1, matrix products: none -> 4.61 us  [per_device(): jnp.dot(jnp.concatenate([hard_matrix[b * query_rows_dev:(b + 1) * query_r...]
    ppermute x3, waiting for transfers between devices: 49.6 us -> 51.8 us  [hop(): lax.ppermute(part.astype(jnp.bfloat16), 'slab', perm).astype(jnp.float32)]
where the time goes in v17:
time: 191 us
  waiting for transfers between devices  109 us (57%)
  matrix products  29.7 us (16%)
  starting transfers between devices  22.8 us (12%)
  between operations  14.3 us (7%)
  other arithmetic  12.8 us (7%)
  local copies, waits for them, and re-layouts  2.11 us (1%)
    ppermute x3, waiting for transfers between devices, hop(): lax.ppermute(part.astype(jnp.bfloat16), 'slab', perm).astype(jnp.float32)  51.8 us
    ppermute x4, waiting for transfers between devices, ring_gather(): current = lax.ppermute(current, 'slab', ring_down)  50 us
    ppermute x4, starting transfers between devices, ring_gather(): current = lax.ppermute(current, 'slab', ring_down)  14.1 us
    dot_general x4, matrix products, per_device(): lax.dot_general(block, pool, contract_rows, preferred_element_type=jnp.fl...  13.1 us
    dot_general x1, matrix products, per_device(): lax.dot_general(jnp.concatenate([own_coef, hard_matrix[query_rows_dev:]],...  7.58 us
    ppermute x3, starting transfers between devices, per_device(): lax.ppermute(payload, 'slab', [(i, (i - t) % slabs) for i in range(slabs)])  4.89 us
    dot_general x1, matrix products, per_device(): jnp.dot(jnp.concatenate([hard_matrix[b * query_rows_dev:(b + 1) * query_r...  4.61 us
  transfers between devices with their start and end apart: 14, of which 10 were waited for; matrix products, arithmetic and copies ran while one was open for 14% of the time, Pallas kernels for 0%

profile of v17, /device:TPU:0, one launch (start us, length us, event | category | flops | bytes accessed | tf_op | source)
XLA Modules:
  0.0 191.0 jit_solution(7829790089144045377)
XLA Ops:
  7.2 0.0 copy-start.5
  7.2 0.0 all-gather.2.cloned.1.call-start
  7.2 0.7 all-gather.2.cloned.1.call-update
  7.9 0.0 reduce-scatter.2.cloned.1.call-start
  8.0 5.1 %collective-permute-start.3 = (bf16[128,4096]{1,0:T(8,128)(2,1)}, bf16[128,4096]{1,0:T(8,128)(2,1)}, u32[]{:S(2)}, u32[]{:S(2)}) collective-permute-start(bf16[128,4096]{1,0:T(8,128)(2,1)} %param.4), channel_id=1, source_target_pairs={{0,3},{1,0},{2,1},{3,2},{4,7},{5,4},{6,5},{7,6},{8,11},{9,8},{10,9... | collective-permute-start | bytes 3145736 | tf_op jit(solution)/shard_map/ppermute | solution.py:31
  13.1 0.4 collective-permute-start
  13.5 1.6 collective-permute-start.2
  15.1 0.0 collective-permute-start.5
  15.1 0.7 constant_dynamic-update-slice_fusion.3
  15.8 21.2 %collective-permute-done = s32[128,8]{0,1:T(8,128)S(1)} collective-permute-done((s32[128,8]{0,1:T(8,128)}, s32[128,8]{0,1:T(8,128)S(1)}, u32[]{:S(2)}, u32[]{:S(2)}) %collective-permute-start) | collective-permute-done | bytes 4128 | tf_op jit(solution)/shard_map/ppermute | solution.py:31
  37.0 4.3 %collective-permute-start.1 = (s32[128,8]{0,1:T(8,128)S(1)}, s32[128,8]{0,1:T(8,128)S(1)}, u32[]{:S(2)}, u32[]{:S(2)}) collective-permute-start(s32[128,8]{0,1:T(8,128)S(1)} %collective-permute-done), channel_id=1, source_target_pairs={{0,3},{1,0},{2,1},{3,2},{4,7},{5,4},{6,5},{7,6},{8,11},{9,8},{10,9... | collective-permute-start | bytes 12296 | tf_op jit(solution)/shard_map/ppermute | solution.py:31
  41.3 17.3 %collective-permute-done.1 = s32[128,8]{0,1:T(8,128)S(1)} collective-permute-done((s32[128,8]{0,1:T(8,128)S(1)}, s32[128,8]{0,1:T(8,128)S(1)}, u32[]{:S(2)}, u32[]{:S(2)}) %collective-permute-start.1) | collective-permute-done | bytes 4128 | tf_op jit(solution)/shard_map/ppermute | solution.py:31
  58.5 0.0 collective-permute-done.2
  58.6 0.0 collective-permute-done.3
  58.6 4.3 %collective-permute-start.4 = (bf16[128,4096]{1,0:T(8,128)(2,1)}, bf16[128,4096]{1,0:T(8,128)(2,1)}, u32[]{:S(2)}, u32[]{:S(2)}) collective-permute-start(bf16[128,4096]{1,0:T(8,128)(2,1)} %collective-permute-done.3), channel_id=1, source_target_pairs={{0,3},{1,0},{2,1},{3,2},{4,7},{5,4},{6,5},{7,6},{8,11},{9,8},{10,9... | collective-permute-start | bytes 3145736 | tf_op jit(solution)/shard_map/ppermute | solution.py:31
  62.9 2.6 %convert_reduce_fusion = f32[512,704]{0,1:T(8,128)S(1)} fusion(s32[512,8]{0,1:T(8,128)S(1)} %fusion.19, pred[512,8]{0,1:T(8,128)(4,1)S(1)} %fusion.20), kind=kLoop, calls=%fused_computation | loop fusion | flops 11173888 | bytes 1462272 | tf_op jit(solution)/shard_map/reduce_sum | solution.py:66
  65.5 0.0 all-gather.2.cloned.1.call-done
  65.6 0.0 copy-done.5
  65.6 0.0 copy-start
  65.6 4.4 %fusion.34 = f32[128,704]{0,1:T(8,128)S(1)} fusion(bf16[128,4096]{1,0:T(8,128)(2,1)S(1)} %copy-done.5, bf16[704,4096]{1,0:T(8,128)(2,1)} %all-gather.2.cloned.1.call-done), kind=kOutput, calls=%fused_computation.75 | convolution fusion | flops 738197504 | bytes 7176192 | tf_op jit(solution)/shard_map/dot_general | solution.py:52
  70.0 2.9 %fusion.35 = f32[128,704]{0,1:T(8,128)S(1)} fusion(bf16[128,4096]{1,0:T(8,128)(2,1)} %collective-permute-done.3, bf16[704,4096]{1,0:T(8,128)(2,1)S(1)} %copy-done), kind=kOutput, calls=%fused_computation.76 | convolution fusion | flops 738197504 | bytes 7176192 | tf_op jit(solution)/shard_map/dot_general | solution.py:52
  72.9 11.5 %collective-permute-done.4 = bf16[128,4096]{1,0:T(8,128)(2,1)} collective-permute-done((bf16[128,4096]{1,0:T(8,128)(2,1)}, bf16[128,4096]{1,0:T(8,128)(2,1)}, u32[]{:S(2)}, u32[]{:S(2)}) %collective-permute-start.4) | collective-permute-done | bytes 1048608 | tf_op jit(solution)/shard_map/ppermute | solution.py:31
  84.5 2.9 %fusion.36 = f32[128,704]{0,1:T(8,128)S(1)} fusion(bf16[128,4096]{1,0:T(8,128)(2,1)} %collective-permute-done.4, bf16[704,4096]{1,0:T(8,128)(2,1)S(1)} %copy-done), kind=kOutput, calls=%fused_computation.77 | convolution fusion | flops 738197504 | bytes 7176192 | tf_op jit(solution)/shard_map/dot_general | solution.py:52
  87.3 0.0 collective-permute-done.5
  87.4 2.9 %fusion.37 = f32[128,704]{0,1:T(8,128)S(1)} fusion(bf16[128,4096]{1,0:T(8,128)(2,1)} %collective-permute-done.5, bf16[704,4096]{1,0:T(8,128)(2,1)S(1)} %copy-done), kind=kOutput, calls=%fused_computation.78 | convolution fusion | flops 738197504 | bytes 7176192 | tf_op jit(solution)/shard_map/dot_general | solution.py:52
  90.2 0.0 copy-start.3
  90.3 0.3 select_reduce_fusion.1
  90.6 0.4 select_reduce_fusion
  91.0 0.0 copy-start.4
  91.0 0.1 slice_reduce_fusion
  91.1 1.0 copy-done.4
  92.1 0.1 exponential_reduce_fusion
  92.2 0.1 collective-permute-start.8
  92.3 4.8 %collective-permute-start.7 = (f32[1280]{0:T(1024)S(1)}, f32[1280]{0:T(1024)S(1)}, u32[]{:S(2)}, u32[]{:S(2)}) collective-permute-start(f32[1280]{0:T(1024)S(1)} %pad_maximum_fusion), channel_id=1, source_target_pairs={{0,2},{1,3},{2,0},{3,1},{4,6},{5,7},{6,4},{7,5},{8,10},{9,11},{10,... | collective-permute-start | bytes 15368 | tf_op jit(solution)/shard_map/ppermute | solution.py:90
  97.1 0.0 collective-permute-start.6
  97.1 1.1 collective-permute-done.8
  98.2 0.6 collective-permute-done.7
  98.8 2.0 %collective-permute-done.6 = f32[1280]{0:T(1024)S(1)} collective-permute-done((f32[1280]{0:T(1024)S(1)}, f32[1280]{0:T(1024)S(1)}, u32[]{:S(2)}, u32[]{:S(2)}) %collective-permute-start.6) | collective-permute-done | bytes 5152 | tf_op jit(solution)/shard_map/ppermute | solution.py:90
  100.8 0.1 concatenate.53
  100.9 0.1 fusion.28
  101.0 0.1 fusion.24
  101.1 0.1 fusion.27
  101.2 0.0 copy-start.6
  101.2 1.4 select_convert_fusion
  102.7 0.1 slice.65
  102.7 1.1 add_convert_fusion.1
  103.8 7.6 %convolution_convert_fusion = bf16[704,4096]{1,0:T(8,128)(2,1)} fusion(bf16[128,4096]{1,0:T(8,128)(2,1)} %collective-permute-done.5, bf16[128,4096]{1,0:T(8,128)(2,1)} %collective-permute-done.4, bf16[128,4096]{1,0:T(8,128)(2,1)} %collective-permute-done.3, bf16[128,4096]{1,0:T(8,128)(2,1)S(1)} %copy-done.6, bf16[384,704]{0,1:T(8,128)(2,1)S(1)} %slice.65, ...), kind=kOutput, calls=%fused_computation.3 | convolution fusion | flops 2973892608 | bytes 10682368 | tf_op jit(solution)/shard_map/dot_general | solution.py:148
  111.4 0.0 reduce-scatter.2.cloned.1.call-update
  111.5 0.0 slice-start.1
  111.5 4.6 %convolution_convert_fusion.1 = bf16[256,4096]{1,0:T(8,128)(2,1)S(1)} fusion(bf16[704,4096]{1,0:T(8,128)(2,1)} %all-gather.2.cloned.1.call-done, bf16[128,704]{0,1:T(8,128)(2,1)S(1)} %get-tuple-element.14, bf16[128,704]{0,1:T(8,128)(2,1)S(1)} %get-tuple-element.13), kind=kOutput, calls=%fused_computation.4 | convolution fusion | flops 1478164480 | bytes 8224768 | tf_op jit(solution)/shard_map/dot_general | solution.py:130
  116.1 0.2 fusion.32
  116.3 1.9 %collective-permute-start.9 = (bf16[128,4096]{1,0:T(8,128)(2,1)S(1)}, bf16[128,4096]{1,0:T(8,128)(2,1)S(1)}, u32[]{:S(2)}, u32[]{:S(2)}) collective-permute-start(bf16[128,4096]{1,0:T(8,128)(2,1)S(1)} %get-tuple-element.9), channel_id=1, source_target_pairs={{0,3},{1,0},{2,1},{3,2},{4,7},{5,4},{6,5},{7,6},{8,11},{9,8},{10,9... | collective-permute-start | bytes 3145736 | tf_op jit(solution)/shard_map/ppermute | solution.py:122
  118.3 0.1 collective-permute-start.11
  118.4 40.1 %collective-permute-done.9 = bf16[128,4096]{1,0:T(8,128)(2,1)S(1)} collective-permute-done((bf16[128,4096]{1,0:T(8,128)(2,1)S(1)}, bf16[128,4096]{1,0:T(8,128)(2,1)S(1)}, u32[]{:S(2)}, u32[]{:S(2)}) %collective-permute-start.9) | collective-permute-done | bytes 1048608 | tf_op jit(solution)/shard_map/ppermute | solution.py:122
  158.5 2.0 %add_convert_fusion = bf16[128,4096]{1,0:T(8,128)(2,1)} fusion(bf16[128,4096]{1,0:T(8,128)(2,1)S(1)} %collective-permute-done.9, bf16[704,4096]{1,0:T(8,128)(2,1)S(1)} %bitcast.35, bf16[512,704]{0,1:T(8,128)(2,1)S(1)} %select_convert_fusion), kind=kOutput, calls=%fused_computation.13 | convolution fusion | flops 739770368 | bytes 8044544 | tf_op jit(solution)/shard_map/dot_general | solution.py:119
  160.5 0.0 collective-permute-start.10
  160.5 0.5 fusion.31
  161.0 2.4 %fusion.38 = f32[128,4096]{1,0:T(8,128)} fusion(bf16[128,704]{0,1:T(8,128)(2,1)S(1)} %add_convert_fusion.1, bf16[704,4096]{1,0:T(8,128)(2,1)S(1)} %bitcast.35), kind=kOutput, calls=%fused_computation.79 | convolution fusion | flops 738197504 | bytes 8044544 | tf_op jit(solution)/shard_map/dot_general | solution.py:127
  163.4 2.0 %collective-permute-done.11 = bf16[128,4096]{1,0:T(8,128)(2,1)S(1)} collective-permute-done((bf16[128,4096]{1,0:T(8,128)(2,1)S(1)}, bf16[128,4096]{1,0:T(8,128)(2,1)S(1)}, u32[]{:S(2)}, u32[]{:S(2)}) %collective-permute-start.11) | collective-permute-done | bytes 1048608 | tf_op jit(solution)/shard_map/ppermute | solution.py:122
  165.4 1.5 convert_element_type.51
  166.9 3.3 %reduce-scatter.2.cloned.1.call-done = bf16[88,4096]{1,0:T(8,128)(2,1)} async-done(((bf16[704,4096]{1,0:T(8,128)(2,1)}), bf16[88,4096]{1,0:T(8,128)(2,1)}) %reduce-scatter.2.cloned.1.call-update) | async-done | bytes 720912 | tf_op jit(solution)/shard_map/reduce_scatter | solution.py:154
  170.2 2.5 %convert_element_type.53 = f32[88,4096]{1,0:T(8,128)} convert(bf16[88,4096]{1,0:T(8,128)(2,1)} %reduce-scatter.2.cloned.1.call-done) | non-fusion elementwise | flops 360448 | bytes 2162688 | tf_op jit(solution)/shard_map/convert_element_type | solution.py:156
  172.7 9.7 %collective-permute-done.10 = bf16[128,4096]{1,0:T(8,128)(2,1)S(1)} collective-permute-done((bf16[128,4096]{1,0:T(8,128)(2,1)}, bf16[128,4096]{1,0:T(8,128)(2,1)S(1)}, u32[]{:S(2)}, u32[]{:S(2)}) %collective-permute-start.10) | collective-permute-done | bytes 1048608 | tf_op jit(solution)/shard_map/ppermute | solution.py:122
  182.4 1.7 add_add_fusion
  (32 shorter events, 0.2 us)
Async XLA Ops:
  7.2 58.4 %copy-start.5 = (bf16[128,4096]{1,0:T(8,128)(2,1)S(1)}, bf16[128,4096]{1,0:T(8,128)(2,1)}, u32[]{:S(2)}) copy-start(bf16[128,4096]{1,0:T(8,128)(2,1)} %param.4) | copy-start | bytes 3145732
  7.2 58.4 %all-gather.2.cloned.1.call-start = ((), (), s32[]{:S(2)}) async-start(), calls=%async_computation.1 | async-start | bytes 6488064 | tf_op jit(solution)/shard_map/all_gather | solution.py:19
  7.9 162.3 %reduce-scatter.2.cloned.1.call-start = ((), (), s32[]{:S(2)}) async-start(), calls=%async_computation.2 | async-start | bytes 6488064 | tf_op jit(solution)/shard_map/reduce_scatter | solution.py:154
  8.0 50.6 %collective-permute-start.3 = (bf16[128,4096]{1,0:T(8,128)(2,1)}, bf16[128,4096]{1,0:T(8,128)(2,1)}, u32[]{:S(2)}, u32[]{:S(2)}) collective-permute-start(bf16[128,4096]{1,0:T(8,128)(2,1)} %param.4), channel_id=1, source_target_pairs={{0,3},{1,0},{2,1},{3,2},{4,7},{5,4},{6,5},{7,6},{8,11},{9,8},{10,9... | collective-permute-start | bytes 3145736 | tf_op jit(solution)/shard_map/ppermute | solution.py:31
  13.1 23.9 %collective-permute-start = (s32[128,8]{0,1:T(8,128)}, s32[128,8]{0,1:T(8,128)S(1)}, u32[]{:S(2)}, u32[]{:S(2)}) collective-permute-start(s32[128,8]{0,1:T(8,128)} %param.7), channel_id=1, source_target_pairs={{0,3},{1,0},{2,1},{3,2},{4,7},{5,4},{6,5},{7,6},{8,11},{9,8},{10,9... | collective-permute-start | bytes 12296 | tf_op jit(solution)/shard_map/ppermute | solution.py:31
  13.5 45.0 %collective-permute-start.2 = (s32[128,8]{0,1:T(8,128)}, s32[128,8]{0,1:T(8,128)S(1)}, u32[]{:S(2)}, u32[]{:S(2)}) collective-permute-start(s32[128,8]{0,1:T(8,128)} %param.7), channel_id=1, source_target_pairs={{0,1},{1,2},{2,3},{3,0},{4,5},{5,6},{6,7},{7,4},{8,9},{9,10},{10,1... | collective-permute-start | bytes 12296 | tf_op jit(solution)/shard_map/ppermute | solution.py:35
  15.1 72.3 %collective-permute-start.5 = (bf16[128,4096]{1,0:T(8,128)(2,1)}, bf16[128,4096]{1,0:T(8,128)(2,1)}, u32[]{:S(2)}, u32[]{:S(2)}) collective-permute-start(bf16[128,4096]{1,0:T(8,128)(2,1)} %param.4), channel_id=1, source_target_pairs={{0,1},{1,2},{2,3},{3,0},{4,5},{5,6},{6,7},{7,4},{8,9},{9,10},{10,1... | collective-permute-start | bytes 3145736 | tf_op jit(solution)/shard_map/ppermute | solution.py:35
  37.0 21.5 %collective-permute-start.1 = (s32[128,8]{0,1:T(8,128)S(1)}, s32[128,8]{0,1:T(8,128)S(1)}, u32[]{:S(2)}, u32[]{:S(2)}) collective-permute-start(s32[128,8]{0,1:T(8,128)S(1)} %collective-permute-done), channel_id=1, source_target_pairs={{0,3},{1,0},{2,1},{3,2},{4,7},{5,4},{6,5},{7,6},{8,11},{9,8},{10,9... | collective-permute-start | bytes 12296 | tf_op jit(solution)/shard_map/ppermute | solution.py:31
  58.6 25.8 %collective-permute-start.4 = (bf16[128,4096]{1,0:T(8,128)(2,1)}, bf16[128,4096]{1,0:T(8,128)(2,1)}, u32[]{:S(2)}, u32[]{:S(2)}) collective-permute-start(bf16[128,4096]{1,0:T(8,128)(2,1)} %collective-permute-done.3), channel_id=1, source_target_pairs={{0,3},{1,0},{2,1},{3,2},{4,7},{5,4},{6,5},{7,6},{8,11},{9,8},{10,9... | collective-permute-start | bytes 3145736 | tf_op jit(solution)/shard_map/ppermute | solution.py:31
  65.6 4.5 %copy-start = (bf16[704,4096]{1,0:T(8,128)(2,1)S(1)}, bf16[704,4096]{1,0:T(8,128)(2,1)}, u32[]{:S(2)}) copy-start(bf16[704,4096]{1,0:T(8,128)(2,1)} %all-gather.2.cloned.1.call-done) | copy-start | bytes 17301508
  90.2 0.7 copy-start.3
  90.6 1.5 copy-start.7
  91.0 1.1 copy-start.4
  92.2 6.0 %collective-permute-start.8 = (f32[1280]{0:T(1024)S(1)}, f32[1280]{0:T(1024)S(1)}, u32[]{:S(2)}, u32[]{:S(2)}) collective-permute-start(f32[1280]{0:T(1024)S(1)} %pad_maximum_fusion), channel_id=1, source_target_pairs={{0,1},{1,2},{2,3},{3,0},{4,5},{5,6},{6,7},{7,4},{8,9},{9,10},{10,1... | collective-permute-start | bytes 15368 | tf_op jit(solution)/shard_map/ppermute | solution.py:90
  92.3 6.5 %collective-permute-start.7 = (f32[1280]{0:T(1024)S(1)}, f32[1280]{0:T(1024)S(1)}, u32[]{:S(2)}, u32[]{:S(2)}) collective-permute-start(f32[1280]{0:T(1024)S(1)} %pad_maximum_fusion), channel_id=1, source_target_pairs={{0,2},{1,3},{2,0},{3,1},{4,6},{5,7},{6,4},{7,5},{8,10},{9,11},{10,... | collective-permute-start | bytes 15368 | tf_op jit(solution)/shard_map/ppermute | solution.py:90
  97.1 3.7 %collective-permute-start.6 = (f32[1280]{0:T(1024)S(1)}, f32[1280]{0:T(1024)S(1)}, u32[]{:S(2)}, u32[]{:S(2)}) collective-permute-start(f32[1280]{0:T(1024)S(1)} %pad_maximum_fusion), channel_id=1, source_target_pairs={{0,3},{1,0},{2,1},{3,2},{4,7},{5,4},{6,5},{7,6},{8,11},{9,8},{10,9... | collective-permute-start | bytes 15368 | tf_op jit(solution)/shard_map/ppermute | solution.py:90
  101.2 2.6 %copy-start.6 = (bf16[128,4096]{1,0:T(8,128)(2,1)S(1)}, bf16[128,4096]{1,0:T(8,128)(2,1)}, u32[]{:S(2)}) copy-start(bf16[128,4096]{1,0:T(8,128)(2,1)} %param.4) | copy-start | bytes 3145732
  111.4 47.1 %slice-start = ((s8[5767168]{0:T(1024)(128)(4,1)}), s8[1572864]{0:T(1024)(128)(4,1)S(1)}, s32[]{:S(2)}) async-start(s8[5767168]{0:T(1024)(128)(4,1)} %bitcast.34), calls=%async_computation.3 | async-start | bytes 3145728
  111.5 47.0 %slice-start.1 = ((s8[5767168]{0:T(1024)(128)(4,1)}), s8[4194304]{0:T(1024)(128)(4,1)S(1)}, s32[]{:S(2)}) async-start(s8[5767168]{0:T(1024)(128)(4,1)} %bitcast.34), calls=%async_computation.4 | async-start | bytes 8388608
  116.3 42.2 %collective-permute-start.9 = (bf16[128,4096]{1,0:T(8,128)(2,1)S(1)}, bf16[128,4096]{1,0:T(8,128)(2,1)S(1)}, u32[]{:S(2)}, u32[]{:S(2)}) collective-permute-start(bf16[128,4096]{1,0:T(8,128)(2,1)S(1)} %get-tuple-element.9), channel_id=1, source_target_pairs={{0,3},{1,0},{2,1},{3,2},{4,7},{5,4},{6,5},{7,6},{8,11},{9,8},{10,9... | collective-permute-start | bytes 3145736 | tf_op jit(solution)/shard_map/ppermute | solution.py:122
  118.3 47.1 %collective-permute-start.11 = (bf16[128,4096]{1,0:T(8,128)(2,1)S(1)}, bf16[128,4096]{1,0:T(8,128)(2,1)S(1)}, u32[]{:S(2)}, u32[]{:S(2)}) collective-permute-start(bf16[128,4096]{1,0:T(8,128)(2,1)S(1)} %get-tuple-element.10), channel_id=1, source_target_pairs={{0,1},{1,2},{2,3},{3,0},{4,5},{5,6},{6,7},{7,4},{8,9},{9,10},{10,1... | collective-permute-start | bytes 3145736 | tf_op jit(solution)/shard_map/ppermute | solution.py:122
  160.5 21.9 %collective-permute-start.10 = (bf16[128,4096]{1,0:T(8,128)(2,1)}, bf16[128,4096]{1,0:T(8,128)(2,1)S(1)}, u32[]{:S(2)}, u32[]{:S(2)}) collective-permute-start(bf16[128,4096]{1,0:T(8,128)(2,1)} %add_convert_fusion), channel_id=1, source_target_pairs={{0,3},{1,0},{2,1},{3,2},{4,7},{5,4},{6,5},{7,6},{8,11},{9,8},{10,9... | collective-permute-start | bytes 3145736 | tf_op jit(solution)/shard_map/ppermute | solution.py:122
  163.4 19.0 %copy-start.1 = (f32[128,4096]{1,0:T(8,128)S(1)}, f32[128,4096]{1,0:T(8,128)}, u32[]{:S(2)}) copy-start(f32[128,4096]{1,0:T(8,128)} %fusion.38) | copy-start | bytes 6291460
  170.2 12.2 %copy-start.2 = (f32[128,4096]{1,0:T(8,128)S(1)}, f32[128,4096]{1,0:T(8,128)}, u32[]{:S(2)}) copy-start(f32[128,4096]{1,0:T(8,128)} %convert_element_type.51) | copy-start | bytes 6291460
Sparse Core Ops, SparseCore 0:
  9.9 46.0 all-gather.1
  111.6 58.6 reduce-scatter.1

commit v18 on v14

--- a/solution.py
+++ b/solution.py
@@ -24,19 +24,21 @@
     steps_down = slabs // 2
     steps_up = slabs - 1 - steps_down
 
-    def ring_gather(x):
+    def ring_gather(x, after_first_down=False):
         blocks = [x] * slabs
         current = x
         for step in range(1, steps_down + 1):
             current = lax.ppermute(current, "slab", ring_down)
             blocks[step] = current
         current = x
+        if after_first_down and steps_down and steps_up:
+            current, _ = lax.optimization_barrier((current, blocks[1]))
         for step in range(1, steps_up + 1):
             current = lax.ppermute(current, "slab", ring_up)
             blocks[slabs - step] = current
         return blocks
 
-    query_blocks = ring_gather(queries)
+    query_blocks = ring_gather(queries, after_first_down=True)
     id_blocks = ring_gather(hard_ids)
 
     def to_origin(x):

time: 190 us -> 194 us (1.021)
  starting transfers between devices: 22.8 us -> 28.1 us
  waiting for transfers between devices: 108 us -> 106 us
    ppermute x4, waiting for transfers between devices: 50 us -> 37.9 us  [ring_gather(): current = lax.ppermute(current, 'slab', ring_down)]
    all_gather x1, waiting for transfers between devices: 0.02 us -> 7.39 us  [per_device(): pool = lax.all_gather(passages, 'blk', axis=0, tiled=True)]
    ppermute x2, waiting for transfers between devices: 0.01 us -> 7.03 us  [ring_gather(): current = lax.ppermute(current, 'slab', ring_up)]
    ppermute x3, starting transfers between devices: 2.16 us -> 6.65 us  [hop(): lax.ppermute(part.astype(jnp.bfloat16), 'slab', perm).astype(jnp.float32)]
    ppermute x3, waiting for transfers between devices: 49.6 us -> 45.4 us  [hop(): lax.ppermute(part.astype(jnp.bfloat16), 'slab', perm).astype(jnp.float32)]
  transfers between devices with their start and end apart: 14 -> 14, of which waited for: 10 -> 12; matrix products, arithmetic and copies ran while one was open for 14% -> 14% of each run, Pallas kernels for 0% -> 0%
where the time goes in v18:
time: 194 us; the launch traced here: 193 us
  waiting for transfers between devices  106 us (55%)
  matrix products  29.9 us (15%)
  starting transfers between devices  28.1 us (14%)
  between operations  14.3 us (7%)
  other arithmetic  12.8 us (7%)
    ppermute x3, waiting for transfers between devices, hop(): lax.ppermute(part.astype(jnp.bfloat16), 'slab', perm).astype(jnp.float32)  45.4 us
    ppermute x4, waiting for transfers between devices, ring_gather(): current = lax.ppermute(current, 'slab', ring_down)  37.9 us
    ppermute x4, starting transfers between devices, ring_gather(): current = lax.ppermute(current, 'slab', ring_down)  14.1 us
    dot_general x4, matrix products, per_device(): lax.dot_general(block, pool, contract_rows, preferred_element_type=jnp.fl...  13.1 us
    dot_general x1, matrix products, per_device(): lax.dot_general(jnp.concatenate([own_coef, hard_matrix[query_rows_dev:]],...  7.59 us
    all_gather x1, waiting for transfers between devices, per_device(): pool = lax.all_gather(passages, 'blk', axis=0, tiled=True)  7.39 us
    ppermute x2, waiting for transfers between devices, ring_gather(): current = lax.ppermute(current, 'slab', ring_up)  7.03 us
    dot_general x3, matrix products, grad_for(): return jnp.dot(rows, pool, preferred_element_type=jnp.float32)  6.84 us
  transfers between devices with their start and end apart: 14, of which 12 were waited for; matrix products, arithmetic and copies ran while one was open for 14% of the time, Pallas kernels for 0%

profile of v18, /device:TPU:0, one launch (start us, length us, event | category | flops | bytes accessed | tf_op | source)
XLA Modules:
  0.0 193.2 jit_solution(12943162576088655650)
XLA Ops:
  7.2 0.0 copy-start.5
  7.2 0.0 all-gather.2.cloned.1.call-start
  7.2 0.7 all-gather.2.cloned.1.call-update
  7.9 0.0 reduce-scatter.2.cloned.1.call-start
  8.0 5.1 %collective-permute-start.3 = (bf16[128,4096]{1,0:T(8,128)(2,1)}, bf16[128,4096]{1,0:T(8,128)(2,1)}, u32[]{:S(2)}, u32[]{:S(2)}) collective-permute-start(bf16[128,4096]{1,0:T(8,128)(2,1)} %param.4), channel_id=1, source_target_pairs={{0,3},{1,0},{2,1},{3,2},{4,7},{5,4},{6,5},{7,6},{8,11},{9,8},{10,9... | collective-permute-start | bytes 3145736 | tf_op jit(solution)/shard_map/ppermute | solution.py:31
  13.1 0.4 collective-permute-start
  13.5 1.6 collective-permute-start.2
  15.1 0.7 constant_dynamic-update-slice_fusion.3
  15.8 20.1 %collective-permute-done = s32[128,8]{0,1:T(8,128)S(1)} collective-permute-done((s32[128,8]{0,1:T(8,128)}, s32[128,8]{0,1:T(8,128)S(1)}, u32[]{:S(2)}, u32[]{:S(2)}) %collective-permute-start) | collective-permute-done | bytes 4128 | tf_op jit(solution)/shard_map/ppermute | solution.py:31
  35.9 4.3 %collective-permute-start.1 = (s32[128,8]{0,1:T(8,128)S(1)}, s32[128,8]{0,1:T(8,128)S(1)}, u32[]{:S(2)}, u32[]{:S(2)}) collective-permute-start(s32[128,8]{0,1:T(8,128)S(1)} %collective-permute-done), channel_id=1, source_target_pairs={{0,3},{1,0},{2,1},{3,2},{4,7},{5,4},{6,5},{7,6},{8,11},{9,8},{10,9... | collective-permute-start | bytes 12296 | tf_op jit(solution)/shard_map/ppermute | solution.py:31
  40.2 1.3 collective-permute-done.1
  41.5 0.0 collective-permute-done.2
  41.6 0.0 collective-permute-done.3
  41.6 0.1 collective-permute-start.5
  41.7 2.6 %convert_reduce_fusion = f32[512,704]{0,1:T(8,128)S(1)} fusion(s32[512,8]{0,1:T(8,128)S(1)} %fusion.18, pred[512,8]{0,1:T(8,128)(4,1)S(1)} %fusion.19), kind=kLoop, calls=%fused_computation | loop fusion | flops 11173888 | bytes 1462272 | tf_op jit(solution)/shard_map/reduce_sum | solution.py:68
  44.3 4.2 %collective-permute-start.4 = (bf16[128,4096]{1,0:T(8,128)(2,1)}, bf16[128,4096]{1,0:T(8,128)(2,1)}, u32[]{:S(2)}, u32[]{:S(2)}) collective-permute-start(bf16[128,4096]{1,0:T(8,128)(2,1)} %collective-permute-done.3), channel_id=1, source_target_pairs={{0,3},{1,0},{2,1},{3,2},{4,7},{5,4},{6,5},{7,6},{8,11},{9,8},{10,9... | collective-permute-start | bytes 3145736 | tf_op jit(solution)/shard_map/ppermute | solution.py:31
  48.6 7.4 %all-gather.2.cloned.1.call-done = bf16[704,4096]{1,0:T(8,128)(2,1)} async-done(((bf16[88,4096]{1,0:T(8,128)(2,1)}), bf16[704,4096]{1,0:T(8,128)(2,1)}) %all-gather.2.cloned.1.call-update) | async-done | bytes 5767184 | tf_op jit(solution)/shard_map/all_gather | solution.py:19
  56.0 4.4 %fusion.30 = f32[128,704]{0,1:T(8,128)S(1)} fusion(bf16[128,4096]{1,0:T(8,128)(2,1)S(1)} %copy-done.5, bf16[704,4096]{1,0:T(8,128)(2,1)} %all-gather.2.cloned.1.call-done), kind=kOutput, calls=%fused_computation.72 | convolution fusion | flops 738197504 | bytes 7176192 | tf_op jit(solution)/shard_map/dot_general | solution.py:54
  60.4 2.9 %fusion.31 = f32[128,704]{0,1:T(8,128)S(1)} fusion(bf16[128,4096]{1,0:T(8,128)(2,1)} %collective-permute-done.3, bf16[704,4096]{1,0:T(8,128)(2,1)S(1)} %copy-done), kind=kOutput, calls=%fused_computation.73 | convolution fusion | flops 738197504 | bytes 7176192 | tf_op jit(solution)/shard_map/dot_general | solution.py:54
  63.3 7.0 %collective-permute-done.5 = bf16[128,4096]{1,0:T(8,128)(2,1)} collective-permute-done((bf16[128,4096]{1,0:T(8,128)(2,1)}, bf16[128,4096]{1,0:T(8,128)(2,1)}, u32[]{:S(2)}, u32[]{:S(2)}) %collective-permute-start.5) | collective-permute-done | bytes 1048608 | tf_op jit(solution)/shard_map/ppermute | solution.py:37
  70.3 2.9 %fusion.33 = f32[128,704]{0,1:T(8,128)S(1)} fusion(bf16[128,4096]{1,0:T(8,128)(2,1)} %collective-permute-done.5, bf16[704,4096]{1,0:T(8,128)(2,1)S(1)} %copy-done), kind=kOutput, calls=%fused_computation.75 | convolution fusion | flops 738197504 | bytes 7176192 | tf_op jit(solution)/shard_map/dot_general | solution.py:54
  73.2 16.4 %collective-permute-done.4 = bf16[128,4096]{1,0:T(8,128)(2,1)} collective-permute-done((bf16[128,4096]{1,0:T(8,128)(2,1)}, bf16[128,4096]{1,0:T(8,128)(2,1)}, u32[]{:S(2)}, u32[]{:S(2)}) %collective-permute-start.4) | collective-permute-done | bytes 1048608 | tf_op jit(solution)/shard_map/ppermute | solution.py:31
  89.7 2.9 %fusion.32 = f32[128,704]{0,1:T(8,128)S(1)} fusion(bf16[128,4096]{1,0:T(8,128)(2,1)} %collective-permute-done.4, bf16[704,4096]{1,0:T(8,128)(2,1)S(1)} %copy-done), kind=kOutput, calls=%fused_computation.74 | convolution fusion | flops 738197504 | bytes 7176192 | tf_op jit(solution)/shard_map/dot_general | solution.py:54
  92.6 0.0 copy-start.3
  92.6 0.3 select_reduce_fusion.1
  92.9 0.4 select_reduce_fusion
  93.3 0.0 copy-done.3
  93.3 0.0 copy-start.4
  93.3 0.1 slice_reduce_fusion
  93.4 1.0 copy-done.4
  94.4 0.1 exponential_reduce_fusion
  94.5 0.7 collective-permute-start.8
  95.2 4.6 %collective-permute-start.7 = (f32[1280]{0:T(1024)S(1)}, f32[1280]{0:T(1024)S(1)}, u32[]{:S(2)}, u32[]{:S(2)}) collective-permute-start(f32[1280]{0:T(1024)S(1)} %pad_maximum_fusion), channel_id=1, source_target_pairs={{0,2},{1,3},{2,0},{3,1},{4,6},{5,7},{6,4},{7,5},{8,10},{9,11},{10,... | collective-permute-start | bytes 15368 | tf_op jit(solution)/shard_map/ppermute | solution.py:92
  99.8 0.4 collective-permute-start.6
  100.3 0.6 collective-permute-done.8
  100.9 0.6 collective-permute-done.7
  101.4 2.0 %collective-permute-done.6 = f32[1280]{0:T(1024)S(1)} collective-permute-done((f32[1280]{0:T(1024)S(1)}, f32[1280]{0:T(1024)S(1)}, u32[]{:S(2)}, u32[]{:S(2)}) %collective-permute-start.6) | collective-permute-done | bytes 5152 | tf_op jit(solution)/shard_map/ppermute | solution.py:92
  103.5 0.1 concatenate.50
  103.6 0.1 fusion.27
  103.6 0.1 fusion.23
  103.7 0.1 fusion.26
  103.9 0.0 copy-start.6
  103.9 1.4 select_convert_fusion
  105.3 0.1 slice.53
  105.4 1.1 add_convert_fusion.1
  106.5 7.6 %convolution_convert_fusion = bf16[704,4096]{1,0:T(8,128)(2,1)} fusion(bf16[128,4096]{1,0:T(8,128)(2,1)} %collective-permute-done.5, bf16[128,4096]{1,0:T(8,128)(2,1)} %collective-permute-done.4, bf16[128,4096]{1,0:T(8,128)(2,1)} %collective-permute-done.3, bf16[128,4096]{1,0:T(8,128)(2,1)S(1)} %copy-done.6, bf16[384,704]{0,1:T(8,128)(2,1)S(1)} %slice.53, ...), kind=kOutput, calls=%fused_computation.3 | convolution fusion | flops 2973892608 | bytes 10682368 | tf_op jit(solution)/shard_map/dot_general | solution.py:136
  114.1 0.0 reduce-scatter.2.cloned.1.call-update
  114.1 0.0 slice-start.1
  114.1 3.8 %convolution_convert_fusion.2 = bf16[128,4096]{1,0:T(8,128)(2,1)S(1)} fusion(bf16[704,4096]{1,0:T(8,128)(2,1)} %all-gather.2.cloned.1.call-done, bf16[512,704]{0,1:T(8,128)(2,1)S(1)} %select_convert_fusion), kind=kOutput, calls=%fused_computation.5 | convolution fusion | flops 738721792 | bytes 6995968 | tf_op jit(solution)/shard_map/dot_general | solution.py:121
  118.0 2.3 %collective-permute-start.9 = (bf16[128,4096]{1,0:T(8,128)(2,1)S(1)}, bf16[128,4096]{1,0:T(8,128)(2,1)S(1)}, u32[]{:S(2)}, u32[]{:S(2)}) collective-permute-start(bf16[128,4096]{1,0:T(8,128)(2,1)S(1)} %convolution_convert_fusion.2), channel_id=1, source_target_pairs={{0,3},{1,0},{2,1},{3,2},{4,7},{5,4},{6,5},{7,6},{8,11},{9,8},{10,9... | collective-permute-start | bytes 3145736 | tf_op jit(solution)/shard_map/ppermute | solution.py:124
  120.3 0.0 slice-done.1
  120.3 1.0 convolution_convert_fusion.1
  121.3 0.1 collective-permute-start.11
  121.3 22.5 %collective-permute-done.9 = bf16[128,4096]{1,0:T(8,128)(2,1)S(1)} collective-permute-done((bf16[128,4096]{1,0:T(8,128)(2,1)S(1)}, bf16[128,4096]{1,0:T(8,128)(2,1)S(1)}, u32[]{:S(2)}, u32[]{:S(2)}) %collective-permute-start.9) | collective-permute-done | bytes 1048608 | tf_op jit(solution)/shard_map/ppermute | solution.py:124
  143.9 2.0 %add_convert_fusion = bf16[128,4096]{1,0:T(8,128)(2,1)} fusion(bf16[128,4096]{1,0:T(8,128)(2,1)S(1)} %collective-permute-done.9, bf16[704,4096]{1,0:T(8,128)(2,1)S(1)} %bitcast.36, bf16[512,704]{0,1:T(8,128)(2,1)S(1)} %select_convert_fusion), kind=kOutput, calls=%fused_computation.14 | convolution fusion | flops 739770368 | bytes 8044544 | tf_op jit(solution)/shard_map/dot_general | solution.py:121
  145.9 4.3 %collective-permute-start.10 = (bf16[128,4096]{1,0:T(8,128)(2,1)}, bf16[128,4096]{1,0:T(8,128)(2,1)S(1)}, u32[]{:S(2)}, u32[]{:S(2)}) collective-permute-start(bf16[128,4096]{1,0:T(8,128)(2,1)} %add_convert_fusion), channel_id=1, source_target_pairs={{0,3},{1,0},{2,1},{3,2},{4,7},{5,4},{6,5},{7,6},{8,11},{9,8},{10,9... | collective-permute-start | bytes 3145736 | tf_op jit(solution)/shard_map/ppermute | solution.py:124
  150.2 0.5 fusion.29
  150.7 2.4 %fusion.34 = f32[128,4096]{1,0:T(8,128)} fusion(bf16[128,704]{0,1:T(8,128)(2,1)S(1)} %add_convert_fusion.1, bf16[704,4096]{1,0:T(8,128)(2,1)S(1)} %bitcast.36), kind=kOutput, calls=%fused_computation.76 | convolution fusion | flops 738197504 | bytes 8044544 | tf_op jit(solution)/shard_map/dot_general | solution.py:129
  153.1 13.9 %collective-permute-done.11 = bf16[128,4096]{1,0:T(8,128)(2,1)S(1)} collective-permute-done((bf16[128,4096]{1,0:T(8,128)(2,1)S(1)}, bf16[128,4096]{1,0:T(8,128)(2,1)S(1)}, u32[]{:S(2)}, u32[]{:S(2)}) %collective-permute-start.11) | collective-permute-done | bytes 1048608 | tf_op jit(solution)/shard_map/ppermute | solution.py:124
  167.0 1.5 convert_element_type.57
  168.5 4.7 %reduce-scatter.2.cloned.1.call-done = bf16[88,4096]{1,0:T(8,128)(2,1)} async-done(((bf16[704,4096]{1,0:T(8,128)(2,1)}), bf16[88,4096]{1,0:T(8,128)(2,1)}) %reduce-scatter.2.cloned.1.call-update) | async-done | bytes 720912 | tf_op jit(solution)/shard_map/reduce_scatter | solution.py:142
  173.2 2.5 %convert_element_type.59 = f32[88,4096]{1,0:T(8,128)} convert(bf16[88,4096]{1,0:T(8,128)(2,1)} %reduce-scatter.2.cloned.1.call-done) | non-fusion elementwise | flops 360448 | bytes 2162688 | tf_op jit(solution)/shard_map/convert_element_type | solution.py:144
  175.7 8.9 %collective-permute-done.10 = bf16[128,4096]{1,0:T(8,128)(2,1)S(1)} collective-permute-done((bf16[128,4096]{1,0:T(8,128)(2,1)}, bf16[128,4096]{1,0:T(8,128)(2,1)S(1)}, u32[]{:S(2)}, u32[]{:S(2)}) %collective-permute-start.10) | collective-permute-done | bytes 1048608 | tf_op jit(solution)/shard_map/ppermute | solution.py:124
  184.7 1.7 add_add_fusion
  (31 shorter events, 0.2 us)
Async XLA Ops:
  7.2 48.8 %copy-start.5 = (bf16[128,4096]{1,0:T(8,128)(2,1)S(1)}, bf16[128,4096]{1,0:T(8,128)(2,1)}, u32[]{:S(2)}) copy-start(bf16[128,4096]{1,0:T(8,128)(2,1)} %param.4) | copy-start | bytes 3145732
  7.2 48.8 %all-gather.2.cloned.1.call-start = ((), (), s32[]{:S(2)}) async-start(), calls=%async_computation.1 | async-start | bytes 6488064 | tf_op jit(solution)/shard_map/all_gather | solution.py:19
  7.9 165.3 %reduce-scatter.2.cloned.1.call-start = ((), (), s32[]{:S(2)}) async-start(), calls=%async_computation.2 | async-start | bytes 6488064 | tf_op jit(solution)/shard_map/reduce_scatter | solution.py:142
  8.0 33.7 %collective-permute-start.3 = (bf16[128,4096]{1,0:T(8,128)(2,1)}, bf16[128,4096]{1,0:T(8,128)(2,1)}, u32[]{:S(2)}, u32[]{:S(2)}) collective-permute-start(bf16[128,4096]{1,0:T(8,128)(2,1)} %param.4), channel_id=1, source_target_pairs={{0,3},{1,0},{2,1},{3,2},{4,7},{5,4},{6,5},{7,6},{8,11},{9,8},{10,9... | collective-permute-start | bytes 3145736 | tf_op jit(solution)/shard_map/ppermute | solution.py:31
  13.1 22.9 %collective-permute-start = (s32[128,8]{0,1:T(8,128)}, s32[128,8]{0,1:T(8,128)S(1)}, u32[]{:S(2)}, u32[]{:S(2)}) collective-permute-start(s32[128,8]{0,1:T(8,128)} %param.7), channel_id=1, source_target_pairs={{0,3},{1,0},{2,1},{3,2},{4,7},{5,4},{6,5},{7,6},{8,11},{9,8},{10,9... | collective-permute-start | bytes 12296 | tf_op jit(solution)/shard_map/ppermute | solution.py:31
  13.5 28.0 %collective-permute-start.2 = (s32[128,8]{0,1:T(8,128)}, s32[128,8]{0,1:T(8,128)S(1)}, u32[]{:S(2)}, u32[]{:S(2)}) collective-permute-start(s32[128,8]{0,1:T(8,128)} %param.7), channel_id=1, source_target_pairs={{0,1},{1,2},{2,3},{3,0},{4,5},{5,6},{6,7},{7,4},{8,9},{9,10},{10,1... | collective-permute-start | bytes 12296 | tf_op jit(solution)/shard_map/ppermute | solution.py:37
  35.9 5.6 %collective-permute-start.1 = (s32[128,8]{0,1:T(8,128)S(1)}, s32[128,8]{0,1:T(8,128)S(1)}, u32[]{:S(2)}, u32[]{:S(2)}) collective-permute-start(s32[128,8]{0,1:T(8,128)S(1)} %collective-permute-done), channel_id=1, source_target_pairs={{0,3},{1,0},{2,1},{3,2},{4,7},{5,4},{6,5},{7,6},{8,11},{9,8},{10,9... | collective-permute-start | bytes 12296 | tf_op jit(solution)/shard_map/ppermute | solution.py:31
  41.6 28.7 %collective-permute-start.5 = (bf16[128,4096]{1,0:T(8,128)(2,1)}, bf16[128,4096]{1,0:T(8,128)(2,1)}, u32[]{:S(2)}, u32[]{:S(2)}) collective-permute-start(bf16[128,4096]{1,0:T(8,128)(2,1)} %param.4), channel_id=1, source_target_pairs={{0,1},{1,2},{2,3},{3,0},{4,5},{5,6},{6,7},{7,4},{8,9},{9,10},{10,1... | collective-permute-start | bytes 3145736 | tf_op jit(solution)/shard_map/ppermute | solution.py:37
  44.3 45.3 %collective-permute-start.4 = (bf16[128,4096]{1,0:T(8,128)(2,1)}, bf16[128,4096]{1,0:T(8,128)(2,1)}, u32[]{:S(2)}, u32[]{:S(2)}) collective-permute-start(bf16[128,4096]{1,0:T(8,128)(2,1)} %collective-permute-done.3), channel_id=1, source_target_pairs={{0,3},{1,0},{2,1},{3,2},{4,7},{5,4},{6,5},{7,6},{8,11},{9,8},{10,9... | collective-permute-start | bytes 3145736 | tf_op jit(solution)/shard_map/ppermute | solution.py:31
  56.0 4.5 %copy-start = (bf16[704,4096]{1,0:T(8,128)(2,1)S(1)}, bf16[704,4096]{1,0:T(8,128)(2,1)}, u32[]{:S(2)}) copy-start(bf16[704,4096]{1,0:T(8,128)(2,1)} %all-gather.2.cloned.1.call-done) | copy-start | bytes 17301508
  92.6 0.7 copy-start.3
  92.9 1.5 copy-start.7
  93.3 1.1 copy-start.4
  94.5 6.3 %collective-permute-start.8 = (f32[1280]{0:T(1024)S(1)}, f32[1280]{0:T(1024)S(1)}, u32[]{:S(2)}, u32[]{:S(2)}) collective-permute-start(f32[1280]{0:T(1024)S(1)} %pad_maximum_fusion), channel_id=1, source_target_pairs={{0,1},{1,2},{2,3},{3,0},{4,5},{5,6},{6,7},{7,4},{8,9},{9,10},{10,1... | collective-permute-start | bytes 15368 | tf_op jit(solution)/shard_map/ppermute | solution.py:92
  95.2 6.2 %collective-permute-start.7 = (f32[1280]{0:T(1024)S(1)}, f32[1280]{0:T(1024)S(1)}, u32[]{:S(2)}, u32[]{:S(2)}) collective-permute-start(f32[1280]{0:T(1024)S(1)} %pad_maximum_fusion), channel_id=1, source_target_pairs={{0,2},{1,3},{2,0},{3,1},{4,6},{5,7},{6,4},{7,5},{8,10},{9,11},{10,... | collective-permute-start | bytes 15368 | tf_op jit(solution)/shard_map/ppermute | solution.py:92
  99.8 3.7 %collective-permute-start.6 = (f32[1280]{0:T(1024)S(1)}, f32[1280]{0:T(1024)S(1)}, u32[]{:S(2)}, u32[]{:S(2)}) collective-permute-start(f32[1280]{0:T(1024)S(1)} %pad_maximum_fusion), channel_id=1, source_target_pairs={{0,3},{1,0},{2,1},{3,2},{4,7},{5,4},{6,5},{7,6},{8,11},{9,8},{10,9... | collective-permute-start | bytes 15368 | tf_op jit(solution)/shard_map/ppermute | solution.py:92
  103.9 2.6 %copy-start.6 = (bf16[128,4096]{1,0:T(8,128)(2,1)S(1)}, bf16[128,4096]{1,0:T(8,128)(2,1)}, u32[]{:S(2)}) copy-start(bf16[128,4096]{1,0:T(8,128)(2,1)} %param.4) | copy-start | bytes 3145732
  114.1 6.1 %slice-start = ((s8[5767168]{0:T(1024)(128)(4,1)}), s8[1572864]{0:T(1024)(128)(4,1)S(1)}, s32[]{:S(2)}) async-start(s8[5767168]{0:T(1024)(128)(4,1)} %bitcast.35), calls=%async_computation.3 | async-start | bytes 3145728
  114.1 6.1 %slice-start.1 = ((s8[5767168]{0:T(1024)(128)(4,1)}), s8[4194304]{0:T(1024)(128)(4,1)S(1)}, s32[]{:S(2)}) async-start(s8[5767168]{0:T(1024)(128)(4,1)} %bitcast.35), calls=%async_computation.4 | async-start | bytes 8388608
  118.0 25.9 %collective-permute-start.9 = (bf16[128,4096]{1,0:T(8,128)(2,1)S(1)}, bf16[128,4096]{1,0:T(8,128)(2,1)S(1)}, u32[]{:S(2)}, u32[]{:S(2)}) collective-permute-start(bf16[128,4096]{1,0:T(8,128)(2,1)S(1)} %convolution_convert_fusion.2), channel_id=1, source_target_pairs={{0,3},{1,0},{2,1},{3,2},{4,7},{5,4},{6,5},{7,6},{8,11},{9,8},{10,9... | collective-permute-start | bytes 3145736 | tf_op jit(solution)/shard_map/ppermute | solution.py:124
  121.3 45.7 %collective-permute-start.11 = (bf16[128,4096]{1,0:T(8,128)(2,1)S(1)}, bf16[128,4096]{1,0:T(8,128)(2,1)S(1)}, u32[]{:S(2)}, u32[]{:S(2)}) collective-permute-start(bf16[128,4096]{1,0:T(8,128)(2,1)S(1)} %convolution_convert_fusion.1), channel_id=1, source_target_pairs={{0,1},{1,2},{2,3},{3,0},{4,5},{5,6},{6,7},{7,4},{8,9},{9,10},{10,1... | collective-permute-start | bytes 3145736 | tf_op jit(solution)/shard_map/ppermute | solution.py:124
  145.9 38.8 %collective-permute-start.10 = (bf16[128,4096]{1,0:T(8,128)(2,1)}, bf16[128,4096]{1,0:T(8,128)(2,1)S(1)}, u32[]{:S(2)}, u32[]{:S(2)}) collective-permute-start(bf16[128,4096]{1,0:T(8,128)(2,1)} %add_convert_fusion), channel_id=1, source_target_pairs={{0,3},{1,0},{2,1},{3,2},{4,7},{5,4},{6,5},{7,6},{8,11},{9,8},{10,9... | collective-permute-start | bytes 3145736 | tf_op jit(solution)/shard_map/ppermute | solution.py:124
  153.1 31.6 %copy-start.1 = (f32[128,4096]{1,0:T(8,128)S(1)}, f32[128,4096]{1,0:T(8,128)}, u32[]{:S(2)}) copy-start(f32[128,4096]{1,0:T(8,128)} %fusion.34) | copy-start | bytes 6291460
  173.2 11.4 %copy-start.2 = (f32[128,4096]{1,0:T(8,128)S(1)}, f32[128,4096]{1,0:T(8,128)}, u32[]{:S(2)}) copy-start(f32[128,4096]{1,0:T(8,128)} %convert_element_type.57) | copy-start | bytes 6291460
Sparse Core Ops, SparseCore 0:
  9.9 46.0 all-gather.1
  114.3 58.9 reduce-scatter.1
